TPU v7x, 128 devices: a whole 4x4x4 slice. The times are simulated.
128 devices in a mesh: space: 64 (over y, z_hi, x, core), vec: 2 (over z_lo).
Axes of the slice: x: 4, y: 4, z: 4 (z_hi: 2, z_lo: 2; z = z_hi * 2 + z_lo), core: 2. Of those that a mesh axis runs over, the one named last changes fastest.
Arguments:
- potential: float32 [64, 128, 256], P('space'), may hold values from -8.25 to 8.25
- start_basis: float32 [16, 64, 128, 256], P('vec', 'space'), may hold values from -6 to 6
Outputs:
- new_basis: float32 [16, 64, 128, 256], P('vec', 'space')
- rayleigh: float32 [16, 16], replicated
All inputs are finite; a program needn't handle non-finite values.
Results may differ from a plain program's by a relative error of at most 0.0003.
Values sent between devices are 32-bit elements; how exact they have to be, the bound alone decides.
No kernel may reach another device: no remote copies, remote signals or barrier semaphores. Data moves between devices by JAX's collectives and lax.ppermute only.
A program may use at most 64 MiB of HBM per device.

v0:
```python
import jax
import jax.numpy as jnp
from jax import lax
from jax.sharding import PartitionSpec as P

NSWEEP = 3


SIGMA = 0.5
PREC = lax.Precision.HIGHEST


def extended(value, sides, width):
    for axis, dim in sides:
        peers, length = (lax.axis_size(axis), value.shape[dim])
        up = [(i, (i + 1) % peers) for i in range(peers)]
        down = [(j, i) for i, j in up]
        last = lax.slice_in_dim(value, length - width, length, axis=dim)
        first = lax.slice_in_dim(value, 0, width, axis=dim)
        before = lax.ppermute(last, axis, up)
        after = lax.ppermute(first, axis, down)
        value = jnp.concatenate([before, value, after], axis=dim)
    return value


def local_inner(left, right, scale):
    return jnp.einsum("kzyx,jzyx->kj", left, right, precision=PREC) * scale


def combine(coeff, vectors):
    return jnp.einsum("kj,kzyx->jzyx", coeff, vectors, precision=PREC)


def stencil(padded, potential):
    center = padded[:, 1:-1]
    beside = padded[:, 2:] + padded[:, :-2]
    beside = beside + jnp.roll(center, 1, 2) + jnp.roll(center, -1, 2)
    beside = beside + jnp.roll(center, 1, 3) + jnp.roll(center, -1, 3)
    return potential * center - beside


def inverse_factor(gram):
    lower = jnp.linalg.cholesky(gram)
    return jax.scipy.linalg.solve_triangular(
        lower, jnp.eye(gram.shape[0], dtype=jnp.float32), lower=True
    )


def local(potential, start_basis):
    mine = start_basis.shape[0]
    scale = 1.0 / (
        start_basis.shape[1] * start_basis.shape[2] * start_basis.shape[3] * lax.axis_size("space")
    )
    first = lax.axis_index("vec") * mine
    whole = lax.all_gather(start_basis, "vec", axis=0, tiled=True)
    gram = lax.psum(local_inner(whole, whole, scale), "space")
    basis_all = combine(inverse_factor(gram).T, whole)
    basis = lax.dynamic_slice_in_dim(basis_all, first, mine, 0)
    shifted = jnp.where(potential >= SIGMA, potential - SIGMA + 6.0, potential - SIGMA - 6.0)
    padded = extended(basis, (("space", 1),), 1)
    image = stencil(padded, potential)
    panel = lax.psum(local_inner(basis_all, image, scale), "space")
    rayleigh = lax.all_gather(panel, "vec", axis=1, tiled=True)
    panel_mine = lax.dynamic_slice_in_dim(rayleigh, first, mine, 1)
    resid = image - combine(panel_mine, basis_all)
    correction = jnp.zeros_like(basis)
    for sweep in range(NSWEEP):
        coeff = lax.psum(local_inner(basis_all, correction, scale), "space")
        proj = correction - combine(coeff, basis_all)
        padded = extended(proj, (("space", 1),), 1)
        moved = stencil(padded, potential) - SIGMA * proj
        back = lax.psum(local_inner(basis_all, moved, scale), "space")
        update = -resid - (moved - combine(back, basis_all))
        correction = correction + update / shifted
    proj_two = lax.psum(local_inner(basis_all, correction, scale), "space")
    fresh = correction - combine(proj_two, basis_all)
    fresh_all = lax.all_gather(fresh, "vec", axis=0, tiled=True)
    gram_two = lax.psum(local_inner(fresh_all, fresh_all, scale), "space")
    inverse_two = inverse_factor(gram_two)
    rows_mine = lax.dynamic_slice_in_dim(inverse_two, first, mine, 0)
    new_basis = combine(rows_mine.T, fresh_all)
    return (new_basis, rayleigh)


def solution(mesh):
    in_specs = (P("space", None, None), P("vec", "space", None, None))
    out_specs = (P("vec", "space", None, None), P())
    return jax.shard_map(local, mesh=mesh, in_specs=in_specs, out_specs=out_specs, check_vma=False)
```

profile of v0, /device:TPU:0, one launch (start us, length us, event | category | flops | bytes accessed | tf_op | source)
XLA Modules:
  0.0 1709.0 jit_solution(7013803013438455873)
XLA Ops:
  7.2 2.6 copy.4
  9.9 38.5 %all-gather.3.cloned.1.call-done = f32[16,1,128,256]{2,0,3,1:T(8,128)} async-done(((f32[8,1,128,256]{2,0,3,1:T(8,128)}), f32[16,1,128,256]{2,0,3,1:T(8,128)}) %all-gather.3.cloned.1.call-update) | async-done | bytes 2097168 | tf_op jit(solution)/shard_map/all_gather | solution.py:55
  48.4 5.2 fusion.26
  53.6 171.0 %psum.70 = f32[16,16]{0,1:T(8,128)S(1)} all-reduce(f32[16,16]{0,1:T(8,128)S(1)} %fusion.26), channel_id=1, replica_groups=mesh['space'=64,'vec'=2] {'space'}, use_global_device_ids=true, to_apply=%region_0.0 | all-reduce | flops 256 | bytes 2048 | tf_op jit(solution)/shard_map/psum | solution.py:56
  224.7 1.5 cholesky.44
  226.2 0.6 compare_reduce_fusion.1
  226.8 0.6 fusion.68
  227.5 1.2 custom-call.6
  228.9 2.1 copy.7
  231.0 3.4 fusion.107
  234.5 2.6 fusion.36
  237.1 162.5 %psum.72 = f32[16,8]{0,1:T(8,128)S(1)} all-reduce(f32[16,8]{0,1:T(8,128)S(1)} %fusion.36), channel_id=1, replica_groups=mesh['space'=64,'vec'=2] {'space'}, use_global_device_ids=true, to_apply=%region_4.7 | all-reduce | flops 128 | bytes 1024 | tf_op jit(solution)/shard_map/psum | solution.py:68
  399.6 1.1 convolution_subtract_fusion
  401.1 0.5 collective-permute-start.3
  402.1 7.1 collective-permute-start
  409.2 0.4 collective-permute-start.1
  409.6 0.3 fusion.99
  410.4 3.1 collective-permute-done.2
  413.4 7.7 collective-permute-done.3
  421.1 0.8 fusion.46
  421.9 2.7 fusion.35
  424.7 7.7 collective-permute-done.1
  432.4 0.8 fusion.41
  433.2 2.6 fusion.37
  435.8 164.5 %all-reduce = (f32[16,8]{0,1:T(8,128)S(1)}, f32[16,8]{0,1:T(8,128)S(1)}) all-reduce(f32[16,8]{0,1:T(8,128)S(1)} %fusion.37, f32[16,8]{0,1:T(8,128)S(1)} %fusion.35), channel_id=1, replica_groups=mesh['space'=64,'vec'=2] {'space'}, use_global_device_ids=true, to_apply=%region_3.6 | all-reduce | flops 256 | bytes 2048 | tf_op jit(solution)/shard_map/psum | solution.py:62
  600.3 4.4 all_gather.10
  604.7 1.2 fusion.17
  605.9 1.3 fusion.18
  607.3 2.6 fusion.34
  609.9 162.5 %psum.74 = f32[16,8]{0,1:T(8,128)S(1)} all-reduce(f32[16,8]{0,1:T(8,128)S(1)} %fusion.34), channel_id=1, replica_groups=mesh['space'=64,'vec'=2] {'space'}, use_global_device_ids=true, to_apply=%region_6.9 | all-reduce | flops 128 | bytes 1024 | tf_op jit(solution)/shard_map/psum | solution.py:68
  772.4 1.1 fusion.13
  773.6 0.6 collective-permute-start.5
  775.0 11.0 collective-permute-done.4
  785.9 7.9 collective-permute-done.5
  793.8 0.8 fusion.51
  794.6 1.0 copy-done.5
  795.6 2.7 fusion.33
  798.3 162.5 %psum.75 = f32[16,8]{0,1:T(8,128)S(1)} all-reduce(f32[16,8]{0,1:T(8,128)S(1)} %fusion.33), channel_id=1, replica_groups=mesh['space'=64,'vec'=2] {'space'}, use_global_device_ids=true, to_apply=%region_7.10 | all-reduce | flops 128 | bytes 1024 | tf_op jit(solution)/shard_map/psum | solution.py:72
  960.8 3.1 fusion.20
  963.9 2.6 fusion.32
  966.5 162.5 %psum.76 = f32[16,8]{0,1:T(8,128)S(1)} all-reduce(f32[16,8]{0,1:T(8,128)S(1)} %fusion.32), channel_id=1, replica_groups=mesh['space'=64,'vec'=2] {'space'}, use_global_device_ids=true, to_apply=%region_8.11 | all-reduce | flops 128 | bytes 1024 | tf_op jit(solution)/shard_map/psum | solution.py:68
  1129.0 1.1 fusion.10
  1130.2 0.5 collective-permute-start.7
  1131.4 11.1 collective-permute-done.6
  1142.5 7.7 collective-permute-done.7
  1150.3 0.8 fusion.56
  1151.0 1.0 copy-done.4
  1152.0 2.7 fusion.31
  1154.7 162.7 %psum.77 = f32[16,8]{0,1:T(8,128)S(1)} all-reduce(f32[16,8]{0,1:T(8,128)S(1)} %fusion.31), channel_id=1, replica_groups=mesh['space'=64,'vec'=2] {'space'}, use_global_device_ids=true, to_apply=%region_9.12 | all-reduce | flops 128 | bytes 1024 | tf_op jit(solution)/shard_map/psum | solution.py:72
  1317.4 2.9 fusion.22
  1320.3 1.0 copy-done.6
  1321.2 2.7 fusion.30
  1323.9 162.5 %psum.78 = f32[16,8]{0,1:T(8,128)S(1)} all-reduce(f32[16,8]{0,1:T(8,128)S(1)} %fusion.30), channel_id=1, replica_groups=mesh['space'=64,'vec'=2] {'space'}, use_global_device_ids=true, to_apply=%region_10.13 | all-reduce | flops 128 | bytes 1024 | tf_op jit(solution)/shard_map/psum | solution.py:75
  1486.4 3.3 fusion.7
  1489.7 0.7 copy.15
  1490.4 28.6 %all-gather.5.cloned.1.call-done = f32[16,1,128,256]{3,0,2,1:T(8,128)} async-done(((f32[8,1,128,256]{3,0,2,1:T(8,128)}), f32[16,1,128,256]{3,0,2,1:T(8,128)}) %all-gather.5.cloned.1.call-update) | async-done | bytes 2097168 | tf_op jit(solution)/shard_map/all_gather | solution.py:77
  1518.9 5.2 fusion.27
  1524.2 171.0 %psum.79 = f32[16,16]{0,1:T(8,128)S(1)} all-reduce(f32[16,16]{0,1:T(8,128)S(1)} %fusion.27), channel_id=1, replica_groups=mesh['space'=64,'vec'=2] {'space'}, use_global_device_ids=true, to_apply=%region_11.14 | all-reduce | flops 256 | bytes 2048 | tf_op jit(solution)/shard_map/psum | solution.py:78
  1695.2 1.5 cholesky.55
  1696.7 0.6 compare_reduce_fusion
  1697.4 0.6 fusion.69
  1698.0 1.2 custom-call.7
  1699.5 1.1 fusion.4
  1700.6 1.3 copy.14
  (50 shorter events, 3.7 us)
Async XLA Ops:
  7.2 2.7 copy-start.9
  7.2 41.2 %all-gather.3.cloned.1.call-start = ((), (), s32[]{:S(2)}) async-start(), calls=%async_computation | async-start | bytes 3145728 | tf_op jit(solution)/shard_map/all_gather | solution.py:55
  9.8 1509.1 %all-gather.5.cloned.1.call-start = ((), (), s32[]{:S(2)}) async-start(), calls=%async_computation.1 | async-start | bytes 3145728 | tf_op jit(solution)/shard_map/all_gather | solution.py:77
  48.4 180.5 %copy-start.7 = (f32[16,1,128,256]{2,0,3,1:T(8,128)S(1)}, f32[16,1,128,256]{2,0,3,1:T(8,128)}, u32[]{:S(2)}) copy-start(f32[16,1,128,256]{2,0,3,1:T(8,128)} %all-gather.3.cloned.1.call-done) | copy-start | bytes 6291460
  401.0 12.4 collective-permute-start.2
  401.1 20.0 %collective-permute-start.3 = (f32[8,1,128,256]{3,0,2,1:T(8,128)S(1)}, f32[8,1,128,256]{3,0,2,1:T(8,128)S(1)}, u32[]{:S(2)}, u32[]{:S(2)}) collective-permute-start(f32[8,1,128,256]{3,0,2,1:T(8,128)S(1)} %bitcast.203), channel_id=1, source_target_pairs={{0,2},{2,4},{4,6},{6,8},{8,10},{10,12},{12,14},{14,16},{16,18},{18... | collective-permute-start | bytes 3145736 | tf_op jit(solution)/shard_map/ppermute | solution.py:20
  402.1 22.6 %collective-permute-start = (f32[8,1,128,256]{3,0,2,1:T(8,128)S(1)}, f32[8,1,128,256]{3,0,2,1:T(8,128)S(1)}, u32[]{:S(2)}, u32[]{:S(2)}) collective-permute-start(f32[8,1,128,256]{3,0,2,1:T(8,128)S(1)} %dynamic-slice_bitcast_fusion), channel_id=1, source_target_pairs={{2,0},{4,2},{6,4},{8,6},{10,8},{12,10},{14,12},{16,14},{18,16},{20... | collective-permute-start | bytes 3145736 | tf_op jit(solution)/shard_map/ppermute | solution.py:21
  409.2 23.2 %collective-permute-start.1 = (f32[8,1,128,256]{3,0,2,1:T(8,128)S(1)}, f32[8,1,128,256]{3,0,2,1:T(8,128)S(1)}, u32[]{:S(2)}, u32[]{:S(2)}) collective-permute-start(f32[8,1,128,256]{3,0,2,1:T(8,128)S(1)} %dynamic-slice_bitcast_fusion), channel_id=1, source_target_pairs={{0,2},{2,4},{4,6},{6,8},{8,10},{10,12},{12,14},{14,16},{16,18},{18... | collective-permute-start | bytes 3145736 | tf_op jit(solution)/shard_map/ppermute | solution.py:20
  421.9 11.3 copy-start.2
  604.7 1.2 copy-start.3
  605.9 1.4 copy-start.1
  607.2 166.3 %copy-start = (f32[8,1,128,256]{3,0,2,1:T(8,128)}, f32[8,1,128,256]{3,0,2,1:T(8,128)S(1)}, u32[]{:S(2)}) copy-start(f32[8,1,128,256]{3,0,2,1:T(8,128)S(1)} %fusion.18) | copy-start | bytes 3145732
  773.5 12.4 collective-permute-start.4
  773.6 20.2 %collective-permute-start.5 = (f32[8,1,128,256]{3,0,2,1:T(8,128)S(1)}, f32[8,1,128,256]{3,0,2,1:T(8,128)S(1)}, u32[]{:S(2)}, u32[]{:S(2)}) collective-permute-start(f32[8,1,128,256]{3,0,2,1:T(8,128)S(1)} %fusion.13), channel_id=1, source_target_pairs={{0,2},{2,4},{4,6},{6,8},{8,10},{10,12},{12,14},{14,16},{16,18},{18... | collective-permute-start | bytes 3145736 | tf_op jit(solution)/shard_map/ppermute | solution.py:20
  794.6 1.0 copy-start.5
  1130.2 12.4 collective-permute-start.6
  1130.2 20.0 %collective-permute-start.7 = (f32[8,1,128,256]{3,0,2,1:T(8,128)S(1)}, f32[8,1,128,256]{3,0,2,1:T(8,128)S(1)}, u32[]{:S(2)}, u32[]{:S(2)}) collective-permute-start(f32[8,1,128,256]{3,0,2,1:T(8,128)S(1)} %fusion.10), channel_id=1, source_target_pairs={{0,2},{2,4},{4,6},{6,8},{8,10},{10,12},{12,14},{14,16},{16,18},{18... | collective-permute-start | bytes 3145736 | tf_op jit(solution)/shard_map/ppermute | solution.py:20
  1151.0 1.0 copy-start.4
  1320.2 1.0 copy-start.6
  1518.9 180.5 %copy-start.8 = (f32[16,1,128,256]{3,0,2,1:T(8,128)S(1)}, f32[16,1,128,256]{3,0,2,1:T(8,128)}, u32[]{:S(2)}) copy-start(f32[16,1,128,256]{3,0,2,1:T(8,128)} %all-gather.5.cloned.1.call-done) | copy-start | bytes 6291460
Sparse Core Ops, SparseCore 0:
  10.2 38.1 all-gather.2
  1489.8 29.0 all-gather.4
where the time goes:
time: 1720 us; the launch traced here: 1710 us
  blocking collectives  1490 us (87%)
  waiting for transfers between devices  123 us (7%)
  matrix products  51.6 us (3%)
    psum x3, blocking collectives, local(): coeff = lax.psum(local_inner(basis_all, correction, scale), 'space')  488 us
    psum x2, blocking collectives, local(): back = lax.psum(local_inner(basis_all, moved, scale), 'space')  325 us
    psum x1, blocking collectives, local(): gram_two = lax.psum(local_inner(fresh_all, fresh_all, scale), 'space')  171 us
    psum x1, blocking collectives, local(): gram = lax.psum(local_inner(whole, whole, scale), 'space')  171 us
    psum x1, blocking collectives, local(): panel = lax.psum(local_inner(basis_all, image, scale), 'space')  165 us
    psum x1, blocking collectives, local(): proj_two = lax.psum(local_inner(basis_all, correction, scale), 'space')  163 us
    all_gather x1, waiting for transfers between devices, local(): whole = lax.all_gather(start_basis, 'vec', axis=0, tiled=True)  38.5 us
  transfers between devices with their start and end apart: 10, of which 10 were waited for; matrix products, arithmetic and copies ran while one was open for 0% of the time, Pallas kernels for 0%

commit v1 on v0

v1 whole, which is shorter than its diff:
```python
import jax
import jax.numpy as jnp
from jax import lax
from jax.sharding import PartitionSpec as P

NSWEEP = 3


SIGMA = 0.5
PREC = lax.Precision.HIGHEST
AXES = ("space", "vec")


def allsum(x, groups):
    n = lax.axis_size(AXES)
    for group in groups:
        vals = {0: x}
        for m in range(1, 1 << len(group)):
            mask = sum(1 << b for t, b in enumerate(group) if (m >> t) & 1)
            vals[m] = lax.ppermute(x, AXES, [(i, i ^ mask) for i in range(n)])
        for t in range(len(group)):
            vals = {m: vals[m] + vals[m | (1 << t)] for m in vals if not (m >> t) & 1}
        x = vals[0]
    return x


def radix_groups(n):
    bits = n.bit_length() - 1
    order = list(range(bits))
    return [order[i:i + 2] for i in range(0, bits, 2)]


def local_inner(left, right, scale):
    return jnp.einsum("kzyx,jzyx->kj", left, right, precision=PREC) * scale


def combine(coeff, vectors):
    return jnp.einsum("kj,kzyx->jzyx", coeff, vectors, precision=PREC)


def mm(a, b):
    return jnp.matmul(a, b, precision=PREC)


def swap_vec(value):
    return lax.ppermute(value, "vec", [(0, 1), (1, 0)])


def halo(value):
    peers = lax.axis_size("space")
    up = [(i, (i + 1) % peers) for i in range(peers)]
    down = [(j, i) for i, j in up]
    rows = value.shape[2]
    edge = jnp.concatenate([value[:, :, rows - 1:], value[:, :, :1]], axis=2)
    before = lax.ppermute(value, "space", up)
    after = lax.ppermute(value, "space", down)
    ends = swap_vec(edge)
    return before, after, ends


def stencil(value, pieces, potential):
    before, after, ends = pieces
    ext = jnp.concatenate([ends[:, :, :1], value, ends[:, :, 1:]], axis=2)
    beside = before + after
    beside = beside + ext[:, :, :-2] + ext[:, :, 2:]
    beside = beside + jnp.roll(value, 1, 3) + jnp.roll(value, -1, 3)
    return potential * value - beside


def inverse_factor(gram):
    lower = jnp.linalg.cholesky(gram)
    return jax.scipy.linalg.solve_triangular(
        lower, jnp.eye(gram.shape[0], dtype=jnp.float32), lower=True
    )


def local(potential, start_basis):
    mine = start_basis.shape[0]
    rows = start_basis.shape[2] // 2
    v = lax.axis_index("vec")
    groups = radix_groups(lax.axis_size(AXES))
    scale = 1.0 / (
        start_basis.shape[1] * start_basis.shape[2] * start_basis.shape[3] * lax.axis_size("space")
    )
    keep = lax.dynamic_slice_in_dim(start_basis, v * rows, rows, 2)
    give = lax.dynamic_slice_in_dim(start_basis, (1 - v) * rows, rows, 2)
    got = swap_vec(give)
    whole = jnp.where(v == 0, jnp.concatenate([keep, got], 0), jnp.concatenate([got, keep], 0))
    pot = lax.dynamic_slice_in_dim(potential, v * rows, rows, 1)
    shifted = jnp.where(pot >= SIGMA, pot - SIGMA + 6.0, pot - SIGMA - 6.0)

    h_whole = stencil(whole, halo(whole), pot)
    s_d = whole / shifted
    hs_d = h_whole / shifted
    first = allsum(
        jnp.stack(
            [
                local_inner(whole, whole, scale),
                local_inner(whole, h_whole, scale),
                local_inner(whole, s_d, scale),
                local_inner(whole, hs_d, scale),
                local_inner(h_whole, s_d, scale),
                local_inner(h_whole, hs_d, scale),
            ]
        ),
        groups,
    )
    gram, g_sh, u_ss, u_sh, u_hs, u_hh = (first[i] for i in range(6))
    cmat = inverse_factor(gram).T
    ct = cmat.T
    rayleigh = mm(ct, mm(g_sh, cmat))
    b_b = mm(ct, mm(gram, cmat))
    ab_b = mm(ct, mm(g_sh.T, cmat)) - SIGMA * b_b

    basis = combine(cmat, whole)
    image = combine(cmat, h_whole)
    resid = image - combine(rayleigh, basis)
    a_basis = image - SIGMA * basis

    correction = -resid / shifted
    cr = mm(cmat, rayleigh)
    s_rd = mm(u_sh, cmat) - mm(u_ss, cr)
    h_rd = mm(u_hh, cmat) - mm(u_hs, cr)
    coeff = -mm(ct, s_rd)
    ab_c = -mm(ct, h_rd - SIGMA * s_rd)
    back = ab_c - mm(ab_b, coeff)
    proj = correction - combine(coeff, basis)
    moved = stencil(proj, halo(proj), pot) - SIGMA * proj
    correction = correction + (-resid - (moved - combine(back, basis))) / shifted

    for sweep in range(2, NSWEEP):
        pieces = halo(correction)
        red = allsum(
            jnp.stack([local_inner(basis, correction, scale), local_inner(a_basis, correction, scale)]),
            groups,
        )
        coeff = red[0]
        back = red[1] - mm(ab_b, coeff)
        moved = stencil(correction, pieces, pot) - SIGMA * correction - combine(coeff, a_basis)
        correction = correction + (-resid - (moved - combine(back, basis))) / shifted

    proj_two = allsum(local_inner(basis, correction, scale), groups)
    fresh = correction - combine(proj_two, basis)
    gram_two = allsum(local_inner(fresh, fresh, scale), groups)
    new_all = combine(inverse_factor(gram_two).T, fresh)

    own = lax.dynamic_slice_in_dim(new_all, v * mine, mine, 0)
    out = lax.dynamic_slice_in_dim(new_all, (1 - v) * mine, mine, 0)
    back_rows = swap_vec(out)
    new_basis = jnp.where(v == 0, jnp.concatenate([own, back_rows], 2), jnp.concatenate([back_rows, own], 2))
    return (new_basis, rayleigh)


def solution(mesh):
    in_specs = (P("space", None, None), P("vec", "space", None, None))
    out_specs = (P("vec", "space", None, None), P())
    return jax.shard_map(local, mesh=mesh, in_specs=in_specs, out_specs=out_specs, check_vma=False)
```

time: 1720 us -> 230 us (0.13)
  blocking collectives: 1490 us -> 0 us
  starting transfers between devices: 9.5 us -> 70.9 us
  matrix products: 51.6 us -> 28.4 us
    psum x9 -> x0, blocking collectives: 1480 us -> none  [the longest x3 488 us: local(): coeff = lax.psum(local_inner(basis_all, correction, scale), 'space')]
    all_gather x2 -> x0, waiting for transfers between devices: 67 us -> none  [the longest x1 38.5 us: local(): whole = lax.all_gather(start_basis, 'vec', axis=0, tiled=True)]
    ppermute x8 -> x51, starting transfers between devices: 9.42 us -> 70.9 us  [the longest x40 48.5 us: allsum(): vals[m] = lax.ppermute(x, AXES, [(i, i ^ mask) for i in range(n)])]
    ppermute x8 -> x51, waiting for transfers between devices: 56.2 us -> 110 us  [the longest x40 56.5 us: allsum(): vals[m] = lax.ppermute(x, AXES, [(i, i ^ mask) for i in range(n)])]
  transfers between devices with their start and end apart: 10 -> 51, of which waited for: 10 -> 33; matrix products, arithmetic and copies ran while one was open for 0% -> 3% of each run, Pallas kernels for 0% -> 0%
where the time goes in v1:
time: 230 us; the launch traced here: 226 us
  waiting for transfers between devices  110 us (48%)
  starting transfers between devices  70.9 us (31%)
  matrix products  28.4 us (12%)
  other arithmetic  10.1 us (4%)
  local copies, waits for them, and re-layouts  4.86 us (2%)
    ppermute x40, waiting for transfers between devices, allsum(): vals[m] = lax.ppermute(x, AXES, [(i, i ^ mask) for i in range(n)])  56.5 us
    ppermute x40, starting transfers between devices, allsum(): vals[m] = lax.ppermute(x, AXES, [(i, i ^ mask) for i in range(n)])  48.5 us
    ppermute x5, waiting for transfers between devices, swap_vec(): return lax.ppermute(value, 'vec', [(0, 1), (1, 0)])  32.6 us
    ppermute x3, starting transfers between devices, halo(): after = lax.ppermute(value, 'space', down)  15.9 us
    dot_general x10, matrix products, local_inner(): return jnp.einsum('kzyx,jzyx->kj', left, right, precision=PREC) * scale  14.8 us
    ppermute x3, waiting for transfers between devices, halo(): before = lax.ppermute(value, 'space', up)  13.9 us
    dot_general x9, matrix products, combine(): return jnp.einsum('kj,kzyx->jzyx', coeff, vectors, precision=PREC)  10.6 us
    ppermute x3, waiting for transfers between devices, halo(): after = lax.ppermute(value, 'space', down)  7.34 us
  transfers between devices with their start and end apart: 51, of which 33 were waited for; matrix products, arithmetic and copies ran while one was open for 3% of the time, Pallas kernels for 0%

profile of v1, /device:TPU:0, one launch (start us, length us, event | category | flops | bytes accessed | tf_op | source)
XLA Modules:
  0.0 225.8 jit_solution(17604964276403060093)
XLA Ops:
  0.6 1.3 constant_dynamic-slice_fusion.3
  2.3 2.1 collective-permute-start
  5.3 11.0 %collective-permute-done = f32[8,1,64,256]{3,0,2,1:T(8,128)S(1)} collective-permute-done((f32[8,1,64,256]{3,0,2,1:T(8,128)S(1)}, f32[8,1,64,256]{3,0,2,1:T(8,128)S(1)}, u32[]{:S(2)}, u32[]{:S(2)}) %collective-permute-start) | collective-permute-done | bytes 524320 | tf_op jit(solution)/shard_map/ppermute | solution.py:46
  16.4 7.0 %collective-permute-start.2 = (f32[16,1,64,256]{3,0,2,1:T(8,128)S(1)}, f32[16,1,64,256]{3,0,2,1:T(8,128)S(1)}, u32[]{:S(2)}, u32[]{:S(2)}) collective-permute-start(f32[16,1,64,256]{3,0,2,1:T(8,128)S(1)} %maximum_select_fusion.1), channel_id=1, source_target_pairs={{2,0},{4,2},{6,4},{8,6},{10,8},{12,10},{14,12},{16,14},{18,16},{20... | collective-permute-start | bytes 3145736 | tf_op jit(solution)/shard_map/ppermute | solution.py:56
  23.4 1.1 collective-permute-start.3
  25.1 1.5 fusion.38
  26.5 10.6 %collective-permute-done.3 = f32[16,1,2,256]{3,0,2,1:T(8,128)S(1)} collective-permute-done((f32[16,1,2,256]{3,0,2,1:T(8,128)S(1)}, f32[16,1,2,256]{3,0,2,1:T(8,128)S(1)}, u32[]{:S(2)}, u32[]{:S(2)}) %collective-permute-start.3) | collective-permute-done | bytes 32800 | tf_op jit(solution)/shard_map/ppermute | solution.py:46
  37.2 6.2 %collective-permute-done.1 = f32[16,1,64,256]{3,0,2,1:T(8,128)S(1)} collective-permute-done((f32[16,1,64,256]{3,0,2,1:T(8,128)S(1)}, f32[16,1,64,256]{3,0,2,1:T(8,128)S(1)}, u32[]{:S(2)}, u32[]{:S(2)}) %collective-permute-start.1) | collective-permute-done | bytes 1048608 | tf_op jit(solution)/shard_map/ppermute | solution.py:55
  44.1 1.4 fusion.35
  45.5 1.5 fusion.32
  47.0 1.5 fusion.29
  48.6 1.5 fusion.26
  50.0 1.5 fusion.23
  51.5 1.1 collective-permute-start.5
  53.7 1.5 collective-permute-done.6
  55.2 1.6 collective-permute-done.4
  57.0 4.0 %collective-permute-start.7 = (f32[6,16,16]{1,2,0:T(8,128)S(1)}, f32[6,16,16]{1,2,0:T(8,128)S(1)}, u32[]{:S(2)}, u32[]{:S(2)}) collective-permute-start(f32[6,16,16]{1,2,0:T(8,128)S(1)} %add_add_fusion.2), channel_id=1, source_target_pairs={{0,4},{1,5},{2,6},{3,7},{4,0},{5,1},{6,2},{7,3},{8,12},{9,13},{10,... | collective-permute-start | bytes 18440 | tf_op jit(solution)/shard_map/ppermute | solution.py:20
  61.0 1.7 collective-permute-done.9
  64.0 4.9 %collective-permute-start.10 = (f32[6,16,16]{1,2,0:T(8,128)S(1)}, f32[6,16,16]{1,2,0:T(8,128)S(1)}, u32[]{:S(2)}, u32[]{:S(2)}) collective-permute-start(f32[6,16,16]{1,2,0:T(8,128)S(1)} %add_add_fusion.1), channel_id=1, source_target_pairs={{0,16},{1,17},{2,18},{3,19},{4,20},{5,21},{6,22},{7,23},{8,24},{9,... | collective-permute-start | bytes 18440 | tf_op jit(solution)/shard_map/ppermute | solution.py:20
  68.9 1.3 collective-permute-done.12
  71.2 5.5 %collective-permute-done.13 = f32[6,16,16]{1,2,0:T(8,128)S(1)} collective-permute-done((f32[6,16,16]{1,2,0:T(8,128)S(1)}, f32[6,16,16]{1,2,0:T(8,128)S(1)}, u32[]{:S(2)}, u32[]{:S(2)}) %collective-permute-start.13) | collective-permute-done | bytes 6176 | tf_op jit(solution)/shard_map/ppermute | solution.py:20
  76.7 1.5 cholesky.44
  79.5 1.2 custom-call.6
  85.7 1.1 convolution_subtract_fusion
  89.9 1.9 collective-permute-done.16
  91.8 7.3 %collective-permute-done.15 = f32[16,1,64,256]{3,0,2,1:T(8,128)S(1)} collective-permute-done((f32[16,1,64,256]{3,0,2,1:T(8,128)S(1)}, f32[16,1,64,256]{3,0,2,1:T(8,128)S(1)}, u32[]{:S(2)}, u32[]{:S(2)}) %collective-permute-start.15) | collective-permute-done | bytes 1048608 | tf_op jit(solution)/shard_map/ppermute | solution.py:56
  99.2 7.7 %collective-permute-done.14 = f32[16,1,64,256]{3,0,2,1:T(8,128)S(1)} collective-permute-done((f32[16,1,64,256]{3,0,2,1:T(8,128)S(1)}, f32[16,1,64,256]{3,0,2,1:T(8,128)S(1)}, u32[]{:S(2)}, u32[]{:S(2)}) %collective-permute-start.14) | collective-permute-done | bytes 1048608 | tf_op jit(solution)/shard_map/ppermute | solution.py:55
  106.9 1.8 fusion.4
  108.7 1.5 fusion.17
  110.2 1.5 fusion.15
  111.8 1.1 collective-permute-start.22
  114.1 8.9 %collective-permute-start.18 = (f32[16,1,64,256]{3,0,2,1:T(8,128)S(1)}, f32[16,1,64,256]{3,0,2,1:T(8,128)S(1)}, u32[]{:S(2)}, u32[]{:S(2)}) collective-permute-start(f32[16,1,64,256]{3,0,2,1:T(8,128)S(1)} %fusion.4), channel_id=1, source_target_pairs={{2,0},{4,2},{6,4},{8,6},{10,8},{12,10},{14,12},{16,14},{18,16},{20... | collective-permute-start | bytes 3145736 | tf_op jit(solution)/shard_map/ppermute | solution.py:56
  123.6 3.0 %collective-permute-start.24 = (f32[2,16,16]{1,2,0:T(8,128)S(1)}, f32[2,16,16]{1,2,0:T(8,128)S(1)}, u32[]{:S(2)}, u32[]{:S(2)}) collective-permute-start(f32[2,16,16]{1,2,0:T(8,128)S(1)} %add_add_fusion.5), channel_id=1, source_target_pairs={{0,8},{1,9},{2,10},{3,11},{4,12},{5,13},{6,14},{7,15},{8,0},{9,1},... | collective-permute-start | bytes 6152 | tf_op jit(solution)/shard_map/ppermute | solution.py:20
  126.6 1.1 collective-permute-start.23
  128.1 7.8 %collective-permute-done.25 = f32[2,16,16]{1,2,0:T(8,128)S(1)} collective-permute-done((f32[2,16,16]{1,2,0:T(8,128)S(1)}, f32[2,16,16]{1,2,0:T(8,128)S(1)}, u32[]{:S(2)}, u32[]{:S(2)}) %collective-permute-start.25) | collective-permute-done | bytes 2080 | tf_op jit(solution)/shard_map/ppermute | solution.py:20
  135.8 2.1 collective-permute-done.23
  138.9 1.9 collective-permute-start.27
  140.9 2.1 collective-permute-start.26
  143.0 1.1 collective-permute-done.28
  144.1 2.0 collective-permute-done.26
  147.3 4.1 %collective-permute-done.29 = f32[2,16,16]{1,2,0:T(8,128)S(1)} collective-permute-done((f32[2,16,16]{1,2,0:T(8,128)S(1)}, f32[2,16,16]{1,2,0:T(8,128)S(1)}, u32[]{:S(2)}, u32[]{:S(2)}) %collective-permute-start.29) | collective-permute-done | bytes 2080 | tf_op jit(solution)/shard_map/ppermute | solution.py:20
  152.6 1.6 fusion.9
  154.2 1.5 fusion.13
  156.9 1.2 collective-permute-start.30
  158.8 1.7 collective-permute-done.30
  160.5 2.5 %collective-permute-start.35 = (f32[16,16]{0,1:T(8,128)S(1)}, f32[16,16]{0,1:T(8,128)S(1)}, u32[]{:S(2)}, u32[]{:S(2)}) collective-permute-start(f32[16,16]{0,1:T(8,128)S(1)} %add_add_fusion.11), channel_id=1, source_target_pairs={{0,12},{1,13},{2,14},{3,15},{4,8},{5,9},{6,10},{7,11},{8,4},{9,5},... | collective-permute-start | bytes 3080 | tf_op jit(solution)/shard_map/ppermute | solution.py:20
  163.0 1.6 collective-permute-start.33
  165.4 2.7 %collective-permute-done.34 = f32[16,16]{0,1:T(8,128)S(1)} collective-permute-done((f32[16,16]{0,1:T(8,128)S(1)}, f32[16,16]{0,1:T(8,128)S(1)}, u32[]{:S(2)}, u32[]{:S(2)}) %collective-permute-start.34) | collective-permute-done | bytes 1056 | tf_op jit(solution)/shard_map/ppermute | solution.py:20
  168.1 2.2 collective-permute-start.38
  170.4 2.0 collective-permute-start.37
  174.3 3.3 %collective-permute-done.36 = f32[16,16]{0,1:T(8,128)S(1)} collective-permute-done((f32[16,16]{0,1:T(8,128)S(1)}, f32[16,16]{0,1:T(8,128)S(1)}, u32[]{:S(2)}, u32[]{:S(2)}) %collective-permute-start.36) | collective-permute-done | bytes 1056 | tf_op jit(solution)/shard_map/ppermute | solution.py:20
  178.6 4.1 %collective-permute-done.39 = f32[16,16]{0,1:T(8,128)S(1)} collective-permute-done((f32[16,16]{0,1:T(8,128)S(1)}, f32[16,16]{0,1:T(8,128)S(1)}, u32[]{:S(2)}, u32[]{:S(2)}) %collective-permute-start.39) | collective-permute-done | bytes 1056 | tf_op jit(solution)/shard_map/ppermute | solution.py:20
  183.7 1.5 fusion.12
  185.3 2.2 collective-permute-start.40
  190.0 1.3 collective-permute-start.44
  191.4 2.0 collective-permute-start.43
  195.2 2.4 %collective-permute-start.48 = (f32[16,16]{0,1:T(8,128)S(1)}, f32[16,16]{0,1:T(8,128)S(1)}, u32[]{:S(2)}, u32[]{:S(2)}) collective-permute-start(f32[16,16]{0,1:T(8,128)S(1)} %add_add_fusion.7), channel_id=1, source_target_pairs={{0,48},{1,49},{2,50},{3,51},{4,52},{5,53},{6,54},{7,55},{8,56},{9,... | collective-permute-start | bytes 3080 | tf_op jit(solution)/shard_map/ppermute | solution.py:20
  197.6 1.7 collective-permute-start.47
  201.3 3.1 %collective-permute-done.46 = f32[16,16]{0,1:T(8,128)S(1)} collective-permute-done((f32[16,16]{0,1:T(8,128)S(1)}, f32[16,16]{0,1:T(8,128)S(1)}, u32[]{:S(2)}, u32[]{:S(2)}) %collective-permute-start.46) | collective-permute-done | bytes 1056 | tf_op jit(solution)/shard_map/ppermute | solution.py:20
  204.5 1.1 collective-permute-start.49
  205.6 4.0 %collective-permute-done.49 = f32[16,16]{0,1:T(8,128)S(1)} collective-permute-done((f32[16,16]{0,1:T(8,128)S(1)}, f32[16,16]{0,1:T(8,128)S(1)}, u32[]{:S(2)}, u32[]{:S(2)}) %collective-permute-start.49) | collective-permute-done | bytes 1056 | tf_op jit(solution)/shard_map/ppermute | solution.py:20
  209.7 1.5 cholesky.55
  212.5 1.2 custom-call.7
  215.5 9.0 %collective-permute-done.50 = f32[8,1,64,256]{3,2,0,1:T(8,128)S(1)} collective-permute-done((f32[8,1,64,256]{3,2,0,1:T(8,128)S(1)}, f32[8,1,64,256]{3,2,0,1:T(8,128)S(1)}, u32[]{:S(2)}, u32[]{:S(2)}) %collective-permute-start.50) | collective-permute-done | bytes 524320 | tf_op jit(solution)/shard_map/ppermute | solution.py:46
  (134 shorter events, 38.5 us)
Async XLA Ops:
  2.3 14.0 %collective-permute-start = (f32[8,1,64,256]{3,0,2,1:T(8,128)S(1)}, f32[8,1,64,256]{3,0,2,1:T(8,128)S(1)}, u32[]{:S(2)}, u32[]{:S(2)}) collective-permute-start(f32[8,1,64,256]{3,0,2,1:T(8,128)S(1)} %copy.64), channel_id=1, source_target_pairs={{0,1},{1,0},{2,3},{3,2},{4,5},{5,4},{6,7},{7,6},{8,9},{9,8},{10,11... | collective-permute-start | bytes 1572872 | tf_op jit(solution)/shard_map/ppermute | solution.py:46
  4.4 0.9 copy-start.1
  16.4 20.8 %collective-permute-start.2 = (f32[16,1,64,256]{3,0,2,1:T(8,128)S(1)}, f32[16,1,64,256]{3,0,2,1:T(8,128)S(1)}, u32[]{:S(2)}, u32[]{:S(2)}) collective-permute-start(f32[16,1,64,256]{3,0,2,1:T(8,128)S(1)} %maximum_select_fusion.1), channel_id=1, source_target_pairs={{2,0},{4,2},{6,4},{8,6},{10,8},{12,10},{14,12},{16,14},{18,16},{20... | collective-permute-start | bytes 3145736 | tf_op jit(solution)/shard_map/ppermute | solution.py:56
  23.4 19.9 %collective-permute-start.1 = (f32[16,1,64,256]{3,0,2,1:T(8,128)S(1)}, f32[16,1,64,256]{3,0,2,1:T(8,128)S(1)}, u32[]{:S(2)}, u32[]{:S(2)}) collective-permute-start(f32[16,1,64,256]{3,0,2,1:T(8,128)S(1)} %maximum_select_fusion.1), channel_id=1, source_target_pairs={{0,2},{2,4},{4,6},{6,8},{8,10},{10,12},{12,14},{14,16},{16,18},{18... | collective-permute-start | bytes 3145736 | tf_op jit(solution)/shard_map/ppermute | solution.py:55
  23.4 13.8 %collective-permute-start.3 = (f32[16,1,2,256]{3,0,2,1:T(8,128)S(1)}, f32[16,1,2,256]{3,0,2,1:T(8,128)S(1)}, u32[]{:S(2)}, u32[]{:S(2)}) collective-permute-start(f32[16,1,2,256]{3,0,2,1:T(8,128)S(1)} %pad_maximum_fusion.6), channel_id=1, source_target_pairs={{0,1},{1,0},{2,3},{3,2},{4,5},{5,4},{6,7},{7,6},{8,9},{9,8},{10,11... | collective-permute-start | bytes 98312 | tf_op jit(solution)/shard_map/ppermute | solution.py:46
  51.5 3.6 %collective-permute-start.6 = (f32[6,16,16]{1,2,0:T(8,128)S(1)}, f32[6,16,16]{1,2,0:T(8,128)S(1)}, u32[]{:S(2)}, u32[]{:S(2)}) collective-permute-start(f32[6,16,16]{1,2,0:T(8,128)S(1)} %fusion.23), channel_id=1, source_target_pairs={{0,3},{1,2},{2,1},{3,0},{4,7},{5,6},{6,5},{7,4},{8,11},{9,10},{10,... | collective-permute-start | bytes 18440 | tf_op jit(solution)/shard_map/ppermute | solution.py:20
  51.5 3.6 %collective-permute-start.5 = (f32[6,16,16]{1,2,0:T(8,128)S(1)}, f32[6,16,16]{1,2,0:T(8,128)S(1)}, u32[]{:S(2)}, u32[]{:S(2)}) collective-permute-start(f32[6,16,16]{1,2,0:T(8,128)S(1)} %fusion.23), channel_id=1, source_target_pairs={{0,2},{1,3},{2,0},{3,1},{4,6},{5,7},{6,4},{7,5},{8,10},{9,11},{10,... | collective-permute-start | bytes 18440 | tf_op jit(solution)/shard_map/ppermute | solution.py:20
  52.7 4.1 %collective-permute-start.4 = (f32[6,16,16]{1,2,0:T(8,128)S(1)}, f32[6,16,16]{1,2,0:T(8,128)S(1)}, u32[]{:S(2)}, u32[]{:S(2)}) collective-permute-start(f32[6,16,16]{1,2,0:T(8,128)S(1)} %fusion.23), channel_id=1, source_target_pairs={{0,1},{1,0},{2,3},{3,2},{4,5},{5,4},{6,7},{7,6},{8,9},{9,8},{10,11... | collective-permute-start | bytes 18440 | tf_op jit(solution)/shard_map/ppermute | solution.py:20
  56.8 5.9 %collective-permute-start.9 = (f32[6,16,16]{1,2,0:T(8,128)S(1)}, f32[6,16,16]{1,2,0:T(8,128)S(1)}, u32[]{:S(2)}, u32[]{:S(2)}) collective-permute-start(f32[6,16,16]{1,2,0:T(8,128)S(1)} %add_add_fusion.2), channel_id=1, source_target_pairs={{0,12},{1,13},{2,14},{3,15},{4,8},{5,9},{6,10},{7,11},{8,4},{9,5},... | collective-permute-start | bytes 18440 | tf_op jit(solution)/shard_map/ppermute | solution.py:20
  56.9 5.8 %collective-permute-start.8 = (f32[6,16,16]{1,2,0:T(8,128)S(1)}, f32[6,16,16]{1,2,0:T(8,128)S(1)}, u32[]{:S(2)}, u32[]{:S(2)}) collective-permute-start(f32[6,16,16]{1,2,0:T(8,128)S(1)} %add_add_fusion.2), channel_id=1, source_target_pairs={{0,8},{1,9},{2,10},{3,11},{4,12},{5,13},{6,14},{7,15},{8,0},{9,1},... | collective-permute-start | bytes 18440 | tf_op jit(solution)/shard_map/ppermute | solution.py:20
  57.0 6.6 %collective-permute-start.7 = (f32[6,16,16]{1,2,0:T(8,128)S(1)}, f32[6,16,16]{1,2,0:T(8,128)S(1)}, u32[]{:S(2)}, u32[]{:S(2)}) collective-permute-start(f32[6,16,16]{1,2,0:T(8,128)S(1)} %add_add_fusion.2), channel_id=1, source_target_pairs={{0,4},{1,5},{2,6},{3,7},{4,0},{5,1},{6,2},{7,3},{8,12},{9,13},{10,... | collective-permute-start | bytes 18440 | tf_op jit(solution)/shard_map/ppermute | solution.py:20
  63.6 6.6 %collective-permute-start.12 = (f32[6,16,16]{1,2,0:T(8,128)S(1)}, f32[6,16,16]{1,2,0:T(8,128)S(1)}, u32[]{:S(2)}, u32[]{:S(2)}) collective-permute-start(f32[6,16,16]{1,2,0:T(8,128)S(1)} %add_add_fusion.1), channel_id=1, source_target_pairs={{0,48},{1,49},{2,50},{3,51},{4,52},{5,53},{6,54},{7,55},{8,56},{9,... | collective-permute-start | bytes 18440 | tf_op jit(solution)/shard_map/ppermute | solution.py:20
  63.7 6.5 %collective-permute-start.11 = (f32[6,16,16]{1,2,0:T(8,128)S(1)}, f32[6,16,16]{1,2,0:T(8,128)S(1)}, u32[]{:S(2)}, u32[]{:S(2)}) collective-permute-start(f32[6,16,16]{1,2,0:T(8,128)S(1)} %add_add_fusion.1), channel_id=1, source_target_pairs={{0,32},{1,33},{2,34},{3,35},{4,36},{5,37},{6,38},{7,39},{8,40},{9,... | collective-permute-start | bytes 18440 | tf_op jit(solution)/shard_map/ppermute | solution.py:20
  64.0 6.9 %collective-permute-start.10 = (f32[6,16,16]{1,2,0:T(8,128)S(1)}, f32[6,16,16]{1,2,0:T(8,128)S(1)}, u32[]{:S(2)}, u32[]{:S(2)}) collective-permute-start(f32[6,16,16]{1,2,0:T(8,128)S(1)} %add_add_fusion.1), channel_id=1, source_target_pairs={{0,16},{1,17},{2,18},{3,19},{4,20},{5,21},{6,22},{7,23},{8,24},{9,... | collective-permute-start | bytes 18440 | tf_op jit(solution)/shard_map/ppermute | solution.py:20
  71.0 5.7 %collective-permute-start.13 = (f32[6,16,16]{1,2,0:T(8,128)S(1)}, f32[6,16,16]{1,2,0:T(8,128)S(1)}, u32[]{:S(2)}, u32[]{:S(2)}) collective-permute-start(f32[6,16,16]{1,2,0:T(8,128)S(1)} %add_add_fusion), channel_id=1, source_target_pairs={{0,64},{1,65},{2,66},{3,67},{4,68},{5,69},{6,70},{7,71},{8,72},{9,... | collective-permute-start | bytes 18440 | tf_op jit(solution)/shard_map/ppermute | solution.py:20
  83.6 1.0 copy-start
  86.8 12.4 %collective-permute-start.15 = (f32[16,1,64,256]{3,0,2,1:T(8,128)S(1)}, f32[16,1,64,256]{3,0,2,1:T(8,128)S(1)}, u32[]{:S(2)}, u32[]{:S(2)}) collective-permute-start(f32[16,1,64,256]{3,0,2,1:T(8,128)S(1)} %bitcast.282), channel_id=1, source_target_pairs={{2,0},{4,2},{6,4},{8,6},{10,8},{12,10},{14,12},{16,14},{18,16},{20... | collective-permute-start | bytes 3145736 | tf_op jit(solution)/shard_map/ppermute | solution.py:56
  86.9 20.0 %collective-permute-start.14 = (f32[16,1,64,256]{3,0,2,1:T(8,128)S(1)}, f32[16,1,64,256]{3,0,2,1:T(8,128)S(1)}, u32[]{:S(2)}, u32[]{:S(2)}) collective-permute-start(f32[16,1,64,256]{3,0,2,1:T(8,128)S(1)} %bitcast.283), channel_id=1, source_target_pairs={{0,2},{2,4},{4,6},{6,8},{8,10},{10,12},{12,14},{14,16},{16,18},{18... | collective-permute-start | bytes 3145736 | tf_op jit(solution)/shard_map/ppermute | solution.py:55
  87.7 4.1 %collective-permute-start.16 = (f32[16,1,2,256]{3,0,2,1:T(8,128)S(1)}, f32[16,1,2,256]{3,0,2,1:T(8,128)S(1)}, u32[]{:S(2)}, u32[]{:S(2)}) collective-permute-start(f32[16,1,2,256]{3,0,2,1:T(8,128)S(1)} %pad_maximum_fusion.7), channel_id=1, source_target_pairs={{0,1},{1,0},{2,3},{3,2},{4,5},{5,4},{6,7},{7,6},{8,9},{9,8},{10,11... | collective-permute-start | bytes 98312 | tf_op jit(solution)/shard_map/ppermute | solution.py:46
  111.7 11.8 %collective-permute-start.21 = (f32[2,16,16]{1,2,0:T(8,128)S(1)}, f32[2,16,16]{1,2,0:T(8,128)S(1)}, u32[]{:S(2)}, u32[]{:S(2)}) collective-permute-start(f32[2,16,16]{1,2,0:T(8,128)S(1)} %pad_maximum_fusion.9), channel_id=1, source_target_pairs={{0,2},{1,3},{2,0},{3,1},{4,6},{5,7},{6,4},{7,5},{8,10},{9,11},{10,... | collective-permute-start | bytes 6152 | tf_op jit(solution)/shard_map/ppermute | solution.py:20
  111.8 11.7 %collective-permute-start.22 = (f32[2,16,16]{1,2,0:T(8,128)S(1)}, f32[2,16,16]{1,2,0:T(8,128)S(1)}, u32[]{:S(2)}, u32[]{:S(2)}) collective-permute-start(f32[2,16,16]{1,2,0:T(8,128)S(1)} %pad_maximum_fusion.9), channel_id=1, source_target_pairs={{0,3},{1,2},{2,1},{3,0},{4,7},{5,6},{6,5},{7,4},{8,11},{9,10},{10,... | collective-permute-start | bytes 6152 | tf_op jit(solution)/shard_map/ppermute | solution.py:20
  112.9 10.6 %collective-permute-start.20 = (f32[2,16,16]{1,2,0:T(8,128)S(1)}, f32[2,16,16]{1,2,0:T(8,128)S(1)}, u32[]{:S(2)}, u32[]{:S(2)}) collective-permute-start(f32[2,16,16]{1,2,0:T(8,128)S(1)} %pad_maximum_fusion.9), channel_id=1, source_target_pairs={{0,1},{1,0},{2,3},{3,2},{4,5},{5,4},{6,7},{7,6},{8,9},{9,8},{10,11... | collective-permute-start | bytes 6152 | tf_op jit(solution)/shard_map/ppermute | solution.py:20
  114.1 38.5 %collective-permute-start.18 = (f32[16,1,64,256]{3,0,2,1:T(8,128)S(1)}, f32[16,1,64,256]{3,0,2,1:T(8,128)S(1)}, u32[]{:S(2)}, u32[]{:S(2)}) collective-permute-start(f32[16,1,64,256]{3,0,2,1:T(8,128)S(1)} %fusion.4), channel_id=1, source_target_pairs={{2,0},{4,2},{6,4},{8,6},{10,8},{12,10},{14,12},{16,14},{18,16},{20... | collective-permute-start | bytes 3145736 | tf_op jit(solution)/shard_map/ppermute | solution.py:56
  123.0 29.6 %collective-permute-start.17 = (f32[16,1,64,256]{3,0,2,1:T(8,128)S(1)}, f32[16,1,64,256]{3,0,2,1:T(8,128)S(1)}, u32[]{:S(2)}, u32[]{:S(2)}) collective-permute-start(f32[16,1,64,256]{3,0,2,1:T(8,128)S(1)} %fusion.4), channel_id=1, source_target_pairs={{0,2},{2,4},{4,6},{6,8},{8,10},{10,12},{12,14},{14,16},{16,18},{18... | collective-permute-start | bytes 3145736 | tf_op jit(solution)/shard_map/ppermute | solution.py:55
  123.5 12.3 %collective-permute-start.25 = (f32[2,16,16]{1,2,0:T(8,128)S(1)}, f32[2,16,16]{1,2,0:T(8,128)S(1)}, u32[]{:S(2)}, u32[]{:S(2)}) collective-permute-start(f32[2,16,16]{1,2,0:T(8,128)S(1)} %add_add_fusion.5), channel_id=1, source_target_pairs={{0,12},{1,13},{2,14},{3,15},{4,8},{5,9},{6,10},{7,11},{8,4},{9,5},... | collective-permute-start | bytes 6152 | tf_op jit(solution)/shard_map/ppermute | solution.py:20
  123.6 12.2 %collective-permute-start.24 = (f32[2,16,16]{1,2,0:T(8,128)S(1)}, f32[2,16,16]{1,2,0:T(8,128)S(1)}, u32[]{:S(2)}, u32[]{:S(2)}) collective-permute-start(f32[2,16,16]{1,2,0:T(8,128)S(1)} %add_add_fusion.5), channel_id=1, source_target_pairs={{0,8},{1,9},{2,10},{3,11},{4,12},{5,13},{6,14},{7,15},{8,0},{9,1},... | collective-permute-start | bytes 6152 | tf_op jit(solution)/shard_map/ppermute | solution.py:20
  126.6 11.3 %collective-permute-start.23 = (f32[2,16,16]{1,2,0:T(8,128)S(1)}, f32[2,16,16]{1,2,0:T(8,128)S(1)}, u32[]{:S(2)}, u32[]{:S(2)}) collective-permute-start(f32[2,16,16]{1,2,0:T(8,128)S(1)} %add_add_fusion.5), channel_id=1, source_target_pairs={{0,4},{1,5},{2,6},{3,7},{4,0},{5,1},{6,2},{7,3},{8,12},{9,13},{10,... | collective-permute-start | bytes 6152 | tf_op jit(solution)/shard_map/ppermute | solution.py:20
  137.9 6.2 %collective-permute-start.28 = (f32[2,16,16]{1,2,0:T(8,128)S(1)}, f32[2,16,16]{1,2,0:T(8,128)S(1)}, u32[]{:S(2)}, u32[]{:S(2)}) collective-permute-start(f32[2,16,16]{1,2,0:T(8,128)S(1)} %add_add_fusion.4), channel_id=1, source_target_pairs={{0,48},{1,49},{2,50},{3,51},{4,52},{5,53},{6,54},{7,55},{8,56},{9,... | collective-permute-start | bytes 6152 | tf_op jit(solution)/shard_map/ppermute | solution.py:20
  138.9 5.2 %collective-permute-start.27 = (f32[2,16,16]{1,2,0:T(8,128)S(1)}, f32[2,16,16]{1,2,0:T(8,128)S(1)}, u32[]{:S(2)}, u32[]{:S(2)}) collective-permute-start(f32[2,16,16]{1,2,0:T(8,128)S(1)} %add_add_fusion.4), channel_id=1, source_target_pairs={{0,32},{1,33},{2,34},{3,35},{4,36},{5,37},{6,38},{7,39},{8,40},{9,... | collective-permute-start | bytes 6152 | tf_op jit(solution)/shard_map/ppermute | solution.py:20
  140.9 5.2 %collective-permute-start.26 = (f32[2,16,16]{1,2,0:T(8,128)S(1)}, f32[2,16,16]{1,2,0:T(8,128)S(1)}, u32[]{:S(2)}, u32[]{:S(2)}) collective-permute-start(f32[2,16,16]{1,2,0:T(8,128)S(1)} %add_add_fusion.4), channel_id=1, source_target_pairs={{0,16},{1,17},{2,18},{3,19},{4,20},{5,21},{6,22},{7,23},{8,24},{9,... | collective-permute-start | bytes 6152 | tf_op jit(solution)/shard_map/ppermute | solution.py:20
  146.1 5.3 %collective-permute-start.29 = (f32[2,16,16]{1,2,0:T(8,128)S(1)}, f32[2,16,16]{1,2,0:T(8,128)S(1)}, u32[]{:S(2)}, u32[]{:S(2)}) collective-permute-start(f32[2,16,16]{1,2,0:T(8,128)S(1)} %add_add_fusion.3), channel_id=1, source_target_pairs={{0,64},{1,65},{2,66},{3,67},{4,68},{5,69},{6,70},{7,71},{8,72},{9,... | collective-permute-start | bytes 6152 | tf_op jit(solution)/shard_map/ppermute | solution.py:20
  146.2 6.4 %collective-permute-start.19 = (f32[16,1,2,256]{3,0,2,1:T(8,128)S(1)}, f32[16,1,2,256]{3,0,2,1:T(8,128)S(1)}, u32[]{:S(2)}, u32[]{:S(2)}) collective-permute-start(f32[16,1,2,256]{3,0,2,1:T(8,128)S(1)} %pad_maximum_fusion.8), channel_id=1, source_target_pairs={{0,1},{1,0},{2,3},{3,2},{4,5},{5,4},{6,7},{7,6},{8,9},{9,8},{10,11... | collective-permute-start | bytes 98312 | tf_op jit(solution)/shard_map/ppermute | solution.py:46
  155.7 3.1 %collective-permute-start.32 = (f32[16,16]{0,1:T(8,128)S(1)}, f32[16,16]{0,1:T(8,128)S(1)}, u32[]{:S(2)}, u32[]{:S(2)}) collective-permute-start(f32[16,16]{0,1:T(8,128)S(1)} %fusion.13), channel_id=1, source_target_pairs={{0,3},{1,2},{2,1},{3,0},{4,7},{5,6},{6,5},{7,4},{8,11},{9,10},{10,... | collective-permute-start | bytes 3080 | tf_op jit(solution)/shard_map/ppermute | solution.py:20
  156.3 2.4 %collective-permute-start.31 = (f32[16,16]{0,1:T(8,128)S(1)}, f32[16,16]{0,1:T(8,128)S(1)}, u32[]{:S(2)}, u32[]{:S(2)}) collective-permute-start(f32[16,16]{0,1:T(8,128)S(1)} %fusion.13), channel_id=1, source_target_pairs={{0,2},{1,3},{2,0},{3,1},{4,6},{5,7},{6,4},{7,5},{8,10},{9,11},{10,... | collective-permute-start | bytes 3080 | tf_op jit(solution)/shard_map/ppermute | solution.py:20
  156.9 3.7 %collective-permute-start.30 = (f32[16,16]{0,1:T(8,128)S(1)}, f32[16,16]{0,1:T(8,128)S(1)}, u32[]{:S(2)}, u32[]{:S(2)}) collective-permute-start(f32[16,16]{0,1:T(8,128)S(1)} %fusion.13), channel_id=1, source_target_pairs={{0,1},{1,0},{2,3},{3,2},{4,5},{5,4},{6,7},{7,6},{8,9},{9,8},{10,11... | collective-permute-start | bytes 3080 | tf_op jit(solution)/shard_map/ppermute | solution.py:20
  160.5 4.9 %collective-permute-start.35 = (f32[16,16]{0,1:T(8,128)S(1)}, f32[16,16]{0,1:T(8,128)S(1)}, u32[]{:S(2)}, u32[]{:S(2)}) collective-permute-start(f32[16,16]{0,1:T(8,128)S(1)} %add_add_fusion.11), channel_id=1, source_target_pairs={{0,12},{1,13},{2,14},{3,15},{4,8},{5,9},{6,10},{7,11},{8,4},{9,5},... | collective-permute-start | bytes 3080 | tf_op jit(solution)/shard_map/ppermute | solution.py:20
  163.0 5.2 %collective-permute-start.34 = (f32[16,16]{0,1:T(8,128)S(1)}, f32[16,16]{0,1:T(8,128)S(1)}, u32[]{:S(2)}, u32[]{:S(2)}) collective-permute-start(f32[16,16]{0,1:T(8,128)S(1)} %add_add_fusion.11), channel_id=1, source_target_pairs={{0,8},{1,9},{2,10},{3,11},{4,12},{5,13},{6,14},{7,15},{8,0},{9,1},... | collective-permute-start | bytes 3080 | tf_op jit(solution)/shard_map/ppermute | solution.py:20
  163.0 5.2 %collective-permute-start.33 = (f32[16,16]{0,1:T(8,128)S(1)}, f32[16,16]{0,1:T(8,128)S(1)}, u32[]{:S(2)}, u32[]{:S(2)}) collective-permute-start(f32[16,16]{0,1:T(8,128)S(1)} %add_add_fusion.11), channel_id=1, source_target_pairs={{0,4},{1,5},{2,6},{3,7},{4,0},{5,1},{6,2},{7,3},{8,12},{9,13},{10,... | collective-permute-start | bytes 3080 | tf_op jit(solution)/shard_map/ppermute | solution.py:20
  168.1 6.1 %collective-permute-start.38 = (f32[16,16]{0,1:T(8,128)S(1)}, f32[16,16]{0,1:T(8,128)S(1)}, u32[]{:S(2)}, u32[]{:S(2)}) collective-permute-start(f32[16,16]{0,1:T(8,128)S(1)} %add_add_fusion.10), channel_id=1, source_target_pairs={{0,48},{1,49},{2,50},{3,51},{4,52},{5,53},{6,54},{7,55},{8,56},{9,... | collective-permute-start | bytes 3080 | tf_op jit(solution)/shard_map/ppermute | solution.py:20
  170.4 3.9 %collective-permute-start.37 = (f32[16,16]{0,1:T(8,128)S(1)}, f32[16,16]{0,1:T(8,128)S(1)}, u32[]{:S(2)}, u32[]{:S(2)}) collective-permute-start(f32[16,16]{0,1:T(8,128)S(1)} %add_add_fusion.10), channel_id=1, source_target_pairs={{0,32},{1,33},{2,34},{3,35},{4,36},{5,37},{6,38},{7,39},{8,40},{9,... | collective-permute-start | bytes 3080 | tf_op jit(solution)/shard_map/ppermute | solution.py:20
  172.4 5.2 %collective-permute-start.36 = (f32[16,16]{0,1:T(8,128)S(1)}, f32[16,16]{0,1:T(8,128)S(1)}, u32[]{:S(2)}, u32[]{:S(2)}) collective-permute-start(f32[16,16]{0,1:T(8,128)S(1)} %add_add_fusion.10), channel_id=1, source_target_pairs={{0,16},{1,17},{2,18},{3,19},{4,20},{5,21},{6,22},{7,23},{8,24},{9,... | collective-permute-start | bytes 3080 | tf_op jit(solution)/shard_map/ppermute | solution.py:20
  177.6 5.2 %collective-permute-start.39 = (f32[16,16]{0,1:T(8,128)S(1)}, f32[16,16]{0,1:T(8,128)S(1)}, u32[]{:S(2)}, u32[]{:S(2)}) collective-permute-start(f32[16,16]{0,1:T(8,128)S(1)} %add_add_fusion.9), channel_id=1, source_target_pairs={{0,64},{1,65},{2,66},{3,67},{4,68},{5,69},{6,70},{7,71},{8,72},{9,... | collective-permute-start | bytes 3080 | tf_op jit(solution)/shard_map/ppermute | solution.py:20
  185.2 3.1 %collective-permute-start.42 = (f32[16,16]{0,1:T(8,128)S(1)}, f32[16,16]{0,1:T(8,128)S(1)}, u32[]{:S(2)}, u32[]{:S(2)}) collective-permute-start(f32[16,16]{0,1:T(8,128)S(1)} %fusion.12), channel_id=1, source_target_pairs={{0,3},{1,2},{2,1},{3,0},{4,7},{5,6},{6,5},{7,4},{8,11},{9,10},{10,... | collective-permute-start | bytes 3080 | tf_op jit(solution)/shard_map/ppermute | solution.py:20
  185.2 3.1 %collective-permute-start.41 = (f32[16,16]{0,1:T(8,128)S(1)}, f32[16,16]{0,1:T(8,128)S(1)}, u32[]{:S(2)}, u32[]{:S(2)}) collective-permute-start(f32[16,16]{0,1:T(8,128)S(1)} %fusion.12), channel_id=1, source_target_pairs={{0,2},{1,3},{2,0},{3,1},{4,6},{5,7},{6,4},{7,5},{8,10},{9,11},{10,... | collective-permute-start | bytes 3080 | tf_op jit(solution)/shard_map/ppermute | solution.py:20
  185.3 3.9 %collective-permute-start.40 = (f32[16,16]{0,1:T(8,128)S(1)}, f32[16,16]{0,1:T(8,128)S(1)}, u32[]{:S(2)}, u32[]{:S(2)}) collective-permute-start(f32[16,16]{0,1:T(8,128)S(1)} %fusion.12), channel_id=1, source_target_pairs={{0,1},{1,0},{2,3},{3,2},{4,5},{5,4},{6,7},{7,6},{8,9},{9,8},{10,11... | collective-permute-start | bytes 3080 | tf_op jit(solution)/shard_map/ppermute | solution.py:20
  189.3 4.9 %collective-permute-start.45 = (f32[16,16]{0,1:T(8,128)S(1)}, f32[16,16]{0,1:T(8,128)S(1)}, u32[]{:S(2)}, u32[]{:S(2)}) collective-permute-start(f32[16,16]{0,1:T(8,128)S(1)} %add_add_fusion.8), channel_id=1, source_target_pairs={{0,12},{1,13},{2,14},{3,15},{4,8},{5,9},{6,10},{7,11},{8,4},{9,5},... | collective-permute-start | bytes 3080 | tf_op jit(solution)/shard_map/ppermute | solution.py:20
  190.0 5.2 %collective-permute-start.44 = (f32[16,16]{0,1:T(8,128)S(1)}, f32[16,16]{0,1:T(8,128)S(1)}, u32[]{:S(2)}, u32[]{:S(2)}) collective-permute-start(f32[16,16]{0,1:T(8,128)S(1)} %add_add_fusion.8), channel_id=1, source_target_pairs={{0,8},{1,9},{2,10},{3,11},{4,12},{5,13},{6,14},{7,15},{8,0},{9,1},... | collective-permute-start | bytes 3080 | tf_op jit(solution)/shard_map/ppermute | solution.py:20
  191.4 3.8 %collective-permute-start.43 = (f32[16,16]{0,1:T(8,128)S(1)}, f32[16,16]{0,1:T(8,128)S(1)}, u32[]{:S(2)}, u32[]{:S(2)}) collective-permute-start(f32[16,16]{0,1:T(8,128)S(1)} %add_add_fusion.8), channel_id=1, source_target_pairs={{0,4},{1,5},{2,6},{3,7},{4,0},{5,1},{6,2},{7,3},{8,12},{9,13},{10,... | collective-permute-start | bytes 3080 | tf_op jit(solution)/shard_map/ppermute | solution.py:20
  195.2 6.1 %collective-permute-start.48 = (f32[16,16]{0,1:T(8,128)S(1)}, f32[16,16]{0,1:T(8,128)S(1)}, u32[]{:S(2)}, u32[]{:S(2)}) collective-permute-start(f32[16,16]{0,1:T(8,128)S(1)} %add_add_fusion.7), channel_id=1, source_target_pairs={{0,48},{1,49},{2,50},{3,51},{4,52},{5,53},{6,54},{7,55},{8,56},{9,... | collective-permute-start | bytes 3080 | tf_op jit(solution)/shard_map/ppermute | solution.py:20
  197.6 3.8 %collective-permute-start.47 = (f32[16,16]{0,1:T(8,128)S(1)}, f32[16,16]{0,1:T(8,128)S(1)}, u32[]{:S(2)}, u32[]{:S(2)}) collective-permute-start(f32[16,16]{0,1:T(8,128)S(1)} %add_add_fusion.7), channel_id=1, source_target_pairs={{0,32},{1,33},{2,34},{3,35},{4,36},{5,37},{6,38},{7,39},{8,40},{9,... | collective-permute-start | bytes 3080 | tf_op jit(solution)/shard_map/ppermute | solution.py:20
  199.3 5.2 %collective-permute-start.46 = (f32[16,16]{0,1:T(8,128)S(1)}, f32[16,16]{0,1:T(8,128)S(1)}, u32[]{:S(2)}, u32[]{:S(2)}) collective-permute-start(f32[16,16]{0,1:T(8,128)S(1)} %add_add_fusion.7), channel_id=1, source_target_pairs={{0,16},{1,17},{2,18},{3,19},{4,20},{5,21},{6,22},{7,23},{8,24},{9,... | collective-permute-start | bytes 3080 | tf_op jit(solution)/shard_map/ppermute | solution.py:20
  204.5 5.2 %collective-permute-start.49 = (f32[16,16]{0,1:T(8,128)S(1)}, f32[16,16]{0,1:T(8,128)S(1)}, u32[]{:S(2)}, u32[]{:S(2)}) collective-permute-start(f32[16,16]{0,1:T(8,128)S(1)} %add_add_fusion.6), channel_id=1, source_target_pairs={{0,64},{1,65},{2,66},{3,67},{4,68},{5,69},{6,70},{7,71},{8,72},{9,... | collective-permute-start | bytes 3080 | tf_op jit(solution)/shard_map/ppermute | solution.py:20
  215.2 9.3 %collective-permute-start.50 = (f32[8,1,64,256]{3,2,0,1:T(8,128)S(1)}, f32[8,1,64,256]{3,2,0,1:T(8,128)S(1)}, u32[]{:S(2)}, u32[]{:S(2)}) collective-permute-start(f32[8,1,64,256]{3,2,0,1:T(8,128)S(1)} %bitcast.300), channel_id=1, source_target_pairs={{0,1},{1,0},{2,3},{3,2},{4,5},{5,4},{6,7},{7,6},{8,9},{9,8},{10,11... | collective-permute-start | bytes 1572872 | tf_op jit(solution)/shard_map/ppermute | solution.py:46

commit v2 on v1

--- a/solution.py
+++ b/solution.py
@@ -78,34 +78,44 @@
     mine = start_basis.shape[0]
     rows = start_basis.shape[2] // 2
     v = lax.axis_index("vec")
-    groups = radix_groups(lax.axis_size(AXES))
+    n = lax.axis_size(AXES)
+    groups = radix_groups(n)
     scale = 1.0 / (
         start_basis.shape[1] * start_basis.shape[2] * start_basis.shape[3] * lax.axis_size("space")
     )
-    keep = lax.dynamic_slice_in_dim(start_basis, v * rows, rows, 2)
-    give = lax.dynamic_slice_in_dim(start_basis, (1 - v) * rows, rows, 2)
+
+    def in_order(a, b, axis):
+        return jnp.where(v == 0, jnp.concatenate([a, b], axis), jnp.concatenate([b, a], axis))
+
+    ext = jnp.concatenate([start_basis[:, :, -1:], start_basis, start_basis[:, :, :1]], axis=2)
+    keep = lax.dynamic_slice_in_dim(ext, v * rows, rows + 2, 2)
+    give = lax.dynamic_slice_in_dim(ext, (1 - v) * rows, rows + 2, 2)
     got = swap_vec(give)
-    whole = jnp.where(v == 0, jnp.concatenate([keep, got], 0), jnp.concatenate([got, keep], 0))
+    same_up = [(i, (i + 2) % n) for i in range(n)]
+    same_down = [(j, i) for i, j in same_up]
+    cross_up = [(i, ((i // 2 + 1) * 2 + 1 - i % 2) % n) for i in range(n)]
+    cross_down = [(j, i) for i, j in cross_up]
+    keep_rows = keep[:, :, 1:-1]
+    give_rows = give[:, :, 1:-1]
+    before = in_order(lax.ppermute(keep_rows, AXES, same_up), lax.ppermute(give_rows, AXES, cross_up), 0)
+    after = in_order(lax.ppermute(keep_rows, AXES, same_down), lax.ppermute(give_rows, AXES, cross_down), 0)
+    whole_ext = in_order(keep, got, 0)
+    whole = whole_ext[:, :, 1:-1]
+    ends = jnp.concatenate([whole_ext[:, :, :1], whole_ext[:, :, -1:]], axis=2)
+
     pot = lax.dynamic_slice_in_dim(potential, v * rows, rows, 1)
     shifted = jnp.where(pot >= SIGMA, pot - SIGMA + 6.0, pot - SIGMA - 6.0)
 
-    h_whole = stencil(whole, halo(whole), pot)
-    s_d = whole / shifted
-    hs_d = h_whole / shifted
-    first = allsum(
-        jnp.stack(
-            [
-                local_inner(whole, whole, scale),
-                local_inner(whole, h_whole, scale),
-                local_inner(whole, s_d, scale),
-                local_inner(whole, hs_d, scale),
-                local_inner(h_whole, s_d, scale),
-                local_inner(h_whole, hs_d, scale),
-            ]
-        ),
-        groups,
-    )
-    gram, g_sh, u_ss, u_sh, u_hs, u_hh = (first[i] for i in range(6))
+    h_whole = stencil(whole, (before, after, ends), pot)
+    nb = whole.shape[0]
+    fields = jnp.concatenate([whole, h_whole, whole / shifted, h_whole / shifted], 0)
+    first = allsum(local_inner(fields[: 2 * nb], fields, scale), groups)
+    gram = first[:nb, :nb]
+    g_sh = first[:nb, nb:2 * nb]
+    u_ss = first[:nb, 2 * nb:3 * nb]
+    u_sh = first[:nb, 3 * nb:]
+    u_hs = first[nb:, 2 * nb:3 * nb]
+    u_hh = first[nb:, 3 * nb:]
     cmat = inverse_factor(gram).T
     ct = cmat.T
     rayleigh = mm(ct, mm(g_sh, cmat))
@@ -115,7 +125,8 @@
     basis = combine(cmat, whole)
     image = combine(cmat, h_whole)
     resid = image - combine(rayleigh, basis)
-    a_basis = image - SIGMA * basis
+    both = jnp.concatenate([basis, image - SIGMA * basis], 0)
+    a_basis = both[nb:]
 
     correction = -resid / shifted
     cr = mm(cmat, rayleigh)
@@ -130,24 +141,24 @@
 
     for sweep in range(2, NSWEEP):
         pieces = halo(correction)
-        red = allsum(
-            jnp.stack([local_inner(basis, correction, scale), local_inner(a_basis, correction, scale)]),
-            groups,
-        )
-        coeff = red[0]
-        back = red[1] - mm(ab_b, coeff)
+        red = allsum(local_inner(both, correction, scale), groups)
+        coeff = red[:nb]
+        back = red[nb:] - mm(ab_b, coeff)
         moved = stencil(correction, pieces, pot) - SIGMA * correction - combine(coeff, a_basis)
         correction = correction + (-resid - (moved - combine(back, basis))) / shifted
 
-    proj_two = allsum(local_inner(basis, correction, scale), groups)
+    red = allsum(
+        jnp.concatenate([local_inner(basis, correction, scale), local_inner(correction, correction, scale)], 0),
+        groups,
+    )
+    proj_two = red[:nb]
+    gram_two = red[nb:] - 2.0 * mm(proj_two.T, proj_two) + mm(proj_two.T, mm(b_b, proj_two))
     fresh = correction - combine(proj_two, basis)
-    gram_two = allsum(local_inner(fresh, fresh, scale), groups)
     new_all = combine(inverse_factor(gram_two).T, fresh)
 
     own = lax.dynamic_slice_in_dim(new_all, v * mine, mine, 0)
     out = lax.dynamic_slice_in_dim(new_all, (1 - v) * mine, mine, 0)
-    back_rows = swap_vec(out)
-    new_basis = jnp.where(v == 0, jnp.concatenate([own, back_rows], 2), jnp.concatenate([back_rows, own], 2))
+    new_basis = in_order(own, swap_vec(out), 2)
     return (new_basis, rayleigh)
 
 

time: 230 us -> 198 us (0.86); the launches traced: 226 us -> 198 us
  waiting for transfers between devices: 110 us -> 80.7 us
  matrix products: 28.4 us -> 22.3 us
  starting transfers between devices: 70.9 us -> 76.1 us
  other arithmetic: 10.1 us -> 12.8 us
    ppermute x0 -> x4, starting transfers between devices: none -> 14.6 us  [the longest x1 7.47 us: local(): lax.ppermute(keep_rows, AXES, same_down)]
    ppermute x40 -> x30, waiting for transfers between devices: 56.5 us -> 44.2 us  [allsum(): vals[m] = lax.ppermute(x, AXES, [(i, i ^ mask) for i in range(n)])]
    ppermute x3 -> x2, waiting for transfers between devices: 13.9 us -> 4.42 us  [halo(): before = lax.ppermute(value, 'space', up)]
    ppermute x5 -> x4, waiting for transfers between devices: 32.6 us -> 23.1 us  [swap_vec(): return lax.ppermute(value, 'vec', [(0, 1), (1, 0)])]
    ppermute x0 -> x4, waiting for transfers between devices: none -> 8.98 us  [the longest x1 8.97 us: local(): lax.ppermute(give_rows, AXES, cross_up)]
    ppermute x3 -> x2, waiting for transfers between devices: 7.34 us -> 0.01 us  [halo(): after = lax.ppermute(value, 'space', down)]
    dot_general x10 -> x4, matrix products: 14.8 us -> 8.11 us  [local_inner(): return jnp.einsum('kzyx,jzyx->kj', left, right, precision=PREC) * scale]
    ppermute x40 -> x30, starting transfers between devices: 48.5 us -> 42.7 us  [allsum(): vals[m] = lax.ppermute(x, AXES, [(i, i ^ mask) for i in range(n)])]
  transfers between devices with their start and end apart: 51 -> 42, of which waited for: 33 -> 26; matrix products, arithmetic and copies ran while one was open for 3% -> 3% of each run, Pallas kernels for 0% -> 0%
where the time goes in v2:
time: 198 us
  waiting for transfers between devices  80.7 us (41%)
  starting transfers between devices  76.1 us (38%)
  matrix products  22.3 us (11%)
  other arithmetic  12.8 us (6%)
  local copies, waits for them, and re-layouts  5.39 us (3%)
    ppermute x30, waiting for transfers between devices, allsum(): vals[m] = lax.ppermute(x, AXES, [(i, i ^ mask) for i in range(n)])  44.2 us
    ppermute x30, starting transfers between devices, allsum(): vals[m] = lax.ppermute(x, AXES, [(i, i ^ mask) for i in range(n)])  42.7 us
    ppermute x4, waiting for transfers between devices, swap_vec(): return lax.ppermute(value, 'vec', [(0, 1), (1, 0)])  23.1 us
    ppermute x2, starting transfers between devices, halo(): after = lax.ppermute(value, 'space', down)  14.9 us
    dot_general x9, matrix products, combine(): return jnp.einsum('kj,kzyx->jzyx', coeff, vectors, precision=PREC)  10.6 us
    ppermute x1, waiting for transfers between devices, local(): lax.ppermute(give_rows, AXES, cross_up)  8.97 us
    dot_general x4, matrix products, local_inner(): return jnp.einsum('kzyx,jzyx->kj', left, right, precision=PREC) * scale  8.11 us
    ppermute x1, starting transfers between devices, local(): lax.ppermute(keep_rows, AXES, same_down)  7.47 us
  transfers between devices with their start and end apart: 42, of which 26 were waited for; matrix products, arithmetic and copies ran while one was open for 3% of the time, Pallas kernels for 0%

profile of v2, /device:TPU:0, one launch (start us, length us, event | category | flops | bytes accessed | tf_op | source)
XLA Modules:
  0.0 198.3 jit_solution(8226342159351352477)
XLA Ops:
  0.6 1.8 copy.14
  2.7 2.1 %collective-permute-start = (f32[8,1,66,256]{3,0,2,1:T(8,128)S(1)}, f32[8,1,66,256]{3,0,2,1:T(8,128)S(1)}, u32[]{:S(2)}, u32[]{:S(2)}) collective-permute-start(f32[8,1,66,256]{3,0,2,1:T(8,128)S(1)} %get-tuple-element.16), channel_id=1, source_target_pairs={{0,1},{1,0},{2,3},{3,2},{4,5},{5,4},{6,7},{7,6},{8,9},{9,8},{10,11... | collective-permute-start | bytes 1622024 | tf_op jit(solution)/shard_map/ppermute | solution.py:46
  4.8 1.1 constant_dynamic-slice_fusion
  5.8 7.5 %collective-permute-start.3 = (f32[8,1,64,256]{3,0,2,1:T(8,128)}, f32[8,1,64,256]{3,0,2,1:T(8,128)}, u32[]{:S(2)}, u32[]{:S(2)}) collective-permute-start(f32[8,1,64,256]{3,0,2,1:T(8,128)} %get-tuple-element.14), channel_id=1, source_target_pairs={{2,0},{3,1},{4,2},{5,3},{6,4},{7,5},{8,6},{9,7},{10,8},{11,9},{12,... | collective-permute-start | bytes 1572872 | tf_op jit(solution)/shard_map/ppermute | solution.py:101
  13.3 7.2 %collective-permute-start.4 = (f32[8,1,64,256]{3,0,2,1:T(8,128)}, f32[8,1,64,256]{3,0,2,1:T(8,128)}, u32[]{:S(2)}, u32[]{:S(2)}) collective-permute-start(f32[8,1,64,256]{3,0,2,1:T(8,128)} %get-tuple-element.13), channel_id=1, source_target_pairs={{3,0},{2,1},{5,2},{4,3},{7,4},{6,5},{9,6},{8,7},{11,8},{10,9},{13,... | collective-permute-start | bytes 1572872 | tf_op jit(solution)/shard_map/ppermute | solution.py:101
  20.5 8.6 %collective-permute-done = f32[8,1,66,256]{3,0,2,1:T(8,128)S(1)} collective-permute-done((f32[8,1,66,256]{3,0,2,1:T(8,128)S(1)}, f32[8,1,66,256]{3,0,2,1:T(8,128)S(1)}, u32[]{:S(2)}, u32[]{:S(2)}) %collective-permute-start) | collective-permute-done | bytes 540704 | tf_op jit(solution)/shard_map/ppermute | solution.py:46
  29.9 9.0 %collective-permute-done.2 = f32[8,1,64,256]{3,0,2,1:T(8,128)} collective-permute-done((f32[8,1,64,256]{3,0,2,1:T(8,128)}, f32[8,1,64,256]{3,0,2,1:T(8,128)}, u32[]{:S(2)}, u32[]{:S(2)}) %collective-permute-start.2) | collective-permute-done | bytes 524320 | tf_op jit(solution)/shard_map/ppermute | solution.py:100
  38.9 3.1 %broadcast_divide_fusion.1 = (f32[16,1,64,256]{3,0,2,1:T(8,128)S(1)}, f32[16,1,64,256]{3,0,2,1:T(8,128)S(1)}, f32[16,1,64,256]{3,0,2,1:T(8,128)S(1)}) fusion(f32[64,256]{1,0:T(8,128)S(1)} %get-tuple-element.34, f32[16,1,64,1]{3,0,2,1:T(8,128)S(1)} %get-tuple-element.10, f32[16,1,64,255]{3,0,2,1:T(8,128)S(1)} %get-tuple-element.12, ...), kind=kLoop, calls=%fused_computation.90 | loop fusion | flops 4456448 | bytes 10616833 | tf_op jit(solution)/shard_map/div | solution.py:111
  42.0 3.4 %fusion.55 = f32[32,64]{0,1:T(8,128)S(1)} fusion(f32[16,1,64,256]{3,0,2,1:T(8,128)S(1)} %get-tuple-element.6, f32[16,1,64,256]{3,0,2,1:T(8,128)S(1)} %get-tuple-element.8, f32[16,1,64,256]{3,0,2,1:T(8,128)S(1)} %get-tuple-element.7, f32[16,1,64,256]{3,0,2,1:T(8,128)S(1)} %slice.191), kind=kOutput, calls=%fused_computation.86 | convolution fusion | flops 406325248 | bytes 4202496 | tf_op jit(solution)/shard_map/kzyx,jzyx->kj/dot_general | solution.py:34
  45.4 1.4 collective-permute-start.5
  47.6 1.8 collective-permute-done.5
  49.4 1.6 collective-permute-done.7
  51.0 2.8 %collective-permute-start.10 = (f32[32,64]{0,1:T(8,128)S(1)}, f32[32,64]{0,1:T(8,128)S(1)}, u32[]{:S(2)}, u32[]{:S(2)}) collective-permute-start(f32[32,64]{0,1:T(8,128)S(1)} %add_add_fusion.2), channel_id=1, source_target_pairs={{0,12},{1,13},{2,14},{3,15},{4,8},{5,9},{6,10},{7,11},{8,4},{9,5},... | collective-permute-start | bytes 24584 | tf_op jit(solution)/shard_map/ppermute | solution.py:20
  54.1 1.7 collective-permute-start.9
  56.2 1.5 collective-permute-done.8
  57.7 1.7 collective-permute-done.9
  59.5 3.7 %collective-permute-start.11 = (f32[32,64]{0,1:T(8,128)S(1)}, f32[32,64]{0,1:T(8,128)S(1)}, u32[]{:S(2)}, u32[]{:S(2)}) collective-permute-start(f32[32,64]{0,1:T(8,128)S(1)} %add_add_fusion.1), channel_id=1, source_target_pairs={{0,16},{1,17},{2,18},{3,19},{4,20},{5,21},{6,22},{7,23},{8,24},{9,... | collective-permute-start | bytes 24584 | tf_op jit(solution)/shard_map/ppermute | solution.py:20
  63.2 1.6 collective-permute-start.12
  65.1 2.0 %collective-permute-done.12 = f32[32,64]{0,1:T(8,128)S(1)} collective-permute-done((f32[32,64]{0,1:T(8,128)S(1)}, f32[32,64]{0,1:T(8,128)S(1)}, u32[]{:S(2)}, u32[]{:S(2)}) %collective-permute-start.12) | collective-permute-done | bytes 8224 | tf_op jit(solution)/shard_map/ppermute | solution.py:20
  67.1 4.0 %collective-permute-done.13 = f32[32,64]{0,1:T(8,128)S(1)} collective-permute-done((f32[32,64]{0,1:T(8,128)S(1)}, f32[32,64]{0,1:T(8,128)S(1)}, u32[]{:S(2)}, u32[]{:S(2)}) %collective-permute-start.13) | collective-permute-done | bytes 8224 | tf_op jit(solution)/shard_map/ppermute | solution.py:20
  71.1 3.3 %collective-permute-start.14 = (f32[32,64]{0,1:T(8,128)S(1)}, f32[32,64]{0,1:T(8,128)S(1)}, u32[]{:S(2)}, u32[]{:S(2)}) collective-permute-start(f32[32,64]{0,1:T(8,128)S(1)} %add_add_fusion), channel_id=1, source_target_pairs={{0,64},{1,65},{2,66},{3,67},{4,68},{5,69},{6,70},{7,71},{8,72},{9,... | collective-permute-start | bytes 24584 | tf_op jit(solution)/shard_map/ppermute | solution.py:20
  74.4 2.4 %collective-permute-done.14 = f32[32,64]{0,1:T(8,128)S(1)} collective-permute-done((f32[32,64]{0,1:T(8,128)S(1)}, f32[32,64]{0,1:T(8,128)S(1)}, u32[]{:S(2)}, u32[]{:S(2)}) %collective-permute-start.14) | collective-permute-done | bytes 8224 | tf_op jit(solution)/shard_map/ppermute | solution.py:20
  76.8 1.5 cholesky.44
  79.6 1.2 custom-call.6
  81.1 1.0 fusion.51
  82.1 1.0 fusion.53
  84.2 1.1 fusion.12
  85.3 1.1 convolution_subtract_fusion
  86.4 7.5 %collective-permute-start.16 = (f32[16,1,64,256]{3,0,2,1:T(8,128)S(1)}, f32[16,1,64,256]{3,0,2,1:T(8,128)S(1)}, u32[]{:S(2)}, u32[]{:S(2)}) collective-permute-start(f32[16,1,64,256]{3,0,2,1:T(8,128)S(1)} %bitcast.185), channel_id=1, source_target_pairs={{2,0},{4,2},{6,4},{8,6},{10,8},{12,10},{14,12},{16,14},{18,16},{20... | collective-permute-start | bytes 3145736 | tf_op jit(solution)/shard_map/ppermute | solution.py:56
  96.4 5.6 %collective-permute-done.17 = f32[16,1,2,256]{3,0,2,1:T(8,128)S(1)} collective-permute-done((f32[16,1,2,256]{3,0,2,1:T(8,128)S(1)}, f32[16,1,2,256]{3,0,2,1:T(8,128)S(1)}, u32[]{:S(2)}, u32[]{:S(2)}) %collective-permute-start.17) | collective-permute-done | bytes 32800 | tf_op jit(solution)/shard_map/ppermute | solution.py:46
  102.1 4.4 %collective-permute-done.15 = f32[16,1,64,256]{3,0,2,1:T(8,128)S(1)} collective-permute-done((f32[16,1,64,256]{3,0,2,1:T(8,128)S(1)}, f32[16,1,64,256]{3,0,2,1:T(8,128)S(1)}, u32[]{:S(2)}, u32[]{:S(2)}) %collective-permute-start.15) | collective-permute-done | bytes 1048608 | tf_op jit(solution)/shard_map/ppermute | solution.py:55
  106.5 1.8 fusion.16
  108.3 1.7 fusion.30
  110.1 2.0 %collective-permute-start.23 = (f32[32,16]{0,1:T(8,128)S(1)}, f32[32,16]{0,1:T(8,128)S(1)}, u32[]{:S(2)}, u32[]{:S(2)}) collective-permute-start(f32[32,16]{0,1:T(8,128)S(1)} %fusion.30), channel_id=1, source_target_pairs={{0,3},{1,2},{2,1},{3,0},{4,7},{5,6},{6,5},{7,4},{8,11},{9,10},{10,... | collective-permute-start | bytes 6152 | tf_op jit(solution)/shard_map/ppermute | solution.py:20
  112.6 7.5 %collective-permute-start.19 = (f32[16,1,64,256]{3,0,2,1:T(8,128)S(1)}, f32[16,1,64,256]{3,0,2,1:T(8,128)S(1)}, u32[]{:S(2)}, u32[]{:S(2)}) collective-permute-start(f32[16,1,64,256]{3,0,2,1:T(8,128)S(1)} %fusion.16), channel_id=1, source_target_pairs={{2,0},{4,2},{6,4},{8,6},{10,8},{12,10},{14,12},{16,14},{18,16},{20... | collective-permute-start | bytes 3145736 | tf_op jit(solution)/shard_map/ppermute | solution.py:56
  120.5 4.6 %collective-permute-start.26 = (f32[32,16]{0,1:T(8,128)S(1)}, f32[32,16]{0,1:T(8,128)S(1)}, u32[]{:S(2)}, u32[]{:S(2)}) collective-permute-start(f32[32,16]{0,1:T(8,128)S(1)} %add_add_fusion.8), channel_id=1, source_target_pairs={{0,12},{1,13},{2,14},{3,15},{4,8},{5,9},{6,10},{7,11},{8,4},{9,5},... | collective-permute-start | bytes 6152 | tf_op jit(solution)/shard_map/ppermute | solution.py:20
  125.3 2.1 %collective-permute-done.24 = f32[32,16]{0,1:T(8,128)S(1)} collective-permute-done((f32[32,16]{0,1:T(8,128)S(1)}, f32[32,16]{0,1:T(8,128)S(1)}, u32[]{:S(2)}, u32[]{:S(2)}) %collective-permute-start.24) | collective-permute-done | bytes 2080 | tf_op jit(solution)/shard_map/ppermute | solution.py:20
  127.3 5.2 %collective-permute-done.26 = f32[32,16]{0,1:T(8,128)S(1)} collective-permute-done((f32[32,16]{0,1:T(8,128)S(1)}, f32[32,16]{0,1:T(8,128)S(1)}, u32[]{:S(2)}, u32[]{:S(2)}) %collective-permute-start.26) | collective-permute-done | bytes 2080 | tf_op jit(solution)/shard_map/ppermute | solution.py:20
  132.6 5.0 %collective-permute-start.29 = (f32[32,16]{0,1:T(8,128)S(1)}, f32[32,16]{0,1:T(8,128)S(1)}, u32[]{:S(2)}, u32[]{:S(2)}) collective-permute-start(f32[32,16]{0,1:T(8,128)S(1)} %add_add_fusion.7), channel_id=1, source_target_pairs={{0,48},{1,49},{2,50},{3,51},{4,52},{5,53},{6,54},{7,55},{8,56},{9,... | collective-permute-start | bytes 6152 | tf_op jit(solution)/shard_map/ppermute | solution.py:20
  137.7 1.5 collective-permute-done.29
  139.3 1.0 collective-permute-start.30
  140.8 3.6 %collective-permute-done.30 = f32[32,16]{0,1:T(8,128)S(1)} collective-permute-done((f32[32,16]{0,1:T(8,128)S(1)}, f32[32,16]{0,1:T(8,128)S(1)}, u32[]{:S(2)}, u32[]{:S(2)}) %collective-permute-start.30) | collective-permute-done | bytes 2080 | tf_op jit(solution)/shard_map/ppermute | solution.py:20
  144.6 1.0 convolution_bitcast_fusion.1
  145.7 1.6 fusion.21
  147.2 1.5 fusion.27
  148.7 1.5 fusion.26
  150.4 2.0 %collective-permute-start.33 = (f32[32,16]{0,1:T(8,128)S(1)}, f32[32,16]{0,1:T(8,128)S(1)}, u32[]{:S(2)}, u32[]{:S(2)}) collective-permute-start(f32[32,16]{0,1:T(8,128)S(1)} %pad_maximum_fusion.7), channel_id=1, source_target_pairs={{0,3},{1,2},{2,1},{3,0},{4,7},{5,6},{6,5},{7,4},{8,11},{9,10},{10,... | collective-permute-start | bytes 6152 | tf_op jit(solution)/shard_map/ppermute | solution.py:20
  152.5 1.5 collective-permute-done.31
  154.0 2.3 %collective-permute-start.34 = (f32[32,16]{0,1:T(8,128)S(1)}, f32[32,16]{0,1:T(8,128)S(1)}, u32[]{:S(2)}, u32[]{:S(2)}) collective-permute-start(f32[32,16]{0,1:T(8,128)S(1)} %add_add_fusion.5), channel_id=1, source_target_pairs={{0,4},{1,5},{2,6},{3,7},{4,0},{5,1},{6,2},{7,3},{8,12},{9,13},{10,... | collective-permute-start | bytes 6152 | tf_op jit(solution)/shard_map/ppermute | solution.py:20
  156.3 2.9 %collective-permute-start.35 = (f32[32,16]{0,1:T(8,128)S(1)}, f32[32,16]{0,1:T(8,128)S(1)}, u32[]{:S(2)}, u32[]{:S(2)}) collective-permute-start(f32[32,16]{0,1:T(8,128)S(1)} %add_add_fusion.5), channel_id=1, source_target_pairs={{0,8},{1,9},{2,10},{3,11},{4,12},{5,13},{6,14},{7,15},{8,0},{9,1},... | collective-permute-start | bytes 6152 | tf_op jit(solution)/shard_map/ppermute | solution.py:20
  159.2 2.2 %collective-permute-done.35 = f32[32,16]{0,1:T(8,128)S(1)} collective-permute-done((f32[32,16]{0,1:T(8,128)S(1)}, f32[32,16]{0,1:T(8,128)S(1)}, u32[]{:S(2)}, u32[]{:S(2)}) %collective-permute-start.35) | collective-permute-done | bytes 2080 | tf_op jit(solution)/shard_map/ppermute | solution.py:20
  161.5 2.6 %collective-permute-done.36 = f32[32,16]{0,1:T(8,128)S(1)} collective-permute-done((f32[32,16]{0,1:T(8,128)S(1)}, f32[32,16]{0,1:T(8,128)S(1)}, u32[]{:S(2)}, u32[]{:S(2)}) %collective-permute-start.36) | collective-permute-done | bytes 2080 | tf_op jit(solution)/shard_map/ppermute | solution.py:20
  164.1 2.9 %collective-permute-start.37 = (f32[32,16]{0,1:T(8,128)S(1)}, f32[32,16]{0,1:T(8,128)S(1)}, u32[]{:S(2)}, u32[]{:S(2)}) collective-permute-start(f32[32,16]{0,1:T(8,128)S(1)} %add_add_fusion.4), channel_id=1, source_target_pairs={{0,16},{1,17},{2,18},{3,19},{4,20},{5,21},{6,22},{7,23},{8,24},{9,... | collective-permute-start | bytes 6152 | tf_op jit(solution)/shard_map/ppermute | solution.py:20
  167.0 2.0 %collective-permute-start.38 = (f32[32,16]{0,1:T(8,128)S(1)}, f32[32,16]{0,1:T(8,128)S(1)}, u32[]{:S(2)}, u32[]{:S(2)}) collective-permute-start(f32[32,16]{0,1:T(8,128)S(1)} %add_add_fusion.4), channel_id=1, source_target_pairs={{0,32},{1,33},{2,34},{3,35},{4,36},{5,37},{6,38},{7,39},{8,40},{9,... | collective-permute-start | bytes 6152 | tf_op jit(solution)/shard_map/ppermute | solution.py:20
  169.3 1.4 collective-permute-done.38
  170.7 4.4 %collective-permute-done.39 = f32[32,16]{0,1:T(8,128)S(1)} collective-permute-done((f32[32,16]{0,1:T(8,128)S(1)}, f32[32,16]{0,1:T(8,128)S(1)}, u32[]{:S(2)}, u32[]{:S(2)}) %collective-permute-start.39) | collective-permute-done | bytes 2080 | tf_op jit(solution)/shard_map/ppermute | solution.py:20
  175.1 1.7 collective-permute-start.40
  176.8 3.5 %collective-permute-done.40 = f32[32,16]{0,1:T(8,128)S(1)} collective-permute-done((f32[32,16]{0,1:T(8,128)S(1)}, f32[32,16]{0,1:T(8,128)S(1)}, u32[]{:S(2)}, u32[]{:S(2)}) %collective-permute-start.40) | collective-permute-done | bytes 2080 | tf_op jit(solution)/shard_map/ppermute | solution.py:20
  180.3 1.0 fusion.23
  181.8 1.5 cholesky.55
  184.6 1.2 custom-call.7
  186.1 1.0 fusion.119
  188.4 8.9 %collective-permute-done.41 = f32[8,1,64,256]{3,2,0,1:T(8,128)S(1)} collective-permute-done((f32[8,1,64,256]{3,2,0,1:T(8,128)S(1)}, f32[8,1,64,256]{3,2,0,1:T(8,128)S(1)}, u32[]{:S(2)}, u32[]{:S(2)}) %collective-permute-start.41) | collective-permute-done | bytes 524320 | tf_op jit(solution)/shard_map/ppermute | solution.py:46
  197.2 1.0 fusion.47
  (111 shorter events, 13.9 us)
Async XLA Ops:
  2.7 17.8 %copy-start.1 = (f32[1,128,256]{2,1,0:T(8,128)S(1)}, f32[1,128,256]{2,1,0:T(8,128)}, u32[]{:S(2)}) copy-start(f32[1,128,256]{2,1,0:T(8,128)} %param.5) | copy-start | bytes 393220
  2.7 26.5 %collective-permute-start = (f32[8,1,66,256]{3,0,2,1:T(8,128)S(1)}, f32[8,1,66,256]{3,0,2,1:T(8,128)S(1)}, u32[]{:S(2)}, u32[]{:S(2)}) collective-permute-start(f32[8,1,66,256]{3,0,2,1:T(8,128)S(1)} %get-tuple-element.16), channel_id=1, source_target_pairs={{0,1},{1,0},{2,3},{3,2},{4,5},{5,4},{6,7},{7,6},{8,9},{9,8},{10,11... | collective-permute-start | bytes 1622024 | tf_op jit(solution)/shard_map/ppermute | solution.py:46
  5.8 24.1 %collective-permute-start.1 = (f32[8,1,64,256]{3,0,2,1:T(8,128)}, f32[8,1,64,256]{3,0,2,1:T(8,128)}, u32[]{:S(2)}, u32[]{:S(2)}) collective-permute-start(f32[8,1,64,256]{3,0,2,1:T(8,128)} %get-tuple-element.14), channel_id=1, source_target_pairs={{0,2},{1,3},{2,4},{3,5},{4,6},{5,7},{6,8},{7,9},{8,10},{9,11},{10,... | collective-permute-start | bytes 1572872 | tf_op jit(solution)/shard_map/ppermute | solution.py:100
  5.8 33.1 %collective-permute-start.3 = (f32[8,1,64,256]{3,0,2,1:T(8,128)}, f32[8,1,64,256]{3,0,2,1:T(8,128)}, u32[]{:S(2)}, u32[]{:S(2)}) collective-permute-start(f32[8,1,64,256]{3,0,2,1:T(8,128)} %get-tuple-element.14), channel_id=1, source_target_pairs={{2,0},{3,1},{4,2},{5,3},{6,4},{7,5},{8,6},{9,7},{10,8},{11,9},{12,... | collective-permute-start | bytes 1572872 | tf_op jit(solution)/shard_map/ppermute | solution.py:101
  13.3 25.6 %collective-permute-start.2 = (f32[8,1,64,256]{3,0,2,1:T(8,128)}, f32[8,1,64,256]{3,0,2,1:T(8,128)}, u32[]{:S(2)}, u32[]{:S(2)}) collective-permute-start(f32[8,1,64,256]{3,0,2,1:T(8,128)} %get-tuple-element.13), channel_id=1, source_target_pairs={{0,3},{1,2},{2,5},{3,4},{4,7},{5,6},{6,9},{7,8},{8,11},{9,10},{10,... | collective-permute-start | bytes 1572872 | tf_op jit(solution)/shard_map/ppermute | solution.py:100
  13.3 25.6 %collective-permute-start.4 = (f32[8,1,64,256]{3,0,2,1:T(8,128)}, f32[8,1,64,256]{3,0,2,1:T(8,128)}, u32[]{:S(2)}, u32[]{:S(2)}) collective-permute-start(f32[8,1,64,256]{3,0,2,1:T(8,128)} %get-tuple-element.13), channel_id=1, source_target_pairs={{3,0},{2,1},{5,2},{4,3},{7,4},{6,5},{9,6},{8,7},{11,8},{10,9},{13,... | collective-permute-start | bytes 1572872 | tf_op jit(solution)/shard_map/ppermute | solution.py:101
  45.4 4.0 %collective-permute-start.5 = (f32[32,64]{0,1:T(8,128)S(1)}, f32[32,64]{0,1:T(8,128)S(1)}, u32[]{:S(2)}, u32[]{:S(2)}) collective-permute-start(f32[32,64]{0,1:T(8,128)S(1)} %fusion.55), channel_id=1, source_target_pairs={{0,1},{1,0},{2,3},{3,2},{4,5},{5,4},{6,7},{7,6},{8,9},{9,8},{10,11... | collective-permute-start | bytes 24584 | tf_op jit(solution)/shard_map/ppermute | solution.py:20
  46.8 2.6 %collective-permute-start.6 = (f32[32,64]{0,1:T(8,128)S(1)}, f32[32,64]{0,1:T(8,128)S(1)}, u32[]{:S(2)}, u32[]{:S(2)}) collective-permute-start(f32[32,64]{0,1:T(8,128)S(1)} %fusion.55), channel_id=1, source_target_pairs={{0,2},{1,3},{2,0},{3,1},{4,6},{5,7},{6,4},{7,5},{8,10},{9,11},{10,... | collective-permute-start | bytes 24584 | tf_op jit(solution)/shard_map/ppermute | solution.py:20
  47.5 3.5 %collective-permute-start.7 = (f32[32,64]{0,1:T(8,128)S(1)}, f32[32,64]{0,1:T(8,128)S(1)}, u32[]{:S(2)}, u32[]{:S(2)}) collective-permute-start(f32[32,64]{0,1:T(8,128)S(1)} %fusion.55), channel_id=1, source_target_pairs={{0,3},{1,2},{2,1},{3,0},{4,7},{5,6},{6,5},{7,4},{8,11},{9,10},{10,... | collective-permute-start | bytes 24584 | tf_op jit(solution)/shard_map/ppermute | solution.py:20
  51.0 5.2 %collective-permute-start.10 = (f32[32,64]{0,1:T(8,128)S(1)}, f32[32,64]{0,1:T(8,128)S(1)}, u32[]{:S(2)}, u32[]{:S(2)}) collective-permute-start(f32[32,64]{0,1:T(8,128)S(1)} %add_add_fusion.2), channel_id=1, source_target_pairs={{0,12},{1,13},{2,14},{3,15},{4,8},{5,9},{6,10},{7,11},{8,4},{9,5},... | collective-permute-start | bytes 24584 | tf_op jit(solution)/shard_map/ppermute | solution.py:20
  53.8 3.9 %collective-permute-start.8 = (f32[32,64]{0,1:T(8,128)S(1)}, f32[32,64]{0,1:T(8,128)S(1)}, u32[]{:S(2)}, u32[]{:S(2)}) collective-permute-start(f32[32,64]{0,1:T(8,128)S(1)} %add_add_fusion.2), channel_id=1, source_target_pairs={{0,4},{1,5},{2,6},{3,7},{4,0},{5,1},{6,2},{7,3},{8,12},{9,13},{10,... | collective-permute-start | bytes 24584 | tf_op jit(solution)/shard_map/ppermute | solution.py:20
  54.1 5.4 %collective-permute-start.9 = (f32[32,64]{0,1:T(8,128)S(1)}, f32[32,64]{0,1:T(8,128)S(1)}, u32[]{:S(2)}, u32[]{:S(2)}) collective-permute-start(f32[32,64]{0,1:T(8,128)S(1)} %add_add_fusion.2), channel_id=1, source_target_pairs={{0,8},{1,9},{2,10},{3,11},{4,12},{5,13},{6,14},{7,15},{8,0},{9,1},... | collective-permute-start | bytes 24584 | tf_op jit(solution)/shard_map/ppermute | solution.py:20
  59.5 5.6 %collective-permute-start.11 = (f32[32,64]{0,1:T(8,128)S(1)}, f32[32,64]{0,1:T(8,128)S(1)}, u32[]{:S(2)}, u32[]{:S(2)}) collective-permute-start(f32[32,64]{0,1:T(8,128)S(1)} %add_add_fusion.1), channel_id=1, source_target_pairs={{0,16},{1,17},{2,18},{3,19},{4,20},{5,21},{6,22},{7,23},{8,24},{9,... | collective-permute-start | bytes 24584 | tf_op jit(solution)/shard_map/ppermute | solution.py:20
  63.2 3.9 %collective-permute-start.12 = (f32[32,64]{0,1:T(8,128)S(1)}, f32[32,64]{0,1:T(8,128)S(1)}, u32[]{:S(2)}, u32[]{:S(2)}) collective-permute-start(f32[32,64]{0,1:T(8,128)S(1)} %add_add_fusion.1), channel_id=1, source_target_pairs={{0,32},{1,33},{2,34},{3,35},{4,36},{5,37},{6,38},{7,39},{8,40},{9,... | collective-permute-start | bytes 24584 | tf_op jit(solution)/shard_map/ppermute | solution.py:20
  64.7 6.3 %collective-permute-start.13 = (f32[32,64]{0,1:T(8,128)S(1)}, f32[32,64]{0,1:T(8,128)S(1)}, u32[]{:S(2)}, u32[]{:S(2)}) collective-permute-start(f32[32,64]{0,1:T(8,128)S(1)} %add_add_fusion.1), channel_id=1, source_target_pairs={{0,48},{1,49},{2,50},{3,51},{4,52},{5,53},{6,54},{7,55},{8,56},{9,... | collective-permute-start | bytes 24584 | tf_op jit(solution)/shard_map/ppermute | solution.py:20
  71.1 5.7 %collective-permute-start.14 = (f32[32,64]{0,1:T(8,128)S(1)}, f32[32,64]{0,1:T(8,128)S(1)}, u32[]{:S(2)}, u32[]{:S(2)}) collective-permute-start(f32[32,64]{0,1:T(8,128)S(1)} %add_add_fusion), channel_id=1, source_target_pairs={{0,64},{1,65},{2,66},{3,67},{4,68},{5,69},{6,70},{7,71},{8,72},{9,... | collective-permute-start | bytes 24584 | tf_op jit(solution)/shard_map/ppermute | solution.py:20
  83.4 1.8 copy-start
  86.4 20.1 %collective-permute-start.15 = (f32[16,1,64,256]{3,0,2,1:T(8,128)S(1)}, f32[16,1,64,256]{3,0,2,1:T(8,128)S(1)}, u32[]{:S(2)}, u32[]{:S(2)}) collective-permute-start(f32[16,1,64,256]{3,0,2,1:T(8,128)S(1)} %bitcast.184), channel_id=1, source_target_pairs={{0,2},{2,4},{4,6},{6,8},{8,10},{10,12},{12,14},{14,16},{16,18},{18... | collective-permute-start | bytes 3145736 | tf_op jit(solution)/shard_map/ppermute | solution.py:55
  86.4 20.0 %collective-permute-start.16 = (f32[16,1,64,256]{3,0,2,1:T(8,128)S(1)}, f32[16,1,64,256]{3,0,2,1:T(8,128)S(1)}, u32[]{:S(2)}, u32[]{:S(2)}) collective-permute-start(f32[16,1,64,256]{3,0,2,1:T(8,128)S(1)} %bitcast.185), channel_id=1, source_target_pairs={{2,0},{4,2},{6,4},{8,6},{10,8},{12,10},{14,12},{16,14},{18,16},{20... | collective-permute-start | bytes 3145736 | tf_op jit(solution)/shard_map/ppermute | solution.py:56
  94.7 7.3 %collective-permute-start.17 = (f32[16,1,2,256]{3,0,2,1:T(8,128)S(1)}, f32[16,1,2,256]{3,0,2,1:T(8,128)S(1)}, u32[]{:S(2)}, u32[]{:S(2)}) collective-permute-start(f32[16,1,2,256]{3,0,2,1:T(8,128)S(1)} %pad_maximum_fusion.5), channel_id=1, source_target_pairs={{0,1},{1,0},{2,3},{3,2},{4,5},{5,4},{6,7},{7,6},{8,9},{9,8},{10,11... | collective-permute-start | bytes 98312 | tf_op jit(solution)/shard_map/ppermute | solution.py:46
  110.0 10.1 %collective-permute-start.21 = (f32[32,16]{0,1:T(8,128)S(1)}, f32[32,16]{0,1:T(8,128)S(1)}, u32[]{:S(2)}, u32[]{:S(2)}) collective-permute-start(f32[32,16]{0,1:T(8,128)S(1)} %fusion.30), channel_id=1, source_target_pairs={{0,1},{1,0},{2,3},{3,2},{4,5},{5,4},{6,7},{7,6},{8,9},{9,8},{10,11... | collective-permute-start | bytes 6152 | tf_op jit(solution)/shard_map/ppermute | solution.py:20
  110.1 10.0 %collective-permute-start.22 = (f32[32,16]{0,1:T(8,128)S(1)}, f32[32,16]{0,1:T(8,128)S(1)}, u32[]{:S(2)}, u32[]{:S(2)}) collective-permute-start(f32[32,16]{0,1:T(8,128)S(1)} %fusion.30), channel_id=1, source_target_pairs={{0,2},{1,3},{2,0},{3,1},{4,6},{5,7},{6,4},{7,5},{8,10},{9,11},{10,... | collective-permute-start | bytes 6152 | tf_op jit(solution)/shard_map/ppermute | solution.py:20
  110.1 10.0 %collective-permute-start.23 = (f32[32,16]{0,1:T(8,128)S(1)}, f32[32,16]{0,1:T(8,128)S(1)}, u32[]{:S(2)}, u32[]{:S(2)}) collective-permute-start(f32[32,16]{0,1:T(8,128)S(1)} %fusion.30), channel_id=1, source_target_pairs={{0,3},{1,2},{2,1},{3,0},{4,7},{5,6},{6,5},{7,4},{8,11},{9,10},{10,... | collective-permute-start | bytes 6152 | tf_op jit(solution)/shard_map/ppermute | solution.py:20
  112.5 33.1 %collective-permute-start.18 = (f32[16,1,64,256]{3,0,2,1:T(8,128)S(1)}, f32[16,1,64,256]{3,0,2,1:T(8,128)S(1)}, u32[]{:S(2)}, u32[]{:S(2)}) collective-permute-start(f32[16,1,64,256]{3,0,2,1:T(8,128)S(1)} %fusion.16), channel_id=1, source_target_pairs={{0,2},{2,4},{4,6},{6,8},{8,10},{10,12},{12,14},{14,16},{16,18},{18... | collective-permute-start | bytes 3145736 | tf_op jit(solution)/shard_map/ppermute | solution.py:55
  112.6 33.0 %collective-permute-start.19 = (f32[16,1,64,256]{3,0,2,1:T(8,128)S(1)}, f32[16,1,64,256]{3,0,2,1:T(8,128)S(1)}, u32[]{:S(2)}, u32[]{:S(2)}) collective-permute-start(f32[16,1,64,256]{3,0,2,1:T(8,128)S(1)} %fusion.16), channel_id=1, source_target_pairs={{2,0},{4,2},{6,4},{8,6},{10,8},{12,10},{14,12},{16,14},{18,16},{20... | collective-permute-start | bytes 3145736 | tf_op jit(solution)/shard_map/ppermute | solution.py:56
  120.1 7.3 %collective-permute-start.24 = (f32[32,16]{0,1:T(8,128)S(1)}, f32[32,16]{0,1:T(8,128)S(1)}, u32[]{:S(2)}, u32[]{:S(2)}) collective-permute-start(f32[32,16]{0,1:T(8,128)S(1)} %add_add_fusion.8), channel_id=1, source_target_pairs={{0,4},{1,5},{2,6},{3,7},{4,0},{5,1},{6,2},{7,3},{8,12},{9,13},{10,... | collective-permute-start | bytes 6152 | tf_op jit(solution)/shard_map/ppermute | solution.py:20
  120.4 6.9 %collective-permute-start.25 = (f32[32,16]{0,1:T(8,128)S(1)}, f32[32,16]{0,1:T(8,128)S(1)}, u32[]{:S(2)}, u32[]{:S(2)}) collective-permute-start(f32[32,16]{0,1:T(8,128)S(1)} %add_add_fusion.8), channel_id=1, source_target_pairs={{0,8},{1,9},{2,10},{3,11},{4,12},{5,13},{6,14},{7,15},{8,0},{9,1},... | collective-permute-start | bytes 6152 | tf_op jit(solution)/shard_map/ppermute | solution.py:20
  120.5 12.1 %collective-permute-start.26 = (f32[32,16]{0,1:T(8,128)S(1)}, f32[32,16]{0,1:T(8,128)S(1)}, u32[]{:S(2)}, u32[]{:S(2)}) collective-permute-start(f32[32,16]{0,1:T(8,128)S(1)} %add_add_fusion.8), channel_id=1, source_target_pairs={{0,12},{1,13},{2,14},{3,15},{4,8},{5,9},{6,10},{7,11},{8,4},{9,5},... | collective-permute-start | bytes 6152 | tf_op jit(solution)/shard_map/ppermute | solution.py:20
  132.6 5.2 %collective-permute-start.27 = (f32[32,16]{0,1:T(8,128)S(1)}, f32[32,16]{0,1:T(8,128)S(1)}, u32[]{:S(2)}, u32[]{:S(2)}) collective-permute-start(f32[32,16]{0,1:T(8,128)S(1)} %add_add_fusion.7), channel_id=1, source_target_pairs={{0,16},{1,17},{2,18},{3,19},{4,20},{5,21},{6,22},{7,23},{8,24},{9,... | collective-permute-start | bytes 6152 | tf_op jit(solution)/shard_map/ppermute | solution.py:20
  132.6 5.2 %collective-permute-start.28 = (f32[32,16]{0,1:T(8,128)S(1)}, f32[32,16]{0,1:T(8,128)S(1)}, u32[]{:S(2)}, u32[]{:S(2)}) collective-permute-start(f32[32,16]{0,1:T(8,128)S(1)} %add_add_fusion.7), channel_id=1, source_target_pairs={{0,32},{1,33},{2,34},{3,35},{4,36},{5,37},{6,38},{7,39},{8,40},{9,... | collective-permute-start | bytes 6152 | tf_op jit(solution)/shard_map/ppermute | solution.py:20
  132.6 6.7 %collective-permute-start.29 = (f32[32,16]{0,1:T(8,128)S(1)}, f32[32,16]{0,1:T(8,128)S(1)}, u32[]{:S(2)}, u32[]{:S(2)}) collective-permute-start(f32[32,16]{0,1:T(8,128)S(1)} %add_add_fusion.7), channel_id=1, source_target_pairs={{0,48},{1,49},{2,50},{3,51},{4,52},{5,53},{6,54},{7,55},{8,56},{9,... | collective-permute-start | bytes 6152 | tf_op jit(solution)/shard_map/ppermute | solution.py:20
  139.3 5.2 %collective-permute-start.30 = (f32[32,16]{0,1:T(8,128)S(1)}, f32[32,16]{0,1:T(8,128)S(1)}, u32[]{:S(2)}, u32[]{:S(2)}) collective-permute-start(f32[32,16]{0,1:T(8,128)S(1)} %add_add_fusion.6), channel_id=1, source_target_pairs={{0,64},{1,65},{2,66},{3,67},{4,68},{5,69},{6,70},{7,71},{8,72},{9,... | collective-permute-start | bytes 6152 | tf_op jit(solution)/shard_map/ppermute | solution.py:20
  140.3 5.3 %collective-permute-start.20 = (f32[16,1,2,256]{3,0,2,1:T(8,128)S(1)}, f32[16,1,2,256]{3,0,2,1:T(8,128)S(1)}, u32[]{:S(2)}, u32[]{:S(2)}) collective-permute-start(f32[16,1,2,256]{3,0,2,1:T(8,128)S(1)} %pad_maximum_fusion.6), channel_id=1, source_target_pairs={{0,1},{1,0},{2,3},{3,2},{4,5},{5,4},{6,7},{7,6},{8,9},{9,8},{10,11... | collective-permute-start | bytes 98312 | tf_op jit(solution)/shard_map/ppermute | solution.py:46
  150.3 3.7 %collective-permute-start.31 = (f32[32,16]{0,1:T(8,128)S(1)}, f32[32,16]{0,1:T(8,128)S(1)}, u32[]{:S(2)}, u32[]{:S(2)}) collective-permute-start(f32[32,16]{0,1:T(8,128)S(1)} %pad_maximum_fusion.7), channel_id=1, source_target_pairs={{0,1},{1,0},{2,3},{3,2},{4,5},{5,4},{6,7},{7,6},{8,9},{9,8},{10,11... | collective-permute-start | bytes 6152 | tf_op jit(solution)/shard_map/ppermute | solution.py:20
  150.4 3.6 %collective-permute-start.32 = (f32[32,16]{0,1:T(8,128)S(1)}, f32[32,16]{0,1:T(8,128)S(1)}, u32[]{:S(2)}, u32[]{:S(2)}) collective-permute-start(f32[32,16]{0,1:T(8,128)S(1)} %pad_maximum_fusion.7), channel_id=1, source_target_pairs={{0,2},{1,3},{2,0},{3,1},{4,6},{5,7},{6,4},{7,5},{8,10},{9,11},{10,... | collective-permute-start | bytes 6152 | tf_op jit(solution)/shard_map/ppermute | solution.py:20
  150.4 3.6 %collective-permute-start.33 = (f32[32,16]{0,1:T(8,128)S(1)}, f32[32,16]{0,1:T(8,128)S(1)}, u32[]{:S(2)}, u32[]{:S(2)}) collective-permute-start(f32[32,16]{0,1:T(8,128)S(1)} %pad_maximum_fusion.7), channel_id=1, source_target_pairs={{0,3},{1,2},{2,1},{3,0},{4,7},{5,6},{6,5},{7,4},{8,11},{9,10},{10,... | collective-permute-start | bytes 6152 | tf_op jit(solution)/shard_map/ppermute | solution.py:20
  154.0 5.3 %collective-permute-start.34 = (f32[32,16]{0,1:T(8,128)S(1)}, f32[32,16]{0,1:T(8,128)S(1)}, u32[]{:S(2)}, u32[]{:S(2)}) collective-permute-start(f32[32,16]{0,1:T(8,128)S(1)} %add_add_fusion.5), channel_id=1, source_target_pairs={{0,4},{1,5},{2,6},{3,7},{4,0},{5,1},{6,2},{7,3},{8,12},{9,13},{10,... | collective-permute-start | bytes 6152 | tf_op jit(solution)/shard_map/ppermute | solution.py:20
  156.3 5.2 %collective-permute-start.35 = (f32[32,16]{0,1:T(8,128)S(1)}, f32[32,16]{0,1:T(8,128)S(1)}, u32[]{:S(2)}, u32[]{:S(2)}) collective-permute-start(f32[32,16]{0,1:T(8,128)S(1)} %add_add_fusion.5), channel_id=1, source_target_pairs={{0,8},{1,9},{2,10},{3,11},{4,12},{5,13},{6,14},{7,15},{8,0},{9,1},... | collective-permute-start | bytes 6152 | tf_op jit(solution)/shard_map/ppermute | solution.py:20
  159.2 4.9 %collective-permute-start.36 = (f32[32,16]{0,1:T(8,128)S(1)}, f32[32,16]{0,1:T(8,128)S(1)}, u32[]{:S(2)}, u32[]{:S(2)}) collective-permute-start(f32[32,16]{0,1:T(8,128)S(1)} %add_add_fusion.5), channel_id=1, source_target_pairs={{0,12},{1,13},{2,14},{3,15},{4,8},{5,9},{6,10},{7,11},{8,4},{9,5},... | collective-permute-start | bytes 6152 | tf_op jit(solution)/shard_map/ppermute | solution.py:20
  164.1 5.2 %collective-permute-start.37 = (f32[32,16]{0,1:T(8,128)S(1)}, f32[32,16]{0,1:T(8,128)S(1)}, u32[]{:S(2)}, u32[]{:S(2)}) collective-permute-start(f32[32,16]{0,1:T(8,128)S(1)} %add_add_fusion.4), channel_id=1, source_target_pairs={{0,16},{1,17},{2,18},{3,19},{4,20},{5,21},{6,22},{7,23},{8,24},{9,... | collective-permute-start | bytes 6152 | tf_op jit(solution)/shard_map/ppermute | solution.py:20
  167.0 3.7 %collective-permute-start.38 = (f32[32,16]{0,1:T(8,128)S(1)}, f32[32,16]{0,1:T(8,128)S(1)}, u32[]{:S(2)}, u32[]{:S(2)}) collective-permute-start(f32[32,16]{0,1:T(8,128)S(1)} %add_add_fusion.4), channel_id=1, source_target_pairs={{0,32},{1,33},{2,34},{3,35},{4,36},{5,37},{6,38},{7,39},{8,40},{9,... | collective-permute-start | bytes 6152 | tf_op jit(solution)/shard_map/ppermute | solution.py:20
  169.0 6.1 %collective-permute-start.39 = (f32[32,16]{0,1:T(8,128)S(1)}, f32[32,16]{0,1:T(8,128)S(1)}, u32[]{:S(2)}, u32[]{:S(2)}) collective-permute-start(f32[32,16]{0,1:T(8,128)S(1)} %add_add_fusion.4), channel_id=1, source_target_pairs={{0,48},{1,49},{2,50},{3,51},{4,52},{5,53},{6,54},{7,55},{8,56},{9,... | collective-permute-start | bytes 6152 | tf_op jit(solution)/shard_map/ppermute | solution.py:20
  175.1 5.2 %collective-permute-start.40 = (f32[32,16]{0,1:T(8,128)S(1)}, f32[32,16]{0,1:T(8,128)S(1)}, u32[]{:S(2)}, u32[]{:S(2)}) collective-permute-start(f32[32,16]{0,1:T(8,128)S(1)} %add_add_fusion.3), channel_id=1, source_target_pairs={{0,64},{1,65},{2,66},{3,67},{4,68},{5,69},{6,70},{7,71},{8,72},{9,... | collective-permute-start | bytes 6152 | tf_op jit(solution)/shard_map/ppermute | solution.py:20
  187.4 9.8 %collective-permute-start.41 = (f32[8,1,64,256]{3,2,0,1:T(8,128)S(1)}, f32[8,1,64,256]{3,2,0,1:T(8,128)S(1)}, u32[]{:S(2)}, u32[]{:S(2)}) collective-permute-start(f32[8,1,64,256]{3,2,0,1:T(8,128)S(1)} %bitcast.191), channel_id=1, source_target_pairs={{0,1},{1,0},{2,3},{3,2},{4,5},{5,4},{6,7},{7,6},{8,9},{9,8},{10,11... | collective-permute-start | bytes 1572872 | tf_op jit(solution)/shard_map/ppermute | solution.py:46

commit v3 on v2

--- a/solution.py
+++ b/solution.py
@@ -26,8 +26,7 @@
 
 def radix_groups(n):
     bits = n.bit_length() - 1
-    order = list(range(bits))
-    return [order[i:i + 2] for i in range(0, bits, 2)]
+    return [[0]] + [list(range(i, min(i + 2, bits))) for i in range(1, bits, 2)]
 
 
 def local_inner(left, right, scale):
@@ -122,21 +121,28 @@
     b_b = mm(ct, mm(gram, cmat))
     ab_b = mm(ct, mm(g_sh.T, cmat)) - SIGMA * b_b
 
-    basis = combine(cmat, whole)
-    image = combine(cmat, h_whole)
-    resid = image - combine(rayleigh, basis)
-    both = jnp.concatenate([basis, image - SIGMA * basis], 0)
-    a_basis = both[nb:]
-
-    correction = -resid / shifted
     cr = mm(cmat, rayleigh)
     s_rd = mm(u_sh, cmat) - mm(u_ss, cr)
     h_rd = mm(u_hh, cmat) - mm(u_hs, cr)
     coeff = -mm(ct, s_rd)
     ab_c = -mm(ct, h_rd - SIGMA * s_rd)
     back = ab_c - mm(ab_b, coeff)
-    proj = correction - combine(coeff, basis)
-    moved = stencil(proj, halo(proj), pot) - SIGMA * proj
+    zero = jnp.zeros_like(cmat)
+    weights = jnp.concatenate(
+        [
+            jnp.concatenate([cmat, -SIGMA * cmat, -cr, mm(cmat, coeff)], 1),
+            jnp.concatenate([zero, cmat, cmat, zero], 1),
+        ],
+        0,
+    )
+    parts = combine(weights, jnp.concatenate([whole, h_whole], 0))
+    both = parts[: 2 * nb]
+    basis, a_basis, resid = parts[:nb], parts[nb:2 * nb], parts[2 * nb:3 * nb]
+    correction = -resid / shifted
+    proj = correction - parts[3 * nb:]
+    pieces = halo(proj)
+
+    moved = stencil(proj, pieces, pot) - SIGMA * proj
     correction = correction + (-resid - (moved - combine(back, basis))) / shifted
 
     for sweep in range(2, NSWEEP):

time: 198 us -> 191 us (0.965)
  starting transfers between devices: 76.1 us -> 62.4 us
  waiting for transfers between devices: 80.7 us -> 86.1 us
    ppermute x2, starting transfers between devices: 14.9 us -> 1.29 us  [halo(): after = lax.ppermute(value, 'space', down)]
    ppermute x1, waiting for transfers between devices: 0.01 us -> 8.77 us  [local(): lax.ppermute(give_rows, AXES, cross_down)]
    ppermute x1, waiting for transfers between devices: 8.97 us -> 0.22 us  [local(): lax.ppermute(give_rows, AXES, cross_up)]
    ppermute x2, waiting for transfers between devices: 0.01 us -> 7.83 us  [halo(): after = lax.ppermute(value, 'space', down)]
    ppermute x30, waiting for transfers between devices: 44.2 us -> 38.3 us  [allsum(): vals[m] = lax.ppermute(x, AXES, [(i, i ^ mask) for i in range(n)])]
    ppermute x2, waiting for transfers between devices: 4.42 us -> 7.63 us  [halo(): before = lax.ppermute(value, 'space', up)]
    dot_general x9 -> x6, matrix products: 10.6 us -> 11.9 us  [combine(): return jnp.einsum('kj,kzyx->jzyx', coeff, vectors, precision=PREC)]
  transfers between devices with their start and end apart: 42 -> 42, of which waited for: 26 -> 30; matrix products, arithmetic and copies ran while one was open for 3% -> 3% of each run, Pallas kernels for 0% -> 0%
where the time goes in v3:
time: 191 us
  waiting for transfers between devices  86.1 us (45%)
  starting transfers between devices  62.4 us (33%)
  matrix products  24 us (13%)
  other arithmetic  12.1 us (6%)
  local copies, waits for them, and re-layouts  5.39 us (3%)
    ppermute x30, starting transfers between devices, allsum(): vals[m] = lax.ppermute(x, AXES, [(i, i ^ mask) for i in range(n)])  42.6 us
    ppermute x30, waiting for transfers between devices, allsum(): vals[m] = lax.ppermute(x, AXES, [(i, i ^ mask) for i in range(n)])  38.3 us
    ppermute x4, waiting for transfers between devices, swap_vec(): return lax.ppermute(value, 'vec', [(0, 1), (1, 0)])  23.4 us
    dot_general x6, matrix products, combine(): return jnp.einsum('kj,kzyx->jzyx', coeff, vectors, precision=PREC)  11.9 us
    ppermute x1, waiting for transfers between devices, local(): lax.ppermute(give_rows, AXES, cross_down)  8.77 us
    dot_general x4, matrix products, local_inner(): return jnp.einsum('kzyx,jzyx->kj', left, right, precision=PREC) * scale  8.11 us
    ppermute x2, waiting for transfers between devices, halo(): after = lax.ppermute(value, 'space', down)  7.83 us
    ppermute x2, waiting for transfers between devices, halo(): before = lax.ppermute(value, 'space', up)  7.63 us
  transfers between devices with their start and end apart: 42, of which 30 were waited for; matrix products, arithmetic and copies ran while one was open for 3% of the time, Pallas kernels for 0%

profile of v3, /device:TPU:0, one launch (start us, length us, event | category | flops | bytes accessed | tf_op | source)
XLA Modules:
  0.0 190.9 jit_solution(5618293182161684396)
XLA Ops:
  0.6 1.8 copy.12
  2.7 2.1 %collective-permute-start = (f32[8,1,66,256]{3,0,2,1:T(8,128)S(1)}, f32[8,1,66,256]{3,0,2,1:T(8,128)S(1)}, u32[]{:S(2)}, u32[]{:S(2)}) collective-permute-start(f32[8,1,66,256]{3,0,2,1:T(8,128)S(1)} %get-tuple-element.16), channel_id=1, source_target_pairs={{0,1},{1,0},{2,3},{3,2},{4,5},{5,4},{6,7},{7,6},{8,9},{9,8},{10,11... | collective-permute-start | bytes 1622024 | tf_op jit(solution)/shard_map/ppermute | solution.py:45
  4.8 1.0 constant_dynamic-slice_fusion
  5.8 6.3 %collective-permute-start.4 = (f32[8,1,64,256]{3,0,2,1:T(8,128)}, f32[8,1,64,256]{3,0,2,1:T(8,128)S(1)}, u32[]{:S(2)}, u32[]{:S(2)}) collective-permute-start(f32[8,1,64,256]{3,0,2,1:T(8,128)} %get-tuple-element.13), channel_id=1, source_target_pairs={{3,0},{2,1},{5,2},{4,3},{7,4},{6,5},{9,6},{8,7},{11,8},{10,9},{13,... | collective-permute-start | bytes 1572872 | tf_op jit(solution)/shard_map/ppermute | solution.py:100
  12.1 7.0 %collective-permute-start.3 = (f32[8,1,64,256]{3,0,2,1:T(8,128)}, f32[8,1,64,256]{3,0,2,1:T(8,128)}, u32[]{:S(2)}, u32[]{:S(2)}) collective-permute-start(f32[8,1,64,256]{3,0,2,1:T(8,128)} %get-tuple-element.14), channel_id=1, source_target_pairs={{2,0},{3,1},{4,2},{5,3},{6,4},{7,5},{8,6},{9,7},{10,8},{11,9},{12,... | collective-permute-start | bytes 1572872 | tf_op jit(solution)/shard_map/ppermute | solution.py:100
  19.2 9.9 %collective-permute-done = f32[8,1,66,256]{3,0,2,1:T(8,128)S(1)} collective-permute-done((f32[8,1,66,256]{3,0,2,1:T(8,128)S(1)}, f32[8,1,66,256]{3,0,2,1:T(8,128)S(1)}, u32[]{:S(2)}, u32[]{:S(2)}) %collective-permute-start) | collective-permute-done | bytes 540704 | tf_op jit(solution)/shard_map/ppermute | solution.py:45
  29.9 8.8 %collective-permute-done.4 = f32[8,1,64,256]{3,0,2,1:T(8,128)S(1)} collective-permute-done((f32[8,1,64,256]{3,0,2,1:T(8,128)}, f32[8,1,64,256]{3,0,2,1:T(8,128)S(1)}, u32[]{:S(2)}, u32[]{:S(2)}) %collective-permute-start.4) | collective-permute-done | bytes 524320 | tf_op jit(solution)/shard_map/ppermute | solution.py:100
  38.9 2.3 %broadcast_divide_fusion = (f32[16,1,64,256]{3,0,2,1:T(8,128)S(1)}, f32[16,1,64,256]{3,0,2,1:T(8,128)S(1)}, f32[16,1,64,256]{3,0,2,1:T(8,128)S(1)}) fusion(f32[64,256]{1,0:T(8,128)S(1)} %get-tuple-element.34, f32[16,1,64,1]{3,0,2,1:T(8,128)S(1)} %get-tuple-element.10, f32[16,1,64,255]{3,0,2,1:T(8,128)S(1)} %get-tuple-element.12, ...), kind=kLoop, calls=%fused_computation.86 | loop fusion | flops 4456448 | bytes 10616833 | tf_op jit(solution)/shard_map/div | solution.py:110
  41.2 3.4 %fusion.58 = f32[32,64]{0,1:T(8,128)S(1)} fusion(f32[16,1,64,256]{3,0,2,1:T(8,128)S(1)} %get-tuple-element.6, f32[16,1,64,256]{3,0,2,1:T(8,128)S(1)} %get-tuple-element.8, f32[16,1,64,256]{3,0,2,1:T(8,128)S(1)} %get-tuple-element.7, f32[16,1,64,256]{3,0,2,1:T(8,128)S(1)} %slice.216), kind=kOutput, calls=%fused_computation.83 | convolution fusion | flops 406325248 | bytes 4202496 | tf_op jit(solution)/shard_map/kzyx,jzyx->kj/dot_general | solution.py:33
  44.6 1.3 collective-permute-start.5
  45.9 2.7 %collective-permute-done.5 = f32[32,64]{0,1:T(8,128)S(1)} collective-permute-done((f32[32,64]{0,1:T(8,128)S(1)}, f32[32,64]{0,1:T(8,128)S(1)}, u32[]{:S(2)}, u32[]{:S(2)}) %collective-permute-start.5) | collective-permute-done | bytes 8224 | tf_op jit(solution)/shard_map/ppermute | solution.py:20
  49.0 1.2 collective-permute-start.7
  50.5 1.8 collective-permute-done.8
  52.3 0.8 collective-permute-done.7
  53.1 6.1 %collective-permute-start.11 = (f32[32,64]{0,1:T(8,128)S(1)}, f32[32,64]{0,1:T(8,128)S(1)}, u32[]{:S(2)}, u32[]{:S(2)}) collective-permute-start(f32[32,64]{0,1:T(8,128)S(1)} %add_add_fusion.2), channel_id=1, source_target_pairs={{0,24},{1,25},{2,26},{3,27},{4,28},{5,29},{6,30},{7,31},{8,16},{9,... | collective-permute-start | bytes 24584 | tf_op jit(solution)/shard_map/ppermute | solution.py:20
  59.1 0.8 collective-permute-start.9
  59.9 1.1 collective-permute-done.11
  61.0 3.5 %collective-permute-done.10 = f32[32,64]{0,1:T(8,128)S(1)} collective-permute-done((f32[32,64]{0,1:T(8,128)S(1)}, f32[32,64]{0,1:T(8,128)S(1)}, u32[]{:S(2)}, u32[]{:S(2)}) %collective-permute-start.10) | collective-permute-done | bytes 8224 | tf_op jit(solution)/shard_map/ppermute | solution.py:20
  64.6 3.1 %collective-permute-start.14 = (f32[32,64]{0,1:T(8,128)S(1)}, f32[32,64]{0,1:T(8,128)S(1)}, u32[]{:S(2)}, u32[]{:S(2)}) collective-permute-start(f32[32,64]{0,1:T(8,128)S(1)} %add_add_fusion.1), channel_id=1, source_target_pairs={{0,96},{1,97},{2,98},{3,99},{4,100},{5,101},{6,102},{7,103},{8,104... | collective-permute-start | bytes 24584 | tf_op jit(solution)/shard_map/ppermute | solution.py:20
  68.7 1.0 collective-permute-done.14
  69.8 3.3 %collective-permute-done.13 = f32[32,64]{0,1:T(8,128)S(1)} collective-permute-done((f32[32,64]{0,1:T(8,128)S(1)}, f32[32,64]{0,1:T(8,128)S(1)}, u32[]{:S(2)}, u32[]{:S(2)}) %collective-permute-start.13) | collective-permute-done | bytes 8224 | tf_op jit(solution)/shard_map/ppermute | solution.py:20
  73.2 1.5 cholesky.44
  76.0 1.2 custom-call.6
  79.3 3.6 %fusion.9 = f32[64,64,256]{2,0,1:T(8,128)S(1)} fusion(f32[16,1,64,256]{3,0,2,1:T(8,128)S(1)} %get-tuple-element.7, f32[16,1,64,256]{3,0,2,1:T(8,128)S(1)} %slice.216, f32[16,16]{1,0:T(8,128)S(1)} %cholesky.45, f32[16,16]{1,0:T(8,128)S(1)} %bitcast.162, f32[16,16]{1,0:T(8,128)S(1)} %fusion.128, f32[16,16]{1,0:T(8,128)S(1)} %get-tuple-element.39, ...), kind=kOutput, calls=%fused_computation.11 | convolution fusion | flops 403191808 | bytes 6296576 | tf_op jit(solution)/shard_map/kj,kzyx->jzyx/dot_general | solution.py:37
  83.3 0.9 collective-permute-start.16
  84.7 1.7 collective-permute-start.17
  87.6 1.1 collective-permute-done.17
  88.7 7.8 %collective-permute-done.16 = f32[16,1,64,256]{3,0,2,1:T(8,128)S(1)} collective-permute-done((f32[16,1,64,256]{3,0,2,1:T(8,128)S(1)}, f32[16,1,64,256]{3,0,2,1:T(8,128)S(1)}, u32[]{:S(2)}, u32[]{:S(2)}) %collective-permute-start.16) | collective-permute-done | bytes 1048608 | tf_op jit(solution)/shard_map/ppermute | solution.py:55
  96.5 7.6 %collective-permute-done.15 = f32[16,1,64,256]{3,0,2,1:T(8,128)S(1)} collective-permute-done((f32[16,1,64,256]{3,0,2,1:T(8,128)S(1)}, f32[16,1,64,256]{3,0,2,1:T(8,128)S(1)}, u32[]{:S(2)}, u32[]{:S(2)}) %collective-permute-start.15) | collective-permute-done | bytes 1048608 | tf_op jit(solution)/shard_map/ppermute | solution.py:54
  104.1 1.9 %fusion.13 = f32[16,1,64,256]{3,0,2,1:T(8,128)S(1)} fusion(f32[16,16,1]{0,1,2:T(8,128)S(1)} %fusion.27, f32[16,1,1,256]{3,0,2,1:T(8,128)S(1)} %get-tuple-element.38, f32[16,1,64,256]{3,0,2,1:T(8,128)S(1)} %fusion.53, f32[16,1,1,256]{3,0,2,1:T(8,128)S(1)} %get-tuple-element.37, f32[16,1,64,255]{3,0,2,1:T(8,128)S(1)} %get-tuple-element.26, ...), kind=kOutput, calls=%fused_computation.19 | convolution fusion | flops 55574528 | bytes 10723328 | tf_op jit(solution)/shard_map/kj,kzyx->jzyx/dot_general | solution.py:37
  106.1 1.7 fusion.29
  107.8 1.3 collective-permute-start.21
  109.6 1.9 collective-permute-done.21
  111.5 1.9 collective-permute-start.22
  113.7 0.9 collective-permute-done.24
  114.6 2.1 %collective-permute-done.23 = f32[32,16]{0,1:T(8,128)S(1)} collective-permute-done((f32[32,16]{0,1:T(8,128)S(1)}, f32[32,16]{0,1:T(8,128)S(1)}, u32[]{:S(2)}, u32[]{:S(2)}) %collective-permute-start.23) | collective-permute-done | bytes 2080 | tf_op jit(solution)/shard_map/ppermute | solution.py:20
  116.8 6.0 %collective-permute-start.27 = (f32[32,16]{0,1:T(8,128)S(1)}, f32[32,16]{0,1:T(8,128)S(1)}, u32[]{:S(2)}, u32[]{:S(2)}) collective-permute-start(f32[32,16]{0,1:T(8,128)S(1)} %add_add_fusion.8), channel_id=1, source_target_pairs={{0,24},{1,25},{2,26},{3,27},{4,28},{5,29},{6,30},{7,31},{8,16},{9,... | collective-permute-start | bytes 6152 | tf_op jit(solution)/shard_map/ppermute | solution.py:20
  122.8 0.9 collective-permute-start.26
  124.6 5.2 %collective-permute-done.26 = f32[32,16]{0,1:T(8,128)S(1)} collective-permute-done((f32[32,16]{0,1:T(8,128)S(1)}, f32[32,16]{0,1:T(8,128)S(1)}, u32[]{:S(2)}, u32[]{:S(2)}) %collective-permute-start.26) | collective-permute-done | bytes 2080 | tf_op jit(solution)/shard_map/ppermute | solution.py:20
  129.9 1.2 collective-permute-start.29
  131.1 2.8 %collective-permute-start.28 = (f32[32,16]{0,1:T(8,128)S(1)}, f32[32,16]{0,1:T(8,128)S(1)}, u32[]{:S(2)}, u32[]{:S(2)}) collective-permute-start(f32[32,16]{0,1:T(8,128)S(1)} %add_add_fusion.7), channel_id=1, source_target_pairs={{0,32},{1,33},{2,34},{3,35},{4,36},{5,37},{6,38},{7,39},{8,40},{9,... | collective-permute-start | bytes 6152 | tf_op jit(solution)/shard_map/ppermute | solution.py:20
  135.8 1.0 convolution_bitcast_fusion.1
  136.9 1.8 collective-permute-done.20
  138.7 2.0 %fusion.18 = f32[16,1,64,256]{3,0,2,1:T(8,128)S(1)} fusion(f32[16,1,64,256]{3,0,2,1:T(8,128)S(1)} %fusion.13, f32[16,1,64,256]{3,0,2,1:T(8,128)S(1)} %convolution_bitcast_fusion.1, f32[64,64,256]{2,0,1:T(8,128)S(1)} %fusion.9, f32[16,1,1,256]{3,0,2,1:T(8,128)S(1)} %get-tuple-element.36, f32[16,1,1,256]{3,0,2,1:T(8,128)S(1)} %get-tuple-element.35, ...), kind=kOutput, calls=%fused_computation.24 | convolution fusion | flops 55312384 | bytes 10657792 | tf_op jit(solution)/shard_map/kj,kzyx->jzyx/dot_general | solution.py:37
  140.7 1.5 fusion.25
  142.1 1.5 fusion.26
  144.1 3.3 %collective-permute-done.31 = f32[32,16]{0,1:T(8,128)S(1)} collective-permute-done((f32[32,16]{0,1:T(8,128)S(1)}, f32[32,16]{0,1:T(8,128)S(1)}, u32[]{:S(2)}, u32[]{:S(2)}) %collective-permute-start.31) | collective-permute-done | bytes 2080 | tf_op jit(solution)/shard_map/ppermute | solution.py:20
  147.5 2.4 %collective-permute-start.33 = (f32[32,16]{0,1:T(8,128)S(1)}, f32[32,16]{0,1:T(8,128)S(1)}, u32[]{:S(2)}, u32[]{:S(2)}) collective-permute-start(f32[32,16]{0,1:T(8,128)S(1)} %fusion.160), channel_id=1, source_target_pairs={{0,4},{1,5},{2,6},{3,7},{4,0},{5,1},{6,2},{7,3},{8,12},{9,13},{10,... | collective-permute-start | bytes 6152 | tf_op jit(solution)/shard_map/ppermute | solution.py:20
  150.6 1.0 collective-permute-done.33
  151.6 5.1 %collective-permute-start.37 = (f32[32,16]{0,1:T(8,128)S(1)}, f32[32,16]{0,1:T(8,128)S(1)}, u32[]{:S(2)}, u32[]{:S(2)}) collective-permute-start(f32[32,16]{0,1:T(8,128)S(1)} %add_add_fusion.5), channel_id=1, source_target_pairs={{0,24},{1,25},{2,26},{3,27},{4,28},{5,29},{6,30},{7,31},{8,16},{9,... | collective-permute-start | bytes 6152 | tf_op jit(solution)/shard_map/ppermute | solution.py:20
  156.7 2.1 %collective-permute-start.36 = (f32[32,16]{0,1:T(8,128)S(1)}, f32[32,16]{0,1:T(8,128)S(1)}, u32[]{:S(2)}, u32[]{:S(2)}) collective-permute-start(f32[32,16]{0,1:T(8,128)S(1)} %add_add_fusion.5), channel_id=1, source_target_pairs={{0,16},{1,17},{2,18},{3,19},{4,20},{5,21},{6,22},{7,23},{8,24},{9,... | collective-permute-start | bytes 6152 | tf_op jit(solution)/shard_map/ppermute | solution.py:20
  159.2 2.6 %collective-permute-done.36 = f32[32,16]{0,1:T(8,128)S(1)} collective-permute-done((f32[32,16]{0,1:T(8,128)S(1)}, f32[32,16]{0,1:T(8,128)S(1)}, u32[]{:S(2)}, u32[]{:S(2)}) %collective-permute-start.36) | collective-permute-done | bytes 2080 | tf_op jit(solution)/shard_map/ppermute | solution.py:20
  161.8 2.1 %collective-permute-done.35 = f32[32,16]{0,1:T(8,128)S(1)} collective-permute-done((f32[32,16]{0,1:T(8,128)S(1)}, f32[32,16]{0,1:T(8,128)S(1)}, u32[]{:S(2)}, u32[]{:S(2)}) %collective-permute-start.35) | collective-permute-done | bytes 2080 | tf_op jit(solution)/shard_map/ppermute | solution.py:20
  163.9 0.8 collective-permute-start.40
  164.7 1.4 collective-permute-start.39
  166.2 1.8 collective-permute-start.38
  168.7 1.1 collective-permute-done.39
  169.9 2.2 %fusion.20 = f32[16,64,256]{2,0,1:T(8,128)S(1)} fusion(f32[16,1,64,256]{3,0,2,1:T(8,128)S(1)} %fusion.18, f32[64,64,256]{2,0,1:T(8,128)} %copy-done, f32[32,16]{0,1:T(8,128)S(1)} %add_add_fusion.3), kind=kOutput, calls=%fused_computation.26 | convolution fusion | flops 50593792 | bytes 3147776 | tf_op jit(solution)/shard_map/kj,kzyx->jzyx/dot_general | solution.py:37
  172.7 1.5 cholesky.55
  175.5 1.2 custom-call.7
  176.9 1.0 fusion.130
  178.2 0.9 collective-permute-start.41
  179.3 10.6 %collective-permute-done.41 = f32[8,1,64,256]{3,2,0,1:T(8,128)S(1)} collective-permute-done((f32[8,1,64,256]{3,2,0,1:T(8,128)S(1)}, f32[8,1,64,256]{3,2,0,1:T(8,128)S(1)}, u32[]{:S(2)}, u32[]{:S(2)}) %collective-permute-start.41) | collective-permute-done | bytes 524320 | tf_op jit(solution)/shard_map/ppermute | solution.py:45
  189.9 1.0 fusion.49
  (112 shorter events, 17.1 us)
Async XLA Ops:
  2.6 16.6 %copy-start.1 = (f32[1,128,256]{2,1,0:T(8,128)S(1)}, f32[1,128,256]{2,1,0:T(8,128)}, u32[]{:S(2)}) copy-start(f32[1,128,256]{2,1,0:T(8,128)} %param.5) | copy-start | bytes 393220
  2.7 26.5 %collective-permute-start = (f32[8,1,66,256]{3,0,2,1:T(8,128)S(1)}, f32[8,1,66,256]{3,0,2,1:T(8,128)S(1)}, u32[]{:S(2)}, u32[]{:S(2)}) collective-permute-start(f32[8,1,66,256]{3,0,2,1:T(8,128)S(1)} %get-tuple-element.16), channel_id=1, source_target_pairs={{0,1},{1,0},{2,3},{3,2},{4,5},{5,4},{6,7},{7,6},{8,9},{9,8},{10,11... | collective-permute-start | bytes 1622024 | tf_op jit(solution)/shard_map/ppermute | solution.py:45
  5.8 32.9 %collective-permute-start.4 = (f32[8,1,64,256]{3,0,2,1:T(8,128)}, f32[8,1,64,256]{3,0,2,1:T(8,128)S(1)}, u32[]{:S(2)}, u32[]{:S(2)}) collective-permute-start(f32[8,1,64,256]{3,0,2,1:T(8,128)} %get-tuple-element.13), channel_id=1, source_target_pairs={{3,0},{2,1},{5,2},{4,3},{7,4},{6,5},{9,6},{8,7},{11,8},{10,9},{13,... | collective-permute-start | bytes 1572872 | tf_op jit(solution)/shard_map/ppermute | solution.py:100
  12.1 26.7 %collective-permute-start.2 = (f32[8,1,64,256]{3,0,2,1:T(8,128)}, f32[8,1,64,256]{3,0,2,1:T(8,128)S(1)}, u32[]{:S(2)}, u32[]{:S(2)}) collective-permute-start(f32[8,1,64,256]{3,0,2,1:T(8,128)} %get-tuple-element.13), channel_id=1, source_target_pairs={{0,3},{1,2},{2,5},{3,4},{4,7},{5,6},{6,9},{7,8},{8,11},{9,10},{10,... | collective-permute-start | bytes 1572872 | tf_op jit(solution)/shard_map/ppermute | solution.py:99
  12.1 26.7 %collective-permute-start.3 = (f32[8,1,64,256]{3,0,2,1:T(8,128)}, f32[8,1,64,256]{3,0,2,1:T(8,128)}, u32[]{:S(2)}, u32[]{:S(2)}) collective-permute-start(f32[8,1,64,256]{3,0,2,1:T(8,128)} %get-tuple-element.14), channel_id=1, source_target_pairs={{2,0},{3,1},{4,2},{5,3},{6,4},{7,5},{8,6},{9,7},{10,8},{11,9},{12,... | collective-permute-start | bytes 1572872 | tf_op jit(solution)/shard_map/ppermute | solution.py:100
  19.2 19.7 %collective-permute-start.1 = (f32[8,1,64,256]{3,0,2,1:T(8,128)}, f32[8,1,64,256]{3,0,2,1:T(8,128)}, u32[]{:S(2)}, u32[]{:S(2)}) collective-permute-start(f32[8,1,64,256]{3,0,2,1:T(8,128)} %get-tuple-element.14), channel_id=1, source_target_pairs={{0,2},{1,3},{2,4},{3,5},{4,6},{5,7},{6,8},{7,9},{8,10},{9,11},{10,... | collective-permute-start | bytes 1572872 | tf_op jit(solution)/shard_map/ppermute | solution.py:99
  44.6 4.0 %collective-permute-start.5 = (f32[32,64]{0,1:T(8,128)S(1)}, f32[32,64]{0,1:T(8,128)S(1)}, u32[]{:S(2)}, u32[]{:S(2)}) collective-permute-start(f32[32,64]{0,1:T(8,128)S(1)} %fusion.58), channel_id=1, source_target_pairs={{0,1},{1,0},{2,3},{3,2},{4,5},{5,4},{6,7},{7,6},{8,9},{9,8},{10,11... | collective-permute-start | bytes 24584 | tf_op jit(solution)/shard_map/ppermute | solution.py:20
  48.6 3.6 %collective-permute-start.8 = (f32[32,64]{0,1:T(8,128)S(1)}, f32[32,64]{0,1:T(8,128)S(1)}, u32[]{:S(2)}, u32[]{:S(2)}) collective-permute-start(f32[32,64]{0,1:T(8,128)S(1)} %add.197), channel_id=1, source_target_pairs={{0,6},{1,7},{2,4},{3,5},{4,2},{5,3},{6,0},{7,1},{8,14},{9,15},{10,... | collective-permute-start | bytes 24584 | tf_op jit(solution)/shard_map/ppermute | solution.py:20
  49.0 4.0 %collective-permute-start.7 = (f32[32,64]{0,1:T(8,128)S(1)}, f32[32,64]{0,1:T(8,128)S(1)}, u32[]{:S(2)}, u32[]{:S(2)}) collective-permute-start(f32[32,64]{0,1:T(8,128)S(1)} %add.197), channel_id=1, source_target_pairs={{0,4},{1,5},{2,6},{3,7},{4,0},{5,1},{6,2},{7,3},{8,12},{9,13},{10,... | collective-permute-start | bytes 24584 | tf_op jit(solution)/shard_map/ppermute | solution.py:20
  50.2 2.9 %collective-permute-start.6 = (f32[32,64]{0,1:T(8,128)S(1)}, f32[32,64]{0,1:T(8,128)S(1)}, u32[]{:S(2)}, u32[]{:S(2)}) collective-permute-start(f32[32,64]{0,1:T(8,128)S(1)} %add.197), channel_id=1, source_target_pairs={{0,2},{1,3},{2,0},{3,1},{4,6},{5,7},{6,4},{7,5},{8,10},{9,11},{10,... | collective-permute-start | bytes 24584 | tf_op jit(solution)/shard_map/ppermute | solution.py:20
  53.1 8.0 %collective-permute-start.11 = (f32[32,64]{0,1:T(8,128)S(1)}, f32[32,64]{0,1:T(8,128)S(1)}, u32[]{:S(2)}, u32[]{:S(2)}) collective-permute-start(f32[32,64]{0,1:T(8,128)S(1)} %add_add_fusion.2), channel_id=1, source_target_pairs={{0,24},{1,25},{2,26},{3,27},{4,28},{5,29},{6,30},{7,31},{8,16},{9,... | collective-permute-start | bytes 24584 | tf_op jit(solution)/shard_map/ppermute | solution.py:20
  59.1 5.4 %collective-permute-start.10 = (f32[32,64]{0,1:T(8,128)S(1)}, f32[32,64]{0,1:T(8,128)S(1)}, u32[]{:S(2)}, u32[]{:S(2)}) collective-permute-start(f32[32,64]{0,1:T(8,128)S(1)} %add_add_fusion.2), channel_id=1, source_target_pairs={{0,16},{1,17},{2,18},{3,19},{4,20},{5,21},{6,22},{7,23},{8,24},{9,... | collective-permute-start | bytes 24584 | tf_op jit(solution)/shard_map/ppermute | solution.py:20
  59.1 5.4 %collective-permute-start.9 = (f32[32,64]{0,1:T(8,128)S(1)}, f32[32,64]{0,1:T(8,128)S(1)}, u32[]{:S(2)}, u32[]{:S(2)}) collective-permute-start(f32[32,64]{0,1:T(8,128)S(1)} %add_add_fusion.2), channel_id=1, source_target_pairs={{0,8},{1,9},{2,10},{3,11},{4,12},{5,13},{6,14},{7,15},{8,0},{9,1},... | collective-permute-start | bytes 24584 | tf_op jit(solution)/shard_map/ppermute | solution.py:20
  64.6 5.2 %collective-permute-start.14 = (f32[32,64]{0,1:T(8,128)S(1)}, f32[32,64]{0,1:T(8,128)S(1)}, u32[]{:S(2)}, u32[]{:S(2)}) collective-permute-start(f32[32,64]{0,1:T(8,128)S(1)} %add_add_fusion.1), channel_id=1, source_target_pairs={{0,96},{1,97},{2,98},{3,99},{4,100},{5,101},{6,102},{7,103},{8,104... | collective-permute-start | bytes 24584 | tf_op jit(solution)/shard_map/ppermute | solution.py:20
  67.7 5.4 %collective-permute-start.13 = (f32[32,64]{0,1:T(8,128)S(1)}, f32[32,64]{0,1:T(8,128)S(1)}, u32[]{:S(2)}, u32[]{:S(2)}) collective-permute-start(f32[32,64]{0,1:T(8,128)S(1)} %add_add_fusion.1), channel_id=1, source_target_pairs={{0,64},{1,65},{2,66},{3,67},{4,68},{5,69},{6,70},{7,71},{8,72},{9,... | collective-permute-start | bytes 24584 | tf_op jit(solution)/shard_map/ppermute | solution.py:20
  68.3 4.8 %collective-permute-start.12 = (f32[32,64]{0,1:T(8,128)S(1)}, f32[32,64]{0,1:T(8,128)S(1)}, u32[]{:S(2)}, u32[]{:S(2)}) collective-permute-start(f32[32,64]{0,1:T(8,128)S(1)} %add_add_fusion.1), channel_id=1, source_target_pairs={{0,32},{1,33},{2,34},{3,35},{4,36},{5,37},{6,38},{7,39},{8,40},{9,... | collective-permute-start | bytes 24584 | tf_op jit(solution)/shard_map/ppermute | solution.py:20
  78.2 4.8 %copy-start.2 = (f32[16,16]{1,0:T(8,128)}, f32[16,16]{1,0:T(8,128)S(1)}, u32[]{:S(2)}) copy-start(f32[16,16]{1,0:T(8,128)S(1)} %fusion.127) | copy-start | bytes 3076
  83.0 59.1 %copy-start = (f32[64,64,256]{2,0,1:T(8,128)}, f32[64,64,256]{2,0,1:T(8,128)S(1)}, u32[]{:S(2)}) copy-start(f32[64,64,256]{2,0,1:T(8,128)S(1)} %fusion.9) | copy-start | bytes 12582916
  83.3 13.2 %collective-permute-start.16 = (f32[16,1,64,256]{3,0,2,1:T(8,128)S(1)}, f32[16,1,64,256]{3,0,2,1:T(8,128)S(1)}, u32[]{:S(2)}, u32[]{:S(2)}) collective-permute-start(f32[16,1,64,256]{3,0,2,1:T(8,128)S(1)} %fusion.53), channel_id=1, source_target_pairs={{2,0},{4,2},{6,4},{8,6},{10,8},{12,10},{14,12},{16,14},{18,16},{20... | collective-permute-start | bytes 3145736 | tf_op jit(solution)/shard_map/ppermute | solution.py:55
  84.2 19.9 %collective-permute-start.15 = (f32[16,1,64,256]{3,0,2,1:T(8,128)S(1)}, f32[16,1,64,256]{3,0,2,1:T(8,128)S(1)}, u32[]{:S(2)}, u32[]{:S(2)}) collective-permute-start(f32[16,1,64,256]{3,0,2,1:T(8,128)S(1)} %fusion.53), channel_id=1, source_target_pairs={{0,2},{2,4},{4,6},{6,8},{8,10},{10,12},{12,14},{14,16},{16,18},{18... | collective-permute-start | bytes 3145736 | tf_op jit(solution)/shard_map/ppermute | solution.py:54
  84.7 4.0 %collective-permute-start.17 = (f32[16,1,2,256]{3,0,2,1:T(8,128)S(1)}, f32[16,1,2,256]{3,0,2,1:T(8,128)S(1)}, u32[]{:S(2)}, u32[]{:S(2)}) collective-permute-start(f32[16,1,2,256]{3,0,2,1:T(8,128)S(1)} %pad_maximum_fusion.5), channel_id=1, source_target_pairs={{0,1},{1,0},{2,3},{3,2},{4,5},{5,4},{6,7},{7,6},{8,9},{9,8},{10,11... | collective-permute-start | bytes 98312 | tf_op jit(solution)/shard_map/ppermute | solution.py:45
  107.8 3.7 %collective-permute-start.21 = (f32[32,16]{0,1:T(8,128)S(1)}, f32[32,16]{0,1:T(8,128)S(1)}, u32[]{:S(2)}, u32[]{:S(2)}) collective-permute-start(f32[32,16]{0,1:T(8,128)S(1)} %fusion.29), channel_id=1, source_target_pairs={{0,1},{1,0},{2,3},{3,2},{4,5},{5,4},{6,7},{7,6},{8,9},{9,8},{10,11... | collective-permute-start | bytes 6152 | tf_op jit(solution)/shard_map/ppermute | solution.py:20
  109.1 29.6 %collective-permute-start.19 = (f32[16,1,64,256]{3,0,2,1:T(8,128)S(1)}, f32[16,1,64,256]{3,0,2,1:T(8,128)S(1)}, u32[]{:S(2)}, u32[]{:S(2)}) collective-permute-start(f32[16,1,64,256]{3,0,2,1:T(8,128)S(1)} %fusion.13), channel_id=1, source_target_pairs={{2,0},{4,2},{6,4},{8,6},{10,8},{12,10},{14,12},{16,14},{18,16},{20... | collective-permute-start | bytes 3145736 | tf_op jit(solution)/shard_map/ppermute | solution.py:55
  109.5 29.2 %collective-permute-start.18 = (f32[16,1,64,256]{3,0,2,1:T(8,128)S(1)}, f32[16,1,64,256]{3,0,2,1:T(8,128)S(1)}, u32[]{:S(2)}, u32[]{:S(2)}) collective-permute-start(f32[16,1,64,256]{3,0,2,1:T(8,128)S(1)} %fusion.13), channel_id=1, source_target_pairs={{0,2},{2,4},{4,6},{6,8},{8,10},{10,12},{12,14},{14,16},{16,18},{18... | collective-permute-start | bytes 3145736 | tf_op jit(solution)/shard_map/ppermute | solution.py:54
  111.5 3.2 %collective-permute-start.24 = (f32[32,16]{0,1:T(8,128)S(1)}, f32[32,16]{0,1:T(8,128)S(1)}, u32[]{:S(2)}, u32[]{:S(2)}) collective-permute-start(f32[32,16]{0,1:T(8,128)S(1)} %add.218), channel_id=1, source_target_pairs={{0,6},{1,7},{2,4},{3,5},{4,2},{5,3},{6,0},{7,1},{8,14},{9,15},{10,... | collective-permute-start | bytes 6152 | tf_op jit(solution)/shard_map/ppermute | solution.py:20
  111.5 5.3 %collective-permute-start.23 = (f32[32,16]{0,1:T(8,128)S(1)}, f32[32,16]{0,1:T(8,128)S(1)}, u32[]{:S(2)}, u32[]{:S(2)}) collective-permute-start(f32[32,16]{0,1:T(8,128)S(1)} %add.218), channel_id=1, source_target_pairs={{0,4},{1,5},{2,6},{3,7},{4,0},{5,1},{6,2},{7,3},{8,12},{9,13},{10,... | collective-permute-start | bytes 6152 | tf_op jit(solution)/shard_map/ppermute | solution.py:20
  111.5 5.3 %collective-permute-start.22 = (f32[32,16]{0,1:T(8,128)S(1)}, f32[32,16]{0,1:T(8,128)S(1)}, u32[]{:S(2)}, u32[]{:S(2)}) collective-permute-start(f32[32,16]{0,1:T(8,128)S(1)} %add.218), channel_id=1, source_target_pairs={{0,2},{1,3},{2,0},{3,1},{4,6},{5,7},{6,4},{7,5},{8,10},{9,11},{10,... | collective-permute-start | bytes 6152 | tf_op jit(solution)/shard_map/ppermute | solution.py:20
  116.8 7.8 %collective-permute-start.27 = (f32[32,16]{0,1:T(8,128)S(1)}, f32[32,16]{0,1:T(8,128)S(1)}, u32[]{:S(2)}, u32[]{:S(2)}) collective-permute-start(f32[32,16]{0,1:T(8,128)S(1)} %add_add_fusion.8), channel_id=1, source_target_pairs={{0,24},{1,25},{2,26},{3,27},{4,28},{5,29},{6,30},{7,31},{8,16},{9,... | collective-permute-start | bytes 6152 | tf_op jit(solution)/shard_map/ppermute | solution.py:20
  122.8 7.0 %collective-permute-start.26 = (f32[32,16]{0,1:T(8,128)S(1)}, f32[32,16]{0,1:T(8,128)S(1)}, u32[]{:S(2)}, u32[]{:S(2)}) collective-permute-start(f32[32,16]{0,1:T(8,128)S(1)} %add_add_fusion.8), channel_id=1, source_target_pairs={{0,16},{1,17},{2,18},{3,19},{4,20},{5,21},{6,22},{7,23},{8,24},{9,... | collective-permute-start | bytes 6152 | tf_op jit(solution)/shard_map/ppermute | solution.py:20
  123.8 6.0 %collective-permute-start.25 = (f32[32,16]{0,1:T(8,128)S(1)}, f32[32,16]{0,1:T(8,128)S(1)}, u32[]{:S(2)}, u32[]{:S(2)}) collective-permute-start(f32[32,16]{0,1:T(8,128)S(1)} %add_add_fusion.8), channel_id=1, source_target_pairs={{0,8},{1,9},{2,10},{3,11},{4,12},{5,13},{6,14},{7,15},{8,0},{9,1},... | collective-permute-start | bytes 6152 | tf_op jit(solution)/shard_map/ppermute | solution.py:20
  129.8 4.9 %collective-permute-start.30 = (f32[32,16]{0,1:T(8,128)S(1)}, f32[32,16]{0,1:T(8,128)S(1)}, u32[]{:S(2)}, u32[]{:S(2)}) collective-permute-start(f32[32,16]{0,1:T(8,128)S(1)} %add_add_fusion.7), channel_id=1, source_target_pairs={{0,96},{1,97},{2,98},{3,99},{4,100},{5,101},{6,102},{7,103},{8,104... | collective-permute-start | bytes 6152 | tf_op jit(solution)/shard_map/ppermute | solution.py:20
  129.9 5.2 %collective-permute-start.29 = (f32[32,16]{0,1:T(8,128)S(1)}, f32[32,16]{0,1:T(8,128)S(1)}, u32[]{:S(2)}, u32[]{:S(2)}) collective-permute-start(f32[32,16]{0,1:T(8,128)S(1)} %add_add_fusion.7), channel_id=1, source_target_pairs={{0,64},{1,65},{2,66},{3,67},{4,68},{5,69},{6,70},{7,71},{8,72},{9,... | collective-permute-start | bytes 6152 | tf_op jit(solution)/shard_map/ppermute | solution.py:20
  131.1 4.6 %collective-permute-start.28 = (f32[32,16]{0,1:T(8,128)S(1)}, f32[32,16]{0,1:T(8,128)S(1)}, u32[]{:S(2)}, u32[]{:S(2)}) collective-permute-start(f32[32,16]{0,1:T(8,128)S(1)} %add_add_fusion.7), channel_id=1, source_target_pairs={{0,32},{1,33},{2,34},{3,35},{4,36},{5,37},{6,38},{7,39},{8,40},{9,... | collective-permute-start | bytes 6152 | tf_op jit(solution)/shard_map/ppermute | solution.py:20
  134.7 3.9 %collective-permute-start.20 = (f32[16,1,2,256]{3,0,2,1:T(8,128)S(1)}, f32[16,1,2,256]{3,0,2,1:T(8,128)S(1)}, u32[]{:S(2)}, u32[]{:S(2)}) collective-permute-start(f32[16,1,2,256]{3,0,2,1:T(8,128)S(1)} %pad_maximum_fusion.6), channel_id=1, source_target_pairs={{0,1},{1,0},{2,3},{3,2},{4,5},{5,4},{6,7},{7,6},{8,9},{9,8},{10,11... | collective-permute-start | bytes 98312 | tf_op jit(solution)/shard_map/ppermute | solution.py:45
  143.7 3.7 %collective-permute-start.31 = (f32[32,16]{0,1:T(8,128)S(1)}, f32[32,16]{0,1:T(8,128)S(1)}, u32[]{:S(2)}, u32[]{:S(2)}) collective-permute-start(f32[32,16]{0,1:T(8,128)S(1)} %pad_maximum_fusion.7), channel_id=1, source_target_pairs={{0,1},{1,0},{2,3},{3,2},{4,5},{5,4},{6,7},{7,6},{8,9},{9,8},{10,11... | collective-permute-start | bytes 6152 | tf_op jit(solution)/shard_map/ppermute | solution.py:20
  147.5 3.1 %collective-permute-start.34 = (f32[32,16]{0,1:T(8,128)S(1)}, f32[32,16]{0,1:T(8,128)S(1)}, u32[]{:S(2)}, u32[]{:S(2)}) collective-permute-start(f32[32,16]{0,1:T(8,128)S(1)} %fusion.160), channel_id=1, source_target_pairs={{0,6},{1,7},{2,4},{3,5},{4,2},{5,3},{6,0},{7,1},{8,14},{9,15},{10,... | collective-permute-start | bytes 6152 | tf_op jit(solution)/shard_map/ppermute | solution.py:20
  147.5 4.0 %collective-permute-start.33 = (f32[32,16]{0,1:T(8,128)S(1)}, f32[32,16]{0,1:T(8,128)S(1)}, u32[]{:S(2)}, u32[]{:S(2)}) collective-permute-start(f32[32,16]{0,1:T(8,128)S(1)} %fusion.160), channel_id=1, source_target_pairs={{0,4},{1,5},{2,6},{3,7},{4,0},{5,1},{6,2},{7,3},{8,12},{9,13},{10,... | collective-permute-start | bytes 6152 | tf_op jit(solution)/shard_map/ppermute | solution.py:20
  149.9 1.6 collective-permute-start.32
  151.6 7.6 %collective-permute-start.37 = (f32[32,16]{0,1:T(8,128)S(1)}, f32[32,16]{0,1:T(8,128)S(1)}, u32[]{:S(2)}, u32[]{:S(2)}) collective-permute-start(f32[32,16]{0,1:T(8,128)S(1)} %add_add_fusion.5), channel_id=1, source_target_pairs={{0,24},{1,25},{2,26},{3,27},{4,28},{5,29},{6,30},{7,31},{8,16},{9,... | collective-permute-start | bytes 6152 | tf_op jit(solution)/shard_map/ppermute | solution.py:20
  156.7 5.2 %collective-permute-start.36 = (f32[32,16]{0,1:T(8,128)S(1)}, f32[32,16]{0,1:T(8,128)S(1)}, u32[]{:S(2)}, u32[]{:S(2)}) collective-permute-start(f32[32,16]{0,1:T(8,128)S(1)} %add_add_fusion.5), channel_id=1, source_target_pairs={{0,16},{1,17},{2,18},{3,19},{4,20},{5,21},{6,22},{7,23},{8,24},{9,... | collective-permute-start | bytes 6152 | tf_op jit(solution)/shard_map/ppermute | solution.py:20
  158.7 5.2 %collective-permute-start.35 = (f32[32,16]{0,1:T(8,128)S(1)}, f32[32,16]{0,1:T(8,128)S(1)}, u32[]{:S(2)}, u32[]{:S(2)}) collective-permute-start(f32[32,16]{0,1:T(8,128)S(1)} %add_add_fusion.5), channel_id=1, source_target_pairs={{0,8},{1,9},{2,10},{3,11},{4,12},{5,13},{6,14},{7,15},{8,0},{9,1},... | collective-permute-start | bytes 6152 | tf_op jit(solution)/shard_map/ppermute | solution.py:20
  163.9 4.9 %collective-permute-start.40 = (f32[32,16]{0,1:T(8,128)S(1)}, f32[32,16]{0,1:T(8,128)S(1)}, u32[]{:S(2)}, u32[]{:S(2)}) collective-permute-start(f32[32,16]{0,1:T(8,128)S(1)} %add_add_fusion.4), channel_id=1, source_target_pairs={{0,96},{1,97},{2,98},{3,99},{4,100},{5,101},{6,102},{7,103},{8,104... | collective-permute-start | bytes 6152 | tf_op jit(solution)/shard_map/ppermute | solution.py:20
  164.7 5.2 %collective-permute-start.39 = (f32[32,16]{0,1:T(8,128)S(1)}, f32[32,16]{0,1:T(8,128)S(1)}, u32[]{:S(2)}, u32[]{:S(2)}) collective-permute-start(f32[32,16]{0,1:T(8,128)S(1)} %add_add_fusion.4), channel_id=1, source_target_pairs={{0,64},{1,65},{2,66},{3,67},{4,68},{5,69},{6,70},{7,71},{8,72},{9,... | collective-permute-start | bytes 6152 | tf_op jit(solution)/shard_map/ppermute | solution.py:20
  166.2 3.7 %collective-permute-start.38 = (f32[32,16]{0,1:T(8,128)S(1)}, f32[32,16]{0,1:T(8,128)S(1)}, u32[]{:S(2)}, u32[]{:S(2)}) collective-permute-start(f32[32,16]{0,1:T(8,128)S(1)} %add_add_fusion.4), channel_id=1, source_target_pairs={{0,32},{1,33},{2,34},{3,35},{4,36},{5,37},{6,38},{7,39},{8,40},{9,... | collective-permute-start | bytes 6152 | tf_op jit(solution)/shard_map/ppermute | solution.py:20
  178.2 11.7 %collective-permute-start.41 = (f32[8,1,64,256]{3,2,0,1:T(8,128)S(1)}, f32[8,1,64,256]{3,2,0,1:T(8,128)S(1)}, u32[]{:S(2)}, u32[]{:S(2)}) collective-permute-start(f32[8,1,64,256]{3,2,0,1:T(8,128)S(1)} %bitcast.163), channel_id=1, source_target_pairs={{0,1},{1,0},{2,3},{3,2},{4,5},{5,4},{6,7},{7,6},{8,9},{9,8},{10,11... | collective-permute-start | bytes 1572872 | tf_op jit(solution)/shard_map/ppermute | solution.py:45

commit v4 on v3

--- a/solution.py
+++ b/solution.py
@@ -8,6 +8,7 @@
 
 SIGMA = 0.5
 PREC = lax.Precision.HIGHEST
+FIELD_PREC = lax.Precision.HIGH
 AXES = ("space", "vec")
 
 
@@ -30,11 +31,11 @@
 
 
 def local_inner(left, right, scale):
-    return jnp.einsum("kzyx,jzyx->kj", left, right, precision=PREC) * scale
+    return jnp.einsum("kzyx,jzyx->kj", left, right, precision=FIELD_PREC) * scale
 
 
 def combine(coeff, vectors):
-    return jnp.einsum("kj,kzyx->jzyx", coeff, vectors, precision=PREC)
+    return jnp.einsum("kj,kzyx->jzyx", coeff, vectors, precision=FIELD_PREC)
 
 
 def mm(a, b):

time: 191 us -> 185 us (0.969)
  matrix products: 24 us -> 16.4 us
    dot_general x10, matrix products: 20 us -> 12.4 us  [the longest x6 8.17 us: combine(): return jnp.einsum('kj,kzyx->jzyx', coeff, vectors, precision=FIELD_PREC)]
  transfers between devices with their start and end apart: 42 -> 42, of which waited for: 30 -> 31; matrix products, arithmetic and copies ran while one was open for 3% -> 3% of each run, Pallas kernels for 0% -> 0%
where the time goes in v4:
time: 185 us; the launch traced here: 184 us
  waiting for transfers between devices  86.3 us (47%)
  starting transfers between devices  62.8 us (34%)
  matrix products  16.4 us (9%)
  other arithmetic  12.1 us (7%)
  local copies, waits for them, and re-layouts  5.39 us (3%)
    ppermute x30, starting transfers between devices, allsum(): vals[m] = lax.ppermute(x, AXES, [(i, i ^ mask) for i in range(n)])  42.9 us
    ppermute x30, waiting for transfers between devices, allsum(): vals[m] = lax.ppermute(x, AXES, [(i, i ^ mask) for i in range(n)])  38 us
    ppermute x4, waiting for transfers between devices, swap_vec(): return lax.ppermute(value, 'vec', [(0, 1), (1, 0)])  23.8 us
    ppermute x1, waiting for transfers between devices, local(): lax.ppermute(give_rows, AXES, cross_down)  8.77 us
    dot_general x6, matrix products, combine(): return jnp.einsum('kj,kzyx->jzyx', coeff, vectors, precision=FIELD_PREC)  8.17 us
    ppermute x2, waiting for transfers between devices, halo(): after = lax.ppermute(value, 'space', down)  7.83 us
    ppermute x2, waiting for transfers between devices, halo(): before = lax.ppermute(value, 'space', up)  7.63 us
    ppermute x1, starting transfers between devices, local(): lax.ppermute(keep_rows, AXES, same_down)  7.02 us
  transfers between devices with their start and end apart: 42, of which 31 were waited for; matrix products, arithmetic and copies ran while one was open for 3% of the time, Pallas kernels for 0%

profile of v4, /device:TPU:0, one launch (start us, length us, event | category | flops | bytes accessed | tf_op | source)
XLA Modules:
  0.0 184.0 jit_solution(8992025920635656560)
XLA Ops:
  0.6 1.8 copy.12
  2.7 2.1 %collective-permute-start = (f32[8,1,66,256]{3,0,2,1:T(8,128)S(1)}, f32[8,1,66,256]{3,0,2,1:T(8,128)S(1)}, u32[]{:S(2)}, u32[]{:S(2)}) collective-permute-start(f32[8,1,66,256]{3,0,2,1:T(8,128)S(1)} %get-tuple-element.16), channel_id=1, source_target_pairs={{0,1},{1,0},{2,3},{3,2},{4,5},{5,4},{6,7},{7,6},{8,9},{9,8},{10,11... | collective-permute-start | bytes 1622024 | tf_op jit(solution)/shard_map/ppermute | solution.py:46
  4.8 1.0 constant_dynamic-slice_fusion
  5.8 6.3 %collective-permute-start.4 = (f32[8,1,64,256]{3,0,2,1:T(8,128)}, f32[8,1,64,256]{3,0,2,1:T(8,128)S(1)}, u32[]{:S(2)}, u32[]{:S(2)}) collective-permute-start(f32[8,1,64,256]{3,0,2,1:T(8,128)} %get-tuple-element.13), channel_id=1, source_target_pairs={{3,0},{2,1},{5,2},{4,3},{7,4},{6,5},{9,6},{8,7},{11,8},{10,9},{13,... | collective-permute-start | bytes 1572872 | tf_op jit(solution)/shard_map/ppermute | solution.py:101
  12.1 7.0 %collective-permute-start.3 = (f32[8,1,64,256]{3,0,2,1:T(8,128)}, f32[8,1,64,256]{3,0,2,1:T(8,128)}, u32[]{:S(2)}, u32[]{:S(2)}) collective-permute-start(f32[8,1,64,256]{3,0,2,1:T(8,128)} %get-tuple-element.14), channel_id=1, source_target_pairs={{2,0},{3,1},{4,2},{5,3},{6,4},{7,5},{8,6},{9,7},{10,8},{11,9},{12,... | collective-permute-start | bytes 1572872 | tf_op jit(solution)/shard_map/ppermute | solution.py:101
  19.2 9.9 %collective-permute-done = f32[8,1,66,256]{3,0,2,1:T(8,128)S(1)} collective-permute-done((f32[8,1,66,256]{3,0,2,1:T(8,128)S(1)}, f32[8,1,66,256]{3,0,2,1:T(8,128)S(1)}, u32[]{:S(2)}, u32[]{:S(2)}) %collective-permute-start) | collective-permute-done | bytes 540704 | tf_op jit(solution)/shard_map/ppermute | solution.py:46
  29.9 8.8 %collective-permute-done.4 = f32[8,1,64,256]{3,0,2,1:T(8,128)S(1)} collective-permute-done((f32[8,1,64,256]{3,0,2,1:T(8,128)}, f32[8,1,64,256]{3,0,2,1:T(8,128)S(1)}, u32[]{:S(2)}, u32[]{:S(2)}) %collective-permute-start.4) | collective-permute-done | bytes 524320 | tf_op jit(solution)/shard_map/ppermute | solution.py:101
  38.9 2.3 %broadcast_divide_fusion = (f32[16,1,64,256]{3,0,2,1:T(8,128)S(1)}, f32[16,1,64,256]{3,0,2,1:T(8,128)S(1)}, f32[16,1,64,256]{3,0,2,1:T(8,128)S(1)}) fusion(f32[64,256]{1,0:T(8,128)S(1)} %get-tuple-element.34, f32[16,1,64,1]{3,0,2,1:T(8,128)S(1)} %get-tuple-element.10, f32[16,1,64,255]{3,0,2,1:T(8,128)S(1)} %get-tuple-element.12, ...), kind=kLoop, calls=%fused_computation.86 | loop fusion | flops 4456448 | bytes 10616833 | tf_op jit(solution)/shard_map/div | solution.py:111
  41.2 1.8 fusion.58
  43.0 1.3 collective-permute-start.5
  44.3 2.7 %collective-permute-done.5 = f32[32,64]{0,1:T(8,128)S(1)} collective-permute-done((f32[32,64]{0,1:T(8,128)S(1)}, f32[32,64]{0,1:T(8,128)S(1)}, u32[]{:S(2)}, u32[]{:S(2)}) %collective-permute-start.5) | collective-permute-done | bytes 8224 | tf_op jit(solution)/shard_map/ppermute | solution.py:21
  47.4 1.2 collective-permute-start.7
  48.9 1.8 collective-permute-done.8
  50.6 0.8 collective-permute-done.7
  51.5 6.1 %collective-permute-start.11 = (f32[32,64]{0,1:T(8,128)S(1)}, f32[32,64]{0,1:T(8,128)S(1)}, u32[]{:S(2)}, u32[]{:S(2)}) collective-permute-start(f32[32,64]{0,1:T(8,128)S(1)} %add_add_fusion.2), channel_id=1, source_target_pairs={{0,24},{1,25},{2,26},{3,27},{4,28},{5,29},{6,30},{7,31},{8,16},{9,... | collective-permute-start | bytes 24584 | tf_op jit(solution)/shard_map/ppermute | solution.py:21
  57.5 0.8 collective-permute-start.9
  58.3 1.1 collective-permute-done.11
  59.4 3.5 %collective-permute-done.10 = f32[32,64]{0,1:T(8,128)S(1)} collective-permute-done((f32[32,64]{0,1:T(8,128)S(1)}, f32[32,64]{0,1:T(8,128)S(1)}, u32[]{:S(2)}, u32[]{:S(2)}) %collective-permute-start.10) | collective-permute-done | bytes 8224 | tf_op jit(solution)/shard_map/ppermute | solution.py:21
  62.9 3.1 %collective-permute-start.14 = (f32[32,64]{0,1:T(8,128)S(1)}, f32[32,64]{0,1:T(8,128)S(1)}, u32[]{:S(2)}, u32[]{:S(2)}) collective-permute-start(f32[32,64]{0,1:T(8,128)S(1)} %add_add_fusion.1), channel_id=1, source_target_pairs={{0,96},{1,97},{2,98},{3,99},{4,100},{5,101},{6,102},{7,103},{8,104... | collective-permute-start | bytes 24584 | tf_op jit(solution)/shard_map/ppermute | solution.py:21
  67.1 1.0 collective-permute-done.14
  68.1 3.3 %collective-permute-done.13 = f32[32,64]{0,1:T(8,128)S(1)} collective-permute-done((f32[32,64]{0,1:T(8,128)S(1)}, f32[32,64]{0,1:T(8,128)S(1)}, u32[]{:S(2)}, u32[]{:S(2)}) %collective-permute-start.13) | collective-permute-done | bytes 8224 | tf_op jit(solution)/shard_map/ppermute | solution.py:21
  71.6 1.5 cholesky.44
  74.4 1.2 custom-call.6
  77.7 2.0 %fusion.9 = f32[64,64,256]{2,0,1:T(8,128)S(1)} fusion(f32[16,1,64,256]{3,0,2,1:T(8,128)S(1)} %get-tuple-element.7, f32[16,1,64,256]{3,0,2,1:T(8,128)S(1)} %slice.216, f32[16,16]{1,0:T(8,128)S(1)} %cholesky.45, f32[16,16]{1,0:T(8,128)S(1)} %bitcast.162, f32[16,16]{1,0:T(8,128)S(1)} %fusion.128, f32[16,16]{1,0:T(8,128)S(1)} %get-tuple-element.39, ...), kind=kOutput, calls=%fused_computation.11 | convolution fusion | flops 201865216 | bytes 6296576 | tf_op jit(solution)/shard_map/kj,kzyx->jzyx/dot_general | solution.py:38
  80.0 1.0 collective-permute-start.16
  81.5 1.8 collective-permute-start.17
  84.5 1.1 collective-permute-done.17
  85.5 7.8 %collective-permute-done.16 = f32[16,1,64,256]{3,0,2,1:T(8,128)S(1)} collective-permute-done((f32[16,1,64,256]{3,0,2,1:T(8,128)S(1)}, f32[16,1,64,256]{3,0,2,1:T(8,128)S(1)}, u32[]{:S(2)}, u32[]{:S(2)}) %collective-permute-start.16) | collective-permute-done | bytes 1048608 | tf_op jit(solution)/shard_map/ppermute | solution.py:56
  93.4 7.6 %collective-permute-done.15 = f32[16,1,64,256]{3,0,2,1:T(8,128)S(1)} collective-permute-done((f32[16,1,64,256]{3,0,2,1:T(8,128)S(1)}, f32[16,1,64,256]{3,0,2,1:T(8,128)S(1)}, u32[]{:S(2)}, u32[]{:S(2)}) %collective-permute-start.15) | collective-permute-done | bytes 1048608 | tf_op jit(solution)/shard_map/ppermute | solution.py:55
  101.0 1.6 fusion.13
  102.6 0.9 fusion.29
  103.5 1.3 collective-permute-start.21
  105.3 1.8 collective-permute-done.21
  107.2 1.9 %collective-permute-start.22 = (f32[32,16]{0,1:T(8,128)S(1)}, f32[32,16]{0,1:T(8,128)S(1)}, u32[]{:S(2)}, u32[]{:S(2)}) collective-permute-start(f32[32,16]{0,1:T(8,128)S(1)} %add.218), channel_id=1, source_target_pairs={{0,2},{1,3},{2,0},{3,1},{4,6},{5,7},{6,4},{7,5},{8,10},{9,11},{10,... | collective-permute-start | bytes 6152 | tf_op jit(solution)/shard_map/ppermute | solution.py:21
  109.4 0.9 collective-permute-done.24
  110.3 2.2 %collective-permute-done.23 = f32[32,16]{0,1:T(8,128)S(1)} collective-permute-done((f32[32,16]{0,1:T(8,128)S(1)}, f32[32,16]{0,1:T(8,128)S(1)}, u32[]{:S(2)}, u32[]{:S(2)}) %collective-permute-start.23) | collective-permute-done | bytes 2080 | tf_op jit(solution)/shard_map/ppermute | solution.py:21
  112.5 6.0 %collective-permute-start.27 = (f32[32,16]{0,1:T(8,128)S(1)}, f32[32,16]{0,1:T(8,128)S(1)}, u32[]{:S(2)}, u32[]{:S(2)}) collective-permute-start(f32[32,16]{0,1:T(8,128)S(1)} %add_add_fusion.8), channel_id=1, source_target_pairs={{0,24},{1,25},{2,26},{3,27},{4,28},{5,29},{6,30},{7,31},{8,16},{9,... | collective-permute-start | bytes 6152 | tf_op jit(solution)/shard_map/ppermute | solution.py:21
  118.5 0.9 collective-permute-start.26
  120.3 5.2 %collective-permute-done.26 = f32[32,16]{0,1:T(8,128)S(1)} collective-permute-done((f32[32,16]{0,1:T(8,128)S(1)}, f32[32,16]{0,1:T(8,128)S(1)}, u32[]{:S(2)}, u32[]{:S(2)}) %collective-permute-start.26) | collective-permute-done | bytes 2080 | tf_op jit(solution)/shard_map/ppermute | solution.py:21
  125.6 1.2 collective-permute-start.29
  126.8 2.8 %collective-permute-start.28 = (f32[32,16]{0,1:T(8,128)S(1)}, f32[32,16]{0,1:T(8,128)S(1)}, u32[]{:S(2)}, u32[]{:S(2)}) collective-permute-start(f32[32,16]{0,1:T(8,128)S(1)} %add_add_fusion.7), channel_id=1, source_target_pairs={{0,32},{1,33},{2,34},{3,35},{4,36},{5,37},{6,38},{7,39},{8,40},{9,... | collective-permute-start | bytes 6152 | tf_op jit(solution)/shard_map/ppermute | solution.py:21
  129.7 0.8 collective-permute-done.30
  131.5 0.7 convolution_bitcast_fusion.1
  132.2 2.1 %collective-permute-done.20 = f32[16,1,2,256]{3,0,2,1:T(8,128)S(1)} collective-permute-done((f32[16,1,2,256]{3,0,2,1:T(8,128)S(1)}, f32[16,1,2,256]{3,0,2,1:T(8,128)S(1)}, u32[]{:S(2)}, u32[]{:S(2)}) %collective-permute-start.20) | collective-permute-done | bytes 32800 | tf_op jit(solution)/shard_map/ppermute | solution.py:46
  134.4 1.6 fusion.18
  136.0 0.8 fusion.25
  136.8 0.8 fusion.26
  138.0 3.3 %collective-permute-done.31 = f32[32,16]{0,1:T(8,128)S(1)} collective-permute-done((f32[32,16]{0,1:T(8,128)S(1)}, f32[32,16]{0,1:T(8,128)S(1)}, u32[]{:S(2)}, u32[]{:S(2)}) %collective-permute-start.31) | collective-permute-done | bytes 2080 | tf_op jit(solution)/shard_map/ppermute | solution.py:21
  141.4 2.4 %collective-permute-start.33 = (f32[32,16]{0,1:T(8,128)S(1)}, f32[32,16]{0,1:T(8,128)S(1)}, u32[]{:S(2)}, u32[]{:S(2)}) collective-permute-start(f32[32,16]{0,1:T(8,128)S(1)} %fusion.160), channel_id=1, source_target_pairs={{0,4},{1,5},{2,6},{3,7},{4,0},{5,1},{6,2},{7,3},{8,12},{9,13},{10,... | collective-permute-start | bytes 6152 | tf_op jit(solution)/shard_map/ppermute | solution.py:21
  144.5 1.0 collective-permute-done.33
  145.5 5.4 %collective-permute-start.37 = (f32[32,16]{0,1:T(8,128)S(1)}, f32[32,16]{0,1:T(8,128)S(1)}, u32[]{:S(2)}, u32[]{:S(2)}) collective-permute-start(f32[32,16]{0,1:T(8,128)S(1)} %add_add_fusion.5), channel_id=1, source_target_pairs={{0,24},{1,25},{2,26},{3,27},{4,28},{5,29},{6,30},{7,31},{8,16},{9,... | collective-permute-start | bytes 6152 | tf_op jit(solution)/shard_map/ppermute | solution.py:21
  150.9 2.0 %collective-permute-start.36 = (f32[32,16]{0,1:T(8,128)S(1)}, f32[32,16]{0,1:T(8,128)S(1)}, u32[]{:S(2)}, u32[]{:S(2)}) collective-permute-start(f32[32,16]{0,1:T(8,128)S(1)} %add_add_fusion.5), channel_id=1, source_target_pairs={{0,16},{1,17},{2,18},{3,19},{4,20},{5,21},{6,22},{7,23},{8,24},{9,... | collective-permute-start | bytes 6152 | tf_op jit(solution)/shard_map/ppermute | solution.py:21
  153.4 2.6 %collective-permute-done.36 = f32[32,16]{0,1:T(8,128)S(1)} collective-permute-done((f32[32,16]{0,1:T(8,128)S(1)}, f32[32,16]{0,1:T(8,128)S(1)}, u32[]{:S(2)}, u32[]{:S(2)}) %collective-permute-start.36) | collective-permute-done | bytes 2080 | tf_op jit(solution)/shard_map/ppermute | solution.py:21
  156.0 2.0 %collective-permute-done.35 = f32[32,16]{0,1:T(8,128)S(1)} collective-permute-done((f32[32,16]{0,1:T(8,128)S(1)}, f32[32,16]{0,1:T(8,128)S(1)}, u32[]{:S(2)}, u32[]{:S(2)}) %collective-permute-start.35) | collective-permute-done | bytes 2080 | tf_op jit(solution)/shard_map/ppermute | solution.py:21
  158.6 1.4 collective-permute-start.39
  160.0 2.2 %collective-permute-start.38 = (f32[32,16]{0,1:T(8,128)S(1)}, f32[32,16]{0,1:T(8,128)S(1)}, u32[]{:S(2)}, u32[]{:S(2)}) collective-permute-start(f32[32,16]{0,1:T(8,128)S(1)} %add_add_fusion.4), channel_id=1, source_target_pairs={{0,32},{1,33},{2,34},{3,35},{4,36},{5,37},{6,38},{7,39},{8,40},{9,... | collective-permute-start | bytes 6152 | tf_op jit(solution)/shard_map/ppermute | solution.py:21
  162.1 0.8 collective-permute-done.40
  162.9 0.8 collective-permute-done.39
  163.9 1.8 fusion.20
  166.2 1.5 cholesky.55
  169.0 1.2 custom-call.7
  171.3 0.8 collective-permute-start.41
  172.3 10.7 %collective-permute-done.41 = f32[8,1,64,256]{3,2,0,1:T(8,128)S(1)} collective-permute-done((f32[8,1,64,256]{3,2,0,1:T(8,128)S(1)}, f32[8,1,64,256]{3,2,0,1:T(8,128)S(1)}, u32[]{:S(2)}, u32[]{:S(2)}) %collective-permute-start.41) | collective-permute-done | bytes 524320 | tf_op jit(solution)/shard_map/ppermute | solution.py:46
  183.0 1.0 fusion.49
  (112 shorter events, 16.8 us)
Async XLA Ops:
  2.6 16.6 %copy-start.1 = (f32[1,128,256]{2,1,0:T(8,128)S(1)}, f32[1,128,256]{2,1,0:T(8,128)}, u32[]{:S(2)}) copy-start(f32[1,128,256]{2,1,0:T(8,128)} %param.5) | copy-start | bytes 393220
  2.7 26.5 %collective-permute-start = (f32[8,1,66,256]{3,0,2,1:T(8,128)S(1)}, f32[8,1,66,256]{3,0,2,1:T(8,128)S(1)}, u32[]{:S(2)}, u32[]{:S(2)}) collective-permute-start(f32[8,1,66,256]{3,0,2,1:T(8,128)S(1)} %get-tuple-element.16), channel_id=1, source_target_pairs={{0,1},{1,0},{2,3},{3,2},{4,5},{5,4},{6,7},{7,6},{8,9},{9,8},{10,11... | collective-permute-start | bytes 1622024 | tf_op jit(solution)/shard_map/ppermute | solution.py:46
  5.8 32.9 %collective-permute-start.4 = (f32[8,1,64,256]{3,0,2,1:T(8,128)}, f32[8,1,64,256]{3,0,2,1:T(8,128)S(1)}, u32[]{:S(2)}, u32[]{:S(2)}) collective-permute-start(f32[8,1,64,256]{3,0,2,1:T(8,128)} %get-tuple-element.13), channel_id=1, source_target_pairs={{3,0},{2,1},{5,2},{4,3},{7,4},{6,5},{9,6},{8,7},{11,8},{10,9},{13,... | collective-permute-start | bytes 1572872 | tf_op jit(solution)/shard_map/ppermute | solution.py:101
  12.1 26.7 %collective-permute-start.2 = (f32[8,1,64,256]{3,0,2,1:T(8,128)}, f32[8,1,64,256]{3,0,2,1:T(8,128)S(1)}, u32[]{:S(2)}, u32[]{:S(2)}) collective-permute-start(f32[8,1,64,256]{3,0,2,1:T(8,128)} %get-tuple-element.13), channel_id=1, source_target_pairs={{0,3},{1,2},{2,5},{3,4},{4,7},{5,6},{6,9},{7,8},{8,11},{9,10},{10,... | collective-permute-start | bytes 1572872 | tf_op jit(solution)/shard_map/ppermute | solution.py:100
  12.1 26.7 %collective-permute-start.3 = (f32[8,1,64,256]{3,0,2,1:T(8,128)}, f32[8,1,64,256]{3,0,2,1:T(8,128)}, u32[]{:S(2)}, u32[]{:S(2)}) collective-permute-start(f32[8,1,64,256]{3,0,2,1:T(8,128)} %get-tuple-element.14), channel_id=1, source_target_pairs={{2,0},{3,1},{4,2},{5,3},{6,4},{7,5},{8,6},{9,7},{10,8},{11,9},{12,... | collective-permute-start | bytes 1572872 | tf_op jit(solution)/shard_map/ppermute | solution.py:101
  19.2 19.7 %collective-permute-start.1 = (f32[8,1,64,256]{3,0,2,1:T(8,128)}, f32[8,1,64,256]{3,0,2,1:T(8,128)}, u32[]{:S(2)}, u32[]{:S(2)}) collective-permute-start(f32[8,1,64,256]{3,0,2,1:T(8,128)} %get-tuple-element.14), channel_id=1, source_target_pairs={{0,2},{1,3},{2,4},{3,5},{4,6},{5,7},{6,8},{7,9},{8,10},{9,11},{10,... | collective-permute-start | bytes 1572872 | tf_op jit(solution)/shard_map/ppermute | solution.py:100
  43.0 4.0 %collective-permute-start.5 = (f32[32,64]{0,1:T(8,128)S(1)}, f32[32,64]{0,1:T(8,128)S(1)}, u32[]{:S(2)}, u32[]{:S(2)}) collective-permute-start(f32[32,64]{0,1:T(8,128)S(1)} %fusion.58), channel_id=1, source_target_pairs={{0,1},{1,0},{2,3},{3,2},{4,5},{5,4},{6,7},{7,6},{8,9},{9,8},{10,11... | collective-permute-start | bytes 24584 | tf_op jit(solution)/shard_map/ppermute | solution.py:21
  47.0 3.6 %collective-permute-start.8 = (f32[32,64]{0,1:T(8,128)S(1)}, f32[32,64]{0,1:T(8,128)S(1)}, u32[]{:S(2)}, u32[]{:S(2)}) collective-permute-start(f32[32,64]{0,1:T(8,128)S(1)} %add.197), channel_id=1, source_target_pairs={{0,6},{1,7},{2,4},{3,5},{4,2},{5,3},{6,0},{7,1},{8,14},{9,15},{10,... | collective-permute-start | bytes 24584 | tf_op jit(solution)/shard_map/ppermute | solution.py:21
  47.4 4.0 %collective-permute-start.7 = (f32[32,64]{0,1:T(8,128)S(1)}, f32[32,64]{0,1:T(8,128)S(1)}, u32[]{:S(2)}, u32[]{:S(2)}) collective-permute-start(f32[32,64]{0,1:T(8,128)S(1)} %add.197), channel_id=1, source_target_pairs={{0,4},{1,5},{2,6},{3,7},{4,0},{5,1},{6,2},{7,3},{8,12},{9,13},{10,... | collective-permute-start | bytes 24584 | tf_op jit(solution)/shard_map/ppermute | solution.py:21
  48.6 2.9 %collective-permute-start.6 = (f32[32,64]{0,1:T(8,128)S(1)}, f32[32,64]{0,1:T(8,128)S(1)}, u32[]{:S(2)}, u32[]{:S(2)}) collective-permute-start(f32[32,64]{0,1:T(8,128)S(1)} %add.197), channel_id=1, source_target_pairs={{0,2},{1,3},{2,0},{3,1},{4,6},{5,7},{6,4},{7,5},{8,10},{9,11},{10,... | collective-permute-start | bytes 24584 | tf_op jit(solution)/shard_map/ppermute | solution.py:21
  51.5 7.9 %collective-permute-start.11 = (f32[32,64]{0,1:T(8,128)S(1)}, f32[32,64]{0,1:T(8,128)S(1)}, u32[]{:S(2)}, u32[]{:S(2)}) collective-permute-start(f32[32,64]{0,1:T(8,128)S(1)} %add_add_fusion.2), channel_id=1, source_target_pairs={{0,24},{1,25},{2,26},{3,27},{4,28},{5,29},{6,30},{7,31},{8,16},{9,... | collective-permute-start | bytes 24584 | tf_op jit(solution)/shard_map/ppermute | solution.py:21
  57.5 5.4 %collective-permute-start.10 = (f32[32,64]{0,1:T(8,128)S(1)}, f32[32,64]{0,1:T(8,128)S(1)}, u32[]{:S(2)}, u32[]{:S(2)}) collective-permute-start(f32[32,64]{0,1:T(8,128)S(1)} %add_add_fusion.2), channel_id=1, source_target_pairs={{0,16},{1,17},{2,18},{3,19},{4,20},{5,21},{6,22},{7,23},{8,24},{9,... | collective-permute-start | bytes 24584 | tf_op jit(solution)/shard_map/ppermute | solution.py:21
  57.5 5.4 %collective-permute-start.9 = (f32[32,64]{0,1:T(8,128)S(1)}, f32[32,64]{0,1:T(8,128)S(1)}, u32[]{:S(2)}, u32[]{:S(2)}) collective-permute-start(f32[32,64]{0,1:T(8,128)S(1)} %add_add_fusion.2), channel_id=1, source_target_pairs={{0,8},{1,9},{2,10},{3,11},{4,12},{5,13},{6,14},{7,15},{8,0},{9,1},... | collective-permute-start | bytes 24584 | tf_op jit(solution)/shard_map/ppermute | solution.py:21
  62.9 5.2 %collective-permute-start.14 = (f32[32,64]{0,1:T(8,128)S(1)}, f32[32,64]{0,1:T(8,128)S(1)}, u32[]{:S(2)}, u32[]{:S(2)}) collective-permute-start(f32[32,64]{0,1:T(8,128)S(1)} %add_add_fusion.1), channel_id=1, source_target_pairs={{0,96},{1,97},{2,98},{3,99},{4,100},{5,101},{6,102},{7,103},{8,104... | collective-permute-start | bytes 24584 | tf_op jit(solution)/shard_map/ppermute | solution.py:21
  66.0 5.4 %collective-permute-start.13 = (f32[32,64]{0,1:T(8,128)S(1)}, f32[32,64]{0,1:T(8,128)S(1)}, u32[]{:S(2)}, u32[]{:S(2)}) collective-permute-start(f32[32,64]{0,1:T(8,128)S(1)} %add_add_fusion.1), channel_id=1, source_target_pairs={{0,64},{1,65},{2,66},{3,67},{4,68},{5,69},{6,70},{7,71},{8,72},{9,... | collective-permute-start | bytes 24584 | tf_op jit(solution)/shard_map/ppermute | solution.py:21
  66.7 4.8 %collective-permute-start.12 = (f32[32,64]{0,1:T(8,128)S(1)}, f32[32,64]{0,1:T(8,128)S(1)}, u32[]{:S(2)}, u32[]{:S(2)}) collective-permute-start(f32[32,64]{0,1:T(8,128)S(1)} %add_add_fusion.1), channel_id=1, source_target_pairs={{0,32},{1,33},{2,34},{3,35},{4,36},{5,37},{6,38},{7,39},{8,40},{9,... | collective-permute-start | bytes 24584 | tf_op jit(solution)/shard_map/ppermute | solution.py:21
  76.5 3.2 %copy-start.2 = (f32[16,16]{1,0:T(8,128)}, f32[16,16]{1,0:T(8,128)S(1)}, u32[]{:S(2)}) copy-start(f32[16,16]{1,0:T(8,128)S(1)} %fusion.127) | copy-start | bytes 3076
  79.7 57.1 %copy-start = (f32[64,64,256]{2,0,1:T(8,128)}, f32[64,64,256]{2,0,1:T(8,128)S(1)}, u32[]{:S(2)}) copy-start(f32[64,64,256]{2,0,1:T(8,128)S(1)} %fusion.9) | copy-start | bytes 12582916
  80.0 13.4 %collective-permute-start.16 = (f32[16,1,64,256]{3,0,2,1:T(8,128)S(1)}, f32[16,1,64,256]{3,0,2,1:T(8,128)S(1)}, u32[]{:S(2)}, u32[]{:S(2)}) collective-permute-start(f32[16,1,64,256]{3,0,2,1:T(8,128)S(1)} %fusion.53), channel_id=1, source_target_pairs={{2,0},{4,2},{6,4},{8,6},{10,8},{12,10},{14,12},{16,14},{18,16},{20... | collective-permute-start | bytes 3145736 | tf_op jit(solution)/shard_map/ppermute | solution.py:56
  81.0 19.9 %collective-permute-start.15 = (f32[16,1,64,256]{3,0,2,1:T(8,128)S(1)}, f32[16,1,64,256]{3,0,2,1:T(8,128)S(1)}, u32[]{:S(2)}, u32[]{:S(2)}) collective-permute-start(f32[16,1,64,256]{3,0,2,1:T(8,128)S(1)} %fusion.53), channel_id=1, source_target_pairs={{0,2},{2,4},{4,6},{6,8},{8,10},{10,12},{12,14},{14,16},{16,18},{18... | collective-permute-start | bytes 3145736 | tf_op jit(solution)/shard_map/ppermute | solution.py:55
  81.5 4.0 %collective-permute-start.17 = (f32[16,1,2,256]{3,0,2,1:T(8,128)S(1)}, f32[16,1,2,256]{3,0,2,1:T(8,128)S(1)}, u32[]{:S(2)}, u32[]{:S(2)}) collective-permute-start(f32[16,1,2,256]{3,0,2,1:T(8,128)S(1)} %pad_maximum_fusion.5), channel_id=1, source_target_pairs={{0,1},{1,0},{2,3},{3,2},{4,5},{5,4},{6,7},{7,6},{8,9},{9,8},{10,11... | collective-permute-start | bytes 98312 | tf_op jit(solution)/shard_map/ppermute | solution.py:46
  103.5 3.7 %collective-permute-start.21 = (f32[32,16]{0,1:T(8,128)S(1)}, f32[32,16]{0,1:T(8,128)S(1)}, u32[]{:S(2)}, u32[]{:S(2)}) collective-permute-start(f32[32,16]{0,1:T(8,128)S(1)} %fusion.29), channel_id=1, source_target_pairs={{0,1},{1,0},{2,3},{3,2},{4,5},{5,4},{6,7},{7,6},{8,9},{9,8},{10,11... | collective-permute-start | bytes 6152 | tf_op jit(solution)/shard_map/ppermute | solution.py:21
  104.8 29.5 %collective-permute-start.19 = (f32[16,1,64,256]{3,0,2,1:T(8,128)S(1)}, f32[16,1,64,256]{3,0,2,1:T(8,128)S(1)}, u32[]{:S(2)}, u32[]{:S(2)}) collective-permute-start(f32[16,1,64,256]{3,0,2,1:T(8,128)S(1)} %fusion.13), channel_id=1, source_target_pairs={{2,0},{4,2},{6,4},{8,6},{10,8},{12,10},{14,12},{16,14},{18,16},{20... | collective-permute-start | bytes 3145736 | tf_op jit(solution)/shard_map/ppermute | solution.py:56
  105.2 29.2 %collective-permute-start.18 = (f32[16,1,64,256]{3,0,2,1:T(8,128)S(1)}, f32[16,1,64,256]{3,0,2,1:T(8,128)S(1)}, u32[]{:S(2)}, u32[]{:S(2)}) collective-permute-start(f32[16,1,64,256]{3,0,2,1:T(8,128)S(1)} %fusion.13), channel_id=1, source_target_pairs={{0,2},{2,4},{4,6},{6,8},{8,10},{10,12},{12,14},{14,16},{16,18},{18... | collective-permute-start | bytes 3145736 | tf_op jit(solution)/shard_map/ppermute | solution.py:55
  107.2 3.2 %collective-permute-start.24 = (f32[32,16]{0,1:T(8,128)S(1)}, f32[32,16]{0,1:T(8,128)S(1)}, u32[]{:S(2)}, u32[]{:S(2)}) collective-permute-start(f32[32,16]{0,1:T(8,128)S(1)} %add.218), channel_id=1, source_target_pairs={{0,6},{1,7},{2,4},{3,5},{4,2},{5,3},{6,0},{7,1},{8,14},{9,15},{10,... | collective-permute-start | bytes 6152 | tf_op jit(solution)/shard_map/ppermute | solution.py:21
  107.2 5.3 %collective-permute-start.23 = (f32[32,16]{0,1:T(8,128)S(1)}, f32[32,16]{0,1:T(8,128)S(1)}, u32[]{:S(2)}, u32[]{:S(2)}) collective-permute-start(f32[32,16]{0,1:T(8,128)S(1)} %add.218), channel_id=1, source_target_pairs={{0,4},{1,5},{2,6},{3,7},{4,0},{5,1},{6,2},{7,3},{8,12},{9,13},{10,... | collective-permute-start | bytes 6152 | tf_op jit(solution)/shard_map/ppermute | solution.py:21
  107.2 5.3 %collective-permute-start.22 = (f32[32,16]{0,1:T(8,128)S(1)}, f32[32,16]{0,1:T(8,128)S(1)}, u32[]{:S(2)}, u32[]{:S(2)}) collective-permute-start(f32[32,16]{0,1:T(8,128)S(1)} %add.218), channel_id=1, source_target_pairs={{0,2},{1,3},{2,0},{3,1},{4,6},{5,7},{6,4},{7,5},{8,10},{9,11},{10,... | collective-permute-start | bytes 6152 | tf_op jit(solution)/shard_map/ppermute | solution.py:21
  112.5 7.8 %collective-permute-start.27 = (f32[32,16]{0,1:T(8,128)S(1)}, f32[32,16]{0,1:T(8,128)S(1)}, u32[]{:S(2)}, u32[]{:S(2)}) collective-permute-start(f32[32,16]{0,1:T(8,128)S(1)} %add_add_fusion.8), channel_id=1, source_target_pairs={{0,24},{1,25},{2,26},{3,27},{4,28},{5,29},{6,30},{7,31},{8,16},{9,... | collective-permute-start | bytes 6152 | tf_op jit(solution)/shard_map/ppermute | solution.py:21
  118.5 7.0 %collective-permute-start.26 = (f32[32,16]{0,1:T(8,128)S(1)}, f32[32,16]{0,1:T(8,128)S(1)}, u32[]{:S(2)}, u32[]{:S(2)}) collective-permute-start(f32[32,16]{0,1:T(8,128)S(1)} %add_add_fusion.8), channel_id=1, source_target_pairs={{0,16},{1,17},{2,18},{3,19},{4,20},{5,21},{6,22},{7,23},{8,24},{9,... | collective-permute-start | bytes 6152 | tf_op jit(solution)/shard_map/ppermute | solution.py:21
  119.5 6.0 %collective-permute-start.25 = (f32[32,16]{0,1:T(8,128)S(1)}, f32[32,16]{0,1:T(8,128)S(1)}, u32[]{:S(2)}, u32[]{:S(2)}) collective-permute-start(f32[32,16]{0,1:T(8,128)S(1)} %add_add_fusion.8), channel_id=1, source_target_pairs={{0,8},{1,9},{2,10},{3,11},{4,12},{5,13},{6,14},{7,15},{8,0},{9,1},... | collective-permute-start | bytes 6152 | tf_op jit(solution)/shard_map/ppermute | solution.py:21
  125.5 4.9 %collective-permute-start.30 = (f32[32,16]{0,1:T(8,128)S(1)}, f32[32,16]{0,1:T(8,128)S(1)}, u32[]{:S(2)}, u32[]{:S(2)}) collective-permute-start(f32[32,16]{0,1:T(8,128)S(1)} %add_add_fusion.7), channel_id=1, source_target_pairs={{0,96},{1,97},{2,98},{3,99},{4,100},{5,101},{6,102},{7,103},{8,104... | collective-permute-start | bytes 6152 | tf_op jit(solution)/shard_map/ppermute | solution.py:21
  125.6 5.2 %collective-permute-start.29 = (f32[32,16]{0,1:T(8,128)S(1)}, f32[32,16]{0,1:T(8,128)S(1)}, u32[]{:S(2)}, u32[]{:S(2)}) collective-permute-start(f32[32,16]{0,1:T(8,128)S(1)} %add_add_fusion.7), channel_id=1, source_target_pairs={{0,64},{1,65},{2,66},{3,67},{4,68},{5,69},{6,70},{7,71},{8,72},{9,... | collective-permute-start | bytes 6152 | tf_op jit(solution)/shard_map/ppermute | solution.py:21
  126.8 4.5 %collective-permute-start.28 = (f32[32,16]{0,1:T(8,128)S(1)}, f32[32,16]{0,1:T(8,128)S(1)}, u32[]{:S(2)}, u32[]{:S(2)}) collective-permute-start(f32[32,16]{0,1:T(8,128)S(1)} %add_add_fusion.7), channel_id=1, source_target_pairs={{0,32},{1,33},{2,34},{3,35},{4,36},{5,37},{6,38},{7,39},{8,40},{9,... | collective-permute-start | bytes 6152 | tf_op jit(solution)/shard_map/ppermute | solution.py:21
  130.4 3.9 %collective-permute-start.20 = (f32[16,1,2,256]{3,0,2,1:T(8,128)S(1)}, f32[16,1,2,256]{3,0,2,1:T(8,128)S(1)}, u32[]{:S(2)}, u32[]{:S(2)}) collective-permute-start(f32[16,1,2,256]{3,0,2,1:T(8,128)S(1)} %pad_maximum_fusion.6), channel_id=1, source_target_pairs={{0,1},{1,0},{2,3},{3,2},{4,5},{5,4},{6,7},{7,6},{8,9},{9,8},{10,11... | collective-permute-start | bytes 98312 | tf_op jit(solution)/shard_map/ppermute | solution.py:46
  137.7 3.7 %collective-permute-start.31 = (f32[32,16]{0,1:T(8,128)S(1)}, f32[32,16]{0,1:T(8,128)S(1)}, u32[]{:S(2)}, u32[]{:S(2)}) collective-permute-start(f32[32,16]{0,1:T(8,128)S(1)} %pad_maximum_fusion.7), channel_id=1, source_target_pairs={{0,1},{1,0},{2,3},{3,2},{4,5},{5,4},{6,7},{7,6},{8,9},{9,8},{10,11... | collective-permute-start | bytes 6152 | tf_op jit(solution)/shard_map/ppermute | solution.py:21
  141.4 3.1 %collective-permute-start.34 = (f32[32,16]{0,1:T(8,128)S(1)}, f32[32,16]{0,1:T(8,128)S(1)}, u32[]{:S(2)}, u32[]{:S(2)}) collective-permute-start(f32[32,16]{0,1:T(8,128)S(1)} %fusion.160), channel_id=1, source_target_pairs={{0,6},{1,7},{2,4},{3,5},{4,2},{5,3},{6,0},{7,1},{8,14},{9,15},{10,... | collective-permute-start | bytes 6152 | tf_op jit(solution)/shard_map/ppermute | solution.py:21
  141.4 4.1 %collective-permute-start.33 = (f32[32,16]{0,1:T(8,128)S(1)}, f32[32,16]{0,1:T(8,128)S(1)}, u32[]{:S(2)}, u32[]{:S(2)}) collective-permute-start(f32[32,16]{0,1:T(8,128)S(1)} %fusion.160), channel_id=1, source_target_pairs={{0,4},{1,5},{2,6},{3,7},{4,0},{5,1},{6,2},{7,3},{8,12},{9,13},{10,... | collective-permute-start | bytes 6152 | tf_op jit(solution)/shard_map/ppermute | solution.py:21
  143.9 1.6 collective-permute-start.32
  145.5 7.9 %collective-permute-start.37 = (f32[32,16]{0,1:T(8,128)S(1)}, f32[32,16]{0,1:T(8,128)S(1)}, u32[]{:S(2)}, u32[]{:S(2)}) collective-permute-start(f32[32,16]{0,1:T(8,128)S(1)} %add_add_fusion.5), channel_id=1, source_target_pairs={{0,24},{1,25},{2,26},{3,27},{4,28},{5,29},{6,30},{7,31},{8,16},{9,... | collective-permute-start | bytes 6152 | tf_op jit(solution)/shard_map/ppermute | solution.py:21
  150.9 5.2 %collective-permute-start.36 = (f32[32,16]{0,1:T(8,128)S(1)}, f32[32,16]{0,1:T(8,128)S(1)}, u32[]{:S(2)}, u32[]{:S(2)}) collective-permute-start(f32[32,16]{0,1:T(8,128)S(1)} %add_add_fusion.5), channel_id=1, source_target_pairs={{0,16},{1,17},{2,18},{3,19},{4,20},{5,21},{6,22},{7,23},{8,24},{9,... | collective-permute-start | bytes 6152 | tf_op jit(solution)/shard_map/ppermute | solution.py:21
  152.9 5.2 %collective-permute-start.35 = (f32[32,16]{0,1:T(8,128)S(1)}, f32[32,16]{0,1:T(8,128)S(1)}, u32[]{:S(2)}, u32[]{:S(2)}) collective-permute-start(f32[32,16]{0,1:T(8,128)S(1)} %add_add_fusion.5), channel_id=1, source_target_pairs={{0,8},{1,9},{2,10},{3,11},{4,12},{5,13},{6,14},{7,15},{8,0},{9,1},... | collective-permute-start | bytes 6152 | tf_op jit(solution)/shard_map/ppermute | solution.py:21
  158.0 4.9 %collective-permute-start.40 = (f32[32,16]{0,1:T(8,128)S(1)}, f32[32,16]{0,1:T(8,128)S(1)}, u32[]{:S(2)}, u32[]{:S(2)}) collective-permute-start(f32[32,16]{0,1:T(8,128)S(1)} %add_add_fusion.4), channel_id=1, source_target_pairs={{0,96},{1,97},{2,98},{3,99},{4,100},{5,101},{6,102},{7,103},{8,104... | collective-permute-start | bytes 6152 | tf_op jit(solution)/shard_map/ppermute | solution.py:21
  158.6 5.2 %collective-permute-start.39 = (f32[32,16]{0,1:T(8,128)S(1)}, f32[32,16]{0,1:T(8,128)S(1)}, u32[]{:S(2)}, u32[]{:S(2)}) collective-permute-start(f32[32,16]{0,1:T(8,128)S(1)} %add_add_fusion.4), channel_id=1, source_target_pairs={{0,64},{1,65},{2,66},{3,67},{4,68},{5,69},{6,70},{7,71},{8,72},{9,... | collective-permute-start | bytes 6152 | tf_op jit(solution)/shard_map/ppermute | solution.py:21
  160.0 3.9 %collective-permute-start.38 = (f32[32,16]{0,1:T(8,128)S(1)}, f32[32,16]{0,1:T(8,128)S(1)}, u32[]{:S(2)}, u32[]{:S(2)}) collective-permute-start(f32[32,16]{0,1:T(8,128)S(1)} %add_add_fusion.4), channel_id=1, source_target_pairs={{0,32},{1,33},{2,34},{3,35},{4,36},{5,37},{6,38},{7,39},{8,40},{9,... | collective-permute-start | bytes 6152 | tf_op jit(solution)/shard_map/ppermute | solution.py:21
  171.3 11.7 %collective-permute-start.41 = (f32[8,1,64,256]{3,2,0,1:T(8,128)S(1)}, f32[8,1,64,256]{3,2,0,1:T(8,128)S(1)}, u32[]{:S(2)}, u32[]{:S(2)}) collective-permute-start(f32[8,1,64,256]{3,2,0,1:T(8,128)S(1)} %bitcast.163), channel_id=1, source_target_pairs={{0,1},{1,0},{2,3},{3,2},{4,5},{5,4},{6,7},{7,6},{8,9},{9,8},{10,11... | collective-permute-start | bytes 1572872 | tf_op jit(solution)/shard_map/ppermute | solution.py:46

commit v5 on v4

--- a/solution.py
+++ b/solution.py
@@ -146,7 +146,7 @@
     moved = stencil(proj, pieces, pot) - SIGMA * proj
     correction = correction + (-resid - (moved - combine(back, basis))) / shifted
 
-    for sweep in range(2, NSWEEP):
+    for sweep in range(2, NSWEEP - 1):
         pieces = halo(correction)
         red = allsum(local_inner(both, correction, scale), groups)
         coeff = red[:nb]
@@ -154,12 +154,38 @@
         moved = stencil(correction, pieces, pot) - SIGMA * correction - combine(coeff, a_basis)
         correction = correction + (-resid - (moved - combine(back, basis))) / shifted
 
-    red = allsum(
-        jnp.concatenate([local_inner(basis, correction, scale), local_inner(correction, correction, scale)], 0),
-        groups,
-    )
-    proj_two = red[:nb]
-    gram_two = red[nb:] - 2.0 * mm(proj_two.T, proj_two) + mm(proj_two.T, mm(b_b, proj_two))
+    pieces = halo(correction)
+    y_pre = jnp.concatenate([correction, resid / shifted, a_basis / shifted, basis / shifted], 0)
+    x_pre = jnp.concatenate([both, y_pre], 0)
+    g_pre = local_inner(x_pre, y_pre, scale)
+    a_corr = stencil(correction, pieces, pot) - SIGMA * correction
+    y_a = a_corr / shifted
+    g_a = local_inner(x_pre, y_a, scale)
+    g_aa = local_inner(y_a, y_a, scale)
+    width = y_pre.shape[0]
+    packed = jnp.concatenate(
+        [
+            jnp.concatenate([g_pre, g_a], 1),
+            jnp.concatenate([jnp.zeros((nb, width), jnp.float32), g_aa], 1),
+        ],
+        0,
+    )
+    red = allsum(packed, groups)
+    b_y = red[:nb]
+    coeff = b_y[:, :nb]
+    back = red[nb:2 * nb, :nb] - mm(ab_b, coeff)
+    y_rows = red[2 * nb:2 * nb + width]
+    y_y = jnp.concatenate(
+        [y_rows, jnp.concatenate([y_rows[:, width:].T, red[2 * nb + width:, width:]], 1)], 0
+    )
+    eye = jnp.eye(nb, dtype=jnp.float32)
+    mix = jnp.concatenate([eye, -eye, coeff, back, -eye], 0)
+    proj_two = mm(b_y, mix)
+    c_c = mm(mix.T, mm(y_y, mix))
+    moved = a_corr - combine(coeff, a_basis)
+    correction = correction + (-resid - (moved - combine(back, basis))) / shifted
+
+    gram_two = c_c - 2.0 * mm(proj_two.T, proj_two) + mm(proj_two.T, mm(b_b, proj_two))
     fresh = correction - combine(proj_two, basis)
     new_all = combine(inverse_factor(gram_two).T, fresh)
 

time: 185 us -> 191 us (1.032)
  waiting for transfers between devices: 86.3 us -> 76.8 us
  matrix products: 16.4 us -> 24.8 us
  starting transfers between devices: 62.8 us -> 68.6 us
    ppermute x2, starting transfers between devices: 1.4 us -> 14.9 us  [halo(): after = lax.ppermute(value, 'space', down)]
    ppermute x30 -> x20, starting transfers between devices: 42.9 us -> 32.7 us  [allsum(): vals[m] = lax.ppermute(x, AXES, [(i, i ^ mask) for i in range(n)])]
    ppermute x4, waiting for transfers between devices: 23.8 us -> 33.9 us  [swap_vec(): return lax.ppermute(value, 'vec', [(0, 1), (1, 0)])]
    ppermute x1, waiting for transfers between devices: 8.77 us -> 0.01 us  [local(): lax.ppermute(give_rows, AXES, cross_down)]
    ppermute x1, waiting for transfers between devices: 0.22 us -> 8.98 us  [local(): lax.ppermute(give_rows, AXES, cross_up)]
    ppermute x30 -> x20, waiting for transfers between devices: 38 us -> 29.7 us  [allsum(): vals[m] = lax.ppermute(x, AXES, [(i, i ^ mask) for i in range(n)])]
    ppermute x2, waiting for transfers between devices: 7.83 us -> 0.01 us  [halo(): after = lax.ppermute(value, 'space', down)]
    dot_general x4, matrix products: 4.27 us -> 8.64 us  [local_inner(): jnp.einsum('kzyx,jzyx->kj', left, right, precision=FIELD_PREC) * scale]
  transfers between devices with their start and end apart: 42 -> 32, of which waited for: 31 -> 19; matrix products, arithmetic and copies ran while one was open for 3% -> 2% of each run, Pallas kernels for 0% -> 0%
where the time goes in v5:
time: 191 us
  waiting for transfers between devices  76.8 us (40%)
  starting transfers between devices  68.6 us (36%)
  matrix products  24.8 us (13%)
  other arithmetic  13.8 us (7%)
  local copies, waits for them, and re-layouts  6.06 us (3%)
    ppermute x4, waiting for transfers between devices, swap_vec(): return lax.ppermute(value, 'vec', [(0, 1), (1, 0)])  33.9 us
    ppermute x20, starting transfers between devices, allsum(): vals[m] = lax.ppermute(x, AXES, [(i, i ^ mask) for i in range(n)])  32.7 us
    ppermute x20, waiting for transfers between devices, allsum(): vals[m] = lax.ppermute(x, AXES, [(i, i ^ mask) for i in range(n)])  29.7 us
    ppermute x2, starting transfers between devices, halo(): after = lax.ppermute(value, 'space', down)  14.9 us
    dot_general x6, matrix products, combine(): return jnp.einsum('kj,kzyx->jzyx', coeff, vectors, precision=FIELD_PREC)  11.5 us
    ppermute x1, waiting for transfers between devices, local(): lax.ppermute(give_rows, AXES, cross_up)  8.98 us
    dot_general x4, matrix products, local_inner(): jnp.einsum('kzyx,jzyx->kj', left, right, precision=FIELD_PREC) * scale  8.64 us
    ppermute x1, starting transfers between devices, local(): lax.ppermute(keep_rows, AXES, same_down)  7.47 us
  transfers between devices with their start and end apart: 32, of which 19 were waited for; matrix products, arithmetic and copies ran while one was open for 2% of the time, Pallas kernels for 0%

profile of v5, /device:TPU:0, one launch (start us, length us, event | category | flops | bytes accessed | tf_op | source)
XLA Modules:
  0.0 191.1 jit_solution(8836411972503048453)
XLA Ops:
  0.6 1.9 copy.17
  2.7 2.1 %collective-permute-start = (f32[8,1,66,256]{3,0,2,1:T(8,128)S(1)}, f32[8,1,66,256]{3,0,2,1:T(8,128)S(1)}, u32[]{:S(2)}, u32[]{:S(2)}) collective-permute-start(f32[8,1,66,256]{3,0,2,1:T(8,128)S(1)} %get-tuple-element.22), channel_id=1, source_target_pairs={{0,1},{1,0},{2,3},{3,2},{4,5},{5,4},{6,7},{7,6},{8,9},{9,8},{10,11... | collective-permute-start | bytes 1622024 | tf_op jit(solution)/shard_map/ppermute | solution.py:46
  4.8 1.0 constant_dynamic-slice_fusion
  5.9 7.5 %collective-permute-start.3 = (f32[8,1,64,256]{3,0,2,1:T(8,128)}, f32[8,1,64,256]{3,0,2,1:T(8,128)S(1)}, u32[]{:S(2)}, u32[]{:S(2)}) collective-permute-start(f32[8,1,64,256]{3,0,2,1:T(8,128)} %get-tuple-element.20), channel_id=1, source_target_pairs={{2,0},{3,1},{4,2},{5,3},{6,4},{7,5},{8,6},{9,7},{10,8},{11,9},{12,... | collective-permute-start | bytes 1572872 | tf_op jit(solution)/shard_map/ppermute | solution.py:101
  13.3 7.2 %collective-permute-start.4 = (f32[8,1,64,256]{3,0,2,1:T(8,128)}, f32[8,1,64,256]{3,0,2,1:T(8,128)}, u32[]{:S(2)}, u32[]{:S(2)}) collective-permute-start(f32[8,1,64,256]{3,0,2,1:T(8,128)} %get-tuple-element.19), channel_id=1, source_target_pairs={{3,0},{2,1},{5,2},{4,3},{7,4},{6,5},{9,6},{8,7},{11,8},{10,9},{13,... | collective-permute-start | bytes 1572872 | tf_op jit(solution)/shard_map/ppermute | solution.py:101
  20.5 8.7 %collective-permute-done = f32[8,1,66,256]{3,0,2,1:T(8,128)S(1)} collective-permute-done((f32[8,1,66,256]{3,0,2,1:T(8,128)S(1)}, f32[8,1,66,256]{3,0,2,1:T(8,128)S(1)}, u32[]{:S(2)}, u32[]{:S(2)}) %collective-permute-start) | collective-permute-done | bytes 540704 | tf_op jit(solution)/shard_map/ppermute | solution.py:46
  29.9 9.0 %collective-permute-done.2 = f32[8,1,64,256]{3,0,2,1:T(8,128)} collective-permute-done((f32[8,1,64,256]{3,0,2,1:T(8,128)}, f32[8,1,64,256]{3,0,2,1:T(8,128)}, u32[]{:S(2)}, u32[]{:S(2)}) %collective-permute-start.2) | collective-permute-done | bytes 524320 | tf_op jit(solution)/shard_map/ppermute | solution.py:100
  38.9 2.3 %broadcast_divide_fusion.1 = (f32[16,1,64,256]{3,0,2,1:T(8,128)S(1)}, f32[16,1,64,256]{3,0,2,1:T(8,128)S(1)}, f32[16,1,64,256]{3,0,2,1:T(8,128)S(1)}) fusion(f32[64,256]{1,0:T(8,128)S(1)} %get-tuple-element.42, f32[16,1,64,1]{3,0,2,1:T(8,128)S(1)} %get-tuple-element.16, f32[16,1,64,255]{3,0,2,1:T(8,128)S(1)} %get-tuple-element.18, ...), kind=kLoop, calls=%fused_computation.101 | loop fusion | flops 4456448 | bytes 10616833 | tf_op jit(solution)/shard_map/div | solution.py:111
  41.3 1.8 fusion.70
  43.0 1.4 collective-permute-start.5
  44.5 2.6 %collective-permute-done.5 = f32[32,64]{0,1:T(8,128)S(1)} collective-permute-done((f32[32,64]{0,1:T(8,128)S(1)}, f32[32,64]{0,1:T(8,128)S(1)}, u32[]{:S(2)}, u32[]{:S(2)}) %collective-permute-start.5) | collective-permute-done | bytes 8224 | tf_op jit(solution)/shard_map/ppermute | solution.py:21
  47.0 1.6 collective-permute-start.7
  48.9 2.1 %collective-permute-done.7 = f32[32,64]{0,1:T(8,128)S(1)} collective-permute-done((f32[32,64]{0,1:T(8,128)S(1)}, f32[32,64]{0,1:T(8,128)S(1)}, u32[]{:S(2)}, u32[]{:S(2)}) %collective-permute-start.7) | collective-permute-done | bytes 8224 | tf_op jit(solution)/shard_map/ppermute | solution.py:21
  51.0 0.9 collective-permute-done.8
  52.0 3.7 %collective-permute-start.10 = (f32[32,64]{0,1:T(8,128)S(1)}, f32[32,64]{0,1:T(8,128)S(1)}, u32[]{:S(2)}, u32[]{:S(2)}) collective-permute-start(f32[32,64]{0,1:T(8,128)S(1)} %add_add_fusion.5), channel_id=1, source_target_pairs={{0,16},{1,17},{2,18},{3,19},{4,20},{5,21},{6,22},{7,23},{8,24},{9,... | collective-permute-start | bytes 24584 | tf_op jit(solution)/shard_map/ppermute | solution.py:21
  55.7 2.3 %collective-permute-start.11 = (f32[32,64]{0,1:T(8,128)S(1)}, f32[32,64]{0,1:T(8,128)S(1)}, u32[]{:S(2)}, u32[]{:S(2)}) collective-permute-start(f32[32,64]{0,1:T(8,128)S(1)} %add_add_fusion.5), channel_id=1, source_target_pairs={{0,24},{1,25},{2,26},{3,27},{4,28},{5,29},{6,30},{7,31},{8,16},{9,... | collective-permute-start | bytes 24584 | tf_op jit(solution)/shard_map/ppermute | solution.py:21
  58.0 0.8 collective-permute-start.9
  58.8 4.8 %collective-permute-done.11 = f32[32,64]{0,1:T(8,128)S(1)} collective-permute-done((f32[32,64]{0,1:T(8,128)S(1)}, f32[32,64]{0,1:T(8,128)S(1)}, u32[]{:S(2)}, u32[]{:S(2)}) %collective-permute-start.11) | collective-permute-done | bytes 8224 | tf_op jit(solution)/shard_map/ppermute | solution.py:21
  63.6 1.7 collective-permute-start.12
  65.2 2.9 %collective-permute-start.13 = (f32[32,64]{0,1:T(8,128)S(1)}, f32[32,64]{0,1:T(8,128)S(1)}, u32[]{:S(2)}, u32[]{:S(2)}) collective-permute-start(f32[32,64]{0,1:T(8,128)S(1)} %add_add_fusion.4), channel_id=1, source_target_pairs={{0,64},{1,65},{2,66},{3,67},{4,68},{5,69},{6,70},{7,71},{8,72},{9,... | collective-permute-start | bytes 24584 | tf_op jit(solution)/shard_map/ppermute | solution.py:21
  68.3 2.4 %collective-permute-done.13 = f32[32,64]{0,1:T(8,128)S(1)} collective-permute-done((f32[32,64]{0,1:T(8,128)S(1)}, f32[32,64]{0,1:T(8,128)S(1)}, u32[]{:S(2)}, u32[]{:S(2)}) %collective-permute-start.13) | collective-permute-done | bytes 8224 | tf_op jit(solution)/shard_map/ppermute | solution.py:21
  70.7 2.5 %collective-permute-done.14 = f32[32,64]{0,1:T(8,128)S(1)} collective-permute-done((f32[32,64]{0,1:T(8,128)S(1)}, f32[32,64]{0,1:T(8,128)S(1)}, u32[]{:S(2)}, u32[]{:S(2)}) %collective-permute-start.14) | collective-permute-done | bytes 8224 | tf_op jit(solution)/shard_map/ppermute | solution.py:21
  73.3 1.5 cholesky.44
  74.8 0.6 compare_reduce_fusion.1
  75.5 0.6 fusion.94
  76.1 1.2 custom-call.6
  79.4 2.0 %fusion.18 = f32[64,64,256]{2,0,1:T(8,128)S(1)} fusion(f32[16,1,64,256]{3,0,2,1:T(8,128)S(1)} %get-tuple-element.13, f32[16,1,64,256]{3,0,2,1:T(8,128)S(1)} %slice.229, f32[16,16]{1,0:T(8,128)S(1)} %cholesky.45, f32[16,16]{1,0:T(8,128)S(1)} %bitcast.202, f32[16,16]{1,0:T(8,128)S(1)} %fusion.142, f32[16,16]{1,0:T(8,128)S(1)} %get-tuple-element.49, ...), kind=kOutput, calls=%fused_computation.22 | convolution fusion | flops 201865216 | bytes 6296576 | tf_op jit(solution)/shard_map/kj,kzyx->jzyx/dot_general | solution.py:38
  81.8 7.5 %collective-permute-start.16 = (f32[16,1,64,256]{3,0,2,1:T(8,128)S(1)}, f32[16,1,64,256]{3,0,2,1:T(8,128)S(1)}, u32[]{:S(2)}, u32[]{:S(2)}) collective-permute-start(f32[16,1,64,256]{3,0,2,1:T(8,128)S(1)} %fusion.66), channel_id=1, source_target_pairs={{2,0},{4,2},{6,4},{8,6},{10,8},{12,10},{14,12},{16,14},{18,16},{20... | collective-permute-start | bytes 3145736 | tf_op jit(solution)/shard_map/ppermute | solution.py:56
  89.5 1.4 collective-permute-start.17
  91.8 0.4 fusion.133
  92.5 8.3 %collective-permute-done.17 = f32[16,1,2,256]{3,0,2,1:T(8,128)S(1)} collective-permute-done((f32[16,1,2,256]{3,0,2,1:T(8,128)S(1)}, f32[16,1,2,256]{3,0,2,1:T(8,128)S(1)}, u32[]{:S(2)}, u32[]{:S(2)}) %collective-permute-start.17) | collective-permute-done | bytes 32800 | tf_op jit(solution)/shard_map/ppermute | solution.py:46
  100.8 1.0 collective-permute-done.15
  101.8 1.6 fusion.22
  103.6 7.5 %collective-permute-start.19 = (f32[16,1,64,256]{3,0,2,1:T(8,128)S(1)}, f32[16,1,64,256]{3,0,2,1:T(8,128)S(1)}, u32[]{:S(2)}, u32[]{:S(2)}) collective-permute-start(f32[16,1,64,256]{3,0,2,1:T(8,128)S(1)} %fusion.22), channel_id=1, source_target_pairs={{2,0},{4,2},{6,4},{8,6},{10,8},{12,10},{14,12},{16,14},{18,16},{20... | collective-permute-start | bytes 3145736 | tf_op jit(solution)/shard_map/ppermute | solution.py:56
  111.0 1.4 collective-permute-start.20
  113.0 7.5 %collective-permute-done.20 = f32[16,1,2,256]{3,0,2,1:T(8,128)S(1)} collective-permute-done((f32[16,1,2,256]{3,0,2,1:T(8,128)S(1)}, f32[16,1,2,256]{3,0,2,1:T(8,128)S(1)}, u32[]{:S(2)}, u32[]{:S(2)}) %collective-permute-start.20) | collective-permute-done | bytes 32800 | tf_op jit(solution)/shard_map/ppermute | solution.py:46
  120.4 3.2 %collective-permute-done.18 = f32[16,1,64,256]{3,0,2,1:T(8,128)S(1)} collective-permute-done((f32[16,1,64,256]{3,0,2,1:T(8,128)S(1)}, f32[16,1,64,256]{3,0,2,1:T(8,128)S(1)}, u32[]{:S(2)}, u32[]{:S(2)}) %collective-permute-start.18) | collective-permute-done | bytes 1048608 | tf_op jit(solution)/shard_map/ppermute | solution.py:55
  123.6 0.8 constant_dynamic-update-slice_fusion.3
  125.1 0.9 fusion.40
  126.0 2.6 %fusion.43 = f32[96,16]{0,1:T(8,128)S(1)} fusion(f32[96,1,64,256]{3,0,2,1:T(8,128)S(1)} %get-tuple-element.6, f32[16,1,64,256]{3,0,2,1:T(8,128)S(1)} %get-tuple-element.26, f32[64,256]{1,0:T(8,128)S(1)} %get-tuple-element.42), kind=kOutput, calls=%fused_computation.56 | convolution fusion | flops 151258624 | bytes 7411712 | tf_op jit(solution)/shard_map/kzyx,jzyx->kj/dot_general | solution.py:34
  128.6 3.4 %fusion.34 = f32[96,64]{0,1:T(8,128)S(1)} fusion(f32[16,1,64,256]{3,0,2,1:T(8,128)S(1)} %get-tuple-element.7, f32[16,1,64,256]{3,0,2,1:T(8,128)S(1)} %get-tuple-element.9, f32[16,1,64,256]{3,0,2,1:T(8,128)S(1)} %get-tuple-element.11, f32[16,1,64,256]{3,0,2,1:T(8,128)S(1)} %fusion.22, f32[96,1,64,256]{3,0,2,1:T(8,128)S(1)} %get-tuple-element.6), kind=kOutput, calls=%fused_computation.40 | convolution fusion | flops 607131648 | bytes 10510336 | tf_op jit(solution)/shard_map/kzyx,jzyx->kj/dot_general | solution.py:34
  132.1 1.4 collective-permute-start.21
  133.5 2.6 %collective-permute-done.21 = f32[112,80]{0,1:T(8,128)S(1)} collective-permute-done((f32[112,80]{0,1:T(8,128)S(1)}, f32[112,80]{0,1:T(8,128)S(1)}, u32[]{:S(2)}, u32[]{:S(2)}) %collective-permute-start.21) | collective-permute-done | bytes 35872 | tf_op jit(solution)/shard_map/ppermute | solution.py:21
  136.3 1.8 collective-permute-start.24
  138.1 2.6 %collective-permute-done.23 = f32[112,80]{0,1:T(8,128)S(1)} collective-permute-done((f32[112,80]{0,1:T(8,128)S(1)}, f32[112,80]{0,1:T(8,128)S(1)}, u32[]{:S(2)}, u32[]{:S(2)}) %collective-permute-start.23) | collective-permute-done | bytes 35872 | tf_op jit(solution)/shard_map/ppermute | solution.py:21
  140.6 2.9 %collective-permute-start.25 = (f32[112,80]{0,1:T(8,128)S(1)}, f32[112,80]{0,1:T(8,128)S(1)}, u32[]{:S(2)}, u32[]{:S(2)}) collective-permute-start(f32[112,80]{0,1:T(8,128)S(1)} %add_add_fusion.2), channel_id=1, source_target_pairs={{0,8},{1,9},{2,10},{3,11},{4,12},{5,13},{6,14},{7,15},{8,0},{9,1},... | collective-permute-start | bytes 107528 | tf_op jit(solution)/shard_map/ppermute | solution.py:21
  143.5 3.9 %collective-permute-start.27 = (f32[112,80]{0,1:T(8,128)S(1)}, f32[112,80]{0,1:T(8,128)S(1)}, u32[]{:S(2)}, u32[]{:S(2)}) collective-permute-start(f32[112,80]{0,1:T(8,128)S(1)} %add_add_fusion.2), channel_id=1, source_target_pairs={{0,24},{1,25},{2,26},{3,27},{4,28},{5,29},{6,30},{7,31},{8,16},{9,... | collective-permute-start | bytes 107528 | tf_op jit(solution)/shard_map/ppermute | solution.py:21
  147.5 1.6 collective-permute-done.26
  149.0 2.4 %collective-permute-done.27 = f32[112,80]{0,1:T(8,128)S(1)} collective-permute-done((f32[112,80]{0,1:T(8,128)S(1)}, f32[112,80]{0,1:T(8,128)S(1)}, u32[]{:S(2)}, u32[]{:S(2)}) %collective-permute-start.27) | collective-permute-done | bytes 35872 | tf_op jit(solution)/shard_map/ppermute | solution.py:21
  151.4 0.9 collective-permute-start.28
  152.4 6.9 %collective-permute-start.29 = (f32[112,80]{0,1:T(8,128)S(1)}, f32[112,80]{0,1:T(8,128)S(1)}, u32[]{:S(2)}, u32[]{:S(2)}) collective-permute-start(f32[112,80]{0,1:T(8,128)S(1)} %add_add_fusion.1), channel_id=1, source_target_pairs={{0,64},{1,65},{2,66},{3,67},{4,68},{5,69},{6,70},{7,71},{8,72},{9,... | collective-permute-start | bytes 107528 | tf_op jit(solution)/shard_map/ppermute | solution.py:21
  159.3 2.5 %collective-permute-done.29 = f32[112,80]{0,1:T(8,128)S(1)} collective-permute-done((f32[112,80]{0,1:T(8,128)S(1)}, f32[112,80]{0,1:T(8,128)S(1)}, u32[]{:S(2)}, u32[]{:S(2)}) %collective-permute-start.29) | collective-permute-done | bytes 35872 | tf_op jit(solution)/shard_map/ppermute | solution.py:21
  161.8 2.7 %collective-permute-done.30 = f32[112,80]{0,1:T(8,128)S(1)} collective-permute-done((f32[112,80]{0,1:T(8,128)S(1)}, f32[112,80]{0,1:T(8,128)S(1)}, u32[]{:S(2)}, u32[]{:S(2)}) %collective-permute-start.30) | collective-permute-done | bytes 35872 | tf_op jit(solution)/shard_map/ppermute | solution.py:21
  164.7 1.8 convolution_bitcast_fusion.1
  166.8 2.9 %convolution_bitcast_fusion = f32[16,1,64,256]{3,0,2,1:T(8,128)} fusion(f32[64,64,256]{2,0,1:T(8,128)} %copy-done, f32[16,16]{1,0:T(8,128)S(1)} %fusion.71), kind=kOutput, calls=%fused_computation.23 | convolution fusion | flops 25165824 | bytes 2098176 | tf_op jit(solution)/shard_map/kj,kzyx->jzyx/dot_general | solution.py:38
  171.2 1.5 cholesky.55
  172.7 0.7 compare_reduce_fusion
  173.4 0.6 fusion.95
  174.1 1.2 custom-call.7
  175.5 2.7 %fusion.29 = f32[16,64,256]{2,0,1:T(8,128)S(1)} fusion(f32[16,1,64,256]{3,0,2,1:T(8,128)} %convolution_bitcast_fusion, f32[16,1,64,256]{3,0,2,1:T(8,128)S(1)} %fusion.22, f32[16,1,64,256]{3,0,2,1:T(8,128)S(1)} %convolution_bitcast_fusion.1, f32[16,1,64,256]{3,0,2,1:T(8,128)S(1)} %get-tuple-element.26, f32[64,64,256]{2,0,1:T(8,128)} %copy-done, ...), kind=kOutput, calls=%fused_computation.37 | convolution fusion | flops 27000832 | bytes 7413760 | tf_op jit(solution)/shard_map/kj,kzyx->jzyx/dot_general | solution.py:38
  178.2 0.6 fusion.145
  179.1 1.2 collective-permute-start.31
  180.5 9.5 %collective-permute-done.31 = f32[8,1,64,256]{3,2,0,1:T(8,128)S(1)} collective-permute-done((f32[8,1,64,256]{3,2,0,1:T(8,128)S(1)}, f32[8,1,64,256]{3,2,0,1:T(8,128)S(1)}, u32[]{:S(2)}, u32[]{:S(2)}) %collective-permute-start.31) | collective-permute-done | bytes 524320 | tf_op jit(solution)/shard_map/ppermute | solution.py:46
  190.0 1.0 fusion.62
  (105 shorter events, 9.8 us)
Async XLA Ops:
  0.6 19.9 %copy-start.1 = (f32[1,128,256]{2,1,0:T(8,128)S(1)}, f32[1,128,256]{2,1,0:T(8,128)}, u32[]{:S(2)}) copy-start(f32[1,128,256]{2,1,0:T(8,128)} %param.5) | copy-start | bytes 393220
  2.7 26.5 %collective-permute-start = (f32[8,1,66,256]{3,0,2,1:T(8,128)S(1)}, f32[8,1,66,256]{3,0,2,1:T(8,128)S(1)}, u32[]{:S(2)}, u32[]{:S(2)}) collective-permute-start(f32[8,1,66,256]{3,0,2,1:T(8,128)S(1)} %get-tuple-element.22), channel_id=1, source_target_pairs={{0,1},{1,0},{2,3},{3,2},{4,5},{5,4},{6,7},{7,6},{8,9},{9,8},{10,11... | collective-permute-start | bytes 1622024 | tf_op jit(solution)/shard_map/ppermute | solution.py:46
  5.9 24.1 %collective-permute-start.1 = (f32[8,1,64,256]{3,0,2,1:T(8,128)}, f32[8,1,64,256]{3,0,2,1:T(8,128)S(1)}, u32[]{:S(2)}, u32[]{:S(2)}) collective-permute-start(f32[8,1,64,256]{3,0,2,1:T(8,128)} %get-tuple-element.20), channel_id=1, source_target_pairs={{0,2},{1,3},{2,4},{3,5},{4,6},{5,7},{6,8},{7,9},{8,10},{9,11},{10,... | collective-permute-start | bytes 1572872 | tf_op jit(solution)/shard_map/ppermute | solution.py:100
  5.9 33.1 %collective-permute-start.3 = (f32[8,1,64,256]{3,0,2,1:T(8,128)}, f32[8,1,64,256]{3,0,2,1:T(8,128)S(1)}, u32[]{:S(2)}, u32[]{:S(2)}) collective-permute-start(f32[8,1,64,256]{3,0,2,1:T(8,128)} %get-tuple-element.20), channel_id=1, source_target_pairs={{2,0},{3,1},{4,2},{5,3},{6,4},{7,5},{8,6},{9,7},{10,8},{11,9},{12,... | collective-permute-start | bytes 1572872 | tf_op jit(solution)/shard_map/ppermute | solution.py:101
  13.3 25.6 %collective-permute-start.2 = (f32[8,1,64,256]{3,0,2,1:T(8,128)}, f32[8,1,64,256]{3,0,2,1:T(8,128)}, u32[]{:S(2)}, u32[]{:S(2)}) collective-permute-start(f32[8,1,64,256]{3,0,2,1:T(8,128)} %get-tuple-element.19), channel_id=1, source_target_pairs={{0,3},{1,2},{2,5},{3,4},{4,7},{5,6},{6,9},{7,8},{8,11},{9,10},{10,... | collective-permute-start | bytes 1572872 | tf_op jit(solution)/shard_map/ppermute | solution.py:100
  13.3 25.6 %collective-permute-start.4 = (f32[8,1,64,256]{3,0,2,1:T(8,128)}, f32[8,1,64,256]{3,0,2,1:T(8,128)}, u32[]{:S(2)}, u32[]{:S(2)}) collective-permute-start(f32[8,1,64,256]{3,0,2,1:T(8,128)} %get-tuple-element.19), channel_id=1, source_target_pairs={{3,0},{2,1},{5,2},{4,3},{7,4},{6,5},{9,6},{8,7},{11,8},{10,9},{13,... | collective-permute-start | bytes 1572872 | tf_op jit(solution)/shard_map/ppermute | solution.py:101
  43.0 4.0 %collective-permute-start.5 = (f32[32,64]{0,1:T(8,128)S(1)}, f32[32,64]{0,1:T(8,128)S(1)}, u32[]{:S(2)}, u32[]{:S(2)}) collective-permute-start(f32[32,64]{0,1:T(8,128)S(1)} %fusion.70), channel_id=1, source_target_pairs={{0,1},{1,0},{2,3},{3,2},{4,5},{5,4},{6,7},{7,6},{8,9},{9,8},{10,11... | collective-permute-start | bytes 24584 | tf_op jit(solution)/shard_map/ppermute | solution.py:21
  47.0 1.9 collective-permute-start.6
  47.0 4.0 %collective-permute-start.7 = (f32[32,64]{0,1:T(8,128)S(1)}, f32[32,64]{0,1:T(8,128)S(1)}, u32[]{:S(2)}, u32[]{:S(2)}) collective-permute-start(f32[32,64]{0,1:T(8,128)S(1)} %add.169), channel_id=1, source_target_pairs={{0,4},{1,5},{2,6},{3,7},{4,0},{5,1},{6,2},{7,3},{8,12},{9,13},{10,... | collective-permute-start | bytes 24584 | tf_op jit(solution)/shard_map/ppermute | solution.py:21
  48.6 3.4 %collective-permute-start.8 = (f32[32,64]{0,1:T(8,128)S(1)}, f32[32,64]{0,1:T(8,128)S(1)}, u32[]{:S(2)}, u32[]{:S(2)}) collective-permute-start(f32[32,64]{0,1:T(8,128)S(1)} %add.169), channel_id=1, source_target_pairs={{0,6},{1,7},{2,4},{3,5},{4,2},{5,3},{6,0},{7,1},{8,14},{9,15},{10,... | collective-permute-start | bytes 24584 | tf_op jit(solution)/shard_map/ppermute | solution.py:21
  52.0 6.8 %collective-permute-start.10 = (f32[32,64]{0,1:T(8,128)S(1)}, f32[32,64]{0,1:T(8,128)S(1)}, u32[]{:S(2)}, u32[]{:S(2)}) collective-permute-start(f32[32,64]{0,1:T(8,128)S(1)} %add_add_fusion.5), channel_id=1, source_target_pairs={{0,16},{1,17},{2,18},{3,19},{4,20},{5,21},{6,22},{7,23},{8,24},{9,... | collective-permute-start | bytes 24584 | tf_op jit(solution)/shard_map/ppermute | solution.py:21
  55.7 7.8 %collective-permute-start.11 = (f32[32,64]{0,1:T(8,128)S(1)}, f32[32,64]{0,1:T(8,128)S(1)}, u32[]{:S(2)}, u32[]{:S(2)}) collective-permute-start(f32[32,64]{0,1:T(8,128)S(1)} %add_add_fusion.5), channel_id=1, source_target_pairs={{0,24},{1,25},{2,26},{3,27},{4,28},{5,29},{6,30},{7,31},{8,16},{9,... | collective-permute-start | bytes 24584 | tf_op jit(solution)/shard_map/ppermute | solution.py:21
  58.0 5.6 %collective-permute-start.9 = (f32[32,64]{0,1:T(8,128)S(1)}, f32[32,64]{0,1:T(8,128)S(1)}, u32[]{:S(2)}, u32[]{:S(2)}) collective-permute-start(f32[32,64]{0,1:T(8,128)S(1)} %add_add_fusion.5), channel_id=1, source_target_pairs={{0,8},{1,9},{2,10},{3,11},{4,12},{5,13},{6,14},{7,15},{8,0},{9,1},... | collective-permute-start | bytes 24584 | tf_op jit(solution)/shard_map/ppermute | solution.py:21
  63.6 4.8 %collective-permute-start.12 = (f32[32,64]{0,1:T(8,128)S(1)}, f32[32,64]{0,1:T(8,128)S(1)}, u32[]{:S(2)}, u32[]{:S(2)}) collective-permute-start(f32[32,64]{0,1:T(8,128)S(1)} %add_add_fusion.4), channel_id=1, source_target_pairs={{0,32},{1,33},{2,34},{3,35},{4,36},{5,37},{6,38},{7,39},{8,40},{9,... | collective-permute-start | bytes 24584 | tf_op jit(solution)/shard_map/ppermute | solution.py:21
  65.2 5.5 %collective-permute-start.13 = (f32[32,64]{0,1:T(8,128)S(1)}, f32[32,64]{0,1:T(8,128)S(1)}, u32[]{:S(2)}, u32[]{:S(2)}) collective-permute-start(f32[32,64]{0,1:T(8,128)S(1)} %add_add_fusion.4), channel_id=1, source_target_pairs={{0,64},{1,65},{2,66},{3,67},{4,68},{5,69},{6,70},{7,71},{8,72},{9,... | collective-permute-start | bytes 24584 | tf_op jit(solution)/shard_map/ppermute | solution.py:21
  68.1 5.1 %collective-permute-start.14 = (f32[32,64]{0,1:T(8,128)S(1)}, f32[32,64]{0,1:T(8,128)S(1)}, u32[]{:S(2)}, u32[]{:S(2)}) collective-permute-start(f32[32,64]{0,1:T(8,128)S(1)} %add_add_fusion.4), channel_id=1, source_target_pairs={{0,96},{1,97},{2,98},{3,99},{4,100},{5,101},{6,102},{7,103},{8,104... | collective-permute-start | bytes 24584 | tf_op jit(solution)/shard_map/ppermute | solution.py:21
  78.2 3.5 %copy-start.2 = (f32[16,16]{1,0:T(8,128)}, f32[16,16]{1,0:T(8,128)S(1)}, u32[]{:S(2)}) copy-start(f32[16,16]{1,0:T(8,128)S(1)} %fusion.141) | copy-start | bytes 3076
  81.4 43.5 %copy-start = (f32[64,64,256]{2,0,1:T(8,128)}, f32[64,64,256]{2,0,1:T(8,128)S(1)}, u32[]{:S(2)}) copy-start(f32[64,64,256]{2,0,1:T(8,128)S(1)} %fusion.18) | copy-start | bytes 12582916
  81.7 20.1 %collective-permute-start.15 = (f32[16,1,64,256]{3,0,2,1:T(8,128)S(1)}, f32[16,1,64,256]{3,0,2,1:T(8,128)S(1)}, u32[]{:S(2)}, u32[]{:S(2)}) collective-permute-start(f32[16,1,64,256]{3,0,2,1:T(8,128)S(1)} %fusion.66), channel_id=1, source_target_pairs={{0,2},{2,4},{4,6},{6,8},{8,10},{10,12},{12,14},{14,16},{16,18},{18... | collective-permute-start | bytes 3145736 | tf_op jit(solution)/shard_map/ppermute | solution.py:55
  81.8 20.0 %collective-permute-start.16 = (f32[16,1,64,256]{3,0,2,1:T(8,128)S(1)}, f32[16,1,64,256]{3,0,2,1:T(8,128)S(1)}, u32[]{:S(2)}, u32[]{:S(2)}) collective-permute-start(f32[16,1,64,256]{3,0,2,1:T(8,128)S(1)} %fusion.66), channel_id=1, source_target_pairs={{2,0},{4,2},{6,4},{8,6},{10,8},{12,10},{14,12},{16,14},{18,16},{20... | collective-permute-start | bytes 3145736 | tf_op jit(solution)/shard_map/ppermute | solution.py:56
  89.5 11.3 %collective-permute-start.17 = (f32[16,1,2,256]{3,0,2,1:T(8,128)S(1)}, f32[16,1,2,256]{3,0,2,1:T(8,128)S(1)}, u32[]{:S(2)}, u32[]{:S(2)}) collective-permute-start(f32[16,1,2,256]{3,0,2,1:T(8,128)S(1)} %pad_maximum_fusion.5), channel_id=1, source_target_pairs={{0,1},{1,0},{2,3},{3,2},{4,5},{5,4},{6,7},{7,6},{8,9},{9,8},{10,11... | collective-permute-start | bytes 98312 | tf_op jit(solution)/shard_map/ppermute | solution.py:46
  103.5 20.1 %collective-permute-start.18 = (f32[16,1,64,256]{3,0,2,1:T(8,128)S(1)}, f32[16,1,64,256]{3,0,2,1:T(8,128)S(1)}, u32[]{:S(2)}, u32[]{:S(2)}) collective-permute-start(f32[16,1,64,256]{3,0,2,1:T(8,128)S(1)} %fusion.22), channel_id=1, source_target_pairs={{0,2},{2,4},{4,6},{6,8},{8,10},{10,12},{12,14},{14,16},{16,18},{18... | collective-permute-start | bytes 3145736 | tf_op jit(solution)/shard_map/ppermute | solution.py:55
  103.6 20.0 %collective-permute-start.19 = (f32[16,1,64,256]{3,0,2,1:T(8,128)S(1)}, f32[16,1,64,256]{3,0,2,1:T(8,128)S(1)}, u32[]{:S(2)}, u32[]{:S(2)}) collective-permute-start(f32[16,1,64,256]{3,0,2,1:T(8,128)S(1)} %fusion.22), channel_id=1, source_target_pairs={{2,0},{4,2},{6,4},{8,6},{10,8},{12,10},{14,12},{16,14},{18,16},{20... | collective-permute-start | bytes 3145736 | tf_op jit(solution)/shard_map/ppermute | solution.py:56
  111.0 9.4 %collective-permute-start.20 = (f32[16,1,2,256]{3,0,2,1:T(8,128)S(1)}, f32[16,1,2,256]{3,0,2,1:T(8,128)S(1)}, u32[]{:S(2)}, u32[]{:S(2)}) collective-permute-start(f32[16,1,2,256]{3,0,2,1:T(8,128)S(1)} %pad_maximum_fusion.6), channel_id=1, source_target_pairs={{0,1},{1,0},{2,3},{3,2},{4,5},{5,4},{6,7},{7,6},{8,9},{9,8},{10,11... | collective-permute-start | bytes 98312 | tf_op jit(solution)/shard_map/ppermute | solution.py:46
  132.1 4.0 %collective-permute-start.21 = (f32[112,80]{0,1:T(8,128)S(1)}, f32[112,80]{0,1:T(8,128)S(1)}, u32[]{:S(2)}, u32[]{:S(2)}) collective-permute-start(f32[112,80]{0,1:T(8,128)S(1)} %select_maximum_fusion), channel_id=1, source_target_pairs={{0,1},{1,0},{2,3},{3,2},{4,5},{5,4},{6,7},{7,6},{8,9},{9,8},{10,11... | collective-permute-start | bytes 107528 | tf_op jit(solution)/shard_map/ppermute | solution.py:21
  136.2 1.9 collective-permute-start.22
  136.2 4.4 %collective-permute-start.23 = (f32[112,80]{0,1:T(8,128)S(1)}, f32[112,80]{0,1:T(8,128)S(1)}, u32[]{:S(2)}, u32[]{:S(2)}) collective-permute-start(f32[112,80]{0,1:T(8,128)S(1)} %fusion.183), channel_id=1, source_target_pairs={{0,4},{1,5},{2,6},{3,7},{4,0},{5,1},{6,2},{7,3},{8,12},{9,13},{10,... | collective-permute-start | bytes 107528 | tf_op jit(solution)/shard_map/ppermute | solution.py:21
  136.3 4.3 %collective-permute-start.24 = (f32[112,80]{0,1:T(8,128)S(1)}, f32[112,80]{0,1:T(8,128)S(1)}, u32[]{:S(2)}, u32[]{:S(2)}) collective-permute-start(f32[112,80]{0,1:T(8,128)S(1)} %fusion.183), channel_id=1, source_target_pairs={{0,6},{1,7},{2,4},{3,5},{4,2},{5,3},{6,0},{7,1},{8,14},{9,15},{10,... | collective-permute-start | bytes 107528 | tf_op jit(solution)/shard_map/ppermute | solution.py:21
  140.6 6.8 %collective-permute-start.25 = (f32[112,80]{0,1:T(8,128)S(1)}, f32[112,80]{0,1:T(8,128)S(1)}, u32[]{:S(2)}, u32[]{:S(2)}) collective-permute-start(f32[112,80]{0,1:T(8,128)S(1)} %add_add_fusion.2), channel_id=1, source_target_pairs={{0,8},{1,9},{2,10},{3,11},{4,12},{5,13},{6,14},{7,15},{8,0},{9,1},... | collective-permute-start | bytes 107528 | tf_op jit(solution)/shard_map/ppermute | solution.py:21
  143.5 5.5 %collective-permute-start.26 = (f32[112,80]{0,1:T(8,128)S(1)}, f32[112,80]{0,1:T(8,128)S(1)}, u32[]{:S(2)}, u32[]{:S(2)}) collective-permute-start(f32[112,80]{0,1:T(8,128)S(1)} %add_add_fusion.2), channel_id=1, source_target_pairs={{0,16},{1,17},{2,18},{3,19},{4,20},{5,21},{6,22},{7,23},{8,24},{9,... | collective-permute-start | bytes 107528 | tf_op jit(solution)/shard_map/ppermute | solution.py:21
  143.5 7.9 %collective-permute-start.27 = (f32[112,80]{0,1:T(8,128)S(1)}, f32[112,80]{0,1:T(8,128)S(1)}, u32[]{:S(2)}, u32[]{:S(2)}) collective-permute-start(f32[112,80]{0,1:T(8,128)S(1)} %add_add_fusion.2), channel_id=1, source_target_pairs={{0,24},{1,25},{2,26},{3,27},{4,28},{5,29},{6,30},{7,31},{8,16},{9,... | collective-permute-start | bytes 107528 | tf_op jit(solution)/shard_map/ppermute | solution.py:21
  151.4 7.9 %collective-permute-start.28 = (f32[112,80]{0,1:T(8,128)S(1)}, f32[112,80]{0,1:T(8,128)S(1)}, u32[]{:S(2)}, u32[]{:S(2)}) collective-permute-start(f32[112,80]{0,1:T(8,128)S(1)} %add_add_fusion.1), channel_id=1, source_target_pairs={{0,32},{1,33},{2,34},{3,35},{4,36},{5,37},{6,38},{7,39},{8,40},{9,... | collective-permute-start | bytes 107528 | tf_op jit(solution)/shard_map/ppermute | solution.py:21
  152.4 9.4 %collective-permute-start.29 = (f32[112,80]{0,1:T(8,128)S(1)}, f32[112,80]{0,1:T(8,128)S(1)}, u32[]{:S(2)}, u32[]{:S(2)}) collective-permute-start(f32[112,80]{0,1:T(8,128)S(1)} %add_add_fusion.1), channel_id=1, source_target_pairs={{0,64},{1,65},{2,66},{3,67},{4,68},{5,69},{6,70},{7,71},{8,72},{9,... | collective-permute-start | bytes 107528 | tf_op jit(solution)/shard_map/ppermute | solution.py:21
  159.3 5.2 %collective-permute-start.30 = (f32[112,80]{0,1:T(8,128)S(1)}, f32[112,80]{0,1:T(8,128)S(1)}, u32[]{:S(2)}, u32[]{:S(2)}) collective-permute-start(f32[112,80]{0,1:T(8,128)S(1)} %add_add_fusion.1), channel_id=1, source_target_pairs={{0,96},{1,97},{2,98},{3,99},{4,100},{5,101},{6,102},{7,103},{8,104... | collective-permute-start | bytes 107528 | tf_op jit(solution)/shard_map/ppermute | solution.py:21
  179.1 10.9 %collective-permute-start.31 = (f32[8,1,64,256]{3,2,0,1:T(8,128)S(1)}, f32[8,1,64,256]{3,2,0,1:T(8,128)S(1)}, u32[]{:S(2)}, u32[]{:S(2)}) collective-permute-start(f32[8,1,64,256]{3,2,0,1:T(8,128)S(1)} %bitcast.203), channel_id=1, source_target_pairs={{0,1},{1,0},{2,3},{3,2},{4,5},{5,4},{6,7},{7,6},{8,9},{9,8},{10,11... | collective-permute-start | bytes 1572872 | tf_op jit(solution)/shard_map/ppermute | solution.py:46

commit v6 on v4

--- a/solution.py
+++ b/solution.py
@@ -97,16 +97,34 @@
     cross_down = [(j, i) for i, j in cross_up]
     keep_rows = keep[:, :, 1:-1]
     give_rows = give[:, :, 1:-1]
-    before = in_order(lax.ppermute(keep_rows, AXES, same_up), lax.ppermute(give_rows, AXES, cross_up), 0)
-    after = in_order(lax.ppermute(keep_rows, AXES, same_down), lax.ppermute(give_rows, AXES, cross_down), 0)
+    pot = lax.dynamic_slice_in_dim(potential, v * rows, rows, 1)
+    keep_pot = jnp.concatenate([keep_rows, pot[None]], 0)
+    up_same = lax.ppermute(keep_pot, AXES, same_up)
+    down_same = lax.ppermute(keep_pot, AXES, same_down)
+    before = in_order(up_same[:mine], lax.ppermute(give_rows, AXES, cross_up), 0)
+    after = in_order(down_same[:mine], lax.ppermute(give_rows, AXES, cross_down), 0)
+    pot_nb = jnp.concatenate([up_same[mine], down_same[mine]], 0)
+    pot_ends = jnp.concatenate(
+        [
+            lax.dynamic_slice_in_dim(potential, (v * rows - 1) % (2 * rows), 1, 1),
+            lax.dynamic_slice_in_dim(potential, (v * rows + rows) % (2 * rows), 1, 1),
+        ],
+        axis=1,
+    )
     whole_ext = in_order(keep, got, 0)
     whole = whole_ext[:, :, 1:-1]
     ends = jnp.concatenate([whole_ext[:, :, :1], whole_ext[:, :, -1:]], axis=2)
 
-    pot = lax.dynamic_slice_in_dim(potential, v * rows, rows, 1)
-    shifted = jnp.where(pot >= SIGMA, pot - SIGMA + 6.0, pot - SIGMA - 6.0)
+    def shift_of(p):
+        return jnp.where(p >= SIGMA, p - SIGMA + 6.0, p - SIGMA - 6.0)
+
+    shifted = shift_of(pot)
 
     h_whole = stencil(whole, (before, after, ends), pot)
+    h_nb = jnp.concatenate(
+        [lax.ppermute(h_whole, AXES, same_up), lax.ppermute(h_whole, AXES, same_down)], axis=1
+    )
+    h_ends = swap_vec(jnp.concatenate([h_whole[:, :, rows - 1:], h_whole[:, :, :1]], axis=2))
     nb = whole.shape[0]
     fields = jnp.concatenate([whole, h_whole, whole / shifted, h_whole / shifted], 0)
     first = allsum(local_inner(fields[: 2 * nb], fields, scale), groups)
@@ -141,7 +159,15 @@
     basis, a_basis, resid = parts[:nb], parts[nb:2 * nb], parts[2 * nb:3 * nb]
     correction = -resid / shifted
     proj = correction - parts[3 * nb:]
-    pieces = halo(proj)
+    w_nb = weights[:, 2 * nb:]
+
+    def proj_of(s_part, h_part, d_part):
+        got = combine(w_nb, jnp.concatenate([s_part, h_part], 0))
+        return -got[:nb] / d_part - got[nb:]
+
+    proj_nb = proj_of(jnp.concatenate([before, after], axis=1), h_nb, shift_of(pot_nb))
+    proj_ends = proj_of(ends, h_ends, shift_of(pot_ends))
+    pieces = (proj_nb[:, 0:1], proj_nb[:, 1:2], proj_ends)
 
     moved = stencil(proj, pieces, pot) - SIGMA * proj
     correction = correction + (-resid - (moved - combine(back, basis))) / shifted

time: 185 us -> 190 us (1.027)
  waiting for transfers between devices: 86.3 us -> 69.8 us
  starting transfers between devices: 62.8 us -> 71.5 us
  local copies, waits for them, and re-layouts: 5.39 us -> 10.9 us
  matrix products: 16.4 us -> 20.3 us
  other arithmetic: 12.1 us -> 15.7 us
    ppermute x2 -> x4, starting transfers between devices: 7.02 us -> 15.6 us  [the longest x1 8.51 us: local(): lax.ppermute(h_whole, AXES, same_down)]
    ppermute x2 -> x1, waiting for transfers between devices: 7.83 us -> 0.01 us  [halo(): after = lax.ppermute(value, 'space', down)]
    ppermute x2 -> x1, waiting for transfers between devices: 7.63 us -> 0.01 us  [halo(): before = lax.ppermute(value, 'space', up)]
    ppermute x1, waiting for transfers between devices: 8.77 us -> 4.61 us  [local(): lax.ppermute(give_rows, AXES, cross_down)]
    dot_general x6 -> x8, matrix products: 8.17 us -> 12.1 us  [combine(): return jnp.einsum('kj,kzyx->jzyx', coeff, vectors, precision=FIELD_PREC)]
    ppermute x30, waiting for transfers between devices: 38 us -> 41.8 us  [allsum(): vals[m] = lax.ppermute(x, AXES, [(i, i ^ mask) for i in range(n)])]
    concatenate x0 -> x4, local copies, waits for them, and re-layouts: none -> 2.04 us  [the longest x2 1.69 us: local(): pot_nb = jnp.concatenate([up_same[mine], down_same[mine]], 0)]
  transfers between devices with their start and end apart: 42 -> 42, of which waited for: 31 -> 28; matrix products, arithmetic and copies ran while one was open for 3% -> 11% of each run, Pallas kernels for 0% -> 0%
where the time goes in v6:
time: 190 us; the launch traced here: 189 us
  starting transfers between devices  71.5 us (38%)
  waiting for transfers between devices  69.8 us (37%)
  matrix products  20.3 us (11%)
  other arithmetic  15.7 us (8%)
  local copies, waits for them, and re-layouts  10.9 us (6%)
    ppermute x30, starting transfers between devices, allsum(): vals[m] = lax.ppermute(x, AXES, [(i, i ^ mask) for i in range(n)])  42.6 us
    ppermute x30, waiting for transfers between devices, allsum(): vals[m] = lax.ppermute(x, AXES, [(i, i ^ mask) for i in range(n)])  41.8 us
    ppermute x4, waiting for transfers between devices, swap_vec(): return lax.ppermute(value, 'vec', [(0, 1), (1, 0)])  22 us
    dot_general x8, matrix products, combine(): return jnp.einsum('kj,kzyx->jzyx', coeff, vectors, precision=FIELD_PREC)  12.1 us
    ppermute x1, starting transfers between devices, local(): lax.ppermute(h_whole, AXES, same_down)  8.51 us
    ppermute x1, starting transfers between devices, local(): down_same = lax.ppermute(keep_pot, AXES, same_down)  7.09 us
    ppermute x4, starting transfers between devices, swap_vec(): return lax.ppermute(value, 'vec', [(0, 1), (1, 0)])  6.51 us
    ppermute x1, starting transfers between devices, local(): lax.ppermute(give_rows, AXES, cross_down)  6.33 us
  transfers between devices with their start and end apart: 42, of which 28 were waited for; matrix products, arithmetic and copies ran while one was open for 11% of the time, Pallas kernels for 0%

profile of v6, /device:TPU:0, one launch (start us, length us, event | category | flops | bytes accessed | tf_op | source)
XLA Modules:
  0.0 189.3 jit_solution(3567763969368568479)
XLA Ops:
  0.6 1.8 copy.48
  3.5 2.0 %collective-permute-start = (f32[8,1,66,256]{3,0,2,1:T(8,128)}, f32[8,1,66,256]{3,0,2,1:T(8,128)}, u32[]{:S(2)}, u32[]{:S(2)}) collective-permute-start(f32[8,1,66,256]{3,0,2,1:T(8,128)} %get-tuple-element.26), channel_id=1, source_target_pairs={{0,1},{1,0},{2,3},{3,2},{4,5},{5,4},{6,7},{7,6},{8,9},{9,8},{10,11... | collective-permute-start | bytes 1622024 | tf_op jit(solution)/shard_map/ppermute | solution.py:46
  6.3 6.3 %collective-permute-start.4 = (f32[8,1,64,256]{3,0,2,1:T(8,128)}, f32[8,1,64,256]{3,0,2,1:T(8,128)}, u32[]{:S(2)}, u32[]{:S(2)}) collective-permute-start(f32[8,1,64,256]{3,0,2,1:T(8,128)} %get-tuple-element.23), channel_id=1, source_target_pairs={{3,0},{2,1},{5,2},{4,3},{7,4},{6,5},{9,6},{8,7},{11,8},{10,9},{13,... | collective-permute-start | bytes 1572872 | tf_op jit(solution)/shard_map/ppermute | solution.py:105
  13.2 7.1 %collective-permute-start.3 = (f32[9,1,64,256]{3,2,1,0:T(8,128)S(1)}, f32[9,1,64,256]{3,2,1,0:T(8,128)}, u32[]{:S(2)}, u32[]{:S(2)}) collective-permute-start(f32[9,1,64,256]{3,2,1,0:T(8,128)S(1)} %copy.51), channel_id=1, source_target_pairs={{2,0},{3,1},{4,2},{5,3},{6,4},{7,5},{8,6},{9,7},{10,8},{11,9},{12,... | collective-permute-start | bytes 1769480 | tf_op jit(solution)/shard_map/ppermute | solution.py:103
  20.9 10.0 %collective-permute-done = f32[8,1,66,256]{3,0,2,1:T(8,128)} collective-permute-done((f32[8,1,66,256]{3,0,2,1:T(8,128)}, f32[8,1,66,256]{3,0,2,1:T(8,128)}, u32[]{:S(2)}, u32[]{:S(2)}) %collective-permute-start) | collective-permute-done | bytes 540704 | tf_op jit(solution)/shard_map/ppermute | solution.py:46
  30.9 1.3 maximum_select_fusion
  32.9 1.1 slice.270
  34.3 1.2 collective-permute-done.1
  35.8 4.6 %collective-permute-done.4 = f32[8,1,64,256]{3,0,2,1:T(8,128)} collective-permute-done((f32[8,1,64,256]{3,0,2,1:T(8,128)}, f32[8,1,64,256]{3,0,2,1:T(8,128)}, u32[]{:S(2)}, u32[]{:S(2)}) %collective-permute-start.4) | collective-permute-done | bytes 524320 | tf_op jit(solution)/shard_map/ppermute | solution.py:105
  40.5 3.3 %broadcast_divide_fusion = (f32[16,1,64,256]{3,0,2,1:T(8,128)S(1)}, f32[16,1,64,256]{3,0,2,1:T(8,128)S(1)}, f32[16,1,64,256]{3,0,2,1:T(8,128)S(1)}, f32[16,1,64,256]{3,0,2,1:T(8,128)}, f32[16,1,64,256]{3,0,2,1:T(8,128)S(1)}) fusion(f32[64,256]{1,0:T(8,128)S(1)} %get-tuple-element.14, f32[16,1,64,1]{3,0,2,1:T(8,128)S(1)} %get-tuple-element.20, ...), kind=kLoop, calls=%fused_computation.98 | loop fusion | flops 4456448 | bytes 12713985 | tf_op jit(solution)/shard_map/div | solution.py:129
  43.8 8.5 %collective-permute-start.16 = (f32[16,1,64,256]{3,0,2,1:T(8,128)S(1)}, f32[16,1,64,256]{3,0,2,1:T(8,128)}, u32[]{:S(2)}, u32[]{:S(2)}) collective-permute-start(f32[16,1,64,256]{3,0,2,1:T(8,128)S(1)} %get-tuple-element.11), channel_id=1, source_target_pairs={{2,0},{3,1},{4,2},{5,3},{6,4},{7,5},{8,6},{9,7},{10,8},{11,9},{12,... | collective-permute-start | bytes 3145736 | tf_op jit(solution)/shard_map/ppermute | solution.py:125
  52.3 1.8 fusion.66
  54.1 1.1 collective-permute-start.5
  56.0 10.1 %collective-permute-done.5 = f32[32,64]{0,1:T(8,128)S(1)} collective-permute-done((f32[32,64]{0,1:T(8,128)S(1)}, f32[32,64]{0,1:T(8,128)S(1)}, u32[]{:S(2)}, u32[]{:S(2)}) %collective-permute-start.5) | collective-permute-done | bytes 8224 | tf_op jit(solution)/shard_map/ppermute | solution.py:21
  66.2 1.8 collective-permute-start.6
  70.2 2.6 %collective-permute-start.11 = (f32[32,64]{0,1:T(8,128)S(1)}, f32[32,64]{0,1:T(8,128)S(1)}, u32[]{:S(2)}, u32[]{:S(2)}) collective-permute-start(f32[32,64]{0,1:T(8,128)S(1)} %add_add_fusion.2), channel_id=1, source_target_pairs={{0,24},{1,25},{2,26},{3,27},{4,28},{5,29},{6,30},{7,31},{8,16},{9,... | collective-permute-start | bytes 24584 | tf_op jit(solution)/shard_map/ppermute | solution.py:21
  72.7 2.7 %collective-permute-start.10 = (f32[32,64]{0,1:T(8,128)S(1)}, f32[32,64]{0,1:T(8,128)S(1)}, u32[]{:S(2)}, u32[]{:S(2)}) collective-permute-start(f32[32,64]{0,1:T(8,128)S(1)} %add_add_fusion.2), channel_id=1, source_target_pairs={{0,16},{1,17},{2,18},{3,19},{4,20},{5,21},{6,22},{7,23},{8,24},{9,... | collective-permute-start | bytes 24584 | tf_op jit(solution)/shard_map/ppermute | solution.py:21
  75.5 1.3 collective-permute-start.9
  76.8 1.3 collective-permute-done.11
  78.4 2.5 %collective-permute-done.9 = f32[32,64]{0,1:T(8,128)S(1)} collective-permute-done((f32[32,64]{0,1:T(8,128)S(1)}, f32[32,64]{0,1:T(8,128)S(1)}, u32[]{:S(2)}, u32[]{:S(2)}) %collective-permute-start.9) | collective-permute-done | bytes 8224 | tf_op jit(solution)/shard_map/ppermute | solution.py:21
  80.9 3.1 %collective-permute-start.14 = (f32[32,64]{0,1:T(8,128)S(1)}, f32[32,64]{0,1:T(8,128)S(1)}, u32[]{:S(2)}, u32[]{:S(2)}) collective-permute-start(f32[32,64]{0,1:T(8,128)S(1)} %add_add_fusion.1), channel_id=1, source_target_pairs={{0,96},{1,97},{2,98},{3,99},{4,100},{5,101},{6,102},{7,103},{8,104... | collective-permute-start | bytes 24584 | tf_op jit(solution)/shard_map/ppermute | solution.py:21
  85.1 1.0 collective-permute-done.14
  86.1 2.0 %collective-permute-start.17 = (f32[16,1,2,256]{3,0,2,1:T(8,128)S(1)}, f32[16,1,2,256]{3,0,2,1:T(8,128)S(1)}, u32[]{:S(2)}, u32[]{:S(2)}) collective-permute-start(f32[16,1,2,256]{3,0,2,1:T(8,128)S(1)} %pad_maximum_fusion.7), channel_id=1, source_target_pairs={{0,1},{1,0},{2,3},{3,2},{4,5},{5,4},{6,7},{7,6},{8,9},{9,8},{10,11... | collective-permute-start | bytes 98312 | tf_op jit(solution)/shard_map/ppermute | solution.py:46
  88.1 1.3 collective-permute-done.13
  89.5 1.5 cholesky.44
  92.3 1.2 custom-call.6
  96.5 1.9 fusion.18
  100.0 1.0 copy-done.1
  101.0 3.7 %fusion.7 = f32[32,2,64,256]{3,0,2,1:T(8,128)S(1)} fusion(f32[16,1,64,256]{3,0,2,1:T(8,128)} %collective-permute-done.16, f32[16,1,64,256]{3,0,2,1:T(8,128)} %collective-permute-done.15, f32[16,1,64,256]{3,0,2,1:T(8,128)S(1)} %get-tuple-element.12, f32[16,1,64,256]{3,0,2,1:T(8,128)S(1)} %copy-done.1, f32[32,64]{1,0:T(8,128)S(1)} %maximum_maximum_fusion), kind=kOutput, calls=%fused_computation.8 | convolution fusion | flops 204472320 | bytes 8396800 | tf_op jit(solution)/shard_map/kj,kzyx->jzyx/dot_general | solution.py:38
  105.3 1.6 fusion.22
  106.9 0.9 fusion.38
  107.8 2.2 %collective-permute-start.21 = (f32[32,16]{0,1:T(8,128)S(1)}, f32[32,16]{0,1:T(8,128)S(1)}, u32[]{:S(2)}, u32[]{:S(2)}) collective-permute-start(f32[32,16]{0,1:T(8,128)S(1)} %fusion.38), channel_id=1, source_target_pairs={{0,1},{1,0},{2,3},{3,2},{4,5},{5,4},{6,7},{7,6},{8,9},{9,8},{10,11... | collective-permute-start | bytes 6152 | tf_op jit(solution)/shard_map/ppermute | solution.py:21
  110.6 1.1 collective-permute-done.21
  112.3 1.3 collective-permute-start.22
  113.9 0.9 collective-permute-done.24
  114.8 8.1 %collective-permute-done.23 = f32[32,16]{0,1:T(8,128)S(1)} collective-permute-done((f32[32,16]{0,1:T(8,128)S(1)}, f32[32,16]{0,1:T(8,128)S(1)}, u32[]{:S(2)}, u32[]{:S(2)}) %collective-permute-start.23) | collective-permute-done | bytes 2080 | tf_op jit(solution)/shard_map/ppermute | solution.py:21
  122.9 1.4 collective-permute-start.27
  124.3 2.3 %collective-permute-start.26 = (f32[32,16]{0,1:T(8,128)S(1)}, f32[32,16]{0,1:T(8,128)S(1)}, u32[]{:S(2)}, u32[]{:S(2)}) collective-permute-start(f32[32,16]{0,1:T(8,128)S(1)} %add_add_fusion.8), channel_id=1, source_target_pairs={{0,16},{1,17},{2,18},{3,19},{4,20},{5,21},{6,22},{7,23},{8,24},{9,... | collective-permute-start | bytes 6152 | tf_op jit(solution)/shard_map/ppermute | solution.py:21
  126.6 2.9 %collective-permute-start.25 = (f32[32,16]{0,1:T(8,128)S(1)}, f32[32,16]{0,1:T(8,128)S(1)}, u32[]{:S(2)}, u32[]{:S(2)}) collective-permute-start(f32[32,16]{0,1:T(8,128)S(1)} %add_add_fusion.8), channel_id=1, source_target_pairs={{0,8},{1,9},{2,10},{3,11},{4,12},{5,13},{6,14},{7,15},{8,0},{9,1},... | collective-permute-start | bytes 6152 | tf_op jit(solution)/shard_map/ppermute | solution.py:21
  130.6 1.2 collective-permute-done.25
  131.8 1.3 collective-permute-start.30
  133.9 2.0 %collective-permute-start.28 = (f32[32,16]{0,1:T(8,128)S(1)}, f32[32,16]{0,1:T(8,128)S(1)}, u32[]{:S(2)}, u32[]{:S(2)}) collective-permute-start(f32[32,16]{0,1:T(8,128)S(1)} %add_add_fusion.7), channel_id=1, source_target_pairs={{0,32},{1,33},{2,34},{3,35},{4,36},{5,37},{6,38},{7,39},{8,40},{9,... | collective-permute-start | bytes 6152 | tf_op jit(solution)/shard_map/ppermute | solution.py:21
  136.6 1.6 collective-permute-start.20
  139.0 1.5 collective-permute-done.20
  140.5 1.6 fusion.27
  143.8 1.6 collective-permute-start.31
  145.4 2.1 %collective-permute-done.31 = f32[32,16]{0,1:T(8,128)S(1)} collective-permute-done((f32[32,16]{0,1:T(8,128)S(1)}, f32[32,16]{0,1:T(8,128)S(1)}, u32[]{:S(2)}, u32[]{:S(2)}) %collective-permute-start.31) | collective-permute-done | bytes 2080 | tf_op jit(solution)/shard_map/ppermute | solution.py:21
  147.6 1.5 collective-permute-start.33
  149.4 1.3 collective-permute-done.34
  151.3 3.7 %collective-permute-start.37 = (f32[32,16]{0,1:T(8,128)S(1)}, f32[32,16]{0,1:T(8,128)S(1)}, u32[]{:S(2)}, u32[]{:S(2)}) collective-permute-start(f32[32,16]{0,1:T(8,128)S(1)} %add_add_fusion.5), channel_id=1, source_target_pairs={{0,24},{1,25},{2,26},{3,27},{4,28},{5,29},{6,30},{7,31},{8,16},{9,... | collective-permute-start | bytes 6152 | tf_op jit(solution)/shard_map/ppermute | solution.py:21
  155.0 2.9 %collective-permute-start.36 = (f32[32,16]{0,1:T(8,128)S(1)}, f32[32,16]{0,1:T(8,128)S(1)}, u32[]{:S(2)}, u32[]{:S(2)}) collective-permute-start(f32[32,16]{0,1:T(8,128)S(1)} %add_add_fusion.5), channel_id=1, source_target_pairs={{0,16},{1,17},{2,18},{3,19},{4,20},{5,21},{6,22},{7,23},{8,24},{9,... | collective-permute-start | bytes 6152 | tf_op jit(solution)/shard_map/ppermute | solution.py:21
  157.9 1.1 collective-permute-done.37
  159.0 1.2 collective-permute-done.36
  160.1 2.9 %collective-permute-done.35 = f32[32,16]{0,1:T(8,128)S(1)} collective-permute-done((f32[32,16]{0,1:T(8,128)S(1)}, f32[32,16]{0,1:T(8,128)S(1)}, u32[]{:S(2)}, u32[]{:S(2)}) %collective-permute-start.35) | collective-permute-done | bytes 2080 | tf_op jit(solution)/shard_map/ppermute | solution.py:21
  163.0 0.9 collective-permute-start.40
  163.9 1.0 collective-permute-start.39
  165.0 2.2 %collective-permute-start.38 = (f32[32,16]{0,1:T(8,128)S(1)}, f32[32,16]{0,1:T(8,128)S(1)}, u32[]{:S(2)}, u32[]{:S(2)}) collective-permute-start(f32[32,16]{0,1:T(8,128)S(1)} %add_add_fusion.4), channel_id=1, source_target_pairs={{0,32},{1,33},{2,34},{3,35},{4,36},{5,37},{6,38},{7,39},{8,40},{9,... | collective-permute-start | bytes 6152 | tf_op jit(solution)/shard_map/ppermute | solution.py:21
  167.9 1.2 collective-permute-done.39
  169.1 1.8 fusion.29
  171.5 1.5 cholesky.55
  174.3 1.2 custom-call.7
  176.6 0.9 collective-permute-start.41
  177.6 10.6 %collective-permute-done.41 = f32[8,1,64,256]{3,2,0,1:T(8,128)S(1)} collective-permute-done((f32[8,1,64,256]{3,2,0,1:T(8,128)S(1)}, f32[8,1,64,256]{3,2,0,1:T(8,128)S(1)}, u32[]{:S(2)}, u32[]{:S(2)}) %collective-permute-start.41) | collective-permute-done | bytes 524320 | tf_op jit(solution)/shard_map/ppermute | solution.py:46
  188.2 1.0 fusion.57
  (136 shorter events, 26.9 us)
Async XLA Ops:
  2.6 10.1 %copy-start.3 = (f32[1,128,256]{2,1,0:T(8,128)S(1)}, f32[1,128,256]{2,1,0:T(8,128)}, u32[]{:S(2)}) copy-start(f32[1,128,256]{2,1,0:T(8,128)} %param.5) | copy-start | bytes 393220
  3.5 27.4 %collective-permute-start = (f32[8,1,66,256]{3,0,2,1:T(8,128)}, f32[8,1,66,256]{3,0,2,1:T(8,128)}, u32[]{:S(2)}, u32[]{:S(2)}) collective-permute-start(f32[8,1,66,256]{3,0,2,1:T(8,128)} %get-tuple-element.26), channel_id=1, source_target_pairs={{0,1},{1,0},{2,3},{3,2},{4,5},{5,4},{6,7},{7,6},{8,9},{9,8},{10,11... | collective-permute-start | bytes 1622024 | tf_op jit(solution)/shard_map/ppermute | solution.py:46
  6.3 34.0 %collective-permute-start.4 = (f32[8,1,64,256]{3,0,2,1:T(8,128)}, f32[8,1,64,256]{3,0,2,1:T(8,128)}, u32[]{:S(2)}, u32[]{:S(2)}) collective-permute-start(f32[8,1,64,256]{3,0,2,1:T(8,128)} %get-tuple-element.23), channel_id=1, source_target_pairs={{3,0},{2,1},{5,2},{4,3},{7,4},{6,5},{9,6},{8,7},{11,8},{10,9},{13,... | collective-permute-start | bytes 1572872 | tf_op jit(solution)/shard_map/ppermute | solution.py:105
  12.7 27.8 %collective-permute-start.2 = (f32[8,1,64,256]{3,0,2,1:T(8,128)}, f32[8,1,64,256]{3,0,2,1:T(8,128)}, u32[]{:S(2)}, u32[]{:S(2)}) collective-permute-start(f32[8,1,64,256]{3,0,2,1:T(8,128)} %get-tuple-element.23), channel_id=1, source_target_pairs={{0,3},{1,2},{2,5},{3,4},{4,7},{5,6},{6,9},{7,8},{8,11},{9,10},{10,... | collective-permute-start | bytes 1572872 | tf_op jit(solution)/shard_map/ppermute | solution.py:104
  13.2 19.6 %collective-permute-start.3 = (f32[9,1,64,256]{3,2,1,0:T(8,128)S(1)}, f32[9,1,64,256]{3,2,1,0:T(8,128)}, u32[]{:S(2)}, u32[]{:S(2)}) collective-permute-start(f32[9,1,64,256]{3,2,1,0:T(8,128)S(1)} %copy.51), channel_id=1, source_target_pairs={{2,0},{3,1},{4,2},{5,3},{6,4},{7,5},{8,6},{9,7},{10,8},{11,9},{12,... | collective-permute-start | bytes 1769480 | tf_op jit(solution)/shard_map/ppermute | solution.py:103
  20.3 15.1 %collective-permute-start.1 = (f32[9,1,64,256]{3,2,1,0:T(8,128)S(1)}, f32[9,1,64,256]{3,2,1,0:T(8,128)S(1)}, u32[]{:S(2)}, u32[]{:S(2)}) collective-permute-start(f32[9,1,64,256]{3,2,1,0:T(8,128)S(1)} %copy.51), channel_id=1, source_target_pairs={{0,2},{1,3},{2,4},{3,5},{4,6},{5,7},{6,8},{7,9},{8,10},{9,11},{10,... | collective-permute-start | bytes 1769480 | tf_op jit(solution)/shard_map/ppermute | solution.py:102
  35.4 5.1 %copy-start.2 = (f32[9,1,64,256]{3,2,1,0:T(8,128)}, f32[9,1,64,256]{3,2,1,0:T(8,128)S(1)}, u32[]{:S(2)}) copy-start(f32[9,1,64,256]{3,2,1,0:T(8,128)S(1)} %collective-permute-done.1) | copy-start | bytes 1769476
  43.8 56.2 %collective-permute-start.16 = (f32[16,1,64,256]{3,0,2,1:T(8,128)S(1)}, f32[16,1,64,256]{3,0,2,1:T(8,128)}, u32[]{:S(2)}, u32[]{:S(2)}) collective-permute-start(f32[16,1,64,256]{3,0,2,1:T(8,128)S(1)} %get-tuple-element.11), channel_id=1, source_target_pairs={{2,0},{3,1},{4,2},{5,3},{6,4},{7,5},{8,6},{9,7},{10,8},{11,9},{12,... | collective-permute-start | bytes 3145736 | tf_op jit(solution)/shard_map/ppermute | solution.py:125
  52.3 47.7 %collective-permute-start.15 = (f32[16,1,64,256]{3,0,2,1:T(8,128)S(1)}, f32[16,1,64,256]{3,0,2,1:T(8,128)}, u32[]{:S(2)}, u32[]{:S(2)}) collective-permute-start(f32[16,1,64,256]{3,0,2,1:T(8,128)S(1)} %get-tuple-element.11), channel_id=1, source_target_pairs={{0,2},{1,3},{2,4},{3,5},{4,6},{5,7},{6,8},{7,9},{8,10},{9,11},{10,... | collective-permute-start | bytes 3145736 | tf_op jit(solution)/shard_map/ppermute | solution.py:125
  54.1 12.0 %collective-permute-start.5 = (f32[32,64]{0,1:T(8,128)S(1)}, f32[32,64]{0,1:T(8,128)S(1)}, u32[]{:S(2)}, u32[]{:S(2)}) collective-permute-start(f32[32,64]{0,1:T(8,128)S(1)} %fusion.66), channel_id=1, source_target_pairs={{0,1},{1,0},{2,3},{3,2},{4,5},{5,4},{6,7},{7,6},{8,9},{9,8},{10,11... | collective-permute-start | bytes 24584 | tf_op jit(solution)/shard_map/ppermute | solution.py:21
  66.1 3.3 %collective-permute-start.8 = (f32[32,64]{0,1:T(8,128)S(1)}, f32[32,64]{0,1:T(8,128)S(1)}, u32[]{:S(2)}, u32[]{:S(2)}) collective-permute-start(f32[32,64]{0,1:T(8,128)S(1)} %add.260), channel_id=1, source_target_pairs={{0,6},{1,7},{2,4},{3,5},{4,2},{5,3},{6,0},{7,1},{8,14},{9,15},{10,... | collective-permute-start | bytes 24584 | tf_op jit(solution)/shard_map/ppermute | solution.py:21
  66.1 4.0 %collective-permute-start.7 = (f32[32,64]{0,1:T(8,128)S(1)}, f32[32,64]{0,1:T(8,128)S(1)}, u32[]{:S(2)}, u32[]{:S(2)}) collective-permute-start(f32[32,64]{0,1:T(8,128)S(1)} %add.260), channel_id=1, source_target_pairs={{0,4},{1,5},{2,6},{3,7},{4,0},{5,1},{6,2},{7,3},{8,12},{9,13},{10,... | collective-permute-start | bytes 24584 | tf_op jit(solution)/shard_map/ppermute | solution.py:21
  66.2 3.9 %collective-permute-start.6 = (f32[32,64]{0,1:T(8,128)S(1)}, f32[32,64]{0,1:T(8,128)S(1)}, u32[]{:S(2)}, u32[]{:S(2)}) collective-permute-start(f32[32,64]{0,1:T(8,128)S(1)} %add.260), channel_id=1, source_target_pairs={{0,2},{1,3},{2,0},{3,1},{4,6},{5,7},{6,4},{7,5},{8,10},{9,11},{10,... | collective-permute-start | bytes 24584 | tf_op jit(solution)/shard_map/ppermute | solution.py:21
  70.2 7.9 %collective-permute-start.11 = (f32[32,64]{0,1:T(8,128)S(1)}, f32[32,64]{0,1:T(8,128)S(1)}, u32[]{:S(2)}, u32[]{:S(2)}) collective-permute-start(f32[32,64]{0,1:T(8,128)S(1)} %add_add_fusion.2), channel_id=1, source_target_pairs={{0,24},{1,25},{2,26},{3,27},{4,28},{5,29},{6,30},{7,31},{8,16},{9,... | collective-permute-start | bytes 24584 | tf_op jit(solution)/shard_map/ppermute | solution.py:21
  72.7 5.7 %collective-permute-start.10 = (f32[32,64]{0,1:T(8,128)S(1)}, f32[32,64]{0,1:T(8,128)S(1)}, u32[]{:S(2)}, u32[]{:S(2)}) collective-permute-start(f32[32,64]{0,1:T(8,128)S(1)} %add_add_fusion.2), channel_id=1, source_target_pairs={{0,16},{1,17},{2,18},{3,19},{4,20},{5,21},{6,22},{7,23},{8,24},{9,... | collective-permute-start | bytes 24584 | tf_op jit(solution)/shard_map/ppermute | solution.py:21
  75.5 5.4 %collective-permute-start.9 = (f32[32,64]{0,1:T(8,128)S(1)}, f32[32,64]{0,1:T(8,128)S(1)}, u32[]{:S(2)}, u32[]{:S(2)}) collective-permute-start(f32[32,64]{0,1:T(8,128)S(1)} %add_add_fusion.2), channel_id=1, source_target_pairs={{0,8},{1,9},{2,10},{3,11},{4,12},{5,13},{6,14},{7,15},{8,0},{9,1},... | collective-permute-start | bytes 24584 | tf_op jit(solution)/shard_map/ppermute | solution.py:21
  80.9 5.2 %collective-permute-start.14 = (f32[32,64]{0,1:T(8,128)S(1)}, f32[32,64]{0,1:T(8,128)S(1)}, u32[]{:S(2)}, u32[]{:S(2)}) collective-permute-start(f32[32,64]{0,1:T(8,128)S(1)} %add_add_fusion.1), channel_id=1, source_target_pairs={{0,96},{1,97},{2,98},{3,99},{4,100},{5,101},{6,102},{7,103},{8,104... | collective-permute-start | bytes 24584 | tf_op jit(solution)/shard_map/ppermute | solution.py:21
  84.0 5.4 %collective-permute-start.13 = (f32[32,64]{0,1:T(8,128)S(1)}, f32[32,64]{0,1:T(8,128)S(1)}, u32[]{:S(2)}, u32[]{:S(2)}) collective-permute-start(f32[32,64]{0,1:T(8,128)S(1)} %add_add_fusion.1), channel_id=1, source_target_pairs={{0,64},{1,65},{2,66},{3,67},{4,68},{5,69},{6,70},{7,71},{8,72},{9,... | collective-permute-start | bytes 24584 | tf_op jit(solution)/shard_map/ppermute | solution.py:21
  84.6 4.8 %collective-permute-start.12 = (f32[32,64]{0,1:T(8,128)S(1)}, f32[32,64]{0,1:T(8,128)S(1)}, u32[]{:S(2)}, u32[]{:S(2)}) collective-permute-start(f32[32,64]{0,1:T(8,128)S(1)} %add_add_fusion.1), channel_id=1, source_target_pairs={{0,32},{1,33},{2,34},{3,35},{4,36},{5,37},{6,38},{7,39},{8,40},{9,... | collective-permute-start | bytes 24584 | tf_op jit(solution)/shard_map/ppermute | solution.py:21
  86.1 12.6 %collective-permute-start.17 = (f32[16,1,2,256]{3,0,2,1:T(8,128)S(1)}, f32[16,1,2,256]{3,0,2,1:T(8,128)S(1)}, u32[]{:S(2)}, u32[]{:S(2)}) collective-permute-start(f32[16,1,2,256]{3,0,2,1:T(8,128)S(1)} %pad_maximum_fusion.7), channel_id=1, source_target_pairs={{0,1},{1,0},{2,3},{3,2},{4,5},{5,4},{6,7},{7,6},{8,9},{9,8},{10,11... | collective-permute-start | bytes 98312 | tf_op jit(solution)/shard_map/ppermute | solution.py:46
  94.5 3.9 %copy-start.4 = (f32[16,16]{1,0:T(8,128)}, f32[16,16]{1,0:T(8,128)S(1)}, u32[]{:S(2)}) copy-start(f32[16,16]{1,0:T(8,128)S(1)} %fusion.138) | copy-start | bytes 3076
  96.5 2.6 %copy-start.5 = (f32[2,256]{1,0:T(2,128)S(1)}, f32[2,256]{1,0:T(2,128)}, u32[]{:S(2)}) copy-start(f32[2,256]{1,0:T(2,128)} %compare_select_fusion) | copy-start | bytes 6148
  98.4 44.5 %copy-start = (f32[64,64,256]{2,0,1:T(8,128)}, f32[64,64,256]{2,0,1:T(8,128)S(1)}, u32[]{:S(2)}) copy-start(f32[64,64,256]{2,0,1:T(8,128)S(1)} %fusion.18) | copy-start | bytes 12582916
  99.5 1.5 copy-start.1
  107.8 3.8 %collective-permute-start.21 = (f32[32,16]{0,1:T(8,128)S(1)}, f32[32,16]{0,1:T(8,128)S(1)}, u32[]{:S(2)}, u32[]{:S(2)}) collective-permute-start(f32[32,16]{0,1:T(8,128)S(1)} %fusion.38), channel_id=1, source_target_pairs={{0,1},{1,0},{2,3},{3,2},{4,5},{5,4},{6,7},{7,6},{8,9},{9,8},{10,11... | collective-permute-start | bytes 6152 | tf_op jit(solution)/shard_map/ppermute | solution.py:21
  110.0 30.5 %collective-permute-start.19 = (f32[16,1,64,256]{3,0,2,1:T(8,128)S(1)}, f32[16,1,64,256]{3,0,2,1:T(8,128)S(1)}, u32[]{:S(2)}, u32[]{:S(2)}) collective-permute-start(f32[16,1,64,256]{3,0,2,1:T(8,128)S(1)} %fusion.22), channel_id=1, source_target_pairs={{2,0},{4,2},{6,4},{8,6},{10,8},{12,10},{14,12},{16,14},{18,16},{20... | collective-permute-start | bytes 3145736 | tf_op jit(solution)/shard_map/ppermute | solution.py:56
  110.1 30.5 %collective-permute-start.18 = (f32[16,1,64,256]{3,0,2,1:T(8,128)S(1)}, f32[16,1,64,256]{3,0,2,1:T(8,128)S(1)}, u32[]{:S(2)}, u32[]{:S(2)}) collective-permute-start(f32[16,1,64,256]{3,0,2,1:T(8,128)S(1)} %fusion.22), channel_id=1, source_target_pairs={{0,2},{2,4},{4,6},{6,8},{8,10},{10,12},{12,14},{14,16},{16,18},{18... | collective-permute-start | bytes 3145736 | tf_op jit(solution)/shard_map/ppermute | solution.py:55
  111.7 3.2 %collective-permute-start.24 = (f32[32,16]{0,1:T(8,128)S(1)}, f32[32,16]{0,1:T(8,128)S(1)}, u32[]{:S(2)}, u32[]{:S(2)}) collective-permute-start(f32[32,16]{0,1:T(8,128)S(1)} %add.290), channel_id=1, source_target_pairs={{0,6},{1,7},{2,4},{3,5},{4,2},{5,3},{6,0},{7,1},{8,14},{9,15},{10,... | collective-permute-start | bytes 6152 | tf_op jit(solution)/shard_map/ppermute | solution.py:21
  111.7 11.2 %collective-permute-start.23 = (f32[32,16]{0,1:T(8,128)S(1)}, f32[32,16]{0,1:T(8,128)S(1)}, u32[]{:S(2)}, u32[]{:S(2)}) collective-permute-start(f32[32,16]{0,1:T(8,128)S(1)} %add.290), channel_id=1, source_target_pairs={{0,4},{1,5},{2,6},{3,7},{4,0},{5,1},{6,2},{7,3},{8,12},{9,13},{10,... | collective-permute-start | bytes 6152 | tf_op jit(solution)/shard_map/ppermute | solution.py:21
  112.3 10.6 %collective-permute-start.22 = (f32[32,16]{0,1:T(8,128)S(1)}, f32[32,16]{0,1:T(8,128)S(1)}, u32[]{:S(2)}, u32[]{:S(2)}) collective-permute-start(f32[32,16]{0,1:T(8,128)S(1)} %add.290), channel_id=1, source_target_pairs={{0,2},{1,3},{2,0},{3,1},{4,6},{5,7},{6,4},{7,5},{8,10},{9,11},{10,... | collective-permute-start | bytes 6152 | tf_op jit(solution)/shard_map/ppermute | solution.py:21
  122.9 7.6 %collective-permute-start.27 = (f32[32,16]{0,1:T(8,128)S(1)}, f32[32,16]{0,1:T(8,128)S(1)}, u32[]{:S(2)}, u32[]{:S(2)}) collective-permute-start(f32[32,16]{0,1:T(8,128)S(1)} %add_add_fusion.8), channel_id=1, source_target_pairs={{0,24},{1,25},{2,26},{3,27},{4,28},{5,29},{6,30},{7,31},{8,16},{9,... | collective-permute-start | bytes 6152 | tf_op jit(solution)/shard_map/ppermute | solution.py:21
  124.3 6.3 %collective-permute-start.26 = (f32[32,16]{0,1:T(8,128)S(1)}, f32[32,16]{0,1:T(8,128)S(1)}, u32[]{:S(2)}, u32[]{:S(2)}) collective-permute-start(f32[32,16]{0,1:T(8,128)S(1)} %add_add_fusion.8), channel_id=1, source_target_pairs={{0,16},{1,17},{2,18},{3,19},{4,20},{5,21},{6,22},{7,23},{8,24},{9,... | collective-permute-start | bytes 6152 | tf_op jit(solution)/shard_map/ppermute | solution.py:21
  126.6 5.2 %collective-permute-start.25 = (f32[32,16]{0,1:T(8,128)S(1)}, f32[32,16]{0,1:T(8,128)S(1)}, u32[]{:S(2)}, u32[]{:S(2)}) collective-permute-start(f32[32,16]{0,1:T(8,128)S(1)} %add_add_fusion.8), channel_id=1, source_target_pairs={{0,8},{1,9},{2,10},{3,11},{4,12},{5,13},{6,14},{7,15},{8,0},{9,1},... | collective-permute-start | bytes 6152 | tf_op jit(solution)/shard_map/ppermute | solution.py:21
  131.8 4.9 %collective-permute-start.30 = (f32[32,16]{0,1:T(8,128)S(1)}, f32[32,16]{0,1:T(8,128)S(1)}, u32[]{:S(2)}, u32[]{:S(2)}) collective-permute-start(f32[32,16]{0,1:T(8,128)S(1)} %add_add_fusion.7), channel_id=1, source_target_pairs={{0,96},{1,97},{2,98},{3,99},{4,100},{5,101},{6,102},{7,103},{8,104... | collective-permute-start | bytes 6152 | tf_op jit(solution)/shard_map/ppermute | solution.py:21
  133.0 5.2 %collective-permute-start.29 = (f32[32,16]{0,1:T(8,128)S(1)}, f32[32,16]{0,1:T(8,128)S(1)}, u32[]{:S(2)}, u32[]{:S(2)}) collective-permute-start(f32[32,16]{0,1:T(8,128)S(1)} %add_add_fusion.7), channel_id=1, source_target_pairs={{0,64},{1,65},{2,66},{3,67},{4,68},{5,69},{6,70},{7,71},{8,72},{9,... | collective-permute-start | bytes 6152 | tf_op jit(solution)/shard_map/ppermute | solution.py:21
  133.9 4.3 %collective-permute-start.28 = (f32[32,16]{0,1:T(8,128)S(1)}, f32[32,16]{0,1:T(8,128)S(1)}, u32[]{:S(2)}, u32[]{:S(2)}) collective-permute-start(f32[32,16]{0,1:T(8,128)S(1)} %add_add_fusion.7), channel_id=1, source_target_pairs={{0,32},{1,33},{2,34},{3,35},{4,36},{5,37},{6,38},{7,39},{8,40},{9,... | collective-permute-start | bytes 6152 | tf_op jit(solution)/shard_map/ppermute | solution.py:21
  136.6 3.9 %collective-permute-start.20 = (f32[16,1,2,256]{3,0,2,1:T(8,128)S(1)}, f32[16,1,2,256]{3,0,2,1:T(8,128)S(1)}, u32[]{:S(2)}, u32[]{:S(2)}) collective-permute-start(f32[16,1,2,256]{3,0,2,1:T(8,128)S(1)} %pad_maximum_fusion.8), channel_id=1, source_target_pairs={{0,1},{1,0},{2,3},{3,2},{4,5},{5,4},{6,7},{7,6},{8,9},{9,8},{10,11... | collective-permute-start | bytes 98312 | tf_op jit(solution)/shard_map/ppermute | solution.py:46
  143.8 3.7 %collective-permute-start.31 = (f32[32,16]{0,1:T(8,128)S(1)}, f32[32,16]{0,1:T(8,128)S(1)}, u32[]{:S(2)}, u32[]{:S(2)}) collective-permute-start(f32[32,16]{0,1:T(8,128)S(1)} %pad_maximum_fusion.9), channel_id=1, source_target_pairs={{0,1},{1,0},{2,3},{3,2},{4,5},{5,4},{6,7},{7,6},{8,9},{9,8},{10,11... | collective-permute-start | bytes 6152 | tf_op jit(solution)/shard_map/ppermute | solution.py:21
  147.6 3.1 %collective-permute-start.34 = (f32[32,16]{0,1:T(8,128)S(1)}, f32[32,16]{0,1:T(8,128)S(1)}, u32[]{:S(2)}, u32[]{:S(2)}) collective-permute-start(f32[32,16]{0,1:T(8,128)S(1)} %fusion.171), channel_id=1, source_target_pairs={{0,6},{1,7},{2,4},{3,5},{4,2},{5,3},{6,0},{7,1},{8,14},{9,15},{10,... | collective-permute-start | bytes 6152 | tf_op jit(solution)/shard_map/ppermute | solution.py:21
  147.6 3.7 %collective-permute-start.33 = (f32[32,16]{0,1:T(8,128)S(1)}, f32[32,16]{0,1:T(8,128)S(1)}, u32[]{:S(2)}, u32[]{:S(2)}) collective-permute-start(f32[32,16]{0,1:T(8,128)S(1)} %fusion.171), channel_id=1, source_target_pairs={{0,4},{1,5},{2,6},{3,7},{4,0},{5,1},{6,2},{7,3},{8,12},{9,13},{10,... | collective-permute-start | bytes 6152 | tf_op jit(solution)/shard_map/ppermute | solution.py:21
  149.1 2.2 %collective-permute-start.32 = (f32[32,16]{0,1:T(8,128)S(1)}, f32[32,16]{0,1:T(8,128)S(1)}, u32[]{:S(2)}, u32[]{:S(2)}) collective-permute-start(f32[32,16]{0,1:T(8,128)S(1)} %fusion.171), channel_id=1, source_target_pairs={{0,2},{1,3},{2,0},{3,1},{4,6},{5,7},{6,4},{7,5},{8,10},{9,11},{10,... | collective-permute-start | bytes 6152 | tf_op jit(solution)/shard_map/ppermute | solution.py:21
  151.3 7.6 %collective-permute-start.37 = (f32[32,16]{0,1:T(8,128)S(1)}, f32[32,16]{0,1:T(8,128)S(1)}, u32[]{:S(2)}, u32[]{:S(2)}) collective-permute-start(f32[32,16]{0,1:T(8,128)S(1)} %add_add_fusion.5), channel_id=1, source_target_pairs={{0,24},{1,25},{2,26},{3,27},{4,28},{5,29},{6,30},{7,31},{8,16},{9,... | collective-permute-start | bytes 6152 | tf_op jit(solution)/shard_map/ppermute | solution.py:21
  155.0 5.2 %collective-permute-start.36 = (f32[32,16]{0,1:T(8,128)S(1)}, f32[32,16]{0,1:T(8,128)S(1)}, u32[]{:S(2)}, u32[]{:S(2)}) collective-permute-start(f32[32,16]{0,1:T(8,128)S(1)} %add_add_fusion.5), channel_id=1, source_target_pairs={{0,16},{1,17},{2,18},{3,19},{4,20},{5,21},{6,22},{7,23},{8,24},{9,... | collective-permute-start | bytes 6152 | tf_op jit(solution)/shard_map/ppermute | solution.py:21
  157.9 5.2 %collective-permute-start.35 = (f32[32,16]{0,1:T(8,128)S(1)}, f32[32,16]{0,1:T(8,128)S(1)}, u32[]{:S(2)}, u32[]{:S(2)}) collective-permute-start(f32[32,16]{0,1:T(8,128)S(1)} %add_add_fusion.5), channel_id=1, source_target_pairs={{0,8},{1,9},{2,10},{3,11},{4,12},{5,13},{6,14},{7,15},{8,0},{9,1},... | collective-permute-start | bytes 6152 | tf_op jit(solution)/shard_map/ppermute | solution.py:21
  163.0 4.9 %collective-permute-start.40 = (f32[32,16]{0,1:T(8,128)S(1)}, f32[32,16]{0,1:T(8,128)S(1)}, u32[]{:S(2)}, u32[]{:S(2)}) collective-permute-start(f32[32,16]{0,1:T(8,128)S(1)} %add_add_fusion.4), channel_id=1, source_target_pairs={{0,96},{1,97},{2,98},{3,99},{4,100},{5,101},{6,102},{7,103},{8,104... | collective-permute-start | bytes 6152 | tf_op jit(solution)/shard_map/ppermute | solution.py:21
  163.9 5.2 %collective-permute-start.39 = (f32[32,16]{0,1:T(8,128)S(1)}, f32[32,16]{0,1:T(8,128)S(1)}, u32[]{:S(2)}, u32[]{:S(2)}) collective-permute-start(f32[32,16]{0,1:T(8,128)S(1)} %add_add_fusion.4), channel_id=1, source_target_pairs={{0,64},{1,65},{2,66},{3,67},{4,68},{5,69},{6,70},{7,71},{8,72},{9,... | collective-permute-start | bytes 6152 | tf_op jit(solution)/shard_map/ppermute | solution.py:21
  165.0 4.1 %collective-permute-start.38 = (f32[32,16]{0,1:T(8,128)S(1)}, f32[32,16]{0,1:T(8,128)S(1)}, u32[]{:S(2)}, u32[]{:S(2)}) collective-permute-start(f32[32,16]{0,1:T(8,128)S(1)} %add_add_fusion.4), channel_id=1, source_target_pairs={{0,32},{1,33},{2,34},{3,35},{4,36},{5,37},{6,38},{7,39},{8,40},{9,... | collective-permute-start | bytes 6152 | tf_op jit(solution)/shard_map/ppermute | solution.py:21
  176.6 11.7 %collective-permute-start.41 = (f32[8,1,64,256]{3,2,0,1:T(8,128)S(1)}, f32[8,1,64,256]{3,2,0,1:T(8,128)S(1)}, u32[]{:S(2)}, u32[]{:S(2)}) collective-permute-start(f32[8,1,64,256]{3,2,0,1:T(8,128)S(1)} %bitcast.184), channel_id=1, source_target_pairs={{0,1},{1,0},{2,3},{3,2},{4,5},{5,4},{6,7},{7,6},{8,9},{9,8},{10,11... | collective-permute-start | bytes 1572872 | tf_op jit(solution)/shard_map/ppermute | solution.py:46

commit v7 on v4

--- a/solution.py
+++ b/solution.py
@@ -52,8 +52,13 @@
     down = [(j, i) for i, j in up]
     rows = value.shape[2]
     edge = jnp.concatenate([value[:, :, rows - 1:], value[:, :, :1]], axis=2)
-    before = lax.ppermute(value, "space", up)
-    after = lax.ppermute(value, "space", down)
+    half = value.shape[0] // 2
+    before = jnp.concatenate(
+        [lax.ppermute(value[:half], "space", up), lax.ppermute(value[half:], "space", up)], 0
+    )
+    after = jnp.concatenate(
+        [lax.ppermute(value[:half], "space", down), lax.ppermute(value[half:], "space", down)], 0
+    )
     ends = swap_vec(edge)
     return before, after, ends
 
@@ -165,7 +170,8 @@
 
     own = lax.dynamic_slice_in_dim(new_all, v * mine, mine, 0)
     out = lax.dynamic_slice_in_dim(new_all, (1 - v) * mine, mine, 0)
-    new_basis = in_order(own, swap_vec(out), 2)
+    half = mine // 2
+    new_basis = in_order(own, jnp.concatenate([swap_vec(out[:half]), swap_vec(out[half:])], 0), 2)
     return (new_basis, rayleigh)
 
 

time: 185 us -> 193 us (1.043)
  starting transfers between devices: 62.8 us -> 91 us
  waiting for transfers between devices: 86.3 us -> 66.4 us
    ppermute x4 -> x8, starting transfers between devices: 1.55 us -> 28 us  [the longest x2 14.9 us: halo(): lax.ppermute(value[:half], 'space', down)]
    ppermute x4 -> x8, waiting for transfers between devices: 15.5 us -> 5.27 us  [the longest x2 5.26 us: halo(): lax.ppermute(value[:half], 'space', up)]
    ppermute x30, waiting for transfers between devices: 38 us -> 28.2 us  [allsum(): vals[m] = lax.ppermute(x, AXES, [(i, i ^ mask) for i in range(n)])]
    ppermute x4 -> x5, starting transfers between devices: 5.06 us -> 7.03 us  [swap_vec(): return lax.ppermute(value, 'vec', [(0, 1), (1, 0)])]
    ppermute x4 -> x5, waiting for transfers between devices: 23.8 us -> 23.9 us  [swap_vec(): return lax.ppermute(value, 'vec', [(0, 1), (1, 0)])]
  transfers between devices with their start and end apart: 42 -> 47, of which waited for: 31 -> 23; matrix products, arithmetic and copies ran while one was open for 3% -> 2% of each run, Pallas kernels for 0% -> 0%
where the time goes in v7:
time: 193 us
  starting transfers between devices  91 us (47%)
  waiting for transfers between devices  66.4 us (34%)
  matrix products  16.4 us (8%)
  other arithmetic  11.5 us (6%)
  local copies, waits for them, and re-layouts  6.56 us (3%)
    ppermute x30, starting transfers between devices, allsum(): vals[m] = lax.ppermute(x, AXES, [(i, i ^ mask) for i in range(n)])  42.1 us
    ppermute x30, waiting for transfers between devices, allsum(): vals[m] = lax.ppermute(x, AXES, [(i, i ^ mask) for i in range(n)])  28.2 us
    ppermute x5, waiting for transfers between devices, swap_vec(): return lax.ppermute(value, 'vec', [(0, 1), (1, 0)])  23.9 us
    ppermute x2, starting transfers between devices, halo(): lax.ppermute(value[:half], 'space', down)  14.9 us
    ppermute x2, starting transfers between devices, halo(): lax.ppermute(value[half:], 'space', down)  12.8 us
    ppermute x1, waiting for transfers between devices, local(): lax.ppermute(give_rows, AXES, cross_down)  8.86 us
    dot_general x6, matrix products, combine(): return jnp.einsum('kj,kzyx->jzyx', coeff, vectors, precision=FIELD_PREC)  8.18 us
    ppermute x1, starting transfers between devices, local(): lax.ppermute(keep_rows, AXES, same_down)  7.39 us
  transfers between devices with their start and end apart: 47, of which 23 were waited for; matrix products, arithmetic and copies ran while one was open for 2% of the time, Pallas kernels for 0%

profile of v7, /device:TPU:0, one launch (start us, length us, event | category | flops | bytes accessed | tf_op | source)
XLA Modules:
  0.0 192.9 jit_solution(4541817756665519604)
XLA Ops:
  0.6 1.8 copy.4
  2.7 2.1 %collective-permute-start = (f32[8,1,66,256]{3,0,2,1:T(8,128)S(1)}, f32[8,1,66,256]{3,0,2,1:T(8,128)S(1)}, u32[]{:S(2)}, u32[]{:S(2)}) collective-permute-start(f32[8,1,66,256]{3,0,2,1:T(8,128)S(1)} %get-tuple-element.16), channel_id=1, source_target_pairs={{0,1},{1,0},{2,3},{3,2},{4,5},{5,4},{6,7},{7,6},{8,9},{9,8},{10,11... | collective-permute-start | bytes 1622024 | tf_op jit(solution)/shard_map/ppermute | solution.py:46
  4.8 1.0 constant_dynamic-slice_fusion
  5.8 7.4 %collective-permute-start.3 = (f32[8,1,64,256]{3,0,2,1:T(8,128)}, f32[8,1,64,256]{3,0,2,1:T(8,128)S(1)}, u32[]{:S(2)}, u32[]{:S(2)}) collective-permute-start(f32[8,1,64,256]{3,0,2,1:T(8,128)} %get-tuple-element.14), channel_id=1, source_target_pairs={{2,0},{3,1},{4,2},{5,3},{6,4},{7,5},{8,6},{9,7},{10,8},{11,9},{12,... | collective-permute-start | bytes 1572872 | tf_op jit(solution)/shard_map/ppermute | solution.py:106
  13.2 6.4 %collective-permute-start.4 = (f32[8,1,64,256]{3,0,2,1:T(8,128)}, f32[8,1,64,256]{3,0,2,1:T(8,128)}, u32[]{:S(2)}, u32[]{:S(2)}) collective-permute-start(f32[8,1,64,256]{3,0,2,1:T(8,128)} %get-tuple-element.13), channel_id=1, source_target_pairs={{3,0},{2,1},{5,2},{4,3},{7,4},{6,5},{9,6},{8,7},{11,8},{10,9},{13,... | collective-permute-start | bytes 1572872 | tf_op jit(solution)/shard_map/ppermute | solution.py:106
  19.6 9.5 %collective-permute-done = f32[8,1,66,256]{3,0,2,1:T(8,128)S(1)} collective-permute-done((f32[8,1,66,256]{3,0,2,1:T(8,128)S(1)}, f32[8,1,66,256]{3,0,2,1:T(8,128)S(1)}, u32[]{:S(2)}, u32[]{:S(2)}) %collective-permute-start) | collective-permute-done | bytes 540704 | tf_op jit(solution)/shard_map/ppermute | solution.py:46
  29.9 8.9 %collective-permute-done.4 = f32[8,1,64,256]{3,0,2,1:T(8,128)} collective-permute-done((f32[8,1,64,256]{3,0,2,1:T(8,128)}, f32[8,1,64,256]{3,0,2,1:T(8,128)}, u32[]{:S(2)}, u32[]{:S(2)}) %collective-permute-start.4) | collective-permute-done | bytes 524320 | tf_op jit(solution)/shard_map/ppermute | solution.py:106
  38.9 2.3 %broadcast_divide_fusion = (f32[16,1,64,256]{3,0,2,1:T(8,128)S(1)}, f32[16,1,64,256]{3,0,2,1:T(8,128)S(1)}, f32[16,1,64,256]{3,0,2,1:T(8,128)S(1)}) fusion(f32[64,256]{1,0:T(8,128)S(1)} %get-tuple-element.38, f32[16,1,64,1]{3,0,2,1:T(8,128)S(1)} %get-tuple-element.10, f32[16,1,64,255]{3,0,2,1:T(8,128)S(1)} %get-tuple-element.12, ...), kind=kLoop, calls=%fused_computation.88 | loop fusion | flops 4456448 | bytes 10616833 | tf_op jit(solution)/shard_map/div | solution.py:116
  41.2 1.8 fusion.57
  43.0 1.4 collective-permute-start.5
  44.4 2.6 %collective-permute-done.5 = f32[32,64]{0,1:T(8,128)S(1)} collective-permute-done((f32[32,64]{0,1:T(8,128)S(1)}, f32[32,64]{0,1:T(8,128)S(1)}, u32[]{:S(2)}, u32[]{:S(2)}) %collective-permute-start.5) | collective-permute-done | bytes 8224 | tf_op jit(solution)/shard_map/ppermute | solution.py:21
  47.0 1.5 collective-permute-start.7
  49.1 1.8 collective-permute-done.7
  50.9 0.9 collective-permute-done.8
  51.8 3.8 %collective-permute-start.10 = (f32[32,64]{0,1:T(8,128)S(1)}, f32[32,64]{0,1:T(8,128)S(1)}, u32[]{:S(2)}, u32[]{:S(2)}) collective-permute-start(f32[32,64]{0,1:T(8,128)S(1)} %add_add_fusion.2), channel_id=1, source_target_pairs={{0,16},{1,17},{2,18},{3,19},{4,20},{5,21},{6,22},{7,23},{8,24},{9,... | collective-permute-start | bytes 24584 | tf_op jit(solution)/shard_map/ppermute | solution.py:21
  55.6 2.3 %collective-permute-start.11 = (f32[32,64]{0,1:T(8,128)S(1)}, f32[32,64]{0,1:T(8,128)S(1)}, u32[]{:S(2)}, u32[]{:S(2)}) collective-permute-start(f32[32,64]{0,1:T(8,128)S(1)} %add_add_fusion.2), channel_id=1, source_target_pairs={{0,24},{1,25},{2,26},{3,27},{4,28},{5,29},{6,30},{7,31},{8,16},{9,... | collective-permute-start | bytes 24584 | tf_op jit(solution)/shard_map/ppermute | solution.py:21
  57.9 0.8 collective-permute-start.9
  58.7 4.8 %collective-permute-done.11 = f32[32,64]{0,1:T(8,128)S(1)} collective-permute-done((f32[32,64]{0,1:T(8,128)S(1)}, f32[32,64]{0,1:T(8,128)S(1)}, u32[]{:S(2)}, u32[]{:S(2)}) %collective-permute-start.11) | collective-permute-done | bytes 8224 | tf_op jit(solution)/shard_map/ppermute | solution.py:21
  63.5 3.3 %collective-permute-start.13 = (f32[32,64]{0,1:T(8,128)S(1)}, f32[32,64]{0,1:T(8,128)S(1)}, u32[]{:S(2)}, u32[]{:S(2)}) collective-permute-start(f32[32,64]{0,1:T(8,128)S(1)} %add_add_fusion.1), channel_id=1, source_target_pairs={{0,64},{1,65},{2,66},{3,67},{4,68},{5,69},{6,70},{7,71},{8,72},{9,... | collective-permute-start | bytes 24584 | tf_op jit(solution)/shard_map/ppermute | solution.py:21
  66.7 1.1 collective-permute-start.14
  67.8 1.2 collective-permute-done.13
  69.0 2.9 %collective-permute-done.14 = f32[32,64]{0,1:T(8,128)S(1)} collective-permute-done((f32[32,64]{0,1:T(8,128)S(1)}, f32[32,64]{0,1:T(8,128)S(1)}, u32[]{:S(2)}, u32[]{:S(2)}) %collective-permute-start.14) | collective-permute-done | bytes 8224 | tf_op jit(solution)/shard_map/ppermute | solution.py:21
  72.0 1.5 cholesky.44
  74.7 1.2 custom-call.6
  78.1 2.0 %fusion.9 = f32[64,64,256]{2,0,1:T(8,128)S(1)} fusion(f32[16,1,64,256]{3,0,2,1:T(8,128)S(1)} %get-tuple-element.7, f32[16,1,64,256]{3,0,2,1:T(8,128)S(1)} %slice.260, f32[16,16]{1,0:T(8,128)S(1)} %cholesky.45, f32[16,16]{1,0:T(8,128)S(1)} %bitcast.163, f32[16,16]{1,0:T(8,128)S(1)} %fusion.128, f32[16,16]{1,0:T(8,128)S(1)} %get-tuple-element.43, ...), kind=kOutput, calls=%fused_computation.11 | convolution fusion | flops 201865216 | bytes 6296576 | tf_op jit(solution)/shard_map/kj,kzyx->jzyx/dot_general | solution.py:38
  81.0 7.5 %collective-permute-start.18 = (f32[8,1,64,256]{3,0,2,1:T(8,128)S(1)}, f32[8,1,64,256]{3,0,2,1:T(8,128)S(1)}, u32[]{:S(2)}, u32[]{:S(2)}) collective-permute-start(f32[8,1,64,256]{3,0,2,1:T(8,128)S(1)} %get-tuple-element.32), channel_id=1, source_target_pairs={{2,0},{4,2},{6,4},{8,6},{10,8},{12,10},{14,12},{16,14},{18,16},{20... | collective-permute-start | bytes 1572872 | tf_op jit(solution)/shard_map/ppermute | solution.py:60
  88.5 7.5 %collective-permute-start.17 = (f32[8,1,64,256]{3,0,2,1:T(8,128)S(1)}, f32[8,1,64,256]{3,0,2,1:T(8,128)S(1)}, u32[]{:S(2)}, u32[]{:S(2)}) collective-permute-start(f32[8,1,64,256]{3,0,2,1:T(8,128)S(1)} %get-tuple-element.31), channel_id=1, source_target_pairs={{2,0},{4,2},{6,4},{8,6},{10,8},{12,10},{14,12},{16,14},{18,16},{20... | collective-permute-start | bytes 1572872 | tf_op jit(solution)/shard_map/ppermute | solution.py:60
  97.0 1.7 collective-permute-start.19
  99.3 1.7 collective-permute-done.19
  101.0 1.9 collective-permute-done.15
  102.9 1.6 fusion.13
  104.5 0.9 fusion.29
  105.8 1.7 collective-permute-start.25
  107.6 2.0 %collective-permute-done.25 = f32[32,16]{0,1:T(8,128)S(1)} collective-permute-done((f32[32,16]{0,1:T(8,128)S(1)}, f32[32,16]{0,1:T(8,128)S(1)}, u32[]{:S(2)}, u32[]{:S(2)}) %collective-permute-start.25) | collective-permute-done | bytes 2080 | tf_op jit(solution)/shard_map/ppermute | solution.py:21
  109.6 2.1 %collective-permute-start.26 = (f32[32,16]{0,1:T(8,128)S(1)}, f32[32,16]{0,1:T(8,128)S(1)}, u32[]{:S(2)}, u32[]{:S(2)}) collective-permute-start(f32[32,16]{0,1:T(8,128)S(1)} %add.234), channel_id=1, source_target_pairs={{0,2},{1,3},{2,0},{3,1},{4,6},{5,7},{6,4},{7,5},{8,10},{9,11},{10,... | collective-permute-start | bytes 6152 | tf_op jit(solution)/shard_map/ppermute | solution.py:21
  111.9 1.3 collective-permute-done.27
  113.2 2.7 %collective-permute-start.30 = (f32[32,16]{0,1:T(8,128)S(1)}, f32[32,16]{0,1:T(8,128)S(1)}, u32[]{:S(2)}, u32[]{:S(2)}) collective-permute-start(f32[32,16]{0,1:T(8,128)S(1)} %add_add_fusion.8), channel_id=1, source_target_pairs={{0,16},{1,17},{2,18},{3,19},{4,20},{5,21},{6,22},{7,23},{8,24},{9,... | collective-permute-start | bytes 6152 | tf_op jit(solution)/shard_map/ppermute | solution.py:21
  116.1 3.7 %collective-permute-start.29 = (f32[32,16]{0,1:T(8,128)S(1)}, f32[32,16]{0,1:T(8,128)S(1)}, u32[]{:S(2)}, u32[]{:S(2)}) collective-permute-start(f32[32,16]{0,1:T(8,128)S(1)} %add_add_fusion.8), channel_id=1, source_target_pairs={{0,8},{1,9},{2,10},{3,11},{4,12},{5,13},{6,14},{7,15},{8,0},{9,1},... | collective-permute-start | bytes 6152 | tf_op jit(solution)/shard_map/ppermute | solution.py:21
  119.8 5.4 %collective-permute-start.23 = (f32[8,1,64,256]{3,0,2,1:T(8,128)S(1)}, f32[8,1,64,256]{3,0,2,1:T(8,128)S(1)}, u32[]{:S(2)}, u32[]{:S(2)}) collective-permute-start(f32[8,1,64,256]{3,0,2,1:T(8,128)S(1)} %get-tuple-element.24), channel_id=1, source_target_pairs={{2,0},{4,2},{6,4},{8,6},{10,8},{12,10},{14,12},{16,14},{18,16},{20... | collective-permute-start | bytes 1572872 | tf_op jit(solution)/shard_map/ppermute | solution.py:60
  125.4 3.4 %collective-permute-start.32 = (f32[32,16]{0,1:T(8,128)S(1)}, f32[32,16]{0,1:T(8,128)S(1)}, u32[]{:S(2)}, u32[]{:S(2)}) collective-permute-start(f32[32,16]{0,1:T(8,128)S(1)} %add_add_fusion.7), channel_id=1, source_target_pairs={{0,32},{1,33},{2,34},{3,35},{4,36},{5,37},{6,38},{7,39},{8,40},{9,... | collective-permute-start | bytes 6152 | tf_op jit(solution)/shard_map/ppermute | solution.py:21
  128.8 1.7 collective-permute-done.33
  130.4 7.5 %collective-permute-start.22 = (f32[8,1,64,256]{3,0,2,1:T(8,128)S(1)}, f32[8,1,64,256]{3,0,2,1:T(8,128)S(1)}, u32[]{:S(2)}, u32[]{:S(2)}) collective-permute-start(f32[8,1,64,256]{3,0,2,1:T(8,128)S(1)} %get-tuple-element.23), channel_id=1, source_target_pairs={{2,0},{4,2},{6,4},{8,6},{10,8},{12,10},{14,12},{16,14},{18,16},{20... | collective-permute-start | bytes 1572872 | tf_op jit(solution)/shard_map/ppermute | solution.py:60
  137.9 1.1 collective-permute-start.24
  139.8 2.0 %collective-permute-done.24 = f32[16,1,2,256]{3,0,2,1:T(8,128)S(1)} collective-permute-done((f32[16,1,2,256]{3,0,2,1:T(8,128)S(1)}, f32[16,1,2,256]{3,0,2,1:T(8,128)S(1)}, u32[]{:S(2)}, u32[]{:S(2)}) %collective-permute-start.24) | collective-permute-done | bytes 32800 | tf_op jit(solution)/shard_map/ppermute | solution.py:46
  141.8 3.4 %collective-permute-done.20 = f32[8,1,64,256]{3,0,2,1:T(8,128)S(1)} collective-permute-done((f32[8,1,64,256]{3,0,2,1:T(8,128)S(1)}, f32[8,1,64,256]{3,0,2,1:T(8,128)S(1)}, u32[]{:S(2)}, u32[]{:S(2)}) %collective-permute-start.20) | collective-permute-done | bytes 524320 | tf_op jit(solution)/shard_map/ppermute | solution.py:57
  145.2 1.6 fusion.18
  148.5 1.2 collective-permute-start.35
  149.6 2.5 %collective-permute-done.35 = f32[32,16]{0,1:T(8,128)S(1)} collective-permute-done((f32[32,16]{0,1:T(8,128)S(1)}, f32[32,16]{0,1:T(8,128)S(1)}, u32[]{:S(2)}, u32[]{:S(2)}) %collective-permute-start.35) | collective-permute-done | bytes 2080 | tf_op jit(solution)/shard_map/ppermute | solution.py:21
  152.3 2.0 %collective-permute-start.36 = (f32[32,16]{0,1:T(8,128)S(1)}, f32[32,16]{0,1:T(8,128)S(1)}, u32[]{:S(2)}, u32[]{:S(2)}) collective-permute-start(f32[32,16]{0,1:T(8,128)S(1)} %fusion.160), channel_id=1, source_target_pairs={{0,2},{1,3},{2,0},{3,1},{4,6},{5,7},{6,4},{7,5},{8,10},{9,11},{10,... | collective-permute-start | bytes 6152 | tf_op jit(solution)/shard_map/ppermute | solution.py:21
  154.4 1.5 collective-permute-done.37
  155.9 2.1 %collective-permute-start.40 = (f32[32,16]{0,1:T(8,128)S(1)}, f32[32,16]{0,1:T(8,128)S(1)}, u32[]{:S(2)}, u32[]{:S(2)}) collective-permute-start(f32[32,16]{0,1:T(8,128)S(1)} %add_add_fusion.5), channel_id=1, source_target_pairs={{0,16},{1,17},{2,18},{3,19},{4,20},{5,21},{6,22},{7,23},{8,24},{9,... | collective-permute-start | bytes 6152 | tf_op jit(solution)/shard_map/ppermute | solution.py:21
  158.0 4.5 %collective-permute-start.39 = (f32[32,16]{0,1:T(8,128)S(1)}, f32[32,16]{0,1:T(8,128)S(1)}, u32[]{:S(2)}, u32[]{:S(2)}) collective-permute-start(f32[32,16]{0,1:T(8,128)S(1)} %add_add_fusion.5), channel_id=1, source_target_pairs={{0,8},{1,9},{2,10},{3,11},{4,12},{5,13},{6,14},{7,15},{8,0},{9,1},... | collective-permute-start | bytes 6152 | tf_op jit(solution)/shard_map/ppermute | solution.py:21
  162.5 3.1 %collective-permute-done.41 = f32[32,16]{0,1:T(8,128)S(1)} collective-permute-done((f32[32,16]{0,1:T(8,128)S(1)}, f32[32,16]{0,1:T(8,128)S(1)}, u32[]{:S(2)}, u32[]{:S(2)}) %collective-permute-start.41) | collective-permute-done | bytes 2080 | tf_op jit(solution)/shard_map/ppermute | solution.py:21
  165.7 1.9 collective-permute-start.44
  167.6 1.6 collective-permute-start.42
  169.1 1.7 collective-permute-done.43
  171.5 1.8 fusion.20
  173.6 1.5 cholesky.55
  176.4 1.2 custom-call.7
  178.5 1.3 collective-permute-start.46
  179.8 0.8 collective-permute-start.45
  180.7 7.1 %collective-permute-done.46 = f32[4,1,64,256]{3,0,2,1:T(4,128)S(1)} collective-permute-done((f32[4,1,64,256]{3,0,2,1:T(4,128)S(1)}, f32[4,1,64,256]{3,0,2,1:T(4,128)S(1)}, u32[]{:S(2)}, u32[]{:S(2)}) %collective-permute-start.46) | collective-permute-done | bytes 262176 | tf_op jit(solution)/shard_map/ppermute | solution.py:46
  187.8 3.6 %collective-permute-done.45 = f32[4,1,64,256]{3,0,2,1:T(4,128)S(1)} collective-permute-done((f32[4,1,64,256]{3,0,2,1:T(4,128)S(1)}, f32[4,1,64,256]{3,0,2,1:T(4,128)S(1)}, u32[]{:S(2)}, u32[]{:S(2)}) %collective-permute-start.45) | collective-permute-done | bytes 262176 | tf_op jit(solution)/shard_map/ppermute | solution.py:46
  191.7 1.3 copy.12
  (125 shorter events, 15.1 us)
Async XLA Ops:
  2.6 17.1 %copy-start.1 = (f32[1,128,256]{2,1,0:T(8,128)S(1)}, f32[1,128,256]{2,1,0:T(8,128)}, u32[]{:S(2)}) copy-start(f32[1,128,256]{2,1,0:T(8,128)} %param.5) | copy-start | bytes 393220
  2.7 26.5 %collective-permute-start = (f32[8,1,66,256]{3,0,2,1:T(8,128)S(1)}, f32[8,1,66,256]{3,0,2,1:T(8,128)S(1)}, u32[]{:S(2)}, u32[]{:S(2)}) collective-permute-start(f32[8,1,66,256]{3,0,2,1:T(8,128)S(1)} %get-tuple-element.16), channel_id=1, source_target_pairs={{0,1},{1,0},{2,3},{3,2},{4,5},{5,4},{6,7},{7,6},{8,9},{9,8},{10,11... | collective-permute-start | bytes 1622024 | tf_op jit(solution)/shard_map/ppermute | solution.py:46
  5.8 24.1 %collective-permute-start.3 = (f32[8,1,64,256]{3,0,2,1:T(8,128)}, f32[8,1,64,256]{3,0,2,1:T(8,128)S(1)}, u32[]{:S(2)}, u32[]{:S(2)}) collective-permute-start(f32[8,1,64,256]{3,0,2,1:T(8,128)} %get-tuple-element.14), channel_id=1, source_target_pairs={{2,0},{3,1},{4,2},{5,3},{6,4},{7,5},{8,6},{9,7},{10,8},{11,9},{12,... | collective-permute-start | bytes 1572872 | tf_op jit(solution)/shard_map/ppermute | solution.py:106
  13.2 25.6 %collective-permute-start.1 = (f32[8,1,64,256]{3,0,2,1:T(8,128)}, f32[8,1,64,256]{3,0,2,1:T(8,128)S(1)}, u32[]{:S(2)}, u32[]{:S(2)}) collective-permute-start(f32[8,1,64,256]{3,0,2,1:T(8,128)} %get-tuple-element.14), channel_id=1, source_target_pairs={{0,2},{1,3},{2,4},{3,5},{4,6},{5,7},{6,8},{7,9},{8,10},{9,11},{10,... | collective-permute-start | bytes 1572872 | tf_op jit(solution)/shard_map/ppermute | solution.py:105
  13.2 25.6 %collective-permute-start.4 = (f32[8,1,64,256]{3,0,2,1:T(8,128)}, f32[8,1,64,256]{3,0,2,1:T(8,128)}, u32[]{:S(2)}, u32[]{:S(2)}) collective-permute-start(f32[8,1,64,256]{3,0,2,1:T(8,128)} %get-tuple-element.13), channel_id=1, source_target_pairs={{3,0},{2,1},{5,2},{4,3},{7,4},{6,5},{9,6},{8,7},{11,8},{10,9},{13,... | collective-permute-start | bytes 1572872 | tf_op jit(solution)/shard_map/ppermute | solution.py:106
  19.6 19.3 %collective-permute-start.2 = (f32[8,1,64,256]{3,0,2,1:T(8,128)}, f32[8,1,64,256]{3,0,2,1:T(8,128)}, u32[]{:S(2)}, u32[]{:S(2)}) collective-permute-start(f32[8,1,64,256]{3,0,2,1:T(8,128)} %get-tuple-element.13), channel_id=1, source_target_pairs={{0,3},{1,2},{2,5},{3,4},{4,7},{5,6},{6,9},{7,8},{8,11},{9,10},{10,... | collective-permute-start | bytes 1572872 | tf_op jit(solution)/shard_map/ppermute | solution.py:105
  43.0 4.0 %collective-permute-start.5 = (f32[32,64]{0,1:T(8,128)S(1)}, f32[32,64]{0,1:T(8,128)S(1)}, u32[]{:S(2)}, u32[]{:S(2)}) collective-permute-start(f32[32,64]{0,1:T(8,128)S(1)} %fusion.57), channel_id=1, source_target_pairs={{0,1},{1,0},{2,3},{3,2},{4,5},{5,4},{6,7},{7,6},{8,9},{9,8},{10,11... | collective-permute-start | bytes 24584 | tf_op jit(solution)/shard_map/ppermute | solution.py:21
  47.0 3.9 %collective-permute-start.7 = (f32[32,64]{0,1:T(8,128)S(1)}, f32[32,64]{0,1:T(8,128)S(1)}, u32[]{:S(2)}, u32[]{:S(2)}) collective-permute-start(f32[32,64]{0,1:T(8,128)S(1)} %add.213), channel_id=1, source_target_pairs={{0,4},{1,5},{2,6},{3,7},{4,0},{5,1},{6,2},{7,3},{8,12},{9,13},{10,... | collective-permute-start | bytes 24584 | tf_op jit(solution)/shard_map/ppermute | solution.py:21
  48.5 3.3 %collective-permute-start.8 = (f32[32,64]{0,1:T(8,128)S(1)}, f32[32,64]{0,1:T(8,128)S(1)}, u32[]{:S(2)}, u32[]{:S(2)}) collective-permute-start(f32[32,64]{0,1:T(8,128)S(1)} %add.213), channel_id=1, source_target_pairs={{0,6},{1,7},{2,4},{3,5},{4,2},{5,3},{6,0},{7,1},{8,14},{9,15},{10,... | collective-permute-start | bytes 24584 | tf_op jit(solution)/shard_map/ppermute | solution.py:21
  48.5 3.3 %collective-permute-start.6 = (f32[32,64]{0,1:T(8,128)S(1)}, f32[32,64]{0,1:T(8,128)S(1)}, u32[]{:S(2)}, u32[]{:S(2)}) collective-permute-start(f32[32,64]{0,1:T(8,128)S(1)} %add.213), channel_id=1, source_target_pairs={{0,2},{1,3},{2,0},{3,1},{4,6},{5,7},{6,4},{7,5},{8,10},{9,11},{10,... | collective-permute-start | bytes 24584 | tf_op jit(solution)/shard_map/ppermute | solution.py:21
  51.8 6.9 %collective-permute-start.10 = (f32[32,64]{0,1:T(8,128)S(1)}, f32[32,64]{0,1:T(8,128)S(1)}, u32[]{:S(2)}, u32[]{:S(2)}) collective-permute-start(f32[32,64]{0,1:T(8,128)S(1)} %add_add_fusion.2), channel_id=1, source_target_pairs={{0,16},{1,17},{2,18},{3,19},{4,20},{5,21},{6,22},{7,23},{8,24},{9,... | collective-permute-start | bytes 24584 | tf_op jit(solution)/shard_map/ppermute | solution.py:21
  55.6 7.8 %collective-permute-start.11 = (f32[32,64]{0,1:T(8,128)S(1)}, f32[32,64]{0,1:T(8,128)S(1)}, u32[]{:S(2)}, u32[]{:S(2)}) collective-permute-start(f32[32,64]{0,1:T(8,128)S(1)} %add_add_fusion.2), channel_id=1, source_target_pairs={{0,24},{1,25},{2,26},{3,27},{4,28},{5,29},{6,30},{7,31},{8,16},{9,... | collective-permute-start | bytes 24584 | tf_op jit(solution)/shard_map/ppermute | solution.py:21
  57.9 5.6 %collective-permute-start.9 = (f32[32,64]{0,1:T(8,128)S(1)}, f32[32,64]{0,1:T(8,128)S(1)}, u32[]{:S(2)}, u32[]{:S(2)}) collective-permute-start(f32[32,64]{0,1:T(8,128)S(1)} %add_add_fusion.2), channel_id=1, source_target_pairs={{0,8},{1,9},{2,10},{3,11},{4,12},{5,13},{6,14},{7,15},{8,0},{9,1},... | collective-permute-start | bytes 24584 | tf_op jit(solution)/shard_map/ppermute | solution.py:21
  63.5 5.5 %collective-permute-start.13 = (f32[32,64]{0,1:T(8,128)S(1)}, f32[32,64]{0,1:T(8,128)S(1)}, u32[]{:S(2)}, u32[]{:S(2)}) collective-permute-start(f32[32,64]{0,1:T(8,128)S(1)} %add_add_fusion.1), channel_id=1, source_target_pairs={{0,64},{1,65},{2,66},{3,67},{4,68},{5,69},{6,70},{7,71},{8,72},{9,... | collective-permute-start | bytes 24584 | tf_op jit(solution)/shard_map/ppermute | solution.py:21
  66.7 5.1 %collective-permute-start.14 = (f32[32,64]{0,1:T(8,128)S(1)}, f32[32,64]{0,1:T(8,128)S(1)}, u32[]{:S(2)}, u32[]{:S(2)}) collective-permute-start(f32[32,64]{0,1:T(8,128)S(1)} %add_add_fusion.1), channel_id=1, source_target_pairs={{0,96},{1,97},{2,98},{3,99},{4,100},{5,101},{6,102},{7,103},{8,104... | collective-permute-start | bytes 24584 | tf_op jit(solution)/shard_map/ppermute | solution.py:21
  67.8 4.1 %collective-permute-start.12 = (f32[32,64]{0,1:T(8,128)S(1)}, f32[32,64]{0,1:T(8,128)S(1)}, u32[]{:S(2)}, u32[]{:S(2)}) collective-permute-start(f32[32,64]{0,1:T(8,128)S(1)} %add_add_fusion.1), channel_id=1, source_target_pairs={{0,32},{1,33},{2,34},{3,35},{4,36},{5,37},{6,38},{7,39},{8,40},{9,... | collective-permute-start | bytes 24584 | tf_op jit(solution)/shard_map/ppermute | solution.py:21
  76.6 3.5 %copy-start.2 = (f32[16,16]{1,0:T(8,128)}, f32[16,16]{1,0:T(8,128)S(1)}, u32[]{:S(2)}) copy-start(f32[16,16]{1,0:T(8,128)S(1)} %fusion.127) | copy-start | bytes 3076
  80.1 67.5 %copy-start = (f32[64,64,256]{2,0,1:T(8,128)}, f32[64,64,256]{2,0,1:T(8,128)S(1)}, u32[]{:S(2)}) copy-start(f32[64,64,256]{2,0,1:T(8,128)S(1)} %fusion.9) | copy-start | bytes 12582916
  80.7 20.3 %collective-permute-start.16 = (f32[8,1,64,256]{3,0,2,1:T(8,128)S(1)}, f32[8,1,64,256]{3,0,2,1:T(8,128)S(1)}, u32[]{:S(2)}, u32[]{:S(2)}) collective-permute-start(f32[8,1,64,256]{3,0,2,1:T(8,128)S(1)} %get-tuple-element.32), channel_id=1, source_target_pairs={{0,2},{2,4},{4,6},{6,8},{8,10},{10,12},{12,14},{14,16},{16,18},{18... | collective-permute-start | bytes 1572872 | tf_op jit(solution)/shard_map/ppermute | solution.py:57
  81.0 21.9 %collective-permute-start.18 = (f32[8,1,64,256]{3,0,2,1:T(8,128)S(1)}, f32[8,1,64,256]{3,0,2,1:T(8,128)S(1)}, u32[]{:S(2)}, u32[]{:S(2)}) collective-permute-start(f32[8,1,64,256]{3,0,2,1:T(8,128)S(1)} %get-tuple-element.32), channel_id=1, source_target_pairs={{2,0},{4,2},{6,4},{8,6},{10,8},{12,10},{14,12},{16,14},{18,16},{20... | collective-permute-start | bytes 1572872 | tf_op jit(solution)/shard_map/ppermute | solution.py:60
  88.5 14.4 %collective-permute-start.15 = (f32[8,1,64,256]{3,0,2,1:T(8,128)S(1)}, f32[8,1,64,256]{3,0,2,1:T(8,128)S(1)}, u32[]{:S(2)}, u32[]{:S(2)}) collective-permute-start(f32[8,1,64,256]{3,0,2,1:T(8,128)S(1)} %get-tuple-element.31), channel_id=1, source_target_pairs={{0,2},{2,4},{4,6},{6,8},{8,10},{10,12},{12,14},{14,16},{16,18},{18... | collective-permute-start | bytes 1572872 | tf_op jit(solution)/shard_map/ppermute | solution.py:57
  88.5 14.4 %collective-permute-start.17 = (f32[8,1,64,256]{3,0,2,1:T(8,128)S(1)}, f32[8,1,64,256]{3,0,2,1:T(8,128)S(1)}, u32[]{:S(2)}, u32[]{:S(2)}) collective-permute-start(f32[8,1,64,256]{3,0,2,1:T(8,128)S(1)} %get-tuple-element.31), channel_id=1, source_target_pairs={{2,0},{4,2},{6,4},{8,6},{10,8},{12,10},{14,12},{16,14},{18,16},{20... | collective-permute-start | bytes 1572872 | tf_op jit(solution)/shard_map/ppermute | solution.py:60
  97.0 4.0 %collective-permute-start.19 = (f32[16,1,2,256]{3,0,2,1:T(8,128)S(1)}, f32[16,1,2,256]{3,0,2,1:T(8,128)S(1)}, u32[]{:S(2)}, u32[]{:S(2)}) collective-permute-start(f32[16,1,2,256]{3,0,2,1:T(8,128)S(1)} %pad_maximum_fusion.5), channel_id=1, source_target_pairs={{0,1},{1,0},{2,3},{3,2},{4,5},{5,4},{6,7},{7,6},{8,9},{9,8},{10,11... | collective-permute-start | bytes 98312 | tf_op jit(solution)/shard_map/ppermute | solution.py:46
  105.8 3.7 %collective-permute-start.25 = (f32[32,16]{0,1:T(8,128)S(1)}, f32[32,16]{0,1:T(8,128)S(1)}, u32[]{:S(2)}, u32[]{:S(2)}) collective-permute-start(f32[32,16]{0,1:T(8,128)S(1)} %fusion.29), channel_id=1, source_target_pairs={{0,1},{1,0},{2,3},{3,2},{4,5},{5,4},{6,7},{7,6},{8,9},{9,8},{10,11... | collective-permute-start | bytes 6152 | tf_op jit(solution)/shard_map/ppermute | solution.py:21
  109.5 3.7 %collective-permute-start.27 = (f32[32,16]{0,1:T(8,128)S(1)}, f32[32,16]{0,1:T(8,128)S(1)}, u32[]{:S(2)}, u32[]{:S(2)}) collective-permute-start(f32[32,16]{0,1:T(8,128)S(1)} %add.234), channel_id=1, source_target_pairs={{0,4},{1,5},{2,6},{3,7},{4,0},{5,1},{6,2},{7,3},{8,12},{9,13},{10,... | collective-permute-start | bytes 6152 | tf_op jit(solution)/shard_map/ppermute | solution.py:21
  109.5 3.7 %collective-permute-start.28 = (f32[32,16]{0,1:T(8,128)S(1)}, f32[32,16]{0,1:T(8,128)S(1)}, u32[]{:S(2)}, u32[]{:S(2)}) collective-permute-start(f32[32,16]{0,1:T(8,128)S(1)} %add.234), channel_id=1, source_target_pairs={{0,6},{1,7},{2,4},{3,5},{4,2},{5,3},{6,0},{7,1},{8,14},{9,15},{10,... | collective-permute-start | bytes 6152 | tf_op jit(solution)/shard_map/ppermute | solution.py:21
  109.6 3.6 %collective-permute-start.26 = (f32[32,16]{0,1:T(8,128)S(1)}, f32[32,16]{0,1:T(8,128)S(1)}, u32[]{:S(2)}, u32[]{:S(2)}) collective-permute-start(f32[32,16]{0,1:T(8,128)S(1)} %add.234), channel_id=1, source_target_pairs={{0,2},{1,3},{2,0},{3,1},{4,6},{5,7},{6,4},{7,5},{8,10},{9,11},{10,... | collective-permute-start | bytes 6152 | tf_op jit(solution)/shard_map/ppermute | solution.py:21
  113.2 11.9 %collective-permute-start.30 = (f32[32,16]{0,1:T(8,128)S(1)}, f32[32,16]{0,1:T(8,128)S(1)}, u32[]{:S(2)}, u32[]{:S(2)}) collective-permute-start(f32[32,16]{0,1:T(8,128)S(1)} %add_add_fusion.8), channel_id=1, source_target_pairs={{0,16},{1,17},{2,18},{3,19},{4,20},{5,21},{6,22},{7,23},{8,24},{9,... | collective-permute-start | bytes 6152 | tf_op jit(solution)/shard_map/ppermute | solution.py:21
  115.9 9.3 %collective-permute-start.31 = (f32[32,16]{0,1:T(8,128)S(1)}, f32[32,16]{0,1:T(8,128)S(1)}, u32[]{:S(2)}, u32[]{:S(2)}) collective-permute-start(f32[32,16]{0,1:T(8,128)S(1)} %add_add_fusion.8), channel_id=1, source_target_pairs={{0,24},{1,25},{2,26},{3,27},{4,28},{5,29},{6,30},{7,31},{8,16},{9,... | collective-permute-start | bytes 6152 | tf_op jit(solution)/shard_map/ppermute | solution.py:21
  116.1 9.1 %collective-permute-start.29 = (f32[32,16]{0,1:T(8,128)S(1)}, f32[32,16]{0,1:T(8,128)S(1)}, u32[]{:S(2)}, u32[]{:S(2)}) collective-permute-start(f32[32,16]{0,1:T(8,128)S(1)} %add_add_fusion.8), channel_id=1, source_target_pairs={{0,8},{1,9},{2,10},{3,11},{4,12},{5,13},{6,14},{7,15},{8,0},{9,1},... | collective-permute-start | bytes 6152 | tf_op jit(solution)/shard_map/ppermute | solution.py:21
  119.8 25.4 %collective-permute-start.23 = (f32[8,1,64,256]{3,0,2,1:T(8,128)S(1)}, f32[8,1,64,256]{3,0,2,1:T(8,128)S(1)}, u32[]{:S(2)}, u32[]{:S(2)}) collective-permute-start(f32[8,1,64,256]{3,0,2,1:T(8,128)S(1)} %get-tuple-element.24), channel_id=1, source_target_pairs={{2,0},{4,2},{6,4},{8,6},{10,8},{12,10},{14,12},{16,14},{18,16},{20... | collective-permute-start | bytes 1572872 | tf_op jit(solution)/shard_map/ppermute | solution.py:60
  125.1 16.7 %collective-permute-start.21 = (f32[8,1,64,256]{3,0,2,1:T(8,128)S(1)}, f32[8,1,64,256]{3,0,2,1:T(8,128)S(1)}, u32[]{:S(2)}, u32[]{:S(2)}) collective-permute-start(f32[8,1,64,256]{3,0,2,1:T(8,128)S(1)} %get-tuple-element.24), channel_id=1, source_target_pairs={{0,2},{2,4},{4,6},{6,8},{8,10},{10,12},{12,14},{14,16},{16,18},{18... | collective-permute-start | bytes 1572872 | tf_op jit(solution)/shard_map/ppermute | solution.py:57
  125.2 5.2 %collective-permute-start.33 = (f32[32,16]{0,1:T(8,128)S(1)}, f32[32,16]{0,1:T(8,128)S(1)}, u32[]{:S(2)}, u32[]{:S(2)}) collective-permute-start(f32[32,16]{0,1:T(8,128)S(1)} %add_add_fusion.7), channel_id=1, source_target_pairs={{0,64},{1,65},{2,66},{3,67},{4,68},{5,69},{6,70},{7,71},{8,72},{9,... | collective-permute-start | bytes 6152 | tf_op jit(solution)/shard_map/ppermute | solution.py:21
  125.3 5.1 %collective-permute-start.34 = (f32[32,16]{0,1:T(8,128)S(1)}, f32[32,16]{0,1:T(8,128)S(1)}, u32[]{:S(2)}, u32[]{:S(2)}) collective-permute-start(f32[32,16]{0,1:T(8,128)S(1)} %add_add_fusion.7), channel_id=1, source_target_pairs={{0,96},{1,97},{2,98},{3,99},{4,100},{5,101},{6,102},{7,103},{8,104... | collective-permute-start | bytes 6152 | tf_op jit(solution)/shard_map/ppermute | solution.py:21
  125.4 12.5 %collective-permute-start.32 = (f32[32,16]{0,1:T(8,128)S(1)}, f32[32,16]{0,1:T(8,128)S(1)}, u32[]{:S(2)}, u32[]{:S(2)}) collective-permute-start(f32[32,16]{0,1:T(8,128)S(1)} %add_add_fusion.7), channel_id=1, source_target_pairs={{0,32},{1,33},{2,34},{3,35},{4,36},{5,37},{6,38},{7,39},{8,40},{9,... | collective-permute-start | bytes 6152 | tf_op jit(solution)/shard_map/ppermute | solution.py:21
  130.4 14.8 %collective-permute-start.20 = (f32[8,1,64,256]{3,0,2,1:T(8,128)S(1)}, f32[8,1,64,256]{3,0,2,1:T(8,128)S(1)}, u32[]{:S(2)}, u32[]{:S(2)}) collective-permute-start(f32[8,1,64,256]{3,0,2,1:T(8,128)S(1)} %get-tuple-element.23), channel_id=1, source_target_pairs={{0,2},{2,4},{4,6},{6,8},{8,10},{10,12},{12,14},{14,16},{16,18},{18... | collective-permute-start | bytes 1572872 | tf_op jit(solution)/shard_map/ppermute | solution.py:57
  130.4 14.8 %collective-permute-start.22 = (f32[8,1,64,256]{3,0,2,1:T(8,128)S(1)}, f32[8,1,64,256]{3,0,2,1:T(8,128)S(1)}, u32[]{:S(2)}, u32[]{:S(2)}) collective-permute-start(f32[8,1,64,256]{3,0,2,1:T(8,128)S(1)} %get-tuple-element.23), channel_id=1, source_target_pairs={{2,0},{4,2},{6,4},{8,6},{10,8},{12,10},{14,12},{16,14},{18,16},{20... | collective-permute-start | bytes 1572872 | tf_op jit(solution)/shard_map/ppermute | solution.py:60
  137.9 3.9 %collective-permute-start.24 = (f32[16,1,2,256]{3,0,2,1:T(8,128)S(1)}, f32[16,1,2,256]{3,0,2,1:T(8,128)S(1)}, u32[]{:S(2)}, u32[]{:S(2)}) collective-permute-start(f32[16,1,2,256]{3,0,2,1:T(8,128)S(1)} %pad_maximum_fusion.6), channel_id=1, source_target_pairs={{0,1},{1,0},{2,3},{3,2},{4,5},{5,4},{6,7},{7,6},{8,9},{9,8},{10,11... | collective-permute-start | bytes 98312 | tf_op jit(solution)/shard_map/ppermute | solution.py:46
  148.5 3.7 %collective-permute-start.35 = (f32[32,16]{0,1:T(8,128)S(1)}, f32[32,16]{0,1:T(8,128)S(1)}, u32[]{:S(2)}, u32[]{:S(2)}) collective-permute-start(f32[32,16]{0,1:T(8,128)S(1)} %pad_maximum_fusion.7), channel_id=1, source_target_pairs={{0,1},{1,0},{2,3},{3,2},{4,5},{5,4},{6,7},{7,6},{8,9},{9,8},{10,11... | collective-permute-start | bytes 6152 | tf_op jit(solution)/shard_map/ppermute | solution.py:21
  152.2 3.7 %collective-permute-start.37 = (f32[32,16]{0,1:T(8,128)S(1)}, f32[32,16]{0,1:T(8,128)S(1)}, u32[]{:S(2)}, u32[]{:S(2)}) collective-permute-start(f32[32,16]{0,1:T(8,128)S(1)} %fusion.160), channel_id=1, source_target_pairs={{0,4},{1,5},{2,6},{3,7},{4,0},{5,1},{6,2},{7,3},{8,12},{9,13},{10,... | collective-permute-start | bytes 6152 | tf_op jit(solution)/shard_map/ppermute | solution.py:21
  152.2 3.6 %collective-permute-start.38 = (f32[32,16]{0,1:T(8,128)S(1)}, f32[32,16]{0,1:T(8,128)S(1)}, u32[]{:S(2)}, u32[]{:S(2)}) collective-permute-start(f32[32,16]{0,1:T(8,128)S(1)} %fusion.160), channel_id=1, source_target_pairs={{0,6},{1,7},{2,4},{3,5},{4,2},{5,3},{6,0},{7,1},{8,14},{9,15},{10,... | collective-permute-start | bytes 6152 | tf_op jit(solution)/shard_map/ppermute | solution.py:21
  152.3 3.6 %collective-permute-start.36 = (f32[32,16]{0,1:T(8,128)S(1)}, f32[32,16]{0,1:T(8,128)S(1)}, u32[]{:S(2)}, u32[]{:S(2)}) collective-permute-start(f32[32,16]{0,1:T(8,128)S(1)} %fusion.160), channel_id=1, source_target_pairs={{0,2},{1,3},{2,0},{3,1},{4,6},{5,7},{6,4},{7,5},{8,10},{9,11},{10,... | collective-permute-start | bytes 6152 | tf_op jit(solution)/shard_map/ppermute | solution.py:21
  155.9 6.6 %collective-permute-start.40 = (f32[32,16]{0,1:T(8,128)S(1)}, f32[32,16]{0,1:T(8,128)S(1)}, u32[]{:S(2)}, u32[]{:S(2)}) collective-permute-start(f32[32,16]{0,1:T(8,128)S(1)} %add_add_fusion.5), channel_id=1, source_target_pairs={{0,16},{1,17},{2,18},{3,19},{4,20},{5,21},{6,22},{7,23},{8,24},{9,... | collective-permute-start | bytes 6152 | tf_op jit(solution)/shard_map/ppermute | solution.py:21
  158.0 7.6 %collective-permute-start.41 = (f32[32,16]{0,1:T(8,128)S(1)}, f32[32,16]{0,1:T(8,128)S(1)}, u32[]{:S(2)}, u32[]{:S(2)}) collective-permute-start(f32[32,16]{0,1:T(8,128)S(1)} %add_add_fusion.5), channel_id=1, source_target_pairs={{0,24},{1,25},{2,26},{3,27},{4,28},{5,29},{6,30},{7,31},{8,16},{9,... | collective-permute-start | bytes 6152 | tf_op jit(solution)/shard_map/ppermute | solution.py:21
  158.0 7.6 %collective-permute-start.39 = (f32[32,16]{0,1:T(8,128)S(1)}, f32[32,16]{0,1:T(8,128)S(1)}, u32[]{:S(2)}, u32[]{:S(2)}) collective-permute-start(f32[32,16]{0,1:T(8,128)S(1)} %add_add_fusion.5), channel_id=1, source_target_pairs={{0,8},{1,9},{2,10},{3,11},{4,12},{5,13},{6,14},{7,15},{8,0},{9,1},... | collective-permute-start | bytes 6152 | tf_op jit(solution)/shard_map/ppermute | solution.py:21
  165.6 5.2 %collective-permute-start.43 = (f32[32,16]{0,1:T(8,128)S(1)}, f32[32,16]{0,1:T(8,128)S(1)}, u32[]{:S(2)}, u32[]{:S(2)}) collective-permute-start(f32[32,16]{0,1:T(8,128)S(1)} %add_add_fusion.4), channel_id=1, source_target_pairs={{0,64},{1,65},{2,66},{3,67},{4,68},{5,69},{6,70},{7,71},{8,72},{9,... | collective-permute-start | bytes 6152 | tf_op jit(solution)/shard_map/ppermute | solution.py:21
  165.7 5.1 %collective-permute-start.44 = (f32[32,16]{0,1:T(8,128)S(1)}, f32[32,16]{0,1:T(8,128)S(1)}, u32[]{:S(2)}, u32[]{:S(2)}) collective-permute-start(f32[32,16]{0,1:T(8,128)S(1)} %add_add_fusion.4), channel_id=1, source_target_pairs={{0,96},{1,97},{2,98},{3,99},{4,100},{5,101},{6,102},{7,103},{8,104... | collective-permute-start | bytes 6152 | tf_op jit(solution)/shard_map/ppermute | solution.py:21
  167.6 3.7 %collective-permute-start.42 = (f32[32,16]{0,1:T(8,128)S(1)}, f32[32,16]{0,1:T(8,128)S(1)}, u32[]{:S(2)}, u32[]{:S(2)}) collective-permute-start(f32[32,16]{0,1:T(8,128)S(1)} %add_add_fusion.4), channel_id=1, source_target_pairs={{0,32},{1,33},{2,34},{3,35},{4,36},{5,37},{6,38},{7,39},{8,40},{9,... | collective-permute-start | bytes 6152 | tf_op jit(solution)/shard_map/ppermute | solution.py:21
  178.5 9.3 %collective-permute-start.46 = (f32[4,1,64,256]{3,0,2,1:T(4,128)S(1)}, f32[4,1,64,256]{3,0,2,1:T(4,128)S(1)}, u32[]{:S(2)}, u32[]{:S(2)}) collective-permute-start(f32[4,1,64,256]{3,0,2,1:T(4,128)S(1)} %get-tuple-element.18), channel_id=1, source_target_pairs={{0,1},{1,0},{2,3},{3,2},{4,5},{5,4},{6,7},{7,6},{8,9},{9,8},{10,11... | collective-permute-start | bytes 786440 | tf_op jit(solution)/shard_map/ppermute | solution.py:46
  179.8 11.6 %collective-permute-start.45 = (f32[4,1,64,256]{3,0,2,1:T(4,128)S(1)}, f32[4,1,64,256]{3,0,2,1:T(4,128)S(1)}, u32[]{:S(2)}, u32[]{:S(2)}) collective-permute-start(f32[4,1,64,256]{3,0,2,1:T(4,128)S(1)} %get-tuple-element.17), channel_id=1, source_target_pairs={{0,1},{1,0},{2,3},{3,2},{4,5},{5,4},{6,7},{7,6},{8,9},{9,8},{10,11... | collective-permute-start | bytes 786440 | tf_op jit(solution)/shard_map/ppermute | solution.py:46

commit v8 on v4

--- a/solution.py
+++ b/solution.py
@@ -1,6 +1,8 @@
 import jax
 import jax.numpy as jnp
 from jax import lax
+from jax.experimental import pallas as pl
+from jax.experimental.pallas import tpu as pltpu
 from jax.sharding import PartitionSpec as P
 
 NSWEEP = 3
@@ -67,11 +69,38 @@
     return potential * value - beside
 
 
-def inverse_factor(gram):
-    lower = jnp.linalg.cholesky(gram)
-    return jax.scipy.linalg.solve_triangular(
-        lower, jnp.eye(gram.shape[0], dtype=jnp.float32), lower=True
-    )
+def _upper_inverse_kernel(a_ref, c_ref):
+    n = a_ref.shape[0]
+    a = a_ref[...]
+    rows = lax.broadcasted_iota(jnp.int32, (n, n), 0)
+    cols = lax.broadcasted_iota(jnp.int32, (n, n), 1)
+    colv = lax.broadcasted_iota(jnp.int32, (n, 1), 0)
+    lcols, diags = [], []
+    for j in range(n):
+        col = a[:, j:j + 1]
+        row = a[j:j + 1, :]
+        root = jnp.sqrt(a[j:j + 1, j:j + 1])
+        lcol = jnp.where(colv >= j, col / root, 0.0)
+        lrow = jnp.where(cols[:1] >= j, row / root, 0.0)
+        a = a - lcol * lrow
+        lcols.append(lcol)
+        diags.append(root)
+    c = jnp.zeros((n, n), jnp.float32)
+    for i in reversed(range(n)):
+        part = jnp.sum(jnp.where(colv > i, lcols[i], 0.0) * c, axis=0, keepdims=True)
+        r = jnp.where(cols[:1] == i, 1.0, 0.0) - part
+        c = jnp.where(rows == i, r / diags[i], c)
+    c_ref[...] = c
+
+
+def upper_inverse(gram):
+    sym = 0.5 * (gram + gram.T)
+    return pl.pallas_call(
+        _upper_inverse_kernel,
+        out_shape=jax.ShapeDtypeStruct(gram.shape, jnp.float32),
+        in_specs=[pl.BlockSpec(memory_space=pltpu.VMEM)],
+        out_specs=pl.BlockSpec(memory_space=pltpu.VMEM),
+    )(sym)
 
 
 def local(potential, start_basis):
@@ -116,7 +145,7 @@
     u_sh = first[:nb, 3 * nb:]
     u_hs = first[nb:, 2 * nb:3 * nb]
     u_hh = first[nb:, 3 * nb:]
-    cmat = inverse_factor(gram).T
+    cmat = upper_inverse(gram)
     ct = cmat.T
     rayleigh = mm(ct, mm(g_sh, cmat))
     b_b = mm(ct, mm(gram, cmat))
@@ -161,7 +190,7 @@
     proj_two = red[:nb]
     gram_two = red[nb:] - 2.0 * mm(proj_two.T, proj_two) + mm(proj_two.T, mm(b_b, proj_two))
     fresh = correction - combine(proj_two, basis)
-    new_all = combine(inverse_factor(gram_two).T, fresh)
+    new_all = combine(upper_inverse(gram_two), fresh)
 
     own = lax.dynamic_slice_in_dim(new_all, v * mine, mine, 0)
     out = lax.dynamic_slice_in_dim(new_all, (1 - v) * mine, mine, 0)

time: 185 us -> 192 us (1.038)
  matrix products: 16.4 us -> 23.2 us
  other arithmetic: 12.1 us -> 5.98 us
  Pallas kernels: 0 us -> 5.84 us
    another operation x10 -> x0, other arithmetic: 8.02 us -> none  [the longest x6 4.27 us: inverse_factor(): lower = jnp.linalg.cholesky(gram)]
    pallas_call x0 -> x2, Pallas kernels: none -> 5.84 us  [upper_inverse(): pl.pallas_call(_upper_inverse_kernel, out_shape=jax.ShapeDtypeStruct(gram...]
    dot_general x19, matrix products: 3.58 us -> 9.12 us  [mm(): return jnp.matmul(a, b, precision=PREC)]
    mul x0 -> x3, other arithmetic: none -> 1.93 us  [the longest x2 1.22 us: upper_inverse(): sym = 0.5 * (gram + gram.T)]
where the time goes in v8:
time: 192 us; the launch traced here: 191 us
  waiting for transfers between devices  86.2 us (45%)
  starting transfers between devices  63 us (33%)
  matrix products  23.2 us (12%)
  other arithmetic  5.98 us (3%)
  Pallas kernels  5.84 us (3%)
  local copies, waits for them, and re-layouts  5.4 us (3%)
    ppermute x30, starting transfers between devices, allsum(): vals[m] = lax.ppermute(x, AXES, [(i, i ^ mask) for i in range(n)])  43 us
    ppermute x30, waiting for transfers between devices, allsum(): vals[m] = lax.ppermute(x, AXES, [(i, i ^ mask) for i in range(n)])  37.9 us
    ppermute x4, waiting for transfers between devices, swap_vec(): return lax.ppermute(value, 'vec', [(0, 1), (1, 0)])  23.8 us
    dot_general x6, matrix products, combine(): return jnp.einsum('kj,kzyx->jzyx', coeff, vectors, precision=FIELD_PREC)  9.83 us
    dot_general x19, matrix products, mm(): return jnp.matmul(a, b, precision=PREC)  9.12 us
    ppermute x1, waiting for transfers between devices, local(): lax.ppermute(give_rows, AXES, cross_down)  8.77 us
    ppermute x2, waiting for transfers between devices, halo(): after = lax.ppermute(value, 'space', down)  7.83 us
    ppermute x2, waiting for transfers between devices, halo(): before = lax.ppermute(value, 'space', up)  7.63 us
  transfers between devices with their start and end apart: 42, of which 31 were waited for; matrix products, arithmetic and copies ran while one was open for 3% of the time, Pallas kernels for 0%

profile of v8, /device:TPU:0, one launch (start us, length us, event | category | flops | bytes accessed | tf_op | source)
XLA Modules:
  0.0 190.6 jit_solution(14973078134208719477)
XLA Ops:
  0.6 1.8 copy.13
  2.7 2.1 %collective-permute-start = (f32[8,1,66,256]{3,0,2,1:T(8,128)S(1)}, f32[8,1,66,256]{3,0,2,1:T(8,128)S(1)}, u32[]{:S(2)}, u32[]{:S(2)}) collective-permute-start(f32[8,1,66,256]{3,0,2,1:T(8,128)S(1)} %get-tuple-element.14), channel_id=1, source_target_pairs={{0,1},{1,0},{2,3},{3,2},{4,5},{5,4},{6,7},{7,6},{8,9},{9,8},{10,11... | collective-permute-start | bytes 1622024 | tf_op jit(solution)/shard_map/ppermute | solution.py:48
  4.8 1.0 constant_dynamic-slice_fusion
  5.8 6.3 %collective-permute-start.4 = (f32[8,1,64,256]{3,0,2,1:T(8,128)}, f32[8,1,64,256]{3,0,2,1:T(8,128)S(1)}, u32[]{:S(2)}, u32[]{:S(2)}) collective-permute-start(f32[8,1,64,256]{3,0,2,1:T(8,128)} %get-tuple-element.11), channel_id=1, source_target_pairs={{3,0},{2,1},{5,2},{4,3},{7,4},{6,5},{9,6},{8,7},{11,8},{10,9},{13,... | collective-permute-start | bytes 1572872 | tf_op jit(solution)/shard_map/ppermute | solution.py:130
  12.2 7.0 %collective-permute-start.3 = (f32[8,1,64,256]{3,0,2,1:T(8,128)}, f32[8,1,64,256]{3,0,2,1:T(8,128)}, u32[]{:S(2)}, u32[]{:S(2)}) collective-permute-start(f32[8,1,64,256]{3,0,2,1:T(8,128)} %get-tuple-element.12), channel_id=1, source_target_pairs={{2,0},{3,1},{4,2},{5,3},{6,4},{7,5},{8,6},{9,7},{10,8},{11,9},{12,... | collective-permute-start | bytes 1572872 | tf_op jit(solution)/shard_map/ppermute | solution.py:130
  19.2 9.9 %collective-permute-done = f32[8,1,66,256]{3,0,2,1:T(8,128)S(1)} collective-permute-done((f32[8,1,66,256]{3,0,2,1:T(8,128)S(1)}, f32[8,1,66,256]{3,0,2,1:T(8,128)S(1)}, u32[]{:S(2)}, u32[]{:S(2)}) %collective-permute-start) | collective-permute-done | bytes 540704 | tf_op jit(solution)/shard_map/ppermute | solution.py:48
  29.9 8.8 %collective-permute-done.4 = f32[8,1,64,256]{3,0,2,1:T(8,128)S(1)} collective-permute-done((f32[8,1,64,256]{3,0,2,1:T(8,128)}, f32[8,1,64,256]{3,0,2,1:T(8,128)S(1)}, u32[]{:S(2)}, u32[]{:S(2)}) %collective-permute-start.4) | collective-permute-done | bytes 524320 | tf_op jit(solution)/shard_map/ppermute | solution.py:130
  38.9 2.3 %broadcast_divide_fusion = (f32[16,1,64,256]{3,0,2,1:T(8,128)S(1)}, f32[16,1,64,256]{3,0,2,1:T(8,128)S(1)}, f32[16,1,64,256]{3,0,2,1:T(8,128)S(1)}) fusion(f32[64,256]{1,0:T(8,128)S(1)} %get-tuple-element.32, f32[16,1,64,1]{3,0,2,1:T(8,128)S(1)} %get-tuple-element.8, f32[16,1,64,255]{3,0,2,1:T(8,128)S(1)} %get-tuple-element.10, ...), kind=kLoop, calls=%fused_computation.85 | loop fusion | flops 4456448 | bytes 10616833 | tf_op jit(solution)/shard_map/div | solution.py:140
  41.2 1.8 fusion.58
  43.0 1.3 collective-permute-start.5
  44.3 2.7 %collective-permute-done.5 = f32[32,64]{0,1:T(8,128)S(1)} collective-permute-done((f32[32,64]{0,1:T(8,128)S(1)}, f32[32,64]{0,1:T(8,128)S(1)}, u32[]{:S(2)}, u32[]{:S(2)}) %collective-permute-start.5) | collective-permute-done | bytes 8224 | tf_op jit(solution)/shard_map/ppermute | solution.py:23
  47.4 1.2 collective-permute-start.7
  48.8 1.8 collective-permute-done.8
  50.6 0.8 collective-permute-done.7
  51.4 6.1 %collective-permute-start.11 = (f32[32,64]{0,1:T(8,128)S(1)}, f32[32,64]{0,1:T(8,128)S(1)}, u32[]{:S(2)}, u32[]{:S(2)}) collective-permute-start(f32[32,64]{0,1:T(8,128)S(1)} %add_add_fusion.2), channel_id=1, source_target_pairs={{0,24},{1,25},{2,26},{3,27},{4,28},{5,29},{6,30},{7,31},{8,16},{9,... | collective-permute-start | bytes 24584 | tf_op jit(solution)/shard_map/ppermute | solution.py:23
  58.3 1.1 collective-permute-done.11
  59.4 3.5 %collective-permute-done.10 = f32[32,64]{0,1:T(8,128)S(1)} collective-permute-done((f32[32,64]{0,1:T(8,128)S(1)}, f32[32,64]{0,1:T(8,128)S(1)}, u32[]{:S(2)}, u32[]{:S(2)}) %collective-permute-start.10) | collective-permute-done | bytes 8224 | tf_op jit(solution)/shard_map/ppermute | solution.py:23
  62.9 3.1 %collective-permute-start.14 = (f32[32,64]{0,1:T(8,128)S(1)}, f32[32,64]{0,1:T(8,128)S(1)}, u32[]{:S(2)}, u32[]{:S(2)}) collective-permute-start(f32[32,64]{0,1:T(8,128)S(1)} %add_add_fusion.1), channel_id=1, source_target_pairs={{0,96},{1,97},{2,98},{3,99},{4,100},{5,101},{6,102},{7,103},{8,104... | collective-permute-start | bytes 24584 | tf_op jit(solution)/shard_map/ppermute | solution.py:23
  67.1 1.0 collective-permute-done.14
  68.1 3.3 %collective-permute-done.13 = f32[32,64]{0,1:T(8,128)S(1)} collective-permute-done((f32[32,64]{0,1:T(8,128)S(1)}, f32[32,64]{0,1:T(8,128)S(1)}, u32[]{:S(2)}, u32[]{:S(2)}) %collective-permute-start.13) | collective-permute-done | bytes 8224 | tf_op jit(solution)/shard_map/ppermute | solution.py:23
  72.1 2.9 %shard_map.41 = f32[16,16]{1,0:T(8,128)} custom-call(f32[16,16]{1,0:T(8,128)} %fusion.87.a_ref), custom_call_target="tpu_custom_call" | custom-call | tf_op jit(solution)/shard_map/pallas_call | solution.py:98
  75.1 0.9 fusion.105
  76.0 0.8 fusion.91
  76.8 0.9 fusion.93
  78.4 0.9 fusion.120
  79.3 0.8 fusion.119
  80.6 0.9 convolution_subtract_fusion.3
  81.5 0.9 convolution_negate_fusion.1
  82.4 0.8 fusion.121
  83.2 2.8 %fusion.9 = f32[64,64,256]{2,0,1:T(8,128)S(1)} fusion(f32[16,1,64,256]{3,0,2,1:T(8,128)S(1)} %get-tuple-element.5, f32[16,1,64,256]{3,0,2,1:T(8,128)S(1)} %slice.208, f32[16,16]{1,0:T(8,128)S(1)} %broadcast_in_dim.2, f32[16,16]{1,0:T(8,128)} %shard_map.41, f32[16,16]{1,0:T(8,128)S(1)} %fusion.121, f32[16,16]{1,0:T(8,128)S(1)} %get-tuple-element.37, ...), kind=kOutput, calls=%fused_computation.11 | convolution fusion | flops 201865216 | bytes 6296576 | tf_op jit(solution)/shard_map/kj,kzyx->jzyx/dot_general | solution.py:40
  86.3 1.0 collective-permute-start.16
  87.9 1.8 collective-permute-start.17
  90.8 1.0 collective-permute-done.17
  91.9 7.8 %collective-permute-done.16 = f32[16,1,64,256]{3,0,2,1:T(8,128)S(1)} collective-permute-done((f32[16,1,64,256]{3,0,2,1:T(8,128)S(1)}, f32[16,1,64,256]{3,0,2,1:T(8,128)S(1)}, u32[]{:S(2)}, u32[]{:S(2)}) %collective-permute-start.16) | collective-permute-done | bytes 1048608 | tf_op jit(solution)/shard_map/ppermute | solution.py:58
  99.7 7.6 %collective-permute-done.15 = f32[16,1,64,256]{3,0,2,1:T(8,128)S(1)} collective-permute-done((f32[16,1,64,256]{3,0,2,1:T(8,128)S(1)}, f32[16,1,64,256]{3,0,2,1:T(8,128)S(1)}, u32[]{:S(2)}, u32[]{:S(2)}) %collective-permute-start.15) | collective-permute-done | bytes 1048608 | tf_op jit(solution)/shard_map/ppermute | solution.py:57
  107.3 1.6 fusion.13
  109.0 1.0 fusion.29
  109.9 1.3 collective-permute-start.21
  111.8 1.8 collective-permute-done.21
  113.6 1.9 collective-permute-start.22
  115.9 0.9 collective-permute-done.24
  116.8 2.2 %collective-permute-done.23 = f32[32,16]{0,1:T(8,128)S(1)} collective-permute-done((f32[32,16]{0,1:T(8,128)S(1)}, f32[32,16]{0,1:T(8,128)S(1)}, u32[]{:S(2)}, u32[]{:S(2)}) %collective-permute-start.23) | collective-permute-done | bytes 2080 | tf_op jit(solution)/shard_map/ppermute | solution.py:23
  118.9 6.0 %collective-permute-start.27 = (f32[32,16]{0,1:T(8,128)S(1)}, f32[32,16]{0,1:T(8,128)S(1)}, u32[]{:S(2)}, u32[]{:S(2)}) collective-permute-start(f32[32,16]{0,1:T(8,128)S(1)} %add_add_fusion.8), channel_id=1, source_target_pairs={{0,24},{1,25},{2,26},{3,27},{4,28},{5,29},{6,30},{7,31},{8,16},{9,... | collective-permute-start | bytes 6152 | tf_op jit(solution)/shard_map/ppermute | solution.py:23
  125.0 0.9 collective-permute-start.26
  126.7 5.2 %collective-permute-done.26 = f32[32,16]{0,1:T(8,128)S(1)} collective-permute-done((f32[32,16]{0,1:T(8,128)S(1)}, f32[32,16]{0,1:T(8,128)S(1)}, u32[]{:S(2)}, u32[]{:S(2)}) %collective-permute-start.26) | collective-permute-done | bytes 2080 | tf_op jit(solution)/shard_map/ppermute | solution.py:23
  132.0 1.3 collective-permute-start.29
  133.3 2.8 %collective-permute-start.28 = (f32[32,16]{0,1:T(8,128)S(1)}, f32[32,16]{0,1:T(8,128)S(1)}, u32[]{:S(2)}, u32[]{:S(2)}) collective-permute-start(f32[32,16]{0,1:T(8,128)S(1)} %add_add_fusion.7), channel_id=1, source_target_pairs={{0,32},{1,33},{2,34},{3,35},{4,36},{5,37},{6,38},{7,39},{8,40},{9,... | collective-permute-start | bytes 6152 | tf_op jit(solution)/shard_map/ppermute | solution.py:23
  138.6 2.1 %collective-permute-done.20 = f32[16,1,2,256]{3,0,2,1:T(8,128)S(1)} collective-permute-done((f32[16,1,2,256]{3,0,2,1:T(8,128)S(1)}, f32[16,1,2,256]{3,0,2,1:T(8,128)S(1)}, u32[]{:S(2)}, u32[]{:S(2)}) %collective-permute-start.20) | collective-permute-done | bytes 32800 | tf_op jit(solution)/shard_map/ppermute | solution.py:48
  140.8 1.6 fusion.18
  144.5 3.2 %collective-permute-done.31 = f32[32,16]{0,1:T(8,128)S(1)} collective-permute-done((f32[32,16]{0,1:T(8,128)S(1)}, f32[32,16]{0,1:T(8,128)S(1)}, u32[]{:S(2)}, u32[]{:S(2)}) %collective-permute-start.31) | collective-permute-done | bytes 2080 | tf_op jit(solution)/shard_map/ppermute | solution.py:23
  147.9 2.5 %collective-permute-start.33 = (f32[32,16]{0,1:T(8,128)S(1)}, f32[32,16]{0,1:T(8,128)S(1)}, u32[]{:S(2)}, u32[]{:S(2)}) collective-permute-start(f32[32,16]{0,1:T(8,128)S(1)} %fusion.151), channel_id=1, source_target_pairs={{0,4},{1,5},{2,6},{3,7},{4,0},{5,1},{6,2},{7,3},{8,12},{9,13},{10,... | collective-permute-start | bytes 6152 | tf_op jit(solution)/shard_map/ppermute | solution.py:23
  150.9 1.0 collective-permute-done.33
  152.0 5.4 %collective-permute-start.37 = (f32[32,16]{0,1:T(8,128)S(1)}, f32[32,16]{0,1:T(8,128)S(1)}, u32[]{:S(2)}, u32[]{:S(2)}) collective-permute-start(f32[32,16]{0,1:T(8,128)S(1)} %add_add_fusion.5), channel_id=1, source_target_pairs={{0,24},{1,25},{2,26},{3,27},{4,28},{5,29},{6,30},{7,31},{8,16},{9,... | collective-permute-start | bytes 6152 | tf_op jit(solution)/shard_map/ppermute | solution.py:23
  157.3 2.0 %collective-permute-start.36 = (f32[32,16]{0,1:T(8,128)S(1)}, f32[32,16]{0,1:T(8,128)S(1)}, u32[]{:S(2)}, u32[]{:S(2)}) collective-permute-start(f32[32,16]{0,1:T(8,128)S(1)} %add_add_fusion.5), channel_id=1, source_target_pairs={{0,16},{1,17},{2,18},{3,19},{4,20},{5,21},{6,22},{7,23},{8,24},{9,... | collective-permute-start | bytes 6152 | tf_op jit(solution)/shard_map/ppermute | solution.py:23
  159.8 2.7 %collective-permute-done.36 = f32[32,16]{0,1:T(8,128)S(1)} collective-permute-done((f32[32,16]{0,1:T(8,128)S(1)}, f32[32,16]{0,1:T(8,128)S(1)}, u32[]{:S(2)}, u32[]{:S(2)}) %collective-permute-start.36) | collective-permute-done | bytes 2080 | tf_op jit(solution)/shard_map/ppermute | solution.py:23
  162.5 2.0 %collective-permute-done.35 = f32[32,16]{0,1:T(8,128)S(1)} collective-permute-done((f32[32,16]{0,1:T(8,128)S(1)}, f32[32,16]{0,1:T(8,128)S(1)}, u32[]{:S(2)}, u32[]{:S(2)}) %collective-permute-start.35) | collective-permute-done | bytes 2080 | tf_op jit(solution)/shard_map/ppermute | solution.py:23
  165.0 1.5 collective-permute-start.39
  166.5 2.1 %collective-permute-start.38 = (f32[32,16]{0,1:T(8,128)S(1)}, f32[32,16]{0,1:T(8,128)S(1)}, u32[]{:S(2)}, u32[]{:S(2)}) collective-permute-start(f32[32,16]{0,1:T(8,128)S(1)} %add_add_fusion.4), channel_id=1, source_target_pairs={{0,32},{1,33},{2,34},{3,35},{4,36},{5,37},{6,38},{7,39},{8,40},{9,... | collective-permute-start | bytes 6152 | tf_op jit(solution)/shard_map/ppermute | solution.py:23
  170.3 1.8 fusion.20
  173.3 2.9 %shard_map.42 = f32[16,16]{1,0:T(8,128)} custom-call(f32[16,16]{1,0:T(8,128)} %fusion.85.a_ref), custom_call_target="tpu_custom_call" | custom-call | tf_op jit(solution)/shard_map/pallas_call | solution.py:98
  176.2 1.3 fusion.83
  177.9 0.8 collective-permute-start.41
  178.8 10.7 %collective-permute-done.41 = f32[8,1,64,256]{3,2,0,1:T(8,128)S(1)} collective-permute-done((f32[8,1,64,256]{3,2,0,1:T(8,128)S(1)}, f32[8,1,64,256]{3,2,0,1:T(8,128)S(1)}, u32[]{:S(2)}, u32[]{:S(2)}) %collective-permute-start.41) | collective-permute-done | bytes 524320 | tf_op jit(solution)/shard_map/ppermute | solution.py:48
  189.5 1.0 fusion.49
  (105 shorter events, 19.0 us)
Async XLA Ops:
  2.6 16.6 %copy-start.2 = (f32[1,128,256]{2,1,0:T(8,128)S(1)}, f32[1,128,256]{2,1,0:T(8,128)}, u32[]{:S(2)}) copy-start(f32[1,128,256]{2,1,0:T(8,128)} %param.2) | copy-start | bytes 393220
  2.7 26.5 %collective-permute-start = (f32[8,1,66,256]{3,0,2,1:T(8,128)S(1)}, f32[8,1,66,256]{3,0,2,1:T(8,128)S(1)}, u32[]{:S(2)}, u32[]{:S(2)}) collective-permute-start(f32[8,1,66,256]{3,0,2,1:T(8,128)S(1)} %get-tuple-element.14), channel_id=1, source_target_pairs={{0,1},{1,0},{2,3},{3,2},{4,5},{5,4},{6,7},{7,6},{8,9},{9,8},{10,11... | collective-permute-start | bytes 1622024 | tf_op jit(solution)/shard_map/ppermute | solution.py:48
  5.8 32.8 %collective-permute-start.4 = (f32[8,1,64,256]{3,0,2,1:T(8,128)}, f32[8,1,64,256]{3,0,2,1:T(8,128)S(1)}, u32[]{:S(2)}, u32[]{:S(2)}) collective-permute-start(f32[8,1,64,256]{3,0,2,1:T(8,128)} %get-tuple-element.11), channel_id=1, source_target_pairs={{3,0},{2,1},{5,2},{4,3},{7,4},{6,5},{9,6},{8,7},{11,8},{10,9},{13,... | collective-permute-start | bytes 1572872 | tf_op jit(solution)/shard_map/ppermute | solution.py:130
  12.1 26.7 %collective-permute-start.2 = (f32[8,1,64,256]{3,0,2,1:T(8,128)}, f32[8,1,64,256]{3,0,2,1:T(8,128)S(1)}, u32[]{:S(2)}, u32[]{:S(2)}) collective-permute-start(f32[8,1,64,256]{3,0,2,1:T(8,128)} %get-tuple-element.11), channel_id=1, source_target_pairs={{0,3},{1,2},{2,5},{3,4},{4,7},{5,6},{6,9},{7,8},{8,11},{9,10},{10,... | collective-permute-start | bytes 1572872 | tf_op jit(solution)/shard_map/ppermute | solution.py:129
  12.2 26.7 %collective-permute-start.3 = (f32[8,1,64,256]{3,0,2,1:T(8,128)}, f32[8,1,64,256]{3,0,2,1:T(8,128)}, u32[]{:S(2)}, u32[]{:S(2)}) collective-permute-start(f32[8,1,64,256]{3,0,2,1:T(8,128)} %get-tuple-element.12), channel_id=1, source_target_pairs={{2,0},{3,1},{4,2},{5,3},{6,4},{7,5},{8,6},{9,7},{10,8},{11,9},{12,... | collective-permute-start | bytes 1572872 | tf_op jit(solution)/shard_map/ppermute | solution.py:130
  19.2 19.7 %collective-permute-start.1 = (f32[8,1,64,256]{3,0,2,1:T(8,128)}, f32[8,1,64,256]{3,0,2,1:T(8,128)}, u32[]{:S(2)}, u32[]{:S(2)}) collective-permute-start(f32[8,1,64,256]{3,0,2,1:T(8,128)} %get-tuple-element.12), channel_id=1, source_target_pairs={{0,2},{1,3},{2,4},{3,5},{4,6},{5,7},{6,8},{7,9},{8,10},{9,11},{10,... | collective-permute-start | bytes 1572872 | tf_op jit(solution)/shard_map/ppermute | solution.py:129
  43.0 4.0 %collective-permute-start.5 = (f32[32,64]{0,1:T(8,128)S(1)}, f32[32,64]{0,1:T(8,128)S(1)}, u32[]{:S(2)}, u32[]{:S(2)}) collective-permute-start(f32[32,64]{0,1:T(8,128)S(1)} %fusion.58), channel_id=1, source_target_pairs={{0,1},{1,0},{2,3},{3,2},{4,5},{5,4},{6,7},{7,6},{8,9},{9,8},{10,11... | collective-permute-start | bytes 24584 | tf_op jit(solution)/shard_map/ppermute | solution.py:23
  47.0 3.6 %collective-permute-start.8 = (f32[32,64]{0,1:T(8,128)S(1)}, f32[32,64]{0,1:T(8,128)S(1)}, u32[]{:S(2)}, u32[]{:S(2)}) collective-permute-start(f32[32,64]{0,1:T(8,128)S(1)} %add.194), channel_id=1, source_target_pairs={{0,6},{1,7},{2,4},{3,5},{4,2},{5,3},{6,0},{7,1},{8,14},{9,15},{10,... | collective-permute-start | bytes 24584 | tf_op jit(solution)/shard_map/ppermute | solution.py:23
  47.4 4.0 %collective-permute-start.7 = (f32[32,64]{0,1:T(8,128)S(1)}, f32[32,64]{0,1:T(8,128)S(1)}, u32[]{:S(2)}, u32[]{:S(2)}) collective-permute-start(f32[32,64]{0,1:T(8,128)S(1)} %add.194), channel_id=1, source_target_pairs={{0,4},{1,5},{2,6},{3,7},{4,0},{5,1},{6,2},{7,3},{8,12},{9,13},{10,... | collective-permute-start | bytes 24584 | tf_op jit(solution)/shard_map/ppermute | solution.py:23
  48.6 2.9 %collective-permute-start.6 = (f32[32,64]{0,1:T(8,128)S(1)}, f32[32,64]{0,1:T(8,128)S(1)}, u32[]{:S(2)}, u32[]{:S(2)}) collective-permute-start(f32[32,64]{0,1:T(8,128)S(1)} %add.194), channel_id=1, source_target_pairs={{0,2},{1,3},{2,0},{3,1},{4,6},{5,7},{6,4},{7,5},{8,10},{9,11},{10,... | collective-permute-start | bytes 24584 | tf_op jit(solution)/shard_map/ppermute | solution.py:23
  51.4 8.0 %collective-permute-start.11 = (f32[32,64]{0,1:T(8,128)S(1)}, f32[32,64]{0,1:T(8,128)S(1)}, u32[]{:S(2)}, u32[]{:S(2)}) collective-permute-start(f32[32,64]{0,1:T(8,128)S(1)} %add_add_fusion.2), channel_id=1, source_target_pairs={{0,24},{1,25},{2,26},{3,27},{4,28},{5,29},{6,30},{7,31},{8,16},{9,... | collective-permute-start | bytes 24584 | tf_op jit(solution)/shard_map/ppermute | solution.py:23
  57.5 5.4 %collective-permute-start.10 = (f32[32,64]{0,1:T(8,128)S(1)}, f32[32,64]{0,1:T(8,128)S(1)}, u32[]{:S(2)}, u32[]{:S(2)}) collective-permute-start(f32[32,64]{0,1:T(8,128)S(1)} %add_add_fusion.2), channel_id=1, source_target_pairs={{0,16},{1,17},{2,18},{3,19},{4,20},{5,21},{6,22},{7,23},{8,24},{9,... | collective-permute-start | bytes 24584 | tf_op jit(solution)/shard_map/ppermute | solution.py:23
  57.5 5.4 %collective-permute-start.9 = (f32[32,64]{0,1:T(8,128)S(1)}, f32[32,64]{0,1:T(8,128)S(1)}, u32[]{:S(2)}, u32[]{:S(2)}) collective-permute-start(f32[32,64]{0,1:T(8,128)S(1)} %add_add_fusion.2), channel_id=1, source_target_pairs={{0,8},{1,9},{2,10},{3,11},{4,12},{5,13},{6,14},{7,15},{8,0},{9,1},... | collective-permute-start | bytes 24584 | tf_op jit(solution)/shard_map/ppermute | solution.py:23
  62.9 5.2 %collective-permute-start.14 = (f32[32,64]{0,1:T(8,128)S(1)}, f32[32,64]{0,1:T(8,128)S(1)}, u32[]{:S(2)}, u32[]{:S(2)}) collective-permute-start(f32[32,64]{0,1:T(8,128)S(1)} %add_add_fusion.1), channel_id=1, source_target_pairs={{0,96},{1,97},{2,98},{3,99},{4,100},{5,101},{6,102},{7,103},{8,104... | collective-permute-start | bytes 24584 | tf_op jit(solution)/shard_map/ppermute | solution.py:23
  66.0 5.4 %collective-permute-start.13 = (f32[32,64]{0,1:T(8,128)S(1)}, f32[32,64]{0,1:T(8,128)S(1)}, u32[]{:S(2)}, u32[]{:S(2)}) collective-permute-start(f32[32,64]{0,1:T(8,128)S(1)} %add_add_fusion.1), channel_id=1, source_target_pairs={{0,64},{1,65},{2,66},{3,67},{4,68},{5,69},{6,70},{7,71},{8,72},{9,... | collective-permute-start | bytes 24584 | tf_op jit(solution)/shard_map/ppermute | solution.py:23
  66.7 4.8 %collective-permute-start.12 = (f32[32,64]{0,1:T(8,128)S(1)}, f32[32,64]{0,1:T(8,128)S(1)}, u32[]{:S(2)}, u32[]{:S(2)}) collective-permute-start(f32[32,64]{0,1:T(8,128)S(1)} %add_add_fusion.1), channel_id=1, source_target_pairs={{0,32},{1,33},{2,34},{3,35},{4,36},{5,37},{6,38},{7,39},{8,40},{9,... | collective-permute-start | bytes 24584 | tf_op jit(solution)/shard_map/ppermute | solution.py:23
  79.3 6.7 %copy-start.3 = (f32[16,16]{1,0:T(8,128)}, f32[16,16]{1,0:T(8,128)S(1)}, u32[]{:S(2)}) copy-start(f32[16,16]{1,0:T(8,128)S(1)} %fusion.120) | copy-start | bytes 3076
  86.0 57.2 %copy-start = (f32[64,64,256]{2,0,1:T(8,128)}, f32[64,64,256]{2,0,1:T(8,128)S(1)}, u32[]{:S(2)}) copy-start(f32[64,64,256]{2,0,1:T(8,128)S(1)} %fusion.9) | copy-start | bytes 12582916
  86.0 1.3 copy-start.1
  86.3 13.4 %collective-permute-start.16 = (f32[16,1,64,256]{3,0,2,1:T(8,128)S(1)}, f32[16,1,64,256]{3,0,2,1:T(8,128)S(1)}, u32[]{:S(2)}, u32[]{:S(2)}) collective-permute-start(f32[16,1,64,256]{3,0,2,1:T(8,128)S(1)} %fusion.53), channel_id=1, source_target_pairs={{2,0},{4,2},{6,4},{8,6},{10,8},{12,10},{14,12},{16,14},{18,16},{20... | collective-permute-start | bytes 3145736 | tf_op jit(solution)/shard_map/ppermute | solution.py:58
  87.4 19.9 %collective-permute-start.15 = (f32[16,1,64,256]{3,0,2,1:T(8,128)S(1)}, f32[16,1,64,256]{3,0,2,1:T(8,128)S(1)}, u32[]{:S(2)}, u32[]{:S(2)}) collective-permute-start(f32[16,1,64,256]{3,0,2,1:T(8,128)S(1)} %fusion.53), channel_id=1, source_target_pairs={{0,2},{2,4},{4,6},{6,8},{8,10},{10,12},{12,14},{14,16},{16,18},{18... | collective-permute-start | bytes 3145736 | tf_op jit(solution)/shard_map/ppermute | solution.py:57
  87.9 4.0 %collective-permute-start.17 = (f32[16,1,2,256]{3,0,2,1:T(8,128)S(1)}, f32[16,1,2,256]{3,0,2,1:T(8,128)S(1)}, u32[]{:S(2)}, u32[]{:S(2)}) collective-permute-start(f32[16,1,2,256]{3,0,2,1:T(8,128)S(1)} %pad_maximum_fusion.5), channel_id=1, source_target_pairs={{0,1},{1,0},{2,3},{3,2},{4,5},{5,4},{6,7},{7,6},{8,9},{9,8},{10,11... | collective-permute-start | bytes 98312 | tf_op jit(solution)/shard_map/ppermute | solution.py:48
  109.9 3.7 %collective-permute-start.21 = (f32[32,16]{0,1:T(8,128)S(1)}, f32[32,16]{0,1:T(8,128)S(1)}, u32[]{:S(2)}, u32[]{:S(2)}) collective-permute-start(f32[32,16]{0,1:T(8,128)S(1)} %fusion.29), channel_id=1, source_target_pairs={{0,1},{1,0},{2,3},{3,2},{4,5},{5,4},{6,7},{7,6},{8,9},{9,8},{10,11... | collective-permute-start | bytes 6152 | tf_op jit(solution)/shard_map/ppermute | solution.py:23
  111.3 29.5 %collective-permute-start.19 = (f32[16,1,64,256]{3,0,2,1:T(8,128)S(1)}, f32[16,1,64,256]{3,0,2,1:T(8,128)S(1)}, u32[]{:S(2)}, u32[]{:S(2)}) collective-permute-start(f32[16,1,64,256]{3,0,2,1:T(8,128)S(1)} %fusion.13), channel_id=1, source_target_pairs={{2,0},{4,2},{6,4},{8,6},{10,8},{12,10},{14,12},{16,14},{18,16},{20... | collective-permute-start | bytes 3145736 | tf_op jit(solution)/shard_map/ppermute | solution.py:58
  111.6 29.2 %collective-permute-start.18 = (f32[16,1,64,256]{3,0,2,1:T(8,128)S(1)}, f32[16,1,64,256]{3,0,2,1:T(8,128)S(1)}, u32[]{:S(2)}, u32[]{:S(2)}) collective-permute-start(f32[16,1,64,256]{3,0,2,1:T(8,128)S(1)} %fusion.13), channel_id=1, source_target_pairs={{0,2},{2,4},{4,6},{6,8},{8,10},{10,12},{12,14},{14,16},{16,18},{18... | collective-permute-start | bytes 3145736 | tf_op jit(solution)/shard_map/ppermute | solution.py:57
  113.6 3.2 %collective-permute-start.24 = (f32[32,16]{0,1:T(8,128)S(1)}, f32[32,16]{0,1:T(8,128)S(1)}, u32[]{:S(2)}, u32[]{:S(2)}) collective-permute-start(f32[32,16]{0,1:T(8,128)S(1)} %add.216), channel_id=1, source_target_pairs={{0,6},{1,7},{2,4},{3,5},{4,2},{5,3},{6,0},{7,1},{8,14},{9,15},{10,... | collective-permute-start | bytes 6152 | tf_op jit(solution)/shard_map/ppermute | solution.py:23
  113.6 5.3 %collective-permute-start.23 = (f32[32,16]{0,1:T(8,128)S(1)}, f32[32,16]{0,1:T(8,128)S(1)}, u32[]{:S(2)}, u32[]{:S(2)}) collective-permute-start(f32[32,16]{0,1:T(8,128)S(1)} %add.216), channel_id=1, source_target_pairs={{0,4},{1,5},{2,6},{3,7},{4,0},{5,1},{6,2},{7,3},{8,12},{9,13},{10,... | collective-permute-start | bytes 6152 | tf_op jit(solution)/shard_map/ppermute | solution.py:23
  113.6 5.3 %collective-permute-start.22 = (f32[32,16]{0,1:T(8,128)S(1)}, f32[32,16]{0,1:T(8,128)S(1)}, u32[]{:S(2)}, u32[]{:S(2)}) collective-permute-start(f32[32,16]{0,1:T(8,128)S(1)} %add.216), channel_id=1, source_target_pairs={{0,2},{1,3},{2,0},{3,1},{4,6},{5,7},{6,4},{7,5},{8,10},{9,11},{10,... | collective-permute-start | bytes 6152 | tf_op jit(solution)/shard_map/ppermute | solution.py:23
  118.9 7.8 %collective-permute-start.27 = (f32[32,16]{0,1:T(8,128)S(1)}, f32[32,16]{0,1:T(8,128)S(1)}, u32[]{:S(2)}, u32[]{:S(2)}) collective-permute-start(f32[32,16]{0,1:T(8,128)S(1)} %add_add_fusion.8), channel_id=1, source_target_pairs={{0,24},{1,25},{2,26},{3,27},{4,28},{5,29},{6,30},{7,31},{8,16},{9,... | collective-permute-start | bytes 6152 | tf_op jit(solution)/shard_map/ppermute | solution.py:23
  125.0 7.0 %collective-permute-start.26 = (f32[32,16]{0,1:T(8,128)S(1)}, f32[32,16]{0,1:T(8,128)S(1)}, u32[]{:S(2)}, u32[]{:S(2)}) collective-permute-start(f32[32,16]{0,1:T(8,128)S(1)} %add_add_fusion.8), channel_id=1, source_target_pairs={{0,16},{1,17},{2,18},{3,19},{4,20},{5,21},{6,22},{7,23},{8,24},{9,... | collective-permute-start | bytes 6152 | tf_op jit(solution)/shard_map/ppermute | solution.py:23
  125.9 6.0 %collective-permute-start.25 = (f32[32,16]{0,1:T(8,128)S(1)}, f32[32,16]{0,1:T(8,128)S(1)}, u32[]{:S(2)}, u32[]{:S(2)}) collective-permute-start(f32[32,16]{0,1:T(8,128)S(1)} %add_add_fusion.8), channel_id=1, source_target_pairs={{0,8},{1,9},{2,10},{3,11},{4,12},{5,13},{6,14},{7,15},{8,0},{9,1},... | collective-permute-start | bytes 6152 | tf_op jit(solution)/shard_map/ppermute | solution.py:23
  131.9 4.9 %collective-permute-start.30 = (f32[32,16]{0,1:T(8,128)S(1)}, f32[32,16]{0,1:T(8,128)S(1)}, u32[]{:S(2)}, u32[]{:S(2)}) collective-permute-start(f32[32,16]{0,1:T(8,128)S(1)} %add_add_fusion.7), channel_id=1, source_target_pairs={{0,96},{1,97},{2,98},{3,99},{4,100},{5,101},{6,102},{7,103},{8,104... | collective-permute-start | bytes 6152 | tf_op jit(solution)/shard_map/ppermute | solution.py:23
  132.0 5.2 %collective-permute-start.29 = (f32[32,16]{0,1:T(8,128)S(1)}, f32[32,16]{0,1:T(8,128)S(1)}, u32[]{:S(2)}, u32[]{:S(2)}) collective-permute-start(f32[32,16]{0,1:T(8,128)S(1)} %add_add_fusion.7), channel_id=1, source_target_pairs={{0,64},{1,65},{2,66},{3,67},{4,68},{5,69},{6,70},{7,71},{8,72},{9,... | collective-permute-start | bytes 6152 | tf_op jit(solution)/shard_map/ppermute | solution.py:23
  133.3 4.5 %collective-permute-start.28 = (f32[32,16]{0,1:T(8,128)S(1)}, f32[32,16]{0,1:T(8,128)S(1)}, u32[]{:S(2)}, u32[]{:S(2)}) collective-permute-start(f32[32,16]{0,1:T(8,128)S(1)} %add_add_fusion.7), channel_id=1, source_target_pairs={{0,32},{1,33},{2,34},{3,35},{4,36},{5,37},{6,38},{7,39},{8,40},{9,... | collective-permute-start | bytes 6152 | tf_op jit(solution)/shard_map/ppermute | solution.py:23
  136.9 3.9 %collective-permute-start.20 = (f32[16,1,2,256]{3,0,2,1:T(8,128)S(1)}, f32[16,1,2,256]{3,0,2,1:T(8,128)S(1)}, u32[]{:S(2)}, u32[]{:S(2)}) collective-permute-start(f32[16,1,2,256]{3,0,2,1:T(8,128)S(1)} %pad_maximum_fusion.6), channel_id=1, source_target_pairs={{0,1},{1,0},{2,3},{3,2},{4,5},{5,4},{6,7},{7,6},{8,9},{9,8},{10,11... | collective-permute-start | bytes 98312 | tf_op jit(solution)/shard_map/ppermute | solution.py:48
  144.1 3.7 %collective-permute-start.31 = (f32[32,16]{0,1:T(8,128)S(1)}, f32[32,16]{0,1:T(8,128)S(1)}, u32[]{:S(2)}, u32[]{:S(2)}) collective-permute-start(f32[32,16]{0,1:T(8,128)S(1)} %pad_maximum_fusion.7), channel_id=1, source_target_pairs={{0,1},{1,0},{2,3},{3,2},{4,5},{5,4},{6,7},{7,6},{8,9},{9,8},{10,11... | collective-permute-start | bytes 6152 | tf_op jit(solution)/shard_map/ppermute | solution.py:23
  147.8 3.1 %collective-permute-start.34 = (f32[32,16]{0,1:T(8,128)S(1)}, f32[32,16]{0,1:T(8,128)S(1)}, u32[]{:S(2)}, u32[]{:S(2)}) collective-permute-start(f32[32,16]{0,1:T(8,128)S(1)} %fusion.151), channel_id=1, source_target_pairs={{0,6},{1,7},{2,4},{3,5},{4,2},{5,3},{6,0},{7,1},{8,14},{9,15},{10,... | collective-permute-start | bytes 6152 | tf_op jit(solution)/shard_map/ppermute | solution.py:23
  147.9 4.1 %collective-permute-start.33 = (f32[32,16]{0,1:T(8,128)S(1)}, f32[32,16]{0,1:T(8,128)S(1)}, u32[]{:S(2)}, u32[]{:S(2)}) collective-permute-start(f32[32,16]{0,1:T(8,128)S(1)} %fusion.151), channel_id=1, source_target_pairs={{0,4},{1,5},{2,6},{3,7},{4,0},{5,1},{6,2},{7,3},{8,12},{9,13},{10,... | collective-permute-start | bytes 6152 | tf_op jit(solution)/shard_map/ppermute | solution.py:23
  150.3 1.6 collective-permute-start.32
  152.0 7.9 %collective-permute-start.37 = (f32[32,16]{0,1:T(8,128)S(1)}, f32[32,16]{0,1:T(8,128)S(1)}, u32[]{:S(2)}, u32[]{:S(2)}) collective-permute-start(f32[32,16]{0,1:T(8,128)S(1)} %add_add_fusion.5), channel_id=1, source_target_pairs={{0,24},{1,25},{2,26},{3,27},{4,28},{5,29},{6,30},{7,31},{8,16},{9,... | collective-permute-start | bytes 6152 | tf_op jit(solution)/shard_map/ppermute | solution.py:23
  157.3 5.2 %collective-permute-start.36 = (f32[32,16]{0,1:T(8,128)S(1)}, f32[32,16]{0,1:T(8,128)S(1)}, u32[]{:S(2)}, u32[]{:S(2)}) collective-permute-start(f32[32,16]{0,1:T(8,128)S(1)} %add_add_fusion.5), channel_id=1, source_target_pairs={{0,16},{1,17},{2,18},{3,19},{4,20},{5,21},{6,22},{7,23},{8,24},{9,... | collective-permute-start | bytes 6152 | tf_op jit(solution)/shard_map/ppermute | solution.py:23
  159.4 5.2 %collective-permute-start.35 = (f32[32,16]{0,1:T(8,128)S(1)}, f32[32,16]{0,1:T(8,128)S(1)}, u32[]{:S(2)}, u32[]{:S(2)}) collective-permute-start(f32[32,16]{0,1:T(8,128)S(1)} %add_add_fusion.5), channel_id=1, source_target_pairs={{0,8},{1,9},{2,10},{3,11},{4,12},{5,13},{6,14},{7,15},{8,0},{9,1},... | collective-permute-start | bytes 6152 | tf_op jit(solution)/shard_map/ppermute | solution.py:23
  164.5 4.9 %collective-permute-start.40 = (f32[32,16]{0,1:T(8,128)S(1)}, f32[32,16]{0,1:T(8,128)S(1)}, u32[]{:S(2)}, u32[]{:S(2)}) collective-permute-start(f32[32,16]{0,1:T(8,128)S(1)} %add_add_fusion.4), channel_id=1, source_target_pairs={{0,96},{1,97},{2,98},{3,99},{4,100},{5,101},{6,102},{7,103},{8,104... | collective-permute-start | bytes 6152 | tf_op jit(solution)/shard_map/ppermute | solution.py:23
  165.0 5.2 %collective-permute-start.39 = (f32[32,16]{0,1:T(8,128)S(1)}, f32[32,16]{0,1:T(8,128)S(1)}, u32[]{:S(2)}, u32[]{:S(2)}) collective-permute-start(f32[32,16]{0,1:T(8,128)S(1)} %add_add_fusion.4), channel_id=1, source_target_pairs={{0,64},{1,65},{2,66},{3,67},{4,68},{5,69},{6,70},{7,71},{8,72},{9,... | collective-permute-start | bytes 6152 | tf_op jit(solution)/shard_map/ppermute | solution.py:23
  166.5 3.9 %collective-permute-start.38 = (f32[32,16]{0,1:T(8,128)S(1)}, f32[32,16]{0,1:T(8,128)S(1)}, u32[]{:S(2)}, u32[]{:S(2)}) collective-permute-start(f32[32,16]{0,1:T(8,128)S(1)} %add_add_fusion.4), channel_id=1, source_target_pairs={{0,32},{1,33},{2,34},{3,35},{4,36},{5,37},{6,38},{7,39},{8,40},{9,... | collective-permute-start | bytes 6152 | tf_op jit(solution)/shard_map/ppermute | solution.py:23
  177.9 11.7 %collective-permute-start.41 = (f32[8,1,64,256]{3,2,0,1:T(8,128)S(1)}, f32[8,1,64,256]{3,2,0,1:T(8,128)S(1)}, u32[]{:S(2)}, u32[]{:S(2)}) collective-permute-start(f32[8,1,64,256]{3,2,0,1:T(8,128)S(1)} %bitcast.148), channel_id=1, source_target_pairs={{0,1},{1,0},{2,3},{3,2},{4,5},{5,4},{6,7},{7,6},{8,9},{9,8},{10,11... | collective-permute-start | bytes 1572872 | tf_op jit(solution)/shard_map/ppermute | solution.py:48

commit v9 on v4

--- a/solution.py
+++ b/solution.py
@@ -163,9 +163,7 @@
     fresh = correction - combine(proj_two, basis)
     new_all = combine(inverse_factor(gram_two).T, fresh)
 
-    own = lax.dynamic_slice_in_dim(new_all, v * mine, mine, 0)
-    out = lax.dynamic_slice_in_dim(new_all, (1 - v) * mine, mine, 0)
-    new_basis = in_order(own, swap_vec(out), 2)
+    new_basis = lax.all_to_all(new_all, "vec", 0, 2, tiled=True)
     return (new_basis, rayleigh)
 
 

time: 185 us -> 186 us (level)
  blocking collectives: 0 us -> 14.2 us
  waiting for transfers between devices: 86.3 us -> 75.6 us
    all_to_all x0 -> x1, blocking collectives: none -> 14.2 us  [local(): new_basis = lax.all_to_all(new_all, 'vec', 0, 2, tiled=True)]
    ppermute x4 -> x3, waiting for transfers between devices: 23.8 us -> 13.2 us  [swap_vec(): return lax.ppermute(value, 'vec', [(0, 1), (1, 0)])]
    ppermute x4 -> x3, starting transfers between devices: 5.06 us -> 4.2 us  [swap_vec(): return lax.ppermute(value, 'vec', [(0, 1), (1, 0)])]
  transfers between devices with their start and end apart: 42 -> 41, of which waited for: 31 -> 30; matrix products, arithmetic and copies ran while one was open for 3% -> 3% of each run, Pallas kernels for 0% -> 0%
where the time goes in v9:
time: 186 us
  waiting for transfers between devices  75.6 us (41%)
  starting transfers between devices  62.1 us (33%)
  matrix products  15.3 us (8%)
  blocking collectives  14.2 us (8%)
  other arithmetic  11.1 us (6%)
  local copies, waits for them, and re-layouts  6.61 us (4%)
    ppermute x30, starting transfers between devices, allsum(): vals[m] = lax.ppermute(x, AXES, [(i, i ^ mask) for i in range(n)])  43.2 us
    ppermute x30, waiting for transfers between devices, allsum(): vals[m] = lax.ppermute(x, AXES, [(i, i ^ mask) for i in range(n)])  38 us
    all_to_all x1, blocking collectives, local(): new_basis = lax.all_to_all(new_all, 'vec', 0, 2, tiled=True)  14.2 us
    ppermute x3, waiting for transfers between devices, swap_vec(): return lax.ppermute(value, 'vec', [(0, 1), (1, 0)])  13.2 us
    ppermute x1, waiting for transfers between devices, local(): lax.ppermute(give_rows, AXES, cross_down)  8.77 us
    ppermute x2, waiting for transfers between devices, halo(): after = lax.ppermute(value, 'space', down)  7.83 us
    ppermute x2, waiting for transfers between devices, halo(): before = lax.ppermute(value, 'space', up)  7.63 us
    ppermute x1, starting transfers between devices, local(): lax.ppermute(keep_rows, AXES, same_down)  7.02 us
  transfers between devices with their start and end apart: 41, of which 30 were waited for; matrix products, arithmetic and copies ran while one was open for 3% of the time, Pallas kernels for 0%

profile of v9, /device:TPU:0, one launch (start us, length us, event | category | flops | bytes accessed | tf_op | source)
XLA Modules:
  0.0 185.8 jit_solution(501699465305700168)
XLA Ops:
  0.6 1.8 copy.13
  2.7 2.1 %collective-permute-start = (f32[8,1,66,256]{3,0,2,1:T(8,128)S(1)}, f32[8,1,66,256]{3,0,2,1:T(8,128)S(1)}, u32[]{:S(2)}, u32[]{:S(2)}) collective-permute-start(f32[8,1,66,256]{3,0,2,1:T(8,128)S(1)} %get-tuple-element.14), channel_id=1, source_target_pairs={{0,1},{1,0},{2,3},{3,2},{4,5},{5,4},{6,7},{7,6},{8,9},{9,8},{10,11... | collective-permute-start | bytes 1622024 | tf_op jit(solution)/shard_map/ppermute | solution.py:46
  4.8 1.0 constant_dynamic-slice_fusion
  5.8 6.3 %collective-permute-start.4 = (f32[8,1,64,256]{3,0,2,1:T(8,128)}, f32[8,1,64,256]{3,0,2,1:T(8,128)S(1)}, u32[]{:S(2)}, u32[]{:S(2)}) collective-permute-start(f32[8,1,64,256]{3,0,2,1:T(8,128)} %get-tuple-element.11), channel_id=1, source_target_pairs={{3,0},{2,1},{5,2},{4,3},{7,4},{6,5},{9,6},{8,7},{11,8},{10,9},{13,... | collective-permute-start | bytes 1572872 | tf_op jit(solution)/shard_map/ppermute | solution.py:101
  12.1 7.0 %collective-permute-start.3 = (f32[8,1,64,256]{3,0,2,1:T(8,128)}, f32[8,1,64,256]{3,0,2,1:T(8,128)}, u32[]{:S(2)}, u32[]{:S(2)}) collective-permute-start(f32[8,1,64,256]{3,0,2,1:T(8,128)} %get-tuple-element.12), channel_id=1, source_target_pairs={{2,0},{3,1},{4,2},{5,3},{6,4},{7,5},{8,6},{9,7},{10,8},{11,9},{12,... | collective-permute-start | bytes 1572872 | tf_op jit(solution)/shard_map/ppermute | solution.py:101
  19.2 9.9 %collective-permute-done = f32[8,1,66,256]{3,0,2,1:T(8,128)S(1)} collective-permute-done((f32[8,1,66,256]{3,0,2,1:T(8,128)S(1)}, f32[8,1,66,256]{3,0,2,1:T(8,128)S(1)}, u32[]{:S(2)}, u32[]{:S(2)}) %collective-permute-start) | collective-permute-done | bytes 540704 | tf_op jit(solution)/shard_map/ppermute | solution.py:46
  29.9 8.8 %collective-permute-done.4 = f32[8,1,64,256]{3,0,2,1:T(8,128)S(1)} collective-permute-done((f32[8,1,64,256]{3,0,2,1:T(8,128)}, f32[8,1,64,256]{3,0,2,1:T(8,128)S(1)}, u32[]{:S(2)}, u32[]{:S(2)}) %collective-permute-start.4) | collective-permute-done | bytes 524320 | tf_op jit(solution)/shard_map/ppermute | solution.py:101
  38.9 2.3 %broadcast_divide_fusion = (f32[16,1,64,256]{3,0,2,1:T(8,128)S(1)}, f32[16,1,64,256]{3,0,2,1:T(8,128)S(1)}, f32[16,1,64,256]{3,0,2,1:T(8,128)S(1)}) fusion(f32[64,256]{1,0:T(8,128)S(1)} %get-tuple-element.30, f32[16,1,64,1]{3,0,2,1:T(8,128)S(1)} %get-tuple-element.8, f32[16,1,64,255]{3,0,2,1:T(8,128)S(1)} %get-tuple-element.10, ...), kind=kLoop, calls=%fused_computation.83 | loop fusion | flops 4456448 | bytes 10616833 | tf_op jit(solution)/shard_map/div | solution.py:111
  41.2 1.8 fusion.57
  43.0 1.3 collective-permute-start.5
  44.3 2.7 %collective-permute-done.5 = f32[32,64]{0,1:T(8,128)S(1)} collective-permute-done((f32[32,64]{0,1:T(8,128)S(1)}, f32[32,64]{0,1:T(8,128)S(1)}, u32[]{:S(2)}, u32[]{:S(2)}) %collective-permute-start.5) | collective-permute-done | bytes 8224 | tf_op jit(solution)/shard_map/ppermute | solution.py:21
  47.4 1.2 collective-permute-start.7
  48.9 1.8 collective-permute-done.8
  50.7 0.8 collective-permute-done.7
  51.5 6.1 %collective-permute-start.11 = (f32[32,64]{0,1:T(8,128)S(1)}, f32[32,64]{0,1:T(8,128)S(1)}, u32[]{:S(2)}, u32[]{:S(2)}) collective-permute-start(f32[32,64]{0,1:T(8,128)S(1)} %add_add_fusion.2), channel_id=1, source_target_pairs={{0,24},{1,25},{2,26},{3,27},{4,28},{5,29},{6,30},{7,31},{8,16},{9,... | collective-permute-start | bytes 24584 | tf_op jit(solution)/shard_map/ppermute | solution.py:21
  57.5 0.8 collective-permute-start.9
  58.3 1.1 collective-permute-done.11
  59.4 3.5 %collective-permute-done.10 = f32[32,64]{0,1:T(8,128)S(1)} collective-permute-done((f32[32,64]{0,1:T(8,128)S(1)}, f32[32,64]{0,1:T(8,128)S(1)}, u32[]{:S(2)}, u32[]{:S(2)}) %collective-permute-start.10) | collective-permute-done | bytes 8224 | tf_op jit(solution)/shard_map/ppermute | solution.py:21
  63.0 3.1 %collective-permute-start.14 = (f32[32,64]{0,1:T(8,128)S(1)}, f32[32,64]{0,1:T(8,128)S(1)}, u32[]{:S(2)}, u32[]{:S(2)}) collective-permute-start(f32[32,64]{0,1:T(8,128)S(1)} %add_add_fusion.1), channel_id=1, source_target_pairs={{0,96},{1,97},{2,98},{3,99},{4,100},{5,101},{6,102},{7,103},{8,104... | collective-permute-start | bytes 24584 | tf_op jit(solution)/shard_map/ppermute | solution.py:21
  67.1 1.0 collective-permute-done.14
  68.2 3.3 %collective-permute-done.13 = f32[32,64]{0,1:T(8,128)S(1)} collective-permute-done((f32[32,64]{0,1:T(8,128)S(1)}, f32[32,64]{0,1:T(8,128)S(1)}, u32[]{:S(2)}, u32[]{:S(2)}) %collective-permute-start.13) | collective-permute-done | bytes 8224 | tf_op jit(solution)/shard_map/ppermute | solution.py:21
  71.6 1.5 cholesky.44
  73.7 0.6 fusion.75
  74.4 1.2 custom-call.6
  77.7 2.0 %fusion.9 = f32[64,64,256]{2,0,1:T(8,128)S(1)} fusion(f32[16,1,64,256]{3,0,2,1:T(8,128)S(1)} %get-tuple-element.5, f32[16,1,64,256]{3,0,2,1:T(8,128)S(1)} %slice.216, f32[16,16]{1,0:T(8,128)S(1)} %cholesky.45, f32[16,16]{1,0:T(8,128)S(1)} %bitcast.160, f32[16,16]{1,0:T(8,128)S(1)} %fusion.127, f32[16,16]{1,0:T(8,128)S(1)} %get-tuple-element.35, ...), kind=kOutput, calls=%fused_computation.11 | convolution fusion | flops 201865216 | bytes 6296576 | tf_op jit(solution)/shard_map/kj,kzyx->jzyx/dot_general | solution.py:38
  80.0 0.9 collective-permute-start.16
  81.4 1.7 collective-permute-start.17
  84.3 1.1 collective-permute-done.17
  85.4 7.8 %collective-permute-done.16 = f32[16,1,64,256]{3,0,2,1:T(8,128)S(1)} collective-permute-done((f32[16,1,64,256]{3,0,2,1:T(8,128)S(1)}, f32[16,1,64,256]{3,0,2,1:T(8,128)S(1)}, u32[]{:S(2)}, u32[]{:S(2)}) %collective-permute-start.16) | collective-permute-done | bytes 1048608 | tf_op jit(solution)/shard_map/ppermute | solution.py:56
  93.2 7.6 %collective-permute-done.15 = f32[16,1,64,256]{3,0,2,1:T(8,128)S(1)} collective-permute-done((f32[16,1,64,256]{3,0,2,1:T(8,128)S(1)}, f32[16,1,64,256]{3,0,2,1:T(8,128)S(1)}, u32[]{:S(2)}, u32[]{:S(2)}) %collective-permute-start.15) | collective-permute-done | bytes 1048608 | tf_op jit(solution)/shard_map/ppermute | solution.py:55
  100.8 1.6 fusion.13
  102.4 0.9 fusion.29
  103.3 1.5 collective-permute-start.21
  105.3 1.6 collective-permute-done.21
  107.1 1.8 collective-permute-start.22
  109.2 0.9 collective-permute-done.24
  110.1 2.2 %collective-permute-done.23 = f32[32,16]{0,1:T(8,128)S(1)} collective-permute-done((f32[32,16]{0,1:T(8,128)S(1)}, f32[32,16]{0,1:T(8,128)S(1)}, u32[]{:S(2)}, u32[]{:S(2)}) %collective-permute-start.23) | collective-permute-done | bytes 2080 | tf_op jit(solution)/shard_map/ppermute | solution.py:21
  112.4 5.9 %collective-permute-start.27 = (f32[32,16]{0,1:T(8,128)S(1)}, f32[32,16]{0,1:T(8,128)S(1)}, u32[]{:S(2)}, u32[]{:S(2)}) collective-permute-start(f32[32,16]{0,1:T(8,128)S(1)} %add_add_fusion.8), channel_id=1, source_target_pairs={{0,24},{1,25},{2,26},{3,27},{4,28},{5,29},{6,30},{7,31},{8,16},{9,... | collective-permute-start | bytes 6152 | tf_op jit(solution)/shard_map/ppermute | solution.py:21
  118.3 0.9 collective-permute-start.26
  119.5 0.7 collective-permute-done.27
  120.2 5.1 %collective-permute-done.26 = f32[32,16]{0,1:T(8,128)S(1)} collective-permute-done((f32[32,16]{0,1:T(8,128)S(1)}, f32[32,16]{0,1:T(8,128)S(1)}, u32[]{:S(2)}, u32[]{:S(2)}) %collective-permute-start.26) | collective-permute-done | bytes 2080 | tf_op jit(solution)/shard_map/ppermute | solution.py:21
  125.4 1.2 collective-permute-start.29
  126.6 2.9 %collective-permute-start.28 = (f32[32,16]{0,1:T(8,128)S(1)}, f32[32,16]{0,1:T(8,128)S(1)}, u32[]{:S(2)}, u32[]{:S(2)}) collective-permute-start(f32[32,16]{0,1:T(8,128)S(1)} %add_add_fusion.7), channel_id=1, source_target_pairs={{0,32},{1,33},{2,34},{3,35},{4,36},{5,37},{6,38},{7,39},{8,40},{9,... | collective-permute-start | bytes 6152 | tf_op jit(solution)/shard_map/ppermute | solution.py:21
  129.5 0.8 collective-permute-done.30
  131.3 0.7 convolution_bitcast_fusion.2
  132.0 2.1 %collective-permute-done.20 = f32[16,1,2,256]{3,0,2,1:T(8,128)S(1)} collective-permute-done((f32[16,1,2,256]{3,0,2,1:T(8,128)S(1)}, f32[16,1,2,256]{3,0,2,1:T(8,128)S(1)}, u32[]{:S(2)}, u32[]{:S(2)}) %collective-permute-start.20) | collective-permute-done | bytes 32800 | tf_op jit(solution)/shard_map/ppermute | solution.py:46
  134.2 1.6 fusion.18
  135.8 0.8 fusion.25
  136.6 0.8 fusion.26
  137.9 3.3 %collective-permute-done.31 = f32[32,16]{0,1:T(8,128)S(1)} collective-permute-done((f32[32,16]{0,1:T(8,128)S(1)}, f32[32,16]{0,1:T(8,128)S(1)}, u32[]{:S(2)}, u32[]{:S(2)}) %collective-permute-start.31) | collective-permute-done | bytes 2080 | tf_op jit(solution)/shard_map/ppermute | solution.py:21
  141.3 2.6 %collective-permute-start.33 = (f32[32,16]{0,1:T(8,128)S(1)}, f32[32,16]{0,1:T(8,128)S(1)}, u32[]{:S(2)}, u32[]{:S(2)}) collective-permute-start(f32[32,16]{0,1:T(8,128)S(1)} %fusion.158), channel_id=1, source_target_pairs={{0,4},{1,5},{2,6},{3,7},{4,0},{5,1},{6,2},{7,3},{8,12},{9,13},{10,... | collective-permute-start | bytes 6152 | tf_op jit(solution)/shard_map/ppermute | solution.py:21
  144.3 1.2 collective-permute-done.33
  145.5 5.4 %collective-permute-start.37 = (f32[32,16]{0,1:T(8,128)S(1)}, f32[32,16]{0,1:T(8,128)S(1)}, u32[]{:S(2)}, u32[]{:S(2)}) collective-permute-start(f32[32,16]{0,1:T(8,128)S(1)} %add_add_fusion.5), channel_id=1, source_target_pairs={{0,24},{1,25},{2,26},{3,27},{4,28},{5,29},{6,30},{7,31},{8,16},{9,... | collective-permute-start | bytes 6152 | tf_op jit(solution)/shard_map/ppermute | solution.py:21
  150.9 2.1 %collective-permute-start.36 = (f32[32,16]{0,1:T(8,128)S(1)}, f32[32,16]{0,1:T(8,128)S(1)}, u32[]{:S(2)}, u32[]{:S(2)}) collective-permute-start(f32[32,16]{0,1:T(8,128)S(1)} %add_add_fusion.5), channel_id=1, source_target_pairs={{0,16},{1,17},{2,18},{3,19},{4,20},{5,21},{6,22},{7,23},{8,24},{9,... | collective-permute-start | bytes 6152 | tf_op jit(solution)/shard_map/ppermute | solution.py:21
  153.4 2.6 %collective-permute-done.36 = f32[32,16]{0,1:T(8,128)S(1)} collective-permute-done((f32[32,16]{0,1:T(8,128)S(1)}, f32[32,16]{0,1:T(8,128)S(1)}, u32[]{:S(2)}, u32[]{:S(2)}) %collective-permute-start.36) | collective-permute-done | bytes 2080 | tf_op jit(solution)/shard_map/ppermute | solution.py:21
  156.0 2.1 %collective-permute-done.35 = f32[32,16]{0,1:T(8,128)S(1)} collective-permute-done((f32[32,16]{0,1:T(8,128)S(1)}, f32[32,16]{0,1:T(8,128)S(1)}, u32[]{:S(2)}, u32[]{:S(2)}) %collective-permute-start.35) | collective-permute-done | bytes 2080 | tf_op jit(solution)/shard_map/ppermute | solution.py:21
  158.6 1.4 collective-permute-start.39
  160.0 2.2 %collective-permute-start.38 = (f32[32,16]{0,1:T(8,128)S(1)}, f32[32,16]{0,1:T(8,128)S(1)}, u32[]{:S(2)}, u32[]{:S(2)}) collective-permute-start(f32[32,16]{0,1:T(8,128)S(1)} %add_add_fusion.4), channel_id=1, source_target_pairs={{0,32},{1,33},{2,34},{3,35},{4,36},{5,37},{6,38},{7,39},{8,40},{9,... | collective-permute-start | bytes 6152 | tf_op jit(solution)/shard_map/ppermute | solution.py:21
  162.2 0.8 collective-permute-done.40
  163.0 0.8 collective-permute-done.39
  165.1 1.5 cholesky.55
  167.9 1.2 custom-call.7
  170.5 14.2 %all_to_all.18 = f32[16,1,64,256]{3,2,1,0:T(8,128)S(1)} all-to-all(f32[16,1,64,256]{3,2,1,0:T(8,128)S(1)} %copy.21), channel_id=1, replica_groups=mesh['space'=64,'vec'=2] {'vec'}, dimensions={0} | all-to-all | bytes 2097152 | tf_op jit(solution)/shard_map/all_to_all | solution.py:166
  184.7 1.1 copy.22
  (107 shorter events, 16.1 us)
Async XLA Ops:
  2.6 16.6 %copy-start = (f32[1,128,256]{2,1,0:T(8,128)S(1)}, f32[1,128,256]{2,1,0:T(8,128)}, u32[]{:S(2)}) copy-start(f32[1,128,256]{2,1,0:T(8,128)} %param.5) | copy-start | bytes 393220
  2.7 26.5 %collective-permute-start = (f32[8,1,66,256]{3,0,2,1:T(8,128)S(1)}, f32[8,1,66,256]{3,0,2,1:T(8,128)S(1)}, u32[]{:S(2)}, u32[]{:S(2)}) collective-permute-start(f32[8,1,66,256]{3,0,2,1:T(8,128)S(1)} %get-tuple-element.14), channel_id=1, source_target_pairs={{0,1},{1,0},{2,3},{3,2},{4,5},{5,4},{6,7},{7,6},{8,9},{9,8},{10,11... | collective-permute-start | bytes 1622024 | tf_op jit(solution)/shard_map/ppermute | solution.py:46
  5.8 32.8 %collective-permute-start.4 = (f32[8,1,64,256]{3,0,2,1:T(8,128)}, f32[8,1,64,256]{3,0,2,1:T(8,128)S(1)}, u32[]{:S(2)}, u32[]{:S(2)}) collective-permute-start(f32[8,1,64,256]{3,0,2,1:T(8,128)} %get-tuple-element.11), channel_id=1, source_target_pairs={{3,0},{2,1},{5,2},{4,3},{7,4},{6,5},{9,6},{8,7},{11,8},{10,9},{13,... | collective-permute-start | bytes 1572872 | tf_op jit(solution)/shard_map/ppermute | solution.py:101
  12.1 26.7 %collective-permute-start.2 = (f32[8,1,64,256]{3,0,2,1:T(8,128)}, f32[8,1,64,256]{3,0,2,1:T(8,128)S(1)}, u32[]{:S(2)}, u32[]{:S(2)}) collective-permute-start(f32[8,1,64,256]{3,0,2,1:T(8,128)} %get-tuple-element.11), channel_id=1, source_target_pairs={{0,3},{1,2},{2,5},{3,4},{4,7},{5,6},{6,9},{7,8},{8,11},{9,10},{10,... | collective-permute-start | bytes 1572872 | tf_op jit(solution)/shard_map/ppermute | solution.py:100
  12.1 26.7 %collective-permute-start.3 = (f32[8,1,64,256]{3,0,2,1:T(8,128)}, f32[8,1,64,256]{3,0,2,1:T(8,128)}, u32[]{:S(2)}, u32[]{:S(2)}) collective-permute-start(f32[8,1,64,256]{3,0,2,1:T(8,128)} %get-tuple-element.12), channel_id=1, source_target_pairs={{2,0},{3,1},{4,2},{5,3},{6,4},{7,5},{8,6},{9,7},{10,8},{11,9},{12,... | collective-permute-start | bytes 1572872 | tf_op jit(solution)/shard_map/ppermute | solution.py:101
  19.2 19.7 %collective-permute-start.1 = (f32[8,1,64,256]{3,0,2,1:T(8,128)}, f32[8,1,64,256]{3,0,2,1:T(8,128)}, u32[]{:S(2)}, u32[]{:S(2)}) collective-permute-start(f32[8,1,64,256]{3,0,2,1:T(8,128)} %get-tuple-element.12), channel_id=1, source_target_pairs={{0,2},{1,3},{2,4},{3,5},{4,6},{5,7},{6,8},{7,9},{8,10},{9,11},{10,... | collective-permute-start | bytes 1572872 | tf_op jit(solution)/shard_map/ppermute | solution.py:100
  43.0 4.0 %collective-permute-start.5 = (f32[32,64]{0,1:T(8,128)S(1)}, f32[32,64]{0,1:T(8,128)S(1)}, u32[]{:S(2)}, u32[]{:S(2)}) collective-permute-start(f32[32,64]{0,1:T(8,128)S(1)} %fusion.57), channel_id=1, source_target_pairs={{0,1},{1,0},{2,3},{3,2},{4,5},{5,4},{6,7},{7,6},{8,9},{9,8},{10,11... | collective-permute-start | bytes 24584 | tf_op jit(solution)/shard_map/ppermute | solution.py:21
  47.0 3.6 %collective-permute-start.8 = (f32[32,64]{0,1:T(8,128)S(1)}, f32[32,64]{0,1:T(8,128)S(1)}, u32[]{:S(2)}, u32[]{:S(2)}) collective-permute-start(f32[32,64]{0,1:T(8,128)S(1)} %add.191), channel_id=1, source_target_pairs={{0,6},{1,7},{2,4},{3,5},{4,2},{5,3},{6,0},{7,1},{8,14},{9,15},{10,... | collective-permute-start | bytes 24584 | tf_op jit(solution)/shard_map/ppermute | solution.py:21
  47.4 4.0 %collective-permute-start.7 = (f32[32,64]{0,1:T(8,128)S(1)}, f32[32,64]{0,1:T(8,128)S(1)}, u32[]{:S(2)}, u32[]{:S(2)}) collective-permute-start(f32[32,64]{0,1:T(8,128)S(1)} %add.191), channel_id=1, source_target_pairs={{0,4},{1,5},{2,6},{3,7},{4,0},{5,1},{6,2},{7,3},{8,12},{9,13},{10,... | collective-permute-start | bytes 24584 | tf_op jit(solution)/shard_map/ppermute | solution.py:21
  48.6 2.9 %collective-permute-start.6 = (f32[32,64]{0,1:T(8,128)S(1)}, f32[32,64]{0,1:T(8,128)S(1)}, u32[]{:S(2)}, u32[]{:S(2)}) collective-permute-start(f32[32,64]{0,1:T(8,128)S(1)} %add.191), channel_id=1, source_target_pairs={{0,2},{1,3},{2,0},{3,1},{4,6},{5,7},{6,4},{7,5},{8,10},{9,11},{10,... | collective-permute-start | bytes 24584 | tf_op jit(solution)/shard_map/ppermute | solution.py:21
  51.5 8.0 %collective-permute-start.11 = (f32[32,64]{0,1:T(8,128)S(1)}, f32[32,64]{0,1:T(8,128)S(1)}, u32[]{:S(2)}, u32[]{:S(2)}) collective-permute-start(f32[32,64]{0,1:T(8,128)S(1)} %add_add_fusion.2), channel_id=1, source_target_pairs={{0,24},{1,25},{2,26},{3,27},{4,28},{5,29},{6,30},{7,31},{8,16},{9,... | collective-permute-start | bytes 24584 | tf_op jit(solution)/shard_map/ppermute | solution.py:21
  57.5 5.4 %collective-permute-start.10 = (f32[32,64]{0,1:T(8,128)S(1)}, f32[32,64]{0,1:T(8,128)S(1)}, u32[]{:S(2)}, u32[]{:S(2)}) collective-permute-start(f32[32,64]{0,1:T(8,128)S(1)} %add_add_fusion.2), channel_id=1, source_target_pairs={{0,16},{1,17},{2,18},{3,19},{4,20},{5,21},{6,22},{7,23},{8,24},{9,... | collective-permute-start | bytes 24584 | tf_op jit(solution)/shard_map/ppermute | solution.py:21
  57.5 5.4 %collective-permute-start.9 = (f32[32,64]{0,1:T(8,128)S(1)}, f32[32,64]{0,1:T(8,128)S(1)}, u32[]{:S(2)}, u32[]{:S(2)}) collective-permute-start(f32[32,64]{0,1:T(8,128)S(1)} %add_add_fusion.2), channel_id=1, source_target_pairs={{0,8},{1,9},{2,10},{3,11},{4,12},{5,13},{6,14},{7,15},{8,0},{9,1},... | collective-permute-start | bytes 24584 | tf_op jit(solution)/shard_map/ppermute | solution.py:21
  63.0 5.2 %collective-permute-start.14 = (f32[32,64]{0,1:T(8,128)S(1)}, f32[32,64]{0,1:T(8,128)S(1)}, u32[]{:S(2)}, u32[]{:S(2)}) collective-permute-start(f32[32,64]{0,1:T(8,128)S(1)} %add_add_fusion.1), channel_id=1, source_target_pairs={{0,96},{1,97},{2,98},{3,99},{4,100},{5,101},{6,102},{7,103},{8,104... | collective-permute-start | bytes 24584 | tf_op jit(solution)/shard_map/ppermute | solution.py:21
  66.1 5.4 %collective-permute-start.13 = (f32[32,64]{0,1:T(8,128)S(1)}, f32[32,64]{0,1:T(8,128)S(1)}, u32[]{:S(2)}, u32[]{:S(2)}) collective-permute-start(f32[32,64]{0,1:T(8,128)S(1)} %add_add_fusion.1), channel_id=1, source_target_pairs={{0,64},{1,65},{2,66},{3,67},{4,68},{5,69},{6,70},{7,71},{8,72},{9,... | collective-permute-start | bytes 24584 | tf_op jit(solution)/shard_map/ppermute | solution.py:21
  66.7 4.8 %collective-permute-start.12 = (f32[32,64]{0,1:T(8,128)S(1)}, f32[32,64]{0,1:T(8,128)S(1)}, u32[]{:S(2)}, u32[]{:S(2)}) collective-permute-start(f32[32,64]{0,1:T(8,128)S(1)} %add_add_fusion.1), channel_id=1, source_target_pairs={{0,32},{1,33},{2,34},{3,35},{4,36},{5,37},{6,38},{7,39},{8,40},{9,... | collective-permute-start | bytes 24584 | tf_op jit(solution)/shard_map/ppermute | solution.py:21
  76.6 3.2 %copy-start.1 = (f32[16,16]{1,0:T(8,128)}, f32[16,16]{1,0:T(8,128)S(1)}, u32[]{:S(2)}) copy-start(f32[16,16]{1,0:T(8,128)S(1)} %fusion.126) | copy-start | bytes 3076
  80.0 13.2 %collective-permute-start.16 = (f32[16,1,64,256]{3,0,2,1:T(8,128)S(1)}, f32[16,1,64,256]{3,0,2,1:T(8,128)S(1)}, u32[]{:S(2)}, u32[]{:S(2)}) collective-permute-start(f32[16,1,64,256]{3,0,2,1:T(8,128)S(1)} %fusion.52), channel_id=1, source_target_pairs={{2,0},{4,2},{6,4},{8,6},{10,8},{12,10},{14,12},{16,14},{18,16},{20... | collective-permute-start | bytes 3145736 | tf_op jit(solution)/shard_map/ppermute | solution.py:56
  80.9 19.9 %collective-permute-start.15 = (f32[16,1,64,256]{3,0,2,1:T(8,128)S(1)}, f32[16,1,64,256]{3,0,2,1:T(8,128)S(1)}, u32[]{:S(2)}, u32[]{:S(2)}) collective-permute-start(f32[16,1,64,256]{3,0,2,1:T(8,128)S(1)} %fusion.52), channel_id=1, source_target_pairs={{0,2},{2,4},{4,6},{6,8},{8,10},{10,12},{12,14},{14,16},{16,18},{18... | collective-permute-start | bytes 3145736 | tf_op jit(solution)/shard_map/ppermute | solution.py:55
  81.4 4.0 %collective-permute-start.17 = (f32[16,1,2,256]{3,0,2,1:T(8,128)S(1)}, f32[16,1,2,256]{3,0,2,1:T(8,128)S(1)}, u32[]{:S(2)}, u32[]{:S(2)}) collective-permute-start(f32[16,1,2,256]{3,0,2,1:T(8,128)S(1)} %pad_maximum_fusion.5), channel_id=1, source_target_pairs={{0,1},{1,0},{2,3},{3,2},{4,5},{5,4},{6,7},{7,6},{8,9},{9,8},{10,11... | collective-permute-start | bytes 98312 | tf_op jit(solution)/shard_map/ppermute | solution.py:46
  103.3 3.7 %collective-permute-start.21 = (f32[32,16]{0,1:T(8,128)S(1)}, f32[32,16]{0,1:T(8,128)S(1)}, u32[]{:S(2)}, u32[]{:S(2)}) collective-permute-start(f32[32,16]{0,1:T(8,128)S(1)} %fusion.29), channel_id=1, source_target_pairs={{0,1},{1,0},{2,3},{3,2},{4,5},{5,4},{6,7},{7,6},{8,9},{9,8},{10,11... | collective-permute-start | bytes 6152 | tf_op jit(solution)/shard_map/ppermute | solution.py:21
  104.8 29.4 %collective-permute-start.19 = (f32[16,1,64,256]{3,0,2,1:T(8,128)S(1)}, f32[16,1,64,256]{3,0,2,1:T(8,128)S(1)}, u32[]{:S(2)}, u32[]{:S(2)}) collective-permute-start(f32[16,1,64,256]{3,0,2,1:T(8,128)S(1)} %fusion.13), channel_id=1, source_target_pairs={{2,0},{4,2},{6,4},{8,6},{10,8},{12,10},{14,12},{16,14},{18,16},{20... | collective-permute-start | bytes 3145736 | tf_op jit(solution)/shard_map/ppermute | solution.py:56
  105.0 29.2 %collective-permute-start.18 = (f32[16,1,64,256]{3,0,2,1:T(8,128)S(1)}, f32[16,1,64,256]{3,0,2,1:T(8,128)S(1)}, u32[]{:S(2)}, u32[]{:S(2)}) collective-permute-start(f32[16,1,64,256]{3,0,2,1:T(8,128)S(1)} %fusion.13), channel_id=1, source_target_pairs={{0,2},{2,4},{4,6},{6,8},{8,10},{10,12},{12,14},{14,16},{16,18},{18... | collective-permute-start | bytes 3145736 | tf_op jit(solution)/shard_map/ppermute | solution.py:55
  107.0 3.2 %collective-permute-start.24 = (f32[32,16]{0,1:T(8,128)S(1)}, f32[32,16]{0,1:T(8,128)S(1)}, u32[]{:S(2)}, u32[]{:S(2)}) collective-permute-start(f32[32,16]{0,1:T(8,128)S(1)} %add.212), channel_id=1, source_target_pairs={{0,6},{1,7},{2,4},{3,5},{4,2},{5,3},{6,0},{7,1},{8,14},{9,15},{10,... | collective-permute-start | bytes 6152 | tf_op jit(solution)/shard_map/ppermute | solution.py:21
  107.0 5.4 %collective-permute-start.23 = (f32[32,16]{0,1:T(8,128)S(1)}, f32[32,16]{0,1:T(8,128)S(1)}, u32[]{:S(2)}, u32[]{:S(2)}) collective-permute-start(f32[32,16]{0,1:T(8,128)S(1)} %add.212), channel_id=1, source_target_pairs={{0,4},{1,5},{2,6},{3,7},{4,0},{5,1},{6,2},{7,3},{8,12},{9,13},{10,... | collective-permute-start | bytes 6152 | tf_op jit(solution)/shard_map/ppermute | solution.py:21
  107.1 5.3 %collective-permute-start.22 = (f32[32,16]{0,1:T(8,128)S(1)}, f32[32,16]{0,1:T(8,128)S(1)}, u32[]{:S(2)}, u32[]{:S(2)}) collective-permute-start(f32[32,16]{0,1:T(8,128)S(1)} %add.212), channel_id=1, source_target_pairs={{0,2},{1,3},{2,0},{3,1},{4,6},{5,7},{6,4},{7,5},{8,10},{9,11},{10,... | collective-permute-start | bytes 6152 | tf_op jit(solution)/shard_map/ppermute | solution.py:21
  112.4 7.8 %collective-permute-start.27 = (f32[32,16]{0,1:T(8,128)S(1)}, f32[32,16]{0,1:T(8,128)S(1)}, u32[]{:S(2)}, u32[]{:S(2)}) collective-permute-start(f32[32,16]{0,1:T(8,128)S(1)} %add_add_fusion.8), channel_id=1, source_target_pairs={{0,24},{1,25},{2,26},{3,27},{4,28},{5,29},{6,30},{7,31},{8,16},{9,... | collective-permute-start | bytes 6152 | tf_op jit(solution)/shard_map/ppermute | solution.py:21
  118.3 7.0 %collective-permute-start.26 = (f32[32,16]{0,1:T(8,128)S(1)}, f32[32,16]{0,1:T(8,128)S(1)}, u32[]{:S(2)}, u32[]{:S(2)}) collective-permute-start(f32[32,16]{0,1:T(8,128)S(1)} %add_add_fusion.8), channel_id=1, source_target_pairs={{0,16},{1,17},{2,18},{3,19},{4,20},{5,21},{6,22},{7,23},{8,24},{9,... | collective-permute-start | bytes 6152 | tf_op jit(solution)/shard_map/ppermute | solution.py:21
  119.3 6.0 %collective-permute-start.25 = (f32[32,16]{0,1:T(8,128)S(1)}, f32[32,16]{0,1:T(8,128)S(1)}, u32[]{:S(2)}, u32[]{:S(2)}) collective-permute-start(f32[32,16]{0,1:T(8,128)S(1)} %add_add_fusion.8), channel_id=1, source_target_pairs={{0,8},{1,9},{2,10},{3,11},{4,12},{5,13},{6,14},{7,15},{8,0},{9,1},... | collective-permute-start | bytes 6152 | tf_op jit(solution)/shard_map/ppermute | solution.py:21
  125.3 4.9 %collective-permute-start.30 = (f32[32,16]{0,1:T(8,128)S(1)}, f32[32,16]{0,1:T(8,128)S(1)}, u32[]{:S(2)}, u32[]{:S(2)}) collective-permute-start(f32[32,16]{0,1:T(8,128)S(1)} %add_add_fusion.7), channel_id=1, source_target_pairs={{0,96},{1,97},{2,98},{3,99},{4,100},{5,101},{6,102},{7,103},{8,104... | collective-permute-start | bytes 6152 | tf_op jit(solution)/shard_map/ppermute | solution.py:21
  125.4 5.2 %collective-permute-start.29 = (f32[32,16]{0,1:T(8,128)S(1)}, f32[32,16]{0,1:T(8,128)S(1)}, u32[]{:S(2)}, u32[]{:S(2)}) collective-permute-start(f32[32,16]{0,1:T(8,128)S(1)} %add_add_fusion.7), channel_id=1, source_target_pairs={{0,64},{1,65},{2,66},{3,67},{4,68},{5,69},{6,70},{7,71},{8,72},{9,... | collective-permute-start | bytes 6152 | tf_op jit(solution)/shard_map/ppermute | solution.py:21
  126.6 4.6 %collective-permute-start.28 = (f32[32,16]{0,1:T(8,128)S(1)}, f32[32,16]{0,1:T(8,128)S(1)}, u32[]{:S(2)}, u32[]{:S(2)}) collective-permute-start(f32[32,16]{0,1:T(8,128)S(1)} %add_add_fusion.7), channel_id=1, source_target_pairs={{0,32},{1,33},{2,34},{3,35},{4,36},{5,37},{6,38},{7,39},{8,40},{9,... | collective-permute-start | bytes 6152 | tf_op jit(solution)/shard_map/ppermute | solution.py:21
  130.3 3.9 %collective-permute-start.20 = (f32[16,1,2,256]{3,0,2,1:T(8,128)S(1)}, f32[16,1,2,256]{3,0,2,1:T(8,128)S(1)}, u32[]{:S(2)}, u32[]{:S(2)}) collective-permute-start(f32[16,1,2,256]{3,0,2,1:T(8,128)S(1)} %pad_maximum_fusion.6), channel_id=1, source_target_pairs={{0,1},{1,0},{2,3},{3,2},{4,5},{5,4},{6,7},{7,6},{8,9},{9,8},{10,11... | collective-permute-start | bytes 98312 | tf_op jit(solution)/shard_map/ppermute | solution.py:46
  137.5 3.7 %collective-permute-start.31 = (f32[32,16]{0,1:T(8,128)S(1)}, f32[32,16]{0,1:T(8,128)S(1)}, u32[]{:S(2)}, u32[]{:S(2)}) collective-permute-start(f32[32,16]{0,1:T(8,128)S(1)} %pad_maximum_fusion.7), channel_id=1, source_target_pairs={{0,1},{1,0},{2,3},{3,2},{4,5},{5,4},{6,7},{7,6},{8,9},{9,8},{10,11... | collective-permute-start | bytes 6152 | tf_op jit(solution)/shard_map/ppermute | solution.py:21
  141.2 3.1 %collective-permute-start.34 = (f32[32,16]{0,1:T(8,128)S(1)}, f32[32,16]{0,1:T(8,128)S(1)}, u32[]{:S(2)}, u32[]{:S(2)}) collective-permute-start(f32[32,16]{0,1:T(8,128)S(1)} %fusion.158), channel_id=1, source_target_pairs={{0,6},{1,7},{2,4},{3,5},{4,2},{5,3},{6,0},{7,1},{8,14},{9,15},{10,... | collective-permute-start | bytes 6152 | tf_op jit(solution)/shard_map/ppermute | solution.py:21
  141.3 4.2 %collective-permute-start.33 = (f32[32,16]{0,1:T(8,128)S(1)}, f32[32,16]{0,1:T(8,128)S(1)}, u32[]{:S(2)}, u32[]{:S(2)}) collective-permute-start(f32[32,16]{0,1:T(8,128)S(1)} %fusion.158), channel_id=1, source_target_pairs={{0,4},{1,5},{2,6},{3,7},{4,0},{5,1},{6,2},{7,3},{8,12},{9,13},{10,... | collective-permute-start | bytes 6152 | tf_op jit(solution)/shard_map/ppermute | solution.py:21
  143.9 1.6 collective-permute-start.32
  145.5 7.9 %collective-permute-start.37 = (f32[32,16]{0,1:T(8,128)S(1)}, f32[32,16]{0,1:T(8,128)S(1)}, u32[]{:S(2)}, u32[]{:S(2)}) collective-permute-start(f32[32,16]{0,1:T(8,128)S(1)} %add_add_fusion.5), channel_id=1, source_target_pairs={{0,24},{1,25},{2,26},{3,27},{4,28},{5,29},{6,30},{7,31},{8,16},{9,... | collective-permute-start | bytes 6152 | tf_op jit(solution)/shard_map/ppermute | solution.py:21
  150.9 5.2 %collective-permute-start.36 = (f32[32,16]{0,1:T(8,128)S(1)}, f32[32,16]{0,1:T(8,128)S(1)}, u32[]{:S(2)}, u32[]{:S(2)}) collective-permute-start(f32[32,16]{0,1:T(8,128)S(1)} %add_add_fusion.5), channel_id=1, source_target_pairs={{0,16},{1,17},{2,18},{3,19},{4,20},{5,21},{6,22},{7,23},{8,24},{9,... | collective-permute-start | bytes 6152 | tf_op jit(solution)/shard_map/ppermute | solution.py:21
  152.9 5.2 %collective-permute-start.35 = (f32[32,16]{0,1:T(8,128)S(1)}, f32[32,16]{0,1:T(8,128)S(1)}, u32[]{:S(2)}, u32[]{:S(2)}) collective-permute-start(f32[32,16]{0,1:T(8,128)S(1)} %add_add_fusion.5), channel_id=1, source_target_pairs={{0,8},{1,9},{2,10},{3,11},{4,12},{5,13},{6,14},{7,15},{8,0},{9,1},... | collective-permute-start | bytes 6152 | tf_op jit(solution)/shard_map/ppermute | solution.py:21
  158.1 4.9 %collective-permute-start.40 = (f32[32,16]{0,1:T(8,128)S(1)}, f32[32,16]{0,1:T(8,128)S(1)}, u32[]{:S(2)}, u32[]{:S(2)}) collective-permute-start(f32[32,16]{0,1:T(8,128)S(1)} %add_add_fusion.4), channel_id=1, source_target_pairs={{0,96},{1,97},{2,98},{3,99},{4,100},{5,101},{6,102},{7,103},{8,104... | collective-permute-start | bytes 6152 | tf_op jit(solution)/shard_map/ppermute | solution.py:21
  158.6 5.2 %collective-permute-start.39 = (f32[32,16]{0,1:T(8,128)S(1)}, f32[32,16]{0,1:T(8,128)S(1)}, u32[]{:S(2)}, u32[]{:S(2)}) collective-permute-start(f32[32,16]{0,1:T(8,128)S(1)} %add_add_fusion.4), channel_id=1, source_target_pairs={{0,64},{1,65},{2,66},{3,67},{4,68},{5,69},{6,70},{7,71},{8,72},{9,... | collective-permute-start | bytes 6152 | tf_op jit(solution)/shard_map/ppermute | solution.py:21
  160.0 3.9 %collective-permute-start.38 = (f32[32,16]{0,1:T(8,128)S(1)}, f32[32,16]{0,1:T(8,128)S(1)}, u32[]{:S(2)}, u32[]{:S(2)}) collective-permute-start(f32[32,16]{0,1:T(8,128)S(1)} %add_add_fusion.4), channel_id=1, source_target_pairs={{0,32},{1,33},{2,34},{3,35},{4,36},{5,37},{6,38},{7,39},{8,40},{9,... | collective-permute-start | bytes 6152 | tf_op jit(solution)/shard_map/ppermute | solution.py:21
